TPU v7x, 768 devices: a whole 4x8x12 slice. The times are simulated.
768 devices in a mesh: tm: 12 (over z), dp: 64 (over y, x, core).
Axes of the slice: x: 4, y: 8, z: 12, core: 2. Of those that a mesh axis runs over, the one named last changes fastest.
Arguments:
- clip_video: bfloat16 [64, 24, 4, 16, 192], P('dp', 'tm'), may hold values from -6 to 6
- clip_ids: int32 [64, 24], P('dp'), may hold values from 0 to 3, never falling along the last dimension, each value on 1 to 12 neighbouring positions
- norm_gain: float32 [192], replicated, may hold values from 0.25 to 1.75
- conv_weight: bfloat16 [5184, 384], replicated, may hold values from -0.078125 to 0.078125
- out_cotangent: bfloat16 [64, 24, 4, 16, 384], P('dp', 'tm'), may hold values from -16 to 16
Outputs:
- conv_out: bfloat16 [64, 24, 4, 16, 384], P('dp', 'tm')
- grad_video: bfloat16 [64, 24, 4, 16, 192], P('dp', 'tm')
- grad_weight: float32 [5184, 384], P('tm', 'dp')
Inputs may be any that keep to these rules, and one draw needn't show every extreme that they name: `clip_ids`: within each group clip numbers never fall along the frames; each clip lasts 1 to 12 frames and one lasts exactly 12.
All inputs are finite; a program needn't handle non-finite values.
Results may differ from a plain program's by a relative error of at most 0.0049.
Values may be sent and summed in bfloat16 or wider, within the bound.
No kernel may reach another device: no remote copies, remote signals or barrier semaphores. Data moves between devices by JAX's collectives and lax.ppermute only.
A program may use at most 32 MiB of HBM per device.

v0:
```python
import math

import jax
import jax.numpy as jnp
from jax import lax
from jax.sharding import PartitionSpec as P


def from_behind(block, axis, distance):
    devices = range(lax.axis_size(axis))
    route = [(i - distance, i) for i in devices if i - distance in devices]
    return lax.ppermute(block, axis, route)


def activate(video, norm_gain):
    values = video.astype(jnp.float32)
    mean_square = jnp.mean(values * values, axis=-1, keepdims=True)
    normed = values * lax.rsqrt(mean_square + 1e-06) * norm_gain
    return jax.nn.silu(normed)


def make_mask(clips, first_frame, count):
    padded_ids = jnp.concatenate([jnp.full((2,), -1, jnp.int32), clips])
    window = lax.dynamic_slice_in_dim(padded_ids, first_frame, count + 2)
    offsets = jnp.arange(count)[:, None] + jnp.arange(3)[None, :]
    current = window[jnp.arange(count) + 2][:, None]
    return (window[offsets] == current).astype(jnp.float32)


def extract(extended, tap_mask):
    frames = tap_mask.shape[0]
    height, width = (extended.shape[1], extended.shape[2])
    padded = jnp.pad(extended, ((0, 0), (1, 1), (1, 1), (0, 0)))
    taps = []
    for tap_t in range(3):
        weight_t = tap_mask[:, tap_t][:, None, None, None].astype(extended.dtype)
        for tap_h in range(3):
            for tap_w in range(3):
                taps.append(
                    padded[tap_t : tap_t + frames, tap_h : tap_h + height, tap_w : tap_w + width]
                    * weight_t
                )
    stacked = jnp.stack(taps, axis=3)
    return stacked.reshape(frames * height * width, -1)


def shards(clip_video, clip_ids, norm_gain, conv_weight, out_cotangent):
    video = clip_video[0]
    frames, height, width, channels = video.shape
    outputs = conv_weight.shape[1]
    activated = activate(video, norm_gain).astype(jnp.bfloat16)
    previous = from_behind(activated, "tm", 1)
    extended = jnp.concatenate([previous, activated])
    first_frame = lax.axis_index("tm") * frames
    tap_mask = make_mask(clip_ids[0], first_frame, frames)
    patches = extract(extended, tap_mask)
    conv_rows = jnp.dot(patches, conv_weight, preferred_element_type=jnp.float32).astype(
        jnp.bfloat16
    )
    cotangent_rows = out_cotangent[0].reshape(-1, outputs)
    patch_grad = jnp.dot(cotangent_rows, conv_weight.T, preferred_element_type=jnp.float32)
    unused, pull_patch = jax.vjp(
        lambda field: extract(field, tap_mask), extended.astype(jnp.float32)
    )
    extended_grad = pull_patch(patch_grad)[0]
    returned = from_behind(extended_grad[:2], "tm", -1)
    own_grad = extended_grad[2:] + returned
    unused, pull_norm = jax.vjp(lambda field: activate(field, norm_gain), video.astype(jnp.float32))
    video_grad = pull_norm(own_grad)[0].astype(jnp.bfloat16)
    chain_len = lax.axis_size("tm")
    scale = 1.0 / math.sqrt(lax.axis_size("dp") * chain_len * frames * height * width)
    kernel_rows = patches.shape[1]
    slab_rows = kernel_rows // chain_len
    slab_start = lax.axis_index("tm") * slab_rows

    def slab_term(block_ext, block_cot, block_mask):
        block_patches = extract(block_ext, block_mask)
        slab_part = lax.dynamic_slice_in_dim(block_patches, slab_start, slab_rows, 1)
        cot_rows = block_cot.reshape(-1, outputs)
        return jnp.dot(slab_part.T, cot_rows, preferred_element_type=jnp.float32)

    start_slab = jnp.zeros((slab_rows, outputs), jnp.float32)

    def add_block(total, block):
        block_ext, block_cot, block_mask = block
        return (total + slab_term(block_ext, block_cot, block_mask), None)

    total = start_slab
    total, unused_out = lax.scan(
        add_block,
        total,
        (
            lax.all_gather(extended[None], "tm", axis=0, tiled=True),
            lax.all_gather(out_cotangent, "tm", axis=0, tiled=True),
            lax.all_gather(tap_mask.astype(jnp.bfloat16)[None], "tm", axis=0, tiled=True),
        ),
    )
    grad_weight = lax.psum_scatter(total * scale, "dp", scatter_dimension=1, tiled=True)
    conv_out = conv_rows.reshape(1, frames, height, width, outputs)
    return (conv_out, video_grad[None], grad_weight)


def solution(mesh):
    in_specs = (
        P("dp", "tm", None, None, None),
        P("dp", None),
        P(),
        P(),
        P("dp", "tm", None, None, None),
    )
    out_specs = (P("dp", "tm", None, None, None), P("dp", "tm", None, None, None), P("tm", "dp"))
    return jax.shard_map(shards, mesh=mesh, in_specs=in_specs, out_specs=out_specs, check_vma=False)
```

profile of v0, /device:TPU:1, one launch (start us, length us, event | category | flops | bytes accessed | tf_op | source)
XLA Modules:
  0.0 711.4 jit_solution(15021511003220087798)
XLA Ops:
  10.5 4.1 fusion.134
  19.4 28.7 %all_gather.10 = bf16[12,2,3]{2,1,0:T(2,128)(2,1)S(1)} all-gather(bf16[1,2,3]{2,1,0:T(2,128)(2,1)S(1)} %fusion.216), channel_id=1, replica_groups=mesh['tm'=12,'dp'=64] {'tm'}, dimensions={0}, use_global_device_ids=true | all-gather | bytes 156 | tf_op jit(solution)/shard_map/all_gather | solution.py:95
  76.4 2.5 copy.94
  78.9 2.9 reshape.209
  81.8 49.5 %all-gather.6.cloned.1.call-done = bf16[48,4,16,192]{3,2,1,0:T(8,128)(2,1)} async-done(((bf16[4,4,16,192]{3,2,1,0:T(8,128)(2,1)}), bf16[48,4,16,192]{3,2,1,0:T(8,128)(2,1)}) %all-gather.6.cloned.1.call-update) | async-done | bytes 1179664 | tf_op jit(solution)/shard_map/all_gather | solution.py:93
  131.3 362.0 %while.13 = (s32[]{:T(128)}, f32[432,384]{1,0:T(8,128)}, bf16[12,4,4,16,192]{4,3,2,1,0:T(8,128)(2,1)}, bf16[12,2,3]{2,1,0:T(2,128)(2,1)S(1)}, s32[]{:T(128)}, /*...) while((s32[]{:T(128)}, f32[432,384]{1,0:T(8,128)}, ...), condition=%wide.region_3.4_spmd.clone, body=%wide.region_2.3_spmd.clone.sunk | while | flops 45453316 | bytes 11585339 | solution.py:89
  153.7 2.5 copy.151
  156.2 2.1 reshape.244
  182.9 2.5 copy.151
  188.4 2.3 convolution_add_fusion.2
  213.1 2.5 copy.151
  218.6 2.3 convolution_add_fusion.2
  243.4 2.5 copy.151
  248.9 2.3 convolution_add_fusion.2
  273.7 2.5 copy.151
  279.1 2.3 convolution_add_fusion.2
  303.9 2.5 copy.151
  309.4 2.3 convolution_add_fusion.2
  334.2 2.5 copy.151
  339.7 2.3 convolution_add_fusion.2
  364.4 2.5 copy.151
  369.9 2.3 convolution_add_fusion.2
  394.7 2.5 copy.151
  400.2 2.3 convolution_add_fusion.2
  425.0 2.5 copy.151
  430.4 2.3 convolution_add_fusion.2
  455.2 2.5 copy.151
  460.7 2.3 convolution_add_fusion.2
  485.5 2.5 copy.151
  491.0 2.3 convolution_add_fusion.2
  495.8 3.6 convolution_convert_fusion
  499.4 204.1 %all-reduce.33.cloned.1.call-done = f32[432,384]{0,1:T(8,128)} async-done(((f32[432,384]{0,1:T(8,128)}), f32[432,384]{0,1:T(8,128)}) %all-reduce.33.cloned.1.call-update) | async-done | bytes 663568
  (465 shorter events, 343.2 us)
Async XLA Ops:
  7.2 3.3 copy-start.4
  7.2 74.6 %all-gather.4.cloned.1.call-start = ((), (), s32[]{:S(2)}) async-start(), calls=%async_computation | async-start | bytes 1277952 | tf_op jit(solution)/shard_map/all_gather | solution.py:94
  7.9 123.4 %all-gather.6.cloned.1.call-start = ((), (), s32[]{:S(2)}) async-start(), calls=%async_computation.1 | async-start | bytes 1703936 | tf_op jit(solution)/shard_map/all_gather | solution.py:93
  15.2 2.0 copy-start.3
  15.2 32.9 %copy-start.5 = (f32[192]{0:T(256)S(1)}, f32[192]{0:T(256)}, u32[]{:S(2)}) copy-start(f32[192]{0:T(256)} %param.9) | copy-start | bytes 2308
  15.8 32.3 %collective-permute-start.1 = (f32[2,4,16,192]{3,2,1,0:T(8,128)S(1)}, f32[2,4,16,192]{3,2,1,0:T(8,128)S(1)}, u32[]{:S(2)}, u32[]{:S(2)}) collective-permute-start(f32[2,4,16,192]{3,2,1,0:T(8,128)S(1)} %slice.363), channel_id=1, source_target_pairs={{64,0},{128,64},{192,128},{256,192},{320,256},{384,320},{448,384},... | collective-permute-start | bytes 294920 | tf_op jit(solution)/shard_map/ppermute | solution.py:12
  48.4 2.6 collective-permute-start
  51.0 11.8 %copy-start = (bf16[4,4,16,192]{3,2,1,0:T(8,128)(2,1)}, bf16[4,4,16,192]{3,2,1,0:T(8,128)(2,1)S(1)}, u32[]{:S(2)}) copy-start(bf16[4,4,16,192]{3,2,1,0:T(8,128)(2,1)S(1)} %pad_maximum_fusion) | copy-start | bytes 294916
  62.9 12.8 %copy-start.1 = (bf16[4,4,16,192]{3,2,1,0:T(8,128)(2,1)S(1)}, bf16[4,4,16,192]{3,2,1,0:T(8,128)(2,1)}, u32[]{:S(2)}) copy-start(bf16[4,4,16,192]{3,2,1,0:T(8,128)(2,1)} %copy-done) | copy-start | bytes 294916
  62.9 640.6 %all-reduce.33.cloned.1.call-start = ((), (), s32[]{:S(2)}) async-start(), calls=%async_computation.2 | async-start | bytes 1572864
  493.3 2.5 copy-start.2
Sparse Core Ops, SparseCore 0:
  10.4 60.7 all-gather.3
  73.6 57.5 all-gather.5
  495.9 207.5 all-reduce.32
where the time goes:
time: 717 us; the launch traced here: 711 us
  other arithmetic  284 us (40%)
  waiting for transfers between devices  255 us (36%)
  local copies, waits for them, and re-layouts  90.9 us (13%)
  matrix products  34.6 us (5%)
  blocking collectives  28.7 us (4%)
  between operations  14.6 us (2%)
    while x312, other arithmetic  247 us
    unnamed x4, waiting for transfers between devices  205 us
    all_gather x1, waiting for transfers between devices, shards(): lax.all_gather(extended[None], 'tm', axis=0, tiled=True)  49.5 us
    another operation x13, local copies, waits for them, and re-layouts, extract(): stacked = jnp.stack(taps, axis=3)  32.4 us
    all_gather x1, blocking collectives, shards(): lax.all_gather(tap_mask.astype(jnp.bfloat16)[None], 'tm', axis=0, tiled=T...  28.7 us
    reshape x13, local copies, waits for them, and re-layouts, extract(): return stacked.reshape(frames * height * width, -1)  27.6 us
    dot_general x12, matrix products, slab_term(): return jnp.dot(slab_part.T, cot_rows, preferred_element_type=jnp.float32)  26.9 us
    unnamed x27, other arithmetic  24.6 us
  transfers between devices with their start and end apart: 5, of which 3 were waited for; matrix products, arithmetic and copies ran while one was open for 6% of the time, Pallas kernels for 0%

commit v1 on v0

--- a/solution.py
+++ b/solution.py
@@ -72,30 +72,32 @@
     kernel_rows = patches.shape[1]
     slab_rows = kernel_rows // chain_len
     slab_start = lax.axis_index("tm") * slab_rows
-
-    def slab_term(block_ext, block_cot, block_mask):
-        block_patches = extract(block_ext, block_mask)
-        slab_part = lax.dynamic_slice_in_dim(block_patches, slab_start, slab_rows, 1)
-        cot_rows = block_cot.reshape(-1, outputs)
-        return jnp.dot(slab_part.T, cot_rows, preferred_element_type=jnp.float32)
-
-    start_slab = jnp.zeros((slab_rows, outputs), jnp.float32)
-
-    def add_block(total, block):
-        block_ext, block_cot, block_mask = block
-        return (total + slab_term(block_ext, block_cot, block_mask), None)
-
-    total = start_slab
-    total, unused_out = lax.scan(
-        add_block,
-        total,
-        (
-            lax.all_gather(extended[None], "tm", axis=0, tiled=True),
-            lax.all_gather(out_cotangent, "tm", axis=0, tiled=True),
-            lax.all_gather(tap_mask.astype(jnp.bfloat16)[None], "tm", axis=0, tiled=True),
-        ),
+    tap_lo = slab_start // channels
+    slab_offset = slab_start - tap_lo * channels
+    group_video = lax.all_gather(activated, "tm", axis=0, tiled=True)
+    group_cot = lax.all_gather(out_cotangent[0], "tm", axis=0, tiled=True)
+    group_frames = group_video.shape[0]
+    group_mask = make_mask(clip_ids[0], 0, group_frames).astype(jnp.bfloat16)
+    group_pad = jnp.pad(group_video, ((2, 0), (1, 1), (1, 1), (0, 0)))
+    tap_count = -(-(slab_rows + channels - 1) // channels)
+    columns = []
+    for step in range(tap_count):
+        tap = jnp.minimum(tap_lo + step, 26)
+        tap_t, tap_h, tap_w = (tap // 9, tap // 3 % 3, tap % 3)
+        window = lax.dynamic_slice(
+            group_pad, (tap_t, tap_h, tap_w, 0), (group_frames, height, width, channels)
+        )
+        weight_t = lax.dynamic_index_in_dim(group_mask, tap_t, 1, keepdims=False)
+        columns.append((window * weight_t[:, None, None, None]).reshape(-1, channels))
+    slab_patches = lax.dynamic_slice_in_dim(jnp.concatenate(columns, axis=1), slab_offset, slab_rows, 1)
+    slab_t = lax.dot_general(
+        group_cot.reshape(-1, outputs),
+        slab_patches,
+        (((0,), (0,)), ((), ())),
+        preferred_element_type=jnp.float32,
     )
-    grad_weight = lax.psum_scatter(total * scale, "dp", scatter_dimension=1, tiled=True)
+    reduced_t = lax.psum_scatter(slab_t, "dp", scatter_dimension=0, tiled=True)
+    grad_weight = reduced_t.T * scale
     conv_out = conv_rows.reshape(1, frames, height, width, outputs)
     return (conv_out, video_grad[None], grad_weight)
 

time: 717 us -> 302 us (0.42)
  other arithmetic: 284 us -> 9.77 us
  local copies, waits for them, and re-layouts: 90.9 us -> 9.84 us
  waiting for transfers between devices: 255 us -> 214 us
  matrix products: 34.6 us -> 14.1 us
    while x312 -> x0, other arithmetic: 247 us -> none
    all_gather x2 -> x1, waiting for transfers between devices: 49.5 us -> 9.69 us  [shards(): group_cot = lax.all_gather(out_cotangent[0], 'tm', axis=0, tiled=True)]
    another operation x13 -> x1, local copies, waits for them, and re-layouts: 32.4 us -> 1.04 us  [extract(): stacked = jnp.stack(taps, axis=3)]
    reshape x13 -> x1, local copies, waits for them, and re-layouts: 27.6 us -> 2 us  [extract(): return stacked.reshape(frames * height * width, -1)]
    unnamed x27 -> x26, other arithmetic: 24.6 us -> 2.07 us
    dot_general x12 -> x1, matrix products: 26.9 us -> 6.31 us  [shards(): lax.dot_general(group_cot.reshape(-1, outputs), slab_patches, (((0,), (0,...]
    squeeze x24 -> x0, local copies, waits for them, and re-layouts: 11.1 us -> none  [shards(): lax.scan(add_block, total, (lax.all_gather(extended[None], 'tm', axis=0,...]
    dynamic_slice x12 -> x1, local copies, waits for them, and re-layouts: 10.9 us -> 0.19 us  [shards(): weight_t = lax.dynamic_index_in_dim(group_mask, tap_t, 1, keepdims=False)]
  transfers between devices with their start and end apart: 5 -> 4, of which waited for: 3 -> 3; matrix products, arithmetic and copies ran while one was open for 6% -> 6% of each run, Pallas kernels for 0% -> 0%
where the time goes in v1:
time: 302 us; the launch traced here: 301 us
  waiting for transfers between devices  214 us (71%)
  blocking collectives  35 us (12%)
  between operations  15.4 us (5%)
  matrix products  14.1 us (5%)
  local copies, waits for them, and re-layouts  9.84 us (3%)
  other arithmetic  9.77 us (3%)
    unnamed x3, waiting for transfers between devices  204 us
    all_gather x1, blocking collectives, shards(): group_video = lax.all_gather(activated, 'tm', axis=0, tiled=True)  35 us
    all_gather x1, waiting for transfers between devices, shards(): group_cot = lax.all_gather(out_cotangent[0], 'tm', axis=0, tiled=True)  9.69 us
    dot_general x1, matrix products, shards(): lax.dot_general(group_cot.reshape(-1, outputs), slab_patches, (((0,), (0,...  6.31 us
  transfers between devices with their start and end apart: 4, of which 3 were waited for; matrix products, arithmetic and copies ran while one was open for 6% of the time, Pallas kernels for 0%

profile of v1, /device:TPU:1, one launch (start us, length us, event | category | flops | bytes accessed | tf_op | source)
XLA Modules:
  0.0 301.2 jit_solution(2106944903656031368)
XLA Ops:
  7.3 0.7 pad_dynamic-slice_fusion.8
  8.1 0.6 gather_fusion
  8.8 0.6 gather_fusion.1
  9.5 0.2 slice_reduce_fusion
  9.7 4.1 %fusion.66 = f32[2,4,16,27,192]{4,2,3,1,0:T(8,128)S(1)} fusion(bf16[27,192,384,1,1]{2,1,0,4,3:T(8,128)(2,1)} %bitcast.373, bf16[1,2,4,16,384]{4,3,2,1,0:T(8,128)(2,1)} %param.9), kind=kOutput, calls=%fused_computation.137 | convolution fusion | flops 509607936 | bytes 6733824 | tf_op jit(solution)/shard_map/dot_general | solution.py:61
  13.9 0.2 fusion.65
  14.1 0.2 fusion.56
  14.3 0.2 fusion.47
  14.6 0.6 pad_add_fusion
  15.2 1.3 collective-permute-start.1
  16.6 0.1 fusion.17
  16.8 0.1 reshape.226
  16.9 1.2 gather_fusion.2
  18.2 0.7 gather_fusion.3
  19.5 1.3 dynamic-slice
  21.4 0.2 dynamic-slice_reduce_fusion
  21.6 0.7 collective-permute-done.1
  22.4 0.2 fusion.29
  22.6 35.0 %all_gather.6 = bf16[24,4,16,192]{3,2,1,0:T(8,128)(2,1)S(1)} all-gather(bf16[2,4,16,192]{3,2,1,0:T(8,128)(2,1)S(1)} %get-tuple-element.51), channel_id=1, replica_groups=mesh['tm'=12,'dp'=64] {'tm'}, dimensions={0}, use_global_device_ids=true | all-gather | bytes 638976 | tf_op jit(solution)/shard_map/all_gather | solution.py:77
  57.6 1.5 collective-permute-start
  59.1 1.4 fusion.8
  60.5 2.5 fusion.11
  63.1 0.7 fusion.68
  65.6 0.1 fusion.70
  66.0 1.0 copy.63
  67.1 2.0 reshape.199
  69.1 9.7 %all-gather.3.cloned.1.call-done = bf16[1,24,4,16,384]{4,3,2,0,1:T(8,128)(2,1)} async-done(((bf16[1,2,4,16,384]{4,3,2,0,1:T(8,128)(2,1)}), bf16[1,24,4,16,384]{4,3,2,0,1:T(8,128)(2,1)}) %all-gather.3.cloned.1.call-update) | async-done | bytes 1179664 | tf_op jit(solution)/shard_map/all_gather | solution.py:78
  78.8 6.3 %fusion.5 = f32[384,432]{0,1:T(8,128)} fusion(bf16[1536,384]{1,0:T(8,128)(2,1)} %bitcast.380, s32[]{:T(128)S(6)} %select_n.196, bf16[1536,192]{1,0:T(8,128)(2,1)} %bitcast.374, bf16[1536,192]{1,0:T(8,128)(2,1)} %bitcast.376, bf16[1536,192]{1,0:T(8,128)(2,1)} %bitcast.377, bf16[1536,192]{1,0:T(8,128)(2,1)} %bitcast.375), kind=kOutput, calls=%fused_computation.40 | convolution fusion | flops 514916352 | bytes 4202500 | tf_op jit(solution)/shard_map/dot_general | solution.py:93
  85.1 3.6 %convolution_convert_fusion = bf16[128,384]{1,0:T(8,128)(2,1)} fusion(bf16[128,5184]{1,0:T(8,128)(2,1)S(1)} %reshape.199, bf16[5184,384]{1,0:T(8,128)(2,1)} %param.8), kind=kOutput, calls=%fused_computation.41 | convolution fusion | flops 509657088 | bytes 5406720 | tf_op jit(solution)/shard_map/dot_general | solution.py:57
  88.7 203.8 %all-reduce.33.cloned.1.call-done = f32[384,432]{0,1:T(8,128)} async-done(((f32[384,432]{0,1:T(8,128)}), f32[384,432]{0,1:T(8,128)}) %all-reduce.33.cloned.1.call-update) | async-done | bytes 663568
  292.5 1.1 fusion.12
  293.7 0.7 copy.91
  (56 shorter events, 2.7 us)
Async XLA Ops:
  7.2 71.6 %all-gather.3.cloned.1.call-start = ((), (), s32[]{:S(2)}) async-start(), calls=%async_computation | async-start | bytes 1277952 | tf_op jit(solution)/shard_map/all_gather | solution.py:78
  14.5 2.0 copy-start
  14.5 2.1 copy-start.2
  15.2 7.2 %collective-permute-start.1 = (f32[2,4,16,192]{3,2,1,0:T(8,128)S(1)}, f32[2,4,16,192]{3,2,1,0:T(8,128)S(1)}, u32[]{:S(2)}, u32[]{:S(2)}) collective-permute-start(f32[2,4,16,192]{3,2,1,0:T(8,128)S(1)} %slice.142), channel_id=1, source_target_pairs={{64,0},{128,64},{192,128},{256,192},{320,256},{384,320},{448,384},... | collective-permute-start | bytes 294920 | tf_op jit(solution)/shard_map/ppermute | solution.py:12
  16.5 276.0 %all-reduce.33.cloned.1.call-start = ((), (), s32[]{:S(2)}) async-start(), calls=%async_computation.1 | async-start | bytes 1327104
  16.9 5.5 %copy-start.1 = (f32[192]{0:T(256)S(1)}, f32[192]{0:T(256)}, u32[]{:S(2)}) copy-start(f32[192]{0:T(256)} %param.7) | copy-start | bytes 2308
  57.6 6.2 %collective-permute-start = (bf16[2,4,16,192]{3,2,1,0:T(8,128)(2,1)S(1)}, bf16[2,4,16,192]{3,2,1,0:T(8,128)(2,1)S(1)}, u32[]{:S(2)}, u32[]{:S(2)}) collective-permute-start(bf16[2,4,16,192]{3,2,1,0:T(8,128)(2,1)S(1)} %get-tuple-element.51), channel_id=1, source_target_pairs={{0,64},{64,128},{128,192},{192,256},{256,320},{320,384},{384,448},... | collective-permute-start | bytes 147464 | tf_op jit(solution)/shard_map/ppermute | solution.py:12
Sparse Core Ops, SparseCore 0:
  16.6 62.0 all-gather.2
  85.2 207.2 all-reduce.32

commit v2 on v1

--- a/solution.py
+++ b/solution.py
@@ -74,8 +74,11 @@
     slab_start = lax.axis_index("tm") * slab_rows
     tap_lo = slab_start // channels
     slab_offset = slab_start - tap_lo * channels
-    group_video = lax.all_gather(activated, "tm", axis=0, tiled=True)
-    group_cot = lax.all_gather(out_cotangent[0], "tm", axis=0, tiled=True)
+    group_both = lax.all_gather(
+        jnp.concatenate([activated, out_cotangent[0]], axis=-1), "tm", axis=0, tiled=True
+    )
+    group_video = group_both[..., :channels]
+    group_cot = group_both[..., channels:]
     group_frames = group_video.shape[0]
     group_mask = make_mask(clip_ids[0], 0, group_frames).astype(jnp.bfloat16)
     group_pad = jnp.pad(group_video, ((2, 0), (1, 1), (1, 1), (0, 0)))
@@ -96,7 +99,9 @@
         (((0,), (0,)), ((), ())),
         preferred_element_type=jnp.float32,
     )
-    reduced_t = lax.psum_scatter(slab_t, "dp", scatter_dimension=0, tiled=True)
+    groups = lax.axis_size("dp")
+    pieces = slab_t.reshape(groups, outputs // groups, slab_rows)
+    reduced_t = lax.all_to_all(pieces, "dp", 0, 0, tiled=False).sum(axis=0)
     grad_weight = reduced_t.T * scale
     conv_out = conv_rows.reshape(1, frames, height, width, outputs)
     return (conv_out, video_grad[None], grad_weight)

time: 302 us -> 161 us (0.53)
  waiting for transfers between devices: 214 us -> 65.7 us
  blocking collectives: 35 us -> 0 us
  starting transfers between devices: 2.83 us -> 23.2 us
  other arithmetic: 9.77 us -> 26.1 us
  local copies, waits for them, and re-layouts: 9.84 us -> 20.3 us
  matrix products: 14.1 us -> 10.9 us
    unnamed x3 -> x1, waiting for transfers between devices: 204 us -> 0.02 us
    all_gather x1, waiting for transfers between devices: 9.69 us -> 46.7 us  [shards(): lax.all_gather(jnp.concatenate([activated, out_cotangent[0]], axis=-1), '...]
    all_gather x1 -> x0, blocking collectives: 35 us -> none  [shards(): group_video = lax.all_gather(activated, 'tm', axis=0, tiled=True)]
    all_to_all x0 -> x1, starting transfers between devices: none -> 17 us  [shards(): reduced_t = lax.all_to_all(pieces, 'dp', 0, 0, tiled=False).sum(axis=0)]
    all_to_all x0 -> x1, waiting for transfers between devices: none -> 16.3 us  [shards(): reduced_t = lax.all_to_all(pieces, 'dp', 0, 0, tiled=False).sum(axis=0)]
    unnamed x26, other arithmetic: 2.07 us -> 18.1 us
    reshape x0 -> x5, local copies, waits for them, and re-layouts: none -> 4.98 us  [the longest x4 4.33 us: shards(): (window * weight_t[:, None, None, None]).reshape(-1, channels)]
    ppermute x2, starting transfers between devices: 2.75 us -> 6.14 us  [from_behind(): return lax.ppermute(block, axis, route)]
  transfers between devices with their start and end apart: 4 -> 4, of which waited for: 3 -> 3; matrix products, arithmetic and copies ran while one was open for 6% -> 19% of each run, Pallas kernels for 0% -> 0%
where the time goes in v2:
time: 161 us
  waiting for transfers between devices  65.7 us (41%)
  other arithmetic  26.1 us (16%)
  starting transfers between devices  23.2 us (14%)
  local copies, waits for them, and re-layouts  20.3 us (13%)
  between operations  14.8 us (9%)
  matrix products  10.9 us (7%)
    all_gather x1, waiting for transfers between devices, shards(): lax.all_gather(jnp.concatenate([activated, out_cotangent[0]], axis=-1), '...  46.7 us
    unnamed x26, other arithmetic  18.1 us
    all_to_all x1, starting transfers between devices, shards(): reduced_t = lax.all_to_all(pieces, 'dp', 0, 0, tiled=False).sum(axis=0)  17 us
    all_to_all x1, waiting for transfers between devices, shards(): reduced_t = lax.all_to_all(pieces, 'dp', 0, 0, tiled=False).sum(axis=0)  16.3 us
    ppermute x2, starting transfers between devices, from_behind(): return lax.ppermute(block, axis, route)  6.14 us
    reshape x4, local copies, waits for them, and re-layouts, shards(): (window * weight_t[:, None, None, None]).reshape(-1, channels)  4.33 us
    dot_general x1, matrix products, shards(): jnp.dot(cotangent_rows, conv_weight.T, preferred_element_type=jnp.float32)  4.14 us
    dot_general x1, matrix products, shards(): jnp.dot(patches, conv_weight, preferred_element_type=jnp.float32)  3.63 us
  transfers between devices with their start and end apart: 4, of which 3 were waited for; matrix products, arithmetic and copies ran while one was open for 19% of the time, Pallas kernels for 0%

profile of v2, /device:TPU:1, one launch (start us, length us, event | category | flops | bytes accessed | tf_op | source)
XLA Modules:
  0.0 160.9 jit_solution(14359559237869275483)
XLA Ops:
  7.3 0.7 pad_dynamic-slice_fusion.11
  9.7 4.1 %fusion.64 = f32[2,4,16,27,192]{4,2,3,1,0:T(8,128)S(1)} fusion(bf16[27,192,384,1,1]{2,1,0,4,3:T(8,128)(2,1)} %bitcast.370, bf16[1,2,4,16,384]{4,3,2,1,0:T(8,128)(2,1)} %param.9), kind=kOutput, calls=%fused_computation.137 | convolution fusion | flops 509607936 | bytes 6733824 | tf_op jit(solution)/shard_map/dot_general | solution.py:61
  15.2 1.3 collective-permute-start.1
  16.8 1.2 gather_fusion.2
  18.2 0.7 gather_fusion.3
  19.6 2.8 %collective-permute-done.1 = f32[2,4,16,192]{3,2,1,0:T(8,128)S(1)} collective-permute-done((f32[2,4,16,192]{3,2,1,0:T(8,128)S(1)}, f32[2,4,16,192]{3,2,1,0:T(8,128)S(1)}, u32[]{:S(2)}, u32[]{:S(2)}) %collective-permute-start.1) | collective-permute-done | bytes 98336 | tf_op jit(solution)/shard_map/ppermute | solution.py:12
  22.6 4.8 %collective-permute-start = (bf16[2,4,16,192]{3,2,1,0:T(8,128)(2,1)S(1)}, bf16[2,4,16,192]{3,2,1,0:T(8,128)(2,1)S(1)}, u32[]{:S(2)}, u32[]{:S(2)}) collective-permute-start(bf16[2,4,16,192]{3,2,1,0:T(8,128)(2,1)S(1)} %get-tuple-element.42), channel_id=1, source_target_pairs={{0,64},{64,128},{128,192},{192,256},{256,320},{320,384},{384,448},... | collective-permute-start | bytes 147464 | tf_op jit(solution)/shard_map/ppermute | solution.py:12
  27.5 0.8 pad_maximum_fusion
  28.3 0.7 fusion.66
  29.0 0.7 fusion.75
  29.7 0.7 fusion.78
  32.5 0.7 fusion.87
  38.1 0.7 fusion.72
  40.1 0.7 fusion.117
  44.3 46.7 %all-gather.2.cloned.1.call-done = bf16[24,4,16,576]{3,2,1,0:T(8,128)(2,1)} async-done(((bf16[2,4,16,576]{3,2,1,0:T(8,128)(2,1)}), bf16[24,4,16,576]{3,2,1,0:T(8,128)(2,1)}) %all-gather.2.cloned.1.call-update) | async-done | bytes 1769488 | tf_op jit(solution)/shard_map/all_gather | solution.py:77
  91.0 1.2 slice.152
  92.2 1.6 fusion.10
  93.8 1.1 copy.100
  94.8 1.1 copy.101
  95.9 1.1 copy.102
  97.5 1.1 copy.99
  98.6 2.0 %slice.151 = bf16[24,4,16,384]{3,2,1,0:T(8,128)(2,1)S(1)} slice(bf16[24,4,16,576]{3,2,1,0:T(8,128)(2,1)} %all-gather.2.cloned.1.call-done), slice={[0:24], [0:4], [0:16], [192:576]} | slice | bytes 2359296 | tf_op jit(solution)/shard_map/slice | solution.py:81
  101.2 1.4 dot_general.22
  102.6 3.1 %fusion.4 = f32[64,6,432]{2,0,1:T(8,128)S(1)} fusion(s32[]{:T(128)S(6)} %select_n.196, bf16[1536,192]{0,1:T(8,128)(2,1)} %copy.99, bf16[1536,192]{0,1:T(8,128)(2,1)S(1)} %copy-done.2, bf16[1536,192]{0,1:T(8,128)(2,1)} %copy.101, bf16[1536,192]{0,1:T(8,128)(2,1)} %copy.102, bf16[64,6,1536]{2,1,0:T(8,128)(2,1)} %dot_general.22), kind=kOutput, calls=%fused_computation.40 | convolution fusion | flops 514916352 | bytes 4202500 | tf_op jit(solution)/shard_map/dot_general | solution.py:96
  105.7 1.5 copy.104
  107.2 17.0 %all-to-all-start = ((f32[64,6,432]{2,1,0:T(8,128)}), f32[64,6,432]{2,1,0:T(8,128)}, u32[]{:S(2)}, u32[]{:S(2)}) async-start(f32[64,6,432]{2,1,0:T(8,128)} %copy.104), calls=%async_computation | async-start | bytes 2097152 | tf_op jit(solution)/shard_map/all_to_all | solution.py:104
  124.2 0.7 fusion.68
  127.7 2.5 %copy.71 = bf16[2,4,16,27,192]{4,3,2,1,0:T(8,128)(2,1)S(1)} copy(bf16[2,4,16,27,192]{4,2,1,0,3:T(8,128)(2,1)} %fusion.144) | data formatting | bytes 2654208 | tf_op jit(solution)/shard_map/stack | solution.py:43
  130.2 2.0 %reshape.201 = bf16[128,5184]{1,0:T(8,128)(2,1)S(1)} reshape(bf16[2,4,16,27,192]{4,3,2,1,0:T(8,128)(2,1)S(1)} %copy.71) | data formatting | bytes 2654208 | tf_op jit(solution)/shard_map/reshape | solution.py:44
  132.2 3.6 %convolution_convert_fusion = bf16[128,384]{1,0:T(8,128)(2,1)} fusion(bf16[128,5184]{1,0:T(8,128)(2,1)S(1)} %reshape.201, bf16[5184,384]{1,0:T(8,128)(2,1)} %param.8), kind=kOutput, calls=%fused_computation.42 | convolution fusion | flops 509657088 | bytes 5406720 | tf_op jit(solution)/shard_map/dot_general | solution.py:57
  135.9 16.3 %all-to-all-done = f32[64,6,432]{2,1,0:T(8,128)} async-done(((f32[64,6,432]{2,1,0:T(8,128)}), f32[64,6,432]{2,1,0:T(8,128)}, u32[]{:S(2)}, u32[]{:S(2)}) %all-to-all-start) | async-done | bytes 663584 | tf_op jit(solution)/shard_map/all_to_all | solution.py:104
  152.1 1.3 reduce_sum.29
  (67 shorter events, 20.3 us)
Async XLA Ops:
  7.2 83.8 %all-gather.2.cloned.1.call-start = ((), (), s32[]{:S(2)}) async-start(), calls=%async_computation.1 | async-start | bytes 2129920 | tf_op jit(solution)/shard_map/all_gather | solution.py:77
  14.5 2.0 %copy-start = (bf16[1,2,4,16,192]{4,3,2,1,0:T(8,128)(2,1)S(1)}, bf16[1,2,4,16,192]{4,3,2,1,0:T(8,128)(2,1)}, u32[]{:S(2)}) copy-start(bf16[1,2,4,16,192]{4,3,2,1,0:T(8,128)(2,1)} %param.5) | copy-start | bytes 147460
  14.5 2.1 %copy-start.4 = (s32[1,24]{1,0:T(1,128)S(1)}, s32[1,24]{1,0:T(1,128)}, u32[]{:S(2)}) copy-start(s32[1,24]{1,0:T(1,128)} %param.6) | copy-start | bytes 292
  15.2 7.2 %collective-permute-start.1 = (f32[2,4,16,192]{3,2,1,0:T(8,128)S(1)}, f32[2,4,16,192]{3,2,1,0:T(8,128)S(1)}, u32[]{:S(2)}, u32[]{:S(2)}) collective-permute-start(f32[2,4,16,192]{3,2,1,0:T(8,128)S(1)} %slice.150), channel_id=1, source_target_pairs={{64,0},{128,64},{192,128},{256,192},{320,256},{384,320},{448,384},... | collective-permute-start | bytes 294920 | tf_op jit(solution)/shard_map/ppermute | solution.py:12
  16.8 5.5 %copy-start.3 = (f32[192]{0:T(256)S(1)}, f32[192]{0:T(256)}, u32[]{:S(2)}) copy-start(f32[192]{0:T(256)} %param.7) | copy-start | bytes 2308
  16.8 10.6 %copy-start.1 = (bf16[1,2,4,16,384]{4,3,2,1,0:T(8,128)(2,1)S(1)}, bf16[1,2,4,16,384]{4,3,2,1,0:T(8,128)(2,1)}, u32[]{:S(2)}) copy-start(bf16[1,2,4,16,384]{4,3,2,1,0:T(8,128)(2,1)} %param.9) | copy-start | bytes 294916
  22.6 6.4 %collective-permute-start = (bf16[2,4,16,192]{3,2,1,0:T(8,128)(2,1)S(1)}, bf16[2,4,16,192]{3,2,1,0:T(8,128)(2,1)S(1)}, u32[]{:S(2)}, u32[]{:S(2)}) collective-permute-start(bf16[2,4,16,192]{3,2,1,0:T(8,128)(2,1)S(1)} %get-tuple-element.42), channel_id=1, source_target_pairs={{0,64},{64,128},{128,192},{192,256},{256,320},{320,384},{384,448},... | collective-permute-start | bytes 147464 | tf_op jit(solution)/shard_map/ppermute | solution.py:12
  101.2 1.4 copy-start.2
  107.2 44.9 %all-to-all-start = ((f32[64,6,432]{2,1,0:T(8,128)}), f32[64,6,432]{2,1,0:T(8,128)}, u32[]{:S(2)}, u32[]{:S(2)}) async-start(f32[64,6,432]{2,1,0:T(8,128)} %copy.104), calls=%async_computation | async-start | bytes 2097152 | tf_op jit(solution)/shard_map/all_to_all | solution.py:104
Sparse Core Ops, SparseCore 0:
  28.4 62.5 all-gather.1

commit v3 on v2

--- a/solution.py
+++ b/solution.py
@@ -75,9 +75,9 @@
     tap_lo = slab_start // channels
     slab_offset = slab_start - tap_lo * channels
     group_both = lax.all_gather(
-        jnp.concatenate([activated, out_cotangent[0]], axis=-1), "tm", axis=0, tiled=True
+        jnp.concatenate([video, out_cotangent[0]], axis=-1), "tm", axis=0, tiled=True
     )
-    group_video = group_both[..., :channels]
+    group_video = activate(group_both[..., :channels], norm_gain).astype(jnp.bfloat16)
     group_cot = group_both[..., channels:]
     group_frames = group_video.shape[0]
     group_mask = make_mask(clip_ids[0], 0, group_frames).astype(jnp.bfloat16)

time: 161 us -> 155 us (0.963)
  waiting for transfers between devices: 65.7 us -> 56.2 us
  other arithmetic: 26.1 us -> 30.1 us
    all_gather x1, waiting for transfers between devices: 46.7 us -> 37.4 us  [shards(): lax.all_gather(jnp.concatenate([video, out_cotangent[0]], axis=-1), 'tm',...]
    convert_element_type x0 -> x1, other arithmetic: none -> 1.66 us  [shards(): activate(group_both[..., :channels], norm_gain).astype(jnp.bfloat16)]
  transfers between devices with their start and end apart: 4 -> 4, of which waited for: 3 -> 4; matrix products, arithmetic and copies ran while one was open for 19% -> 20% of each run, Pallas kernels for 0% -> 0%
where the time goes in v3:
time: 155 us; the launch traced here: 154 us
  waiting for transfers between devices  56.2 us (36%)
  other arithmetic  30.1 us (19%)
  starting transfers between devices  23.5 us (15%)
  local copies, waits for them, and re-layouts  18.8 us (12%)
  between operations  14.7 us (9%)
  matrix products  10.9 us (7%)
    all_gather x1, waiting for transfers between devices, shards(): lax.all_gather(jnp.concatenate([video, out_cotangent[0]], axis=-1), 'tm',...  37.4 us
    unnamed x26, other arithmetic  18.1 us
    all_to_all x1, starting transfers between devices, shards(): reduced_t = lax.all_to_all(pieces, 'dp', 0, 0, tiled=False).sum(axis=0)  17.3 us
    all_to_all x1, waiting for transfers between devices, shards(): reduced_t = lax.all_to_all(pieces, 'dp', 0, 0, tiled=False).sum(axis=0)  16.3 us
    ppermute x2, starting transfers between devices, from_behind(): return lax.ppermute(block, axis, route)  6.14 us
    reshape x4, local copies, waits for them, and re-layouts, shards(): (window * weight_t[:, None, None, None]).reshape(-1, channels)  5.46 us
    dot_general x1, matrix products, shards(): jnp.dot(cotangent_rows, conv_weight.T, preferred_element_type=jnp.float32)  4.14 us
    dot_general x1, matrix products, shards(): jnp.dot(patches, conv_weight, preferred_element_type=jnp.float32)  3.63 us
  transfers between devices with their start and end apart: 4, of which 4 were waited for; matrix products, arithmetic and copies ran while one was open for 20% of the time, Pallas kernels for 0%

profile of v3, /device:TPU:1, one launch (start us, length us, event | category | flops | bytes accessed | tf_op | source)
XLA Modules:
  0.0 154.1 jit_solution(2024976043331382703)
XLA Ops:
  7.3 0.7 pad_dynamic-slice_fusion.11
  9.7 4.1 %fusion.67 = f32[2,4,16,27,192]{4,2,3,1,0:T(8,128)S(1)} fusion(bf16[27,192,384,1,1]{2,1,0,4,3:T(8,128)(2,1)} %bitcast.309, bf16[1,2,4,16,384]{4,3,2,1,0:T(8,128)(2,1)} %param.9), kind=kOutput, calls=%fused_computation.145 | convolution fusion | flops 509607936 | bytes 6733824 | tf_op jit(solution)/shard_map/dot_general | solution.py:61
  15.2 1.3 collective-permute-start.1
  16.5 0.8 pad_maximum_fusion
  17.6 1.2 gather_fusion.2
  19.0 0.7 gather_fusion.3
  20.3 2.0 %collective-permute-done.1 = f32[2,4,16,192]{3,2,1,0:T(8,128)S(1)} collective-permute-done((f32[2,4,16,192]{3,2,1,0:T(8,128)S(1)}, f32[2,4,16,192]{3,2,1,0:T(8,128)S(1)}, u32[]{:S(2)}, u32[]{:S(2)}) %collective-permute-start.1) | collective-permute-done | bytes 98336 | tf_op jit(solution)/shard_map/ppermute | solution.py:12
  22.6 4.8 %collective-permute-start = (bf16[2,4,16,192]{3,2,1,0:T(8,128)(2,1)S(1)}, bf16[2,4,16,192]{3,2,1,0:T(8,128)(2,1)S(1)}, u32[]{:S(2)}, u32[]{:S(2)}) collective-permute-start(bf16[2,4,16,192]{3,2,1,0:T(8,128)(2,1)S(1)} %get-tuple-element.42), channel_id=1, source_target_pairs={{0,64},{64,128},{128,192},{192,256},{256,320},{320,384},{384,448},... | collective-permute-start | bytes 147464 | tf_op jit(solution)/shard_map/ppermute | solution.py:12
  27.5 0.7 fusion.71
  28.8 0.7 fusion.78
  32.3 0.7 fusion.90
  37.8 0.7 fusion.75
  39.9 0.7 fusion.120
  44.1 37.4 %all-gather.2.cloned.1.call-done = bf16[24,4,16,576]{3,2,1,0:T(8,128)(2,1)} async-done(((bf16[2,4,16,576]{3,2,1,0:T(8,128)(2,1)}), bf16[24,4,16,576]{3,2,1,0:T(8,128)(2,1)}) %all-gather.2.cloned.1.call-update) | async-done | bytes 1769488 | tf_op jit(solution)/shard_map/all_gather | solution.py:77
  81.4 1.4 fusion
  82.9 1.7 %fusion.7 = bf16[24,4,16,192]{3,2,1,0:T(8,128)(2,1)S(1)} fusion(f32[192]{0:T(256)S(1)} %copy-done.4, f32[24,4,16]{2,1,0:T(4,128)S(1)} %add_rsqrt_fusion, bf16[24,4,16,576]{3,2,1,0:T(8,128)(2,1)} %all-gather.2.cloned.1.call-done), kind=kLoop, calls=%fused_computation.21 | loop fusion | flops 2359296 | bytes 1186560 | tf_op jit(solution)/shard_map/convert_element_type | solution.py:80
  84.6 1.6 %fusion.18 = (bf16[24,4,16,192]{3,2,1,0:T(8,128)(2,1)S(1)}, bf16[24,4,16,192]{3,2,1,0:T(8,128)(2,1)S(1)}, bf16[24,4,16,192]{3,2,1,0:T(8,128)(2,1)S(1)}) fusion(s32[]{:T(128)S(6)} %select_n.189, s32[]{:T(128)S(6)} %select_n.192, s32[]{:T(128)S(6)} %select_n.194, bf16[24,4,16,192]{3,2,1,0:T(8,128)(2,1)S(1)} %fusion.7, bf16[24]{0:T(256)(128)(2,1)S(1)} %get-tuple-element.3, ...), kind=kLoop, calls=%fused_computation.56 | loop fusion | flops 3538944 | bytes 2359476 | tf_op jit(solution)/shard_map/mul | solution.py:94
  86.2 1.1 copy.100
  87.2 1.1 copy.101
  88.3 1.1 copy.102
  89.4 1.3 fusion.15
  90.8 2.2 %copy.99 = bf16[1536,192]{0,1:T(8,128)(2,1)} copy(bf16[1536,192]{1,0:T(8,128)(2,1)} %bitcast.312) | data formatting | bytes 1179648 | tf_op jit(solution)/shard_map/reshape | solution.py:94
  94.2 1.4 dot_general.22
  95.5 3.1 %fusion.12 = f32[64,6,432]{2,0,1:T(8,128)S(1)} fusion(s32[]{:T(128)S(6)} %select_n.196, bf16[1536,192]{0,1:T(8,128)(2,1)} %copy.99, bf16[1536,192]{0,1:T(8,128)(2,1)S(1)} %copy-done.3, bf16[1536,192]{0,1:T(8,128)(2,1)} %copy.101, bf16[1536,192]{0,1:T(8,128)(2,1)} %copy.102, bf16[64,6,1536]{2,1,0:T(8,128)(2,1)} %dot_general.22), kind=kOutput, calls=%fused_computation.50 | convolution fusion | flops 514916352 | bytes 4202500 | tf_op jit(solution)/shard_map/dot_general | solution.py:96
  98.7 1.5 copy.104
  100.1 17.3 %all-to-all-start = ((f32[64,6,432]{2,1,0:T(8,128)}), f32[64,6,432]{2,1,0:T(8,128)}, u32[]{:S(2)}, u32[]{:S(2)}) async-start(f32[64,6,432]{2,1,0:T(8,128)} %copy.104), calls=%async_computation | async-start | bytes 2097152 | tf_op jit(solution)/shard_map/all_to_all | solution.py:104
  117.5 0.7 fusion.70
  121.0 2.5 %copy.71 = bf16[2,4,16,27,192]{4,3,2,1,0:T(8,128)(2,1)S(1)} copy(bf16[2,4,16,27,192]{4,2,1,0,3:T(8,128)(2,1)} %fusion.147) | data formatting | bytes 2654208 | tf_op jit(solution)/shard_map/stack | solution.py:43
  123.5 2.0 %reshape.207 = bf16[128,5184]{1,0:T(8,128)(2,1)S(1)} reshape(bf16[2,4,16,27,192]{4,3,2,1,0:T(8,128)(2,1)S(1)} %copy.71) | data formatting | bytes 2654208 | tf_op jit(solution)/shard_map/reshape | solution.py:44
  125.5 3.6 %convolution_convert_fusion = bf16[128,384]{1,0:T(8,128)(2,1)} fusion(bf16[128,5184]{1,0:T(8,128)(2,1)S(1)} %reshape.207, bf16[5184,384]{1,0:T(8,128)(2,1)} %param.8), kind=kOutput, calls=%fused_computation.52 | convolution fusion | flops 509657088 | bytes 5406720 | tf_op jit(solution)/shard_map/dot_general | solution.py:57
  129.1 16.3 %all-to-all-done = f32[64,6,432]{2,1,0:T(8,128)} async-done(((f32[64,6,432]{2,1,0:T(8,128)}), f32[64,6,432]{2,1,0:T(8,128)}, u32[]{:S(2)}, u32[]{:S(2)}) %all-to-all-start) | async-done | bytes 663584 | tf_op jit(solution)/shard_map/all_to_all | solution.py:104
  145.4 1.3 reduce_sum.41
  (71 shorter events, 21.6 us)
Async XLA Ops:
  7.2 74.3 %all-gather.2.cloned.1.call-start = ((), (), s32[]{:S(2)}) async-start(), calls=%async_computation.1 | async-start | bytes 2129920 | tf_op jit(solution)/shard_map/all_gather | solution.py:77
  14.5 2.0 %copy-start.1 = (bf16[1,2,4,16,192]{4,3,2,1,0:T(8,128)(2,1)S(1)}, bf16[1,2,4,16,192]{4,3,2,1,0:T(8,128)(2,1)}, u32[]{:S(2)}) copy-start(bf16[1,2,4,16,192]{4,3,2,1,0:T(8,128)(2,1)} %param.5) | copy-start | bytes 147460
  14.5 2.0 %copy-start.2 = (bf16[1,2,4,16,384]{4,3,2,1,0:T(8,128)(2,1)S(1)}, bf16[1,2,4,16,384]{4,3,2,1,0:T(8,128)(2,1)}, u32[]{:S(2)}) copy-start(bf16[1,2,4,16,384]{4,3,2,1,0:T(8,128)(2,1)} %param.9) | copy-start | bytes 294916
  14.6 2.9 %copy-start.5 = (s32[1,24]{1,0:T(1,128)S(1)}, s32[1,24]{1,0:T(1,128)}, u32[]{:S(2)}) copy-start(s32[1,24]{1,0:T(1,128)} %param.6) | copy-start | bytes 292
  15.2 7.2 %collective-permute-start.1 = (f32[2,4,16,192]{3,2,1,0:T(8,128)S(1)}, f32[2,4,16,192]{3,2,1,0:T(8,128)S(1)}, u32[]{:S(2)}, u32[]{:S(2)}) collective-permute-start(f32[2,4,16,192]{3,2,1,0:T(8,128)S(1)} %slice.150), channel_id=1, source_target_pairs={{64,0},{128,64},{192,128},{256,192},{320,256},{384,320},{448,384},... | collective-permute-start | bytes 294920 | tf_op jit(solution)/shard_map/ppermute | solution.py:12
  17.6 4.7 %copy-start.4 = (f32[192]{0:T(256)S(1)}, f32[192]{0:T(256)}, u32[]{:S(2)}) copy-start(f32[192]{0:T(256)} %param.7) | copy-start | bytes 2308
  22.6 6.2 %collective-permute-start = (bf16[2,4,16,192]{3,2,1,0:T(8,128)(2,1)S(1)}, bf16[2,4,16,192]{3,2,1,0:T(8,128)(2,1)S(1)}, u32[]{:S(2)}, u32[]{:S(2)}) collective-permute-start(bf16[2,4,16,192]{3,2,1,0:T(8,128)(2,1)S(1)} %get-tuple-element.42), channel_id=1, source_target_pairs={{0,64},{64,128},{128,192},{192,256},{256,320},{320,384},{384,448},... | collective-permute-start | bytes 147464 | tf_op jit(solution)/shard_map/ppermute | solution.py:12
  89.4 3.6 %copy-start = (bf16[24,4,16,576]{3,2,1,0:T(8,128)(2,1)S(1)}, bf16[24,4,16,576]{3,2,1,0:T(8,128)(2,1)}, u32[]{:S(2)}) copy-start(bf16[24,4,16,576]{3,2,1,0:T(8,128)(2,1)} %all-gather.2.cloned.1.call-done) | copy-start | bytes 5308420
  94.1 1.4 copy-start.3
  100.1 45.2 %all-to-all-start = ((f32[64,6,432]{2,1,0:T(8,128)}), f32[64,6,432]{2,1,0:T(8,128)}, u32[]{:S(2)}, u32[]{:S(2)}) async-start(f32[64,6,432]{2,1,0:T(8,128)} %copy.104), calls=%async_computation | async-start | bytes 2097152 | tf_op jit(solution)/shard_map/all_to_all | solution.py:104
Sparse Core Ops, SparseCore 0:
  17.4 63.9 all-gather.1

commit v4 on v3

--- a/solution.py
+++ b/solution.py
@@ -10,6 +10,27 @@
     devices = range(lax.axis_size(axis))
     route = [(i - distance, i) for i in devices if i - distance in devices]
     return lax.ppermute(block, axis, route)
+
+
+def ring_route(axis, step):
+    size = lax.axis_size(axis)
+    return [(i, (i + step) % size) for i in range(size)]
+
+
+def ring_gather(block, axis, first_behind):
+    size = lax.axis_size(axis)
+    from_ahead = []
+    from_behind_list = [first_behind]
+    for unused in range(size // 2 - 1):
+        from_behind_list.append(lax.ppermute(from_behind_list[-1], axis, ring_route(axis, 1)))
+    moving = block
+    for unused in range(size - 1 - size // 2):
+        moving = lax.ppermute(moving, axis, ring_route(axis, -1))
+        from_ahead.append(moving)
+    relative = [block] + from_ahead + from_behind_list[::-1]
+    stacked = jnp.stack(relative, axis=0)
+    ordered = jnp.roll(stacked, lax.axis_index(axis), axis=0)
+    return ordered.reshape((-1,) + block.shape[1:])
 
 
 def activate(video, norm_gain):
@@ -49,7 +70,9 @@
     frames, height, width, channels = video.shape
     outputs = conv_weight.shape[1]
     activated = activate(video, norm_gain).astype(jnp.bfloat16)
-    previous = from_behind(activated, "tm", 1)
+    both = jnp.concatenate([video, out_cotangent[0]], axis=-1)
+    first_behind = lax.ppermute(both, "tm", ring_route("tm", 1))
+    previous = activate(first_behind[..., :channels], norm_gain).astype(jnp.bfloat16)
     extended = jnp.concatenate([previous, activated])
     first_frame = lax.axis_index("tm") * frames
     tap_mask = make_mask(clip_ids[0], first_frame, frames)
@@ -74,9 +97,7 @@
     slab_start = lax.axis_index("tm") * slab_rows
     tap_lo = slab_start // channels
     slab_offset = slab_start - tap_lo * channels
-    group_both = lax.all_gather(
-        jnp.concatenate([video, out_cotangent[0]], axis=-1), "tm", axis=0, tiled=True
-    )
+    group_both = ring_gather(both, "tm", first_behind)
     group_video = activate(group_both[..., :channels], norm_gain).astype(jnp.bfloat16)
     group_cot = group_both[..., channels:]
     group_frames = group_video.shape[0]

time: 155 us -> 162 us (1.045)
  starting transfers between devices: 23.5 us -> 65.7 us
  waiting for transfers between devices: 56.2 us -> 31 us
  between operations: 14.7 us -> 1.68 us
    ppermute x0 -> x11, starting transfers between devices: none -> 45.6 us  [the longest x5 32.4 us: ring_gather(): moving = lax.ppermute(moving, axis, ring_route(axis, -1))]
    all_gather x1 -> x0, waiting for transfers between devices: 37.4 us -> none  [shards(): lax.all_gather(jnp.concatenate([video, out_cotangent[0]], axis=-1), 'tm',...]
    ppermute x0 -> x11, waiting for transfers between devices: none -> 14.4 us  [the longest x5 11.6 us: ring_gather(): lax.ppermute(from_behind_list[-1], axis, ring_route(axis, 1))]
    ppermute x2 -> x1, starting transfers between devices: 6.14 us -> 1.29 us  [from_behind(): return lax.ppermute(block, axis, route)]
    ppermute x2 -> x1, waiting for transfers between devices: 2.58 us -> 0.53 us  [from_behind(): return lax.ppermute(block, axis, route)]
    dot_general x2 -> x3, local copies, waits for them, and re-layouts: 2.82 us -> 3.48 us  [shards(): lax.dot_general(group_cot.reshape(-1, outputs), slab_patches, (((0,), (0,...]
    unnamed x26 -> x28, other arithmetic: 18.1 us -> 18.3 us
  transfers between devices with their start and end apart: 4 -> 13, of which waited for: 4 -> 7; matrix products, arithmetic and copies ran while one was open for 20% -> 25% of each run, Pallas kernels for 0% -> 0%
where the time goes in v4:
time: 162 us; the launch traced here: 161 us
  starting transfers between devices  65.7 us (41%)
  waiting for transfers between devices  31 us (19%)
  other arithmetic  30.8 us (19%)
  local copies, waits for them, and re-layouts  20.4 us (13%)
  matrix products  11.1 us (7%)
  between operations  1.68 us (1%)
    ppermute x5, starting transfers between devices, ring_gather(): moving = lax.ppermute(moving, axis, ring_route(axis, -1))  32.4 us
    all_to_all x1, starting transfers between devices, shards(): reduced_t = lax.all_to_all(pieces, 'dp', 0, 0, tiled=False).sum(axis=0)  18.8 us
    unnamed x28, other arithmetic  18.3 us
    all_to_all x1, waiting for transfers between devices, shards(): reduced_t = lax.all_to_all(pieces, 'dp', 0, 0, tiled=False).sum(axis=0)  16 us
    ppermute x5, waiting for transfers between devices, ring_gather(): lax.ppermute(from_behind_list[-1], axis, ring_route(axis, 1))  11.6 us
    ppermute x5, starting transfers between devices, ring_gather(): lax.ppermute(from_behind_list[-1], axis, ring_route(axis, 1))  11.3 us
    reshape x4, local copies, waits for them, and re-layouts, shards(): (window * weight_t[:, None, None, None]).reshape(-1, channels)  5.75 us
    dot_general x1, matrix products, shards(): jnp.dot(cotangent_rows, conv_weight.T, preferred_element_type=jnp.float32)  4.05 us
  transfers between devices with their start and end apart: 13, of which 7 were waited for; matrix products, arithmetic and copies ran while one was open for 25% of the time, Pallas kernels for 0%

profile of v4, /device:TPU:1, one launch (start us, length us, event | category | flops | bytes accessed | tf_op | source)
XLA Modules:
  0.0 160.8 jit_solution(6802460676699666208)
XLA Ops:
  1.7 15.1 %collective-permute-start.2 = (bf16[2,4,16,576]{3,2,1,0:T(8,128)(2,1)S(1)}, bf16[2,4,16,576]{3,2,1,0:T(8,128)(2,1)S(1)}, u32[]{:S(2)}, u32[]{:S(2)}) collective-permute-start(bf16[2,4,16,576]{3,2,1,0:T(8,128)(2,1)S(1)} %pad_maximum_fusion), channel_id=1, source_target_pairs={{0,704},{64,0},{128,64},{192,128},{256,192},{320,256},{384,320},{4... | collective-permute-start | bytes 442376 | tf_op jit(solution)/shard_map/ppermute | solution.py:28
  16.9 1.9 %collective-permute-start = (bf16[2,4,16,576]{3,2,1,0:T(8,128)(2,1)S(1)}, bf16[2,4,16,576]{3,2,1,0:T(8,128)(2,1)S(1)}, u32[]{:S(2)}, u32[]{:S(2)}) collective-permute-start(bf16[2,4,16,576]{3,2,1,0:T(8,128)(2,1)S(1)} %pad_maximum_fusion), channel_id=1, source_target_pairs={{0,64},{64,128},{128,192},{192,256},{256,320},{320,384},{384,448},... | collective-permute-start | bytes 442376 | tf_op jit(solution)/shard_map/ppermute | solution.py:74
  21.3 4.0 %fusion.75 = f32[2,4,16,27,192]{4,2,3,1,0:T(8,128)S(1)} fusion(bf16[27,192,384,1,1]{2,1,0,4,3:T(8,128)(2,1)} %bitcast.347, bf16[1,2,4,16,384]{4,3,2,1,0:T(8,128)(2,1)S(1)} %copy-done.1), kind=kOutput, calls=%fused_computation.206 | convolution fusion | flops 509607936 | bytes 6733824 | tf_op jit(solution)/shard_map/dot_general | solution.py:84
  26.7 1.3 collective-permute-start.1
  28.3 1.2 gather_fusion.2
  48.5 3.5 %collective-permute-start.7 = (bf16[2,4,16,576]{3,2,1,0:T(8,128)(2,1)S(1)}, bf16[2,4,16,576]{3,2,1,0:T(8,128)(2,1)S(1)}, u32[]{:S(2)}, u32[]{:S(2)}) collective-permute-start(bf16[2,4,16,576]{3,2,1,0:T(8,128)(2,1)S(1)} %collective-permute-done), channel_id=1, source_target_pairs={{0,64},{64,128},{128,192},{192,256},{256,320},{320,384},{384,448},... | collective-permute-start | bytes 442376 | tf_op jit(solution)/shard_map/ppermute | solution.py:25
  52.7 3.0 %collective-permute-start.3 = (bf16[2,4,16,576]{3,2,1,0:T(8,128)(2,1)S(1)}, bf16[2,4,16,576]{3,2,1,0:T(8,128)(2,1)S(1)}, u32[]{:S(2)}, u32[]{:S(2)}) collective-permute-start(bf16[2,4,16,576]{3,2,1,0:T(8,128)(2,1)S(1)} %collective-permute-done.2), channel_id=1, source_target_pairs={{0,704},{64,0},{128,64},{192,128},{256,192},{320,256},{384,320},{4... | collective-permute-start | bytes 442376 | tf_op jit(solution)/shard_map/ppermute | solution.py:28
  56.5 2.3 %collective-permute-done.3 = bf16[2,4,16,576]{3,2,1,0:T(8,128)(2,1)S(1)} collective-permute-done((bf16[2,4,16,576]{3,2,1,0:T(8,128)(2,1)S(1)}, bf16[2,4,16,576]{3,2,1,0:T(8,128)(2,1)S(1)}, u32[]{:S(2)}, u32[]{:S(2)}) %collective-permute-start.3) | collective-permute-done | bytes 147488 | tf_op jit(solution)/shard_map/ppermute | solution.py:28
  58.8 4.2 %collective-permute-start.4 = (bf16[2,4,16,576]{3,2,1,0:T(8,128)(2,1)S(1)}, bf16[2,4,16,576]{3,2,1,0:T(8,128)(2,1)S(1)}, u32[]{:S(2)}, u32[]{:S(2)}) collective-permute-start(bf16[2,4,16,576]{3,2,1,0:T(8,128)(2,1)S(1)} %collective-permute-done.3), channel_id=1, source_target_pairs={{0,704},{64,0},{128,64},{192,128},{256,192},{320,256},{384,320},{4... | collective-permute-start | bytes 442376 | tf_op jit(solution)/shard_map/ppermute | solution.py:28
  63.0 1.9 %collective-permute-start.8 = (bf16[2,4,16,576]{3,2,1,0:T(8,128)(2,1)S(1)}, bf16[2,4,16,576]{3,2,1,0:T(8,128)(2,1)S(1)}, u32[]{:S(2)}, u32[]{:S(2)}) collective-permute-start(bf16[2,4,16,576]{3,2,1,0:T(8,128)(2,1)S(1)} %collective-permute-done.7), channel_id=1, source_target_pairs={{0,64},{64,128},{128,192},{192,256},{256,320},{320,384},{384,448},... | collective-permute-start | bytes 442376 | tf_op jit(solution)/shard_map/ppermute | solution.py:25
  65.3 5.0 %collective-permute-start.5 = (bf16[2,4,16,576]{3,2,1,0:T(8,128)(2,1)S(1)}, bf16[2,4,16,576]{3,2,1,0:T(8,128)(2,1)S(1)}, u32[]{:S(2)}, u32[]{:S(2)}) collective-permute-start(bf16[2,4,16,576]{3,2,1,0:T(8,128)(2,1)S(1)} %collective-permute-done.4), channel_id=1, source_target_pairs={{0,704},{64,0},{128,64},{192,128},{256,192},{320,256},{384,320},{4... | collective-permute-start | bytes 442376 | tf_op jit(solution)/shard_map/ppermute | solution.py:28
  70.3 1.9 %collective-permute-start.9 = (bf16[2,4,16,576]{3,2,1,0:T(8,128)(2,1)S(1)}, bf16[2,4,16,576]{3,2,1,0:T(8,128)(2,1)S(1)}, u32[]{:S(2)}, u32[]{:S(2)}) collective-permute-start(bf16[2,4,16,576]{3,2,1,0:T(8,128)(2,1)S(1)} %collective-permute-done.8), channel_id=1, source_target_pairs={{0,64},{64,128},{128,192},{192,256},{256,320},{320,384},{384,448},... | collective-permute-start | bytes 442376 | tf_op jit(solution)/shard_map/ppermute | solution.py:25
  72.5 5.0 %collective-permute-start.6 = (bf16[2,4,16,576]{3,2,1,0:T(8,128)(2,1)S(1)}, bf16[2,4,16,576]{3,2,1,0:T(8,128)(2,1)S(1)}, u32[]{:S(2)}, u32[]{:S(2)}) collective-permute-start(bf16[2,4,16,576]{3,2,1,0:T(8,128)(2,1)S(1)} %collective-permute-done.5), channel_id=1, source_target_pairs={{0,704},{64,0},{128,64},{192,128},{256,192},{320,256},{384,320},{4... | collective-permute-start | bytes 442376 | tf_op jit(solution)/shard_map/ppermute | solution.py:28
  77.6 1.9 %collective-permute-start.10 = (bf16[2,4,16,576]{3,2,1,0:T(8,128)(2,1)S(1)}, bf16[2,4,16,576]{3,2,1,0:T(8,128)(2,1)S(1)}, u32[]{:S(2)}, u32[]{:S(2)}) collective-permute-start(bf16[2,4,16,576]{3,2,1,0:T(8,128)(2,1)S(1)} %collective-permute-done.9), channel_id=1, source_target_pairs={{0,64},{64,128},{128,192},{192,256},{256,320},{320,384},{384,448},... | collective-permute-start | bytes 442376 | tf_op jit(solution)/shard_map/ppermute | solution.py:25
  79.5 5.3 %collective-permute-done.10 = bf16[2,4,16,576]{3,2,1,0:T(8,128)(2,1)S(1)} collective-permute-done((bf16[2,4,16,576]{3,2,1,0:T(8,128)(2,1)S(1)}, bf16[2,4,16,576]{3,2,1,0:T(8,128)(2,1)S(1)}, u32[]{:S(2)}, u32[]{:S(2)}) %collective-permute-start.10) | collective-permute-done | bytes 147488 | tf_op jit(solution)/shard_map/ppermute | solution.py:25
  84.8 2.1 %collective-permute-start.11 = (bf16[2,4,16,576]{3,2,1,0:T(8,128)(2,1)S(1)}, bf16[2,4,16,576]{3,2,1,0:T(8,128)(2,1)S(1)}, u32[]{:S(2)}, u32[]{:S(2)}) collective-permute-start(bf16[2,4,16,576]{3,2,1,0:T(8,128)(2,1)S(1)} %collective-permute-done.10), channel_id=1, source_target_pairs={{0,64},{64,128},{128,192},{192,256},{256,320},{320,384},{384,448},... | collective-permute-start | bytes 442376 | tf_op jit(solution)/shard_map/ppermute | solution.py:25
  87.0 6.2 %collective-permute-done.11 = bf16[2,4,16,576]{3,2,1,0:T(8,128)(2,1)S(1)} collective-permute-done((bf16[2,4,16,576]{3,2,1,0:T(8,128)(2,1)S(1)}, bf16[2,4,16,576]{3,2,1,0:T(8,128)(2,1)S(1)}, u32[]{:S(2)}, u32[]{:S(2)}) %collective-permute-start.11) | collective-permute-done | bytes 147488 | tf_op jit(solution)/shard_map/ppermute | solution.py:25
  95.5 2.7 %fusion.18 = (bf16[24,4,16,192]{3,2,1,0:T(8,128)(2,1)S(1)}, bf16[24,4,16,192]{3,2,1,0:T(8,128)(2,1)}, bf16[24,4,16,192]{3,2,1,0:T(8,128)(2,1)}) fusion(s32[]{:T(128)S(6)} %select_n.203, s32[]{:T(128)S(6)} %select_n.206, s32[]{:T(128)S(6)} %select_n.208, bf16[24,4,16,192]{3,2,1,0:T(8,128)(2,1)S(1)} %fusion.7, bf16[24]{0:T(256)(128)(2,1)S(1)} %get-tuple-element.3, ...), kind=kLoop, calls=%fused_computation.56 | loop fusion | flops 3538944 | bytes 2359476 | tf_op jit(solution)/shard_map/mul | solution.py:115
  98.2 1.4 copy.96
  99.6 2.2 %copy.97 = bf16[1536,192]{0,1:T(8,128)(2,1)} copy(bf16[1536,192]{1,0:T(8,128)(2,1)} %bitcast.357) | data formatting | bytes 1179648 | tf_op jit(solution)/shard_map/reshape | solution.py:115
  101.8 1.1 copy.98
  102.8 1.1 fusion.15
  105.7 1.4 dot_general.19
  107.2 3.5 %fusion.12 = f32[64,6,432]{2,0,1:T(8,128)S(1)} fusion(s32[]{:T(128)S(6)} %select_n.210, bf16[1536,192]{0,1:T(8,128)(2,1)} %copy.95, bf16[1536,192]{0,1:T(8,128)(2,1)S(1)} %copy.96, bf16[1536,192]{0,1:T(8,128)(2,1)S(1)} %copy-done.2, bf16[1536,192]{0,1:T(8,128)(2,1)S(1)} %copy-done.3, bf16[64,6,1536]{2,1,0:T(8,128)(2,1)} %dot_general.19), kind=kOutput, calls=%fused_computation.50 | convolution fusion | flops 514916352 | bytes 4202500 | tf_op jit(solution)/shard_map/dot_general | solution.py:117
  110.7 1.5 copy.100
  112.1 18.8 %all-to-all-start = ((f32[64,6,432]{2,1,0:T(8,128)}), f32[64,6,432]{2,1,0:T(8,128)}, u32[]{:S(2)}, u32[]{:S(2)}) async-start(f32[64,6,432]{2,1,0:T(8,128)} %copy.100), calls=%async_computation | async-start | bytes 2097152 | tf_op jit(solution)/shard_map/all_to_all | solution.py:125
  133.0 2.5 %copy.67 = bf16[2,4,16,27,192]{4,3,2,1,0:T(8,128)(2,1)S(1)} copy(bf16[2,4,16,27,192]{4,2,1,0,3:T(8,128)(2,1)} %constant_dynamic-update-slice_fusion) | data formatting | bytes 2654208 | tf_op jit(solution)/shard_map/stack | solution.py:64
  135.5 2.0 %reshape.218 = bf16[128,5184]{1,0:T(8,128)(2,1)S(1)} reshape(bf16[2,4,16,27,192]{4,3,2,1,0:T(8,128)(2,1)S(1)} %copy.67) | data formatting | bytes 2654208 | tf_op jit(solution)/shard_map/reshape | solution.py:65
  137.5 1.6 %fusion.78 = bf16[1,2,4,16,192]{4,3,2,1,0:T(8,128)(2,1)} fusion(f32[2,4,16,192]{3,2,1,0:T(8,128)} %get-tuple-element.11, f32[2,4,16]{2,1,0:T(4,128)S(1)} %multiply_multiply_fusion, f32[2,4,16]{2,1,0:T(4,128)S(1)} %fusion.131, bf16[1,2,4,16,192]{4,3,2,1,0:T(8,128)(2,1)S(1)} %copy-done), kind=kLoop, calls=%fused_computation.209 | loop fusion | flops 147456 | bytes 197632 | tf_op jit(solution)/shard_map/broadcast_in_dim | solution.py:128
  139.2 3.6 %convolution_convert_fusion = bf16[128,384]{1,0:T(8,128)(2,1)} fusion(bf16[128,5184]{1,0:T(8,128)(2,1)S(1)} %reshape.218, bf16[5184,384]{1,0:T(8,128)(2,1)} %param.8), kind=kOutput, calls=%fused_computation.52 | convolution fusion | flops 509657088 | bytes 5406720 | tf_op jit(solution)/shard_map/dot_general | solution.py:80
  142.8 16.0 %all-to-all-done = f32[64,6,432]{2,1,0:T(8,128)} async-done(((f32[64,6,432]{2,1,0:T(8,128)}), f32[64,6,432]{2,1,0:T(8,128)}, u32[]{:S(2)}, u32[]{:S(2)}) %all-to-all-start) | async-done | bytes 663584 | tf_op jit(solution)/shard_map/all_to_all | solution.py:125
  158.8 1.3 reduce_sum.57
  (115 shorter events, 32.4 us)
Async XLA Ops:
  0.6 20.7 %copy-start.1 = (bf16[1,2,4,16,384]{4,3,2,1,0:T(8,128)(2,1)S(1)}, bf16[1,2,4,16,384]{4,3,2,1,0:T(8,128)(2,1)}, u32[]{:S(2)}) copy-start(bf16[1,2,4,16,384]{4,3,2,1,0:T(8,128)(2,1)} %param.9) | copy-start | bytes 294916
  1.7 51.0 %collective-permute-start.2 = (bf16[2,4,16,576]{3,2,1,0:T(8,128)(2,1)S(1)}, bf16[2,4,16,576]{3,2,1,0:T(8,128)(2,1)S(1)}, u32[]{:S(2)}, u32[]{:S(2)}) collective-permute-start(bf16[2,4,16,576]{3,2,1,0:T(8,128)(2,1)S(1)} %pad_maximum_fusion), channel_id=1, source_target_pairs={{0,704},{64,0},{128,64},{192,128},{256,192},{320,256},{384,320},{4... | collective-permute-start | bytes 442376 | tf_op jit(solution)/shard_map/ppermute | solution.py:28
  16.9 14.9 %collective-permute-start = (bf16[2,4,16,576]{3,2,1,0:T(8,128)(2,1)S(1)}, bf16[2,4,16,576]{3,2,1,0:T(8,128)(2,1)S(1)}, u32[]{:S(2)}, u32[]{:S(2)}) collective-permute-start(bf16[2,4,16,576]{3,2,1,0:T(8,128)(2,1)S(1)} %pad_maximum_fusion), channel_id=1, source_target_pairs={{0,64},{64,128},{128,192},{192,256},{256,320},{320,384},{384,448},... | collective-permute-start | bytes 442376 | tf_op jit(solution)/shard_map/ppermute | solution.py:74
  26.0 2.0 %copy-start = (bf16[1,2,4,16,192]{4,3,2,1,0:T(8,128)(2,1)S(1)}, bf16[1,2,4,16,192]{4,3,2,1,0:T(8,128)(2,1)}, u32[]{:S(2)}) copy-start(bf16[1,2,4,16,192]{4,3,2,1,0:T(8,128)(2,1)} %param.5) | copy-start | bytes 147460
  26.0 2.1 %copy-start.5 = (s32[1,24]{1,0:T(1,128)S(1)}, s32[1,24]{1,0:T(1,128)}, u32[]{:S(2)}) copy-start(s32[1,24]{1,0:T(1,128)} %param.6) | copy-start | bytes 292
  26.7 5.7 %collective-permute-start.1 = (f32[2,4,16,192]{3,2,1,0:T(8,128)S(1)}, f32[2,4,16,192]{3,2,1,0:T(8,128)S(1)}, u32[]{:S(2)}, u32[]{:S(2)}) collective-permute-start(f32[2,4,16,192]{3,2,1,0:T(8,128)S(1)} %slice.155), channel_id=1, source_target_pairs={{64,0},{128,64},{192,128},{256,192},{320,256},{384,320},{448,384},... | collective-permute-start | bytes 294920 | tf_op jit(solution)/shard_map/ppermute | solution.py:12
  28.3 4.1 %copy-start.4 = (f32[192]{0:T(256)S(1)}, f32[192]{0:T(256)}, u32[]{:S(2)}) copy-start(f32[192]{0:T(256)} %param.7) | copy-start | bytes 2308
  48.5 14.5 %collective-permute-start.7 = (bf16[2,4,16,576]{3,2,1,0:T(8,128)(2,1)S(1)}, bf16[2,4,16,576]{3,2,1,0:T(8,128)(2,1)S(1)}, u32[]{:S(2)}, u32[]{:S(2)}) collective-permute-start(bf16[2,4,16,576]{3,2,1,0:T(8,128)(2,1)S(1)} %collective-permute-done), channel_id=1, source_target_pairs={{0,64},{64,128},{128,192},{192,256},{256,320},{320,384},{384,448},... | collective-permute-start | bytes 442376 | tf_op jit(solution)/shard_map/ppermute | solution.py:25
  52.7 6.1 %collective-permute-start.3 = (bf16[2,4,16,576]{3,2,1,0:T(8,128)(2,1)S(1)}, bf16[2,4,16,576]{3,2,1,0:T(8,128)(2,1)S(1)}, u32[]{:S(2)}, u32[]{:S(2)}) collective-permute-start(bf16[2,4,16,576]{3,2,1,0:T(8,128)(2,1)S(1)} %collective-permute-done.2), channel_id=1, source_target_pairs={{0,704},{64,0},{128,64},{192,128},{256,192},{320,256},{384,320},{4... | collective-permute-start | bytes 442376 | tf_op jit(solution)/shard_map/ppermute | solution.py:28
  58.8 6.5 %collective-permute-start.4 = (bf16[2,4,16,576]{3,2,1,0:T(8,128)(2,1)S(1)}, bf16[2,4,16,576]{3,2,1,0:T(8,128)(2,1)S(1)}, u32[]{:S(2)}, u32[]{:S(2)}) collective-permute-start(bf16[2,4,16,576]{3,2,1,0:T(8,128)(2,1)S(1)} %collective-permute-done.3), channel_id=1, source_target_pairs={{0,704},{64,0},{128,64},{192,128},{256,192},{320,256},{384,320},{4... | collective-permute-start | bytes 442376 | tf_op jit(solution)/shard_map/ppermute | solution.py:28
  63.0 7.3 %collective-permute-start.8 = (bf16[2,4,16,576]{3,2,1,0:T(8,128)(2,1)S(1)}, bf16[2,4,16,576]{3,2,1,0:T(8,128)(2,1)S(1)}, u32[]{:S(2)}, u32[]{:S(2)}) collective-permute-start(bf16[2,4,16,576]{3,2,1,0:T(8,128)(2,1)S(1)} %collective-permute-done.7), channel_id=1, source_target_pairs={{0,64},{64,128},{128,192},{192,256},{256,320},{320,384},{384,448},... | collective-permute-start | bytes 442376 | tf_op jit(solution)/shard_map/ppermute | solution.py:25
  65.3 7.3 %collective-permute-start.5 = (bf16[2,4,16,576]{3,2,1,0:T(8,128)(2,1)S(1)}, bf16[2,4,16,576]{3,2,1,0:T(8,128)(2,1)S(1)}, u32[]{:S(2)}, u32[]{:S(2)}) collective-permute-start(bf16[2,4,16,576]{3,2,1,0:T(8,128)(2,1)S(1)} %collective-permute-done.4), channel_id=1, source_target_pairs={{0,704},{64,0},{128,64},{192,128},{256,192},{320,256},{384,320},{4... | collective-permute-start | bytes 442376 | tf_op jit(solution)/shard_map/ppermute | solution.py:28
  70.3 7.3 %collective-permute-start.9 = (bf16[2,4,16,576]{3,2,1,0:T(8,128)(2,1)S(1)}, bf16[2,4,16,576]{3,2,1,0:T(8,128)(2,1)S(1)}, u32[]{:S(2)}, u32[]{:S(2)}) collective-permute-start(bf16[2,4,16,576]{3,2,1,0:T(8,128)(2,1)S(1)} %collective-permute-done.8), channel_id=1, source_target_pairs={{0,64},{64,128},{128,192},{192,256},{256,320},{320,384},{384,448},... | collective-permute-start | bytes 442376 | tf_op jit(solution)/shard_map/ppermute | solution.py:25
  72.5 14.4 %collective-permute-start.6 = (bf16[2,4,16,576]{3,2,1,0:T(8,128)(2,1)S(1)}, bf16[2,4,16,576]{3,2,1,0:T(8,128)(2,1)S(1)}, u32[]{:S(2)}, u32[]{:S(2)}) collective-permute-start(bf16[2,4,16,576]{3,2,1,0:T(8,128)(2,1)S(1)} %collective-permute-done.5), channel_id=1, source_target_pairs={{0,704},{64,0},{128,64},{192,128},{256,192},{320,256},{384,320},{4... | collective-permute-start | bytes 442376 | tf_op jit(solution)/shard_map/ppermute | solution.py:28
  77.6 7.3 %collective-permute-start.10 = (bf16[2,4,16,576]{3,2,1,0:T(8,128)(2,1)S(1)}, bf16[2,4,16,576]{3,2,1,0:T(8,128)(2,1)S(1)}, u32[]{:S(2)}, u32[]{:S(2)}) collective-permute-start(bf16[2,4,16,576]{3,2,1,0:T(8,128)(2,1)S(1)} %collective-permute-done.9), channel_id=1, source_target_pairs={{0,64},{64,128},{128,192},{192,256},{256,320},{320,384},{384,448},... | collective-permute-start | bytes 442376 | tf_op jit(solution)/shard_map/ppermute | solution.py:25
  84.8 8.4 %collective-permute-start.11 = (bf16[2,4,16,576]{3,2,1,0:T(8,128)(2,1)S(1)}, bf16[2,4,16,576]{3,2,1,0:T(8,128)(2,1)S(1)}, u32[]{:S(2)}, u32[]{:S(2)}) collective-permute-start(bf16[2,4,16,576]{3,2,1,0:T(8,128)(2,1)S(1)} %collective-permute-done.10), channel_id=1, source_target_pairs={{0,64},{64,128},{128,192},{192,256},{256,320},{320,384},{384,448},... | collective-permute-start | bytes 442376 | tf_op jit(solution)/shard_map/ppermute | solution.py:25
  105.7 1.4 copy-start.2
  105.7 1.5 copy-start.3
  112.1 46.7 %all-to-all-start = ((f32[64,6,432]{2,1,0:T(8,128)}), f32[64,6,432]{2,1,0:T(8,128)}, u32[]{:S(2)}, u32[]{:S(2)}) async-start(f32[64,6,432]{2,1,0:T(8,128)} %copy.100), calls=%async_computation | async-start | bytes 2097152 | tf_op jit(solution)/shard_map/all_to_all | solution.py:125

commit v5 on v4

--- a/solution.py
+++ b/solution.py
@@ -3,7 +3,9 @@
 import jax
 import jax.numpy as jnp
 from jax import lax
-from jax.sharding import PartitionSpec as P
+from jax.sharding import Mesh, PartitionSpec as P
+
+DATA = ("dq", "dc")
 
 
 def from_behind(block, axis, distance):
@@ -91,7 +93,7 @@
     unused, pull_norm = jax.vjp(lambda field: activate(field, norm_gain), video.astype(jnp.float32))
     video_grad = pull_norm(own_grad)[0].astype(jnp.bfloat16)
     chain_len = lax.axis_size("tm")
-    scale = 1.0 / math.sqrt(lax.axis_size("dp") * chain_len * frames * height * width)
+    scale = 1.0 / math.sqrt(lax.axis_size(DATA) * chain_len * frames * height * width)
     kernel_rows = patches.shape[1]
     slab_rows = kernel_rows // chain_len
     slab_start = lax.axis_index("tm") * slab_rows
@@ -120,21 +122,34 @@
         (((0,), (0,)), ((), ())),
         preferred_element_type=jnp.float32,
     )
-    groups = lax.axis_size("dp")
-    pieces = slab_t.reshape(groups, outputs // groups, slab_rows)
-    reduced_t = lax.all_to_all(pieces, "dp", 0, 0, tiled=False).sum(axis=0)
+    chips = lax.axis_size("dq")
+    cores = lax.axis_size("dc")
+    pieces = slab_t.reshape(chips, cores, outputs // (chips * cores), slab_rows)
+    core = lax.axis_index("dc")
+    kept = lax.dynamic_index_in_dim(pieces, core, 1, keepdims=False)
+    sent = lax.dynamic_index_in_dim(pieces, 1 - core, 1, keepdims=False)
+    pair_sum = kept + lax.ppermute(sent, "dc", [(0, 1), (1, 0)])
+    reduced_t = lax.all_to_all(pair_sum, "dq", 0, 0, tiled=False).sum(axis=0)
     grad_weight = reduced_t.T * scale
     conv_out = conv_rows.reshape(1, frames, height, width, outputs)
     return (conv_out, video_grad[None], grad_weight)
 
 
 def solution(mesh):
+    devices = mesh.devices.reshape(mesh.shape["tm"], -1, 2)
+    split_mesh = Mesh(devices, ("tm", "dq", "dc"))
     in_specs = (
-        P("dp", "tm", None, None, None),
-        P("dp", None),
+        P(DATA, "tm", None, None, None),
+        P(DATA, None),
         P(),
         P(),
-        P("dp", "tm", None, None, None),
+        P(DATA, "tm", None, None, None),
     )
-    out_specs = (P("dp", "tm", None, None, None), P("dp", "tm", None, None, None), P("tm", "dp"))
-    return jax.shard_map(shards, mesh=mesh, in_specs=in_specs, out_specs=out_specs, check_vma=False)
+    out_specs = (
+        P(DATA, "tm", None, None, None),
+        P(DATA, "tm", None, None, None),
+        P("tm", DATA),
+    )
+    return jax.shard_map(
+        shards, mesh=split_mesh, in_specs=in_specs, out_specs=out_specs, check_vma=False
+    )

time: 162 us -> 154 us (0.951)
  waiting for transfers between devices: 31 us -> 21.7 us
    ppermute x0 -> x1, starting transfers between devices: none -> 10.4 us  [shards(): pair_sum = kept + lax.ppermute(sent, 'dc', [(0, 1), (1, 0)])]
    all_to_all x1, waiting for transfers between devices: 16 us -> 6.72 us  [shards(): reduced_t = lax.all_to_all(pair_sum, 'dq', 0, 0, tiled=False).sum(axis=0)]
    all_to_all x1, starting transfers between devices: 18.8 us -> 9.75 us  [shards(): reduced_t = lax.all_to_all(pair_sum, 'dq', 0, 0, tiled=False).sum(axis=0)]
    dot_general x3 -> x2, local copies, waits for them, and re-layouts: 3.48 us -> 2 us  [shards(): lax.dot_general(group_cot.reshape(-1, outputs), slab_patches, (((0,), (0,...]
  transfers between devices with their start and end apart: 13 -> 14, of which waited for: 7 -> 7; matrix products, arithmetic and copies ran while one was open for 25% -> 27% of each run, Pallas kernels for 0% -> 0%
where the time goes in v5:
time: 154 us; the launch traced here: 153 us
  starting transfers between devices  67 us (44%)
  other arithmetic  30.7 us (20%)
  waiting for transfers between devices  21.7 us (14%)
  local copies, waits for them, and re-layouts  20 us (13%)
  matrix products  11.3 us (7%)
  between operations  1.71 us (1%)
    ppermute x5, starting transfers between devices, ring_gather(): moving = lax.ppermute(moving, axis, ring_route(axis, -1))  32.4 us
    unnamed x28, other arithmetic  18.3 us
    ppermute x5, waiting for transfers between devices, ring_gather(): lax.ppermute(from_behind_list[-1], axis, ring_route(axis, 1))  11.6 us
    ppermute x5, starting transfers between devices, ring_gather(): lax.ppermute(from_behind_list[-1], axis, ring_route(axis, 1))  11.3 us
    ppermute x1, starting transfers between devices, shards(): pair_sum = kept + lax.ppermute(sent, 'dc', [(0, 1), (1, 0)])  10.4 us
    all_to_all x1, starting transfers between devices, shards(): reduced_t = lax.all_to_all(pair_sum, 'dq', 0, 0, tiled=False).sum(axis=0)  9.75 us
    all_to_all x1, waiting for transfers between devices, shards(): reduced_t = lax.all_to_all(pair_sum, 'dq', 0, 0, tiled=False).sum(axis=0)  6.72 us
    reshape x4, local copies, waits for them, and re-layouts, shards(): (window * weight_t[:, None, None, None]).reshape(-1, channels)  5.75 us
  transfers between devices with their start and end apart: 14, of which 7 were waited for; matrix products, arithmetic and copies ran while one was open for 27% of the time, Pallas kernels for 0%

profile of v5, /device:TPU:1, one launch (start us, length us, event | category | flops | bytes accessed | tf_op | source)
XLA Modules:
  0.0 152.5 jit_solution(18365243496871221059)
XLA Ops:
  1.7 15.1 %collective-permute-start.2 = (bf16[2,4,16,576]{3,2,1,0:T(8,128)(2,1)S(1)}, bf16[2,4,16,576]{3,2,1,0:T(8,128)(2,1)S(1)}, u32[]{:S(2)}, u32[]{:S(2)}) collective-permute-start(bf16[2,4,16,576]{3,2,1,0:T(8,128)(2,1)S(1)} %pad_maximum_fusion), channel_id=1, source_target_pairs={{0,704},{64,0},{128,64},{192,128},{256,192},{320,256},{384,320},{4... | collective-permute-start | bytes 442376 | tf_op jit(solution)/shard_map/ppermute | solution.py:30
  16.9 1.9 %collective-permute-start = (bf16[2,4,16,576]{3,2,1,0:T(8,128)(2,1)S(1)}, bf16[2,4,16,576]{3,2,1,0:T(8,128)(2,1)S(1)}, u32[]{:S(2)}, u32[]{:S(2)}) collective-permute-start(bf16[2,4,16,576]{3,2,1,0:T(8,128)(2,1)S(1)} %pad_maximum_fusion), channel_id=1, source_target_pairs={{0,64},{64,128},{128,192},{192,256},{256,320},{320,384},{384,448},... | collective-permute-start | bytes 442376 | tf_op jit(solution)/shard_map/ppermute | solution.py:76
  21.3 4.0 %fusion.75 = f32[2,4,16,27,192]{4,2,3,1,0:T(8,128)S(1)} fusion(bf16[27,192,384,1,1]{2,1,0,4,3:T(8,128)(2,1)} %bitcast.353, bf16[1,2,4,16,384]{4,3,2,1,0:T(8,128)(2,1)S(1)} %copy-done.1), kind=kOutput, calls=%fused_computation.208 | convolution fusion | flops 509607936 | bytes 6733824 | tf_op jit(solution)/shard_map/dot_general | solution.py:86
  26.7 1.3 collective-permute-start.1
  28.3 1.2 gather_fusion.2
  49.3 3.5 %collective-permute-start.7 = (bf16[2,4,16,576]{3,2,1,0:T(8,128)(2,1)S(1)}, bf16[2,4,16,576]{3,2,1,0:T(8,128)(2,1)S(1)}, u32[]{:S(2)}, u32[]{:S(2)}) collective-permute-start(bf16[2,4,16,576]{3,2,1,0:T(8,128)(2,1)S(1)} %collective-permute-done), channel_id=1, source_target_pairs={{0,64},{64,128},{128,192},{192,256},{256,320},{320,384},{384,448},... | collective-permute-start | bytes 442376 | tf_op jit(solution)/shard_map/ppermute | solution.py:27
  53.4 3.0 %collective-permute-start.3 = (bf16[2,4,16,576]{3,2,1,0:T(8,128)(2,1)S(1)}, bf16[2,4,16,576]{3,2,1,0:T(8,128)(2,1)S(1)}, u32[]{:S(2)}, u32[]{:S(2)}) collective-permute-start(bf16[2,4,16,576]{3,2,1,0:T(8,128)(2,1)S(1)} %collective-permute-done.2), channel_id=1, source_target_pairs={{0,704},{64,0},{128,64},{192,128},{256,192},{320,256},{384,320},{4... | collective-permute-start | bytes 442376 | tf_op jit(solution)/shard_map/ppermute | solution.py:30
  57.2 2.3 %collective-permute-done.3 = bf16[2,4,16,576]{3,2,1,0:T(8,128)(2,1)S(1)} collective-permute-done((bf16[2,4,16,576]{3,2,1,0:T(8,128)(2,1)S(1)}, bf16[2,4,16,576]{3,2,1,0:T(8,128)(2,1)S(1)}, u32[]{:S(2)}, u32[]{:S(2)}) %collective-permute-start.3) | collective-permute-done | bytes 147488 | tf_op jit(solution)/shard_map/ppermute | solution.py:30
  59.5 4.2 %collective-permute-start.4 = (bf16[2,4,16,576]{3,2,1,0:T(8,128)(2,1)S(1)}, bf16[2,4,16,576]{3,2,1,0:T(8,128)(2,1)S(1)}, u32[]{:S(2)}, u32[]{:S(2)}) collective-permute-start(bf16[2,4,16,576]{3,2,1,0:T(8,128)(2,1)S(1)} %collective-permute-done.3), channel_id=1, source_target_pairs={{0,704},{64,0},{128,64},{192,128},{256,192},{320,256},{384,320},{4... | collective-permute-start | bytes 442376 | tf_op jit(solution)/shard_map/ppermute | solution.py:30
  63.7 1.9 %collective-permute-start.8 = (bf16[2,4,16,576]{3,2,1,0:T(8,128)(2,1)S(1)}, bf16[2,4,16,576]{3,2,1,0:T(8,128)(2,1)S(1)}, u32[]{:S(2)}, u32[]{:S(2)}) collective-permute-start(bf16[2,4,16,576]{3,2,1,0:T(8,128)(2,1)S(1)} %collective-permute-done.7), channel_id=1, source_target_pairs={{0,64},{64,128},{128,192},{192,256},{256,320},{320,384},{384,448},... | collective-permute-start | bytes 442376 | tf_op jit(solution)/shard_map/ppermute | solution.py:27
  66.0 5.0 %collective-permute-start.5 = (bf16[2,4,16,576]{3,2,1,0:T(8,128)(2,1)S(1)}, bf16[2,4,16,576]{3,2,1,0:T(8,128)(2,1)S(1)}, u32[]{:S(2)}, u32[]{:S(2)}) collective-permute-start(bf16[2,4,16,576]{3,2,1,0:T(8,128)(2,1)S(1)} %collective-permute-done.4), channel_id=1, source_target_pairs={{0,704},{64,0},{128,64},{192,128},{256,192},{320,256},{384,320},{4... | collective-permute-start | bytes 442376 | tf_op jit(solution)/shard_map/ppermute | solution.py:30
  71.0 1.9 %collective-permute-start.9 = (bf16[2,4,16,576]{3,2,1,0:T(8,128)(2,1)S(1)}, bf16[2,4,16,576]{3,2,1,0:T(8,128)(2,1)S(1)}, u32[]{:S(2)}, u32[]{:S(2)}) collective-permute-start(bf16[2,4,16,576]{3,2,1,0:T(8,128)(2,1)S(1)} %collective-permute-done.8), channel_id=1, source_target_pairs={{0,64},{64,128},{128,192},{192,256},{256,320},{320,384},{384,448},... | collective-permute-start | bytes 442376 | tf_op jit(solution)/shard_map/ppermute | solution.py:27
  73.2 5.0 %collective-permute-start.6 = (bf16[2,4,16,576]{3,2,1,0:T(8,128)(2,1)S(1)}, bf16[2,4,16,576]{3,2,1,0:T(8,128)(2,1)S(1)}, u32[]{:S(2)}, u32[]{:S(2)}) collective-permute-start(bf16[2,4,16,576]{3,2,1,0:T(8,128)(2,1)S(1)} %collective-permute-done.5), channel_id=1, source_target_pairs={{0,704},{64,0},{128,64},{192,128},{256,192},{320,256},{384,320},{4... | collective-permute-start | bytes 442376 | tf_op jit(solution)/shard_map/ppermute | solution.py:30
  78.3 1.9 %collective-permute-start.10 = (bf16[2,4,16,576]{3,2,1,0:T(8,128)(2,1)S(1)}, bf16[2,4,16,576]{3,2,1,0:T(8,128)(2,1)S(1)}, u32[]{:S(2)}, u32[]{:S(2)}) collective-permute-start(bf16[2,4,16,576]{3,2,1,0:T(8,128)(2,1)S(1)} %collective-permute-done.9), channel_id=1, source_target_pairs={{0,64},{64,128},{128,192},{192,256},{256,320},{320,384},{384,448},... | collective-permute-start | bytes 442376 | tf_op jit(solution)/shard_map/ppermute | solution.py:27
  80.2 5.3 %collective-permute-done.10 = bf16[2,4,16,576]{3,2,1,0:T(8,128)(2,1)S(1)} collective-permute-done((bf16[2,4,16,576]{3,2,1,0:T(8,128)(2,1)S(1)}, bf16[2,4,16,576]{3,2,1,0:T(8,128)(2,1)S(1)}, u32[]{:S(2)}, u32[]{:S(2)}) %collective-permute-start.10) | collective-permute-done | bytes 147488 | tf_op jit(solution)/shard_map/ppermute | solution.py:27
  85.5 2.1 %collective-permute-start.11 = (bf16[2,4,16,576]{3,2,1,0:T(8,128)(2,1)S(1)}, bf16[2,4,16,576]{3,2,1,0:T(8,128)(2,1)S(1)}, u32[]{:S(2)}, u32[]{:S(2)}) collective-permute-start(bf16[2,4,16,576]{3,2,1,0:T(8,128)(2,1)S(1)} %collective-permute-done.10), channel_id=1, source_target_pairs={{0,64},{64,128},{128,192},{192,256},{256,320},{320,384},{384,448},... | collective-permute-start | bytes 442376 | tf_op jit(solution)/shard_map/ppermute | solution.py:27
  87.7 6.2 %collective-permute-done.11 = bf16[2,4,16,576]{3,2,1,0:T(8,128)(2,1)S(1)} collective-permute-done((bf16[2,4,16,576]{3,2,1,0:T(8,128)(2,1)S(1)}, bf16[2,4,16,576]{3,2,1,0:T(8,128)(2,1)S(1)}, u32[]{:S(2)}, u32[]{:S(2)}) %collective-permute-start.11) | collective-permute-done | bytes 147488 | tf_op jit(solution)/shard_map/ppermute | solution.py:27
  96.2 2.7 %fusion.18 = (bf16[24,4,16,192]{3,2,1,0:T(8,128)(2,1)S(1)}, bf16[24,4,16,192]{3,2,1,0:T(8,128)(2,1)}, bf16[24,4,16,192]{3,2,1,0:T(8,128)(2,1)}) fusion(s32[]{:T(128)S(6)} %select_n.210, s32[]{:T(128)S(6)} %select_n.213, s32[]{:T(128)S(6)} %select_n.215, bf16[24,4,16,192]{3,2,1,0:T(8,128)(2,1)S(1)} %fusion.7, bf16[24]{0:T(256)(128)(2,1)S(1)} %get-tuple-element.3, ...), kind=kLoop, calls=%fused_computation.56 | loop fusion | flops 3538944 | bytes 2359476 | tf_op jit(solution)/shard_map/mul | solution.py:117
  98.9 1.4 copy.129
  100.3 2.2 %copy.130 = bf16[1536,192]{0,1:T(8,128)(2,1)} copy(bf16[1536,192]{1,0:T(8,128)(2,1)} %bitcast.363) | data formatting | bytes 1179648 | tf_op jit(solution)/shard_map/reshape | solution.py:117
  102.5 1.1 copy.131
  103.6 1.1 fusion.15
  106.4 1.4 dot_general.19
  107.9 3.7 %fusion.12 = f32[32,2,6,432]{3,0,2,1:T(8,128)S(1)} fusion(s32[]{:T(128)S(6)} %select_n.217, bf16[1536,192]{0,1:T(8,128)(2,1)} %copy.128, bf16[1536,192]{0,1:T(8,128)(2,1)S(1)} %copy.129, bf16[1536,192]{0,1:T(8,128)(2,1)S(1)} %copy-done.2, bf16[1536,192]{0,1:T(8,128)(2,1)S(1)} %copy-done.3, bf16[32,2,6,1536]{3,2,1,0:T(8,128)(2,1)} %dot_general.19), kind=kOutput, calls=%fused_computation.50 | convolution fusion | flops 514916352 | bytes 4202500 | tf_op jit(solution)/shard_map/dot_general | solution.py:119
  111.6 10.4 %collective-permute-start.12 = (f32[32,6,432]{2,0,1:T(8,128)S(1)}, f32[32,6,432]{2,0,1:T(8,128)S(1)}, u32[]{:S(2)}, u32[]{:S(2)}) collective-permute-start(f32[32,6,432]{2,0,1:T(8,128)S(1)} %dynamic-slice_bitcast_fusion), channel_id=1, source_target_pairs={{0,1},{1,0},{2,3},{3,2},{4,5},{5,4},{6,7},{7,6},{8,9},{9,8},{10,11... | collective-permute-start | bytes 995336 | tf_op jit(solution)/shard_map/ppermute | solution.py:131
  124.5 9.7 %all-to-all-start = ((f32[32,6,432]{2,1,0:T(8,128)}), f32[32,6,432]{2,1,0:T(8,128)}, u32[]{:S(2)}, u32[]{:S(2)}) async-start(f32[32,6,432]{2,1,0:T(8,128)} %copy.133), calls=%async_computation | async-start | bytes 1048576 | tf_op jit(solution)/shard_map/all_to_all | solution.py:132
  134.3 2.5 %copy.100 = bf16[2,4,16,27,192]{4,3,2,1,0:T(8,128)(2,1)S(1)} copy(bf16[2,4,16,27,192]{4,2,1,0,3:T(8,128)(2,1)} %constant_dynamic-update-slice_fusion) | data formatting | bytes 2654208 | tf_op jit(solution)/shard_map/stack | solution.py:66
  136.8 2.0 %reshape.218 = bf16[128,5184]{1,0:T(8,128)(2,1)S(1)} reshape(bf16[2,4,16,27,192]{4,3,2,1,0:T(8,128)(2,1)S(1)} %copy.100) | data formatting | bytes 2654208 | tf_op jit(solution)/shard_map/reshape | solution.py:67
  138.8 1.6 %fusion.78 = bf16[1,2,4,16,192]{4,3,2,1,0:T(8,128)(2,1)} fusion(f32[2,4,16,192]{3,2,1,0:T(8,128)} %get-tuple-element.11, f32[2,4,16]{2,1,0:T(4,128)S(1)} %multiply_multiply_fusion, f32[2,4,16]{2,1,0:T(4,128)S(1)} %fusion.131, bf16[1,2,4,16,192]{4,3,2,1,0:T(8,128)(2,1)S(1)} %copy-done), kind=kLoop, calls=%fused_computation.211 | loop fusion | flops 147456 | bytes 197632 | tf_op jit(solution)/shard_map/broadcast_in_dim | solution.py:135
  140.5 3.6 %convolution_convert_fusion = bf16[128,384]{1,0:T(8,128)(2,1)} fusion(bf16[128,5184]{1,0:T(8,128)(2,1)S(1)} %reshape.218, bf16[5184,384]{1,0:T(8,128)(2,1)} %param.8), kind=kOutput, calls=%fused_computation.52 | convolution fusion | flops 509657088 | bytes 5406720 | tf_op jit(solution)/shard_map/dot_general | solution.py:82
  144.1 6.7 %all-to-all-done = f32[32,6,432]{2,1,0:T(8,128)} async-done(((f32[32,6,432]{2,1,0:T(8,128)}), f32[32,6,432]{2,1,0:T(8,128)}, u32[]{:S(2)}, u32[]{:S(2)}) %all-to-all-start) | async-done | bytes 331808 | tf_op jit(solution)/shard_map/all_to_all | solution.py:132
  150.8 1.1 reduce_sum.57
  (120 shorter events, 33.5 us)
Async XLA Ops:
  0.6 20.7 %copy-start.1 = (bf16[1,2,4,16,384]{4,3,2,1,0:T(8,128)(2,1)S(1)}, bf16[1,2,4,16,384]{4,3,2,1,0:T(8,128)(2,1)}, u32[]{:S(2)}) copy-start(bf16[1,2,4,16,384]{4,3,2,1,0:T(8,128)(2,1)} %param.9) | copy-start | bytes 294916
  1.7 51.7 %collective-permute-start.2 = (bf16[2,4,16,576]{3,2,1,0:T(8,128)(2,1)S(1)}, bf16[2,4,16,576]{3,2,1,0:T(8,128)(2,1)S(1)}, u32[]{:S(2)}, u32[]{:S(2)}) collective-permute-start(bf16[2,4,16,576]{3,2,1,0:T(8,128)(2,1)S(1)} %pad_maximum_fusion), channel_id=1, source_target_pairs={{0,704},{64,0},{128,64},{192,128},{256,192},{320,256},{384,320},{4... | collective-permute-start | bytes 442376 | tf_op jit(solution)/shard_map/ppermute | solution.py:30
  16.9 14.9 %collective-permute-start = (bf16[2,4,16,576]{3,2,1,0:T(8,128)(2,1)S(1)}, bf16[2,4,16,576]{3,2,1,0:T(8,128)(2,1)S(1)}, u32[]{:S(2)}, u32[]{:S(2)}) collective-permute-start(bf16[2,4,16,576]{3,2,1,0:T(8,128)(2,1)S(1)} %pad_maximum_fusion), channel_id=1, source_target_pairs={{0,64},{64,128},{128,192},{192,256},{256,320},{320,384},{384,448},... | collective-permute-start | bytes 442376 | tf_op jit(solution)/shard_map/ppermute | solution.py:76
  26.0 2.0 %copy-start = (bf16[1,2,4,16,192]{4,3,2,1,0:T(8,128)(2,1)S(1)}, bf16[1,2,4,16,192]{4,3,2,1,0:T(8,128)(2,1)}, u32[]{:S(2)}) copy-start(bf16[1,2,4,16,192]{4,3,2,1,0:T(8,128)(2,1)} %param.5) | copy-start | bytes 147460
  26.0 2.1 %copy-start.5 = (s32[1,24]{1,0:T(1,128)S(1)}, s32[1,24]{1,0:T(1,128)}, u32[]{:S(2)}) copy-start(s32[1,24]{1,0:T(1,128)} %param.6) | copy-start | bytes 292
  26.7 5.7 %collective-permute-start.1 = (f32[2,4,16,192]{3,2,1,0:T(8,128)S(1)}, f32[2,4,16,192]{3,2,1,0:T(8,128)S(1)}, u32[]{:S(2)}, u32[]{:S(2)}) collective-permute-start(f32[2,4,16,192]{3,2,1,0:T(8,128)S(1)} %slice.155), channel_id=1, source_target_pairs={{64,0},{128,64},{192,128},{256,192},{320,256},{384,320},{448,384},... | collective-permute-start | bytes 294920 | tf_op jit(solution)/shard_map/ppermute | solution.py:14
  28.3 4.1 %copy-start.4 = (f32[192]{0:T(256)S(1)}, f32[192]{0:T(256)}, u32[]{:S(2)}) copy-start(f32[192]{0:T(256)} %param.7) | copy-start | bytes 2308
  49.3 14.5 %collective-permute-start.7 = (bf16[2,4,16,576]{3,2,1,0:T(8,128)(2,1)S(1)}, bf16[2,4,16,576]{3,2,1,0:T(8,128)(2,1)S(1)}, u32[]{:S(2)}, u32[]{:S(2)}) collective-permute-start(bf16[2,4,16,576]{3,2,1,0:T(8,128)(2,1)S(1)} %collective-permute-done), channel_id=1, source_target_pairs={{0,64},{64,128},{128,192},{192,256},{256,320},{320,384},{384,448},... | collective-permute-start | bytes 442376 | tf_op jit(solution)/shard_map/ppermute | solution.py:27
  53.4 6.1 %collective-permute-start.3 = (bf16[2,4,16,576]{3,2,1,0:T(8,128)(2,1)S(1)}, bf16[2,4,16,576]{3,2,1,0:T(8,128)(2,1)S(1)}, u32[]{:S(2)}, u32[]{:S(2)}) collective-permute-start(bf16[2,4,16,576]{3,2,1,0:T(8,128)(2,1)S(1)} %collective-permute-done.2), channel_id=1, source_target_pairs={{0,704},{64,0},{128,64},{192,128},{256,192},{320,256},{384,320},{4... | collective-permute-start | bytes 442376 | tf_op jit(solution)/shard_map/ppermute | solution.py:30
  59.5 6.5 %collective-permute-start.4 = (bf16[2,4,16,576]{3,2,1,0:T(8,128)(2,1)S(1)}, bf16[2,4,16,576]{3,2,1,0:T(8,128)(2,1)S(1)}, u32[]{:S(2)}, u32[]{:S(2)}) collective-permute-start(bf16[2,4,16,576]{3,2,1,0:T(8,128)(2,1)S(1)} %collective-permute-done.3), channel_id=1, source_target_pairs={{0,704},{64,0},{128,64},{192,128},{256,192},{320,256},{384,320},{4... | collective-permute-start | bytes 442376 | tf_op jit(solution)/shard_map/ppermute | solution.py:30
  63.7 7.3 %collective-permute-start.8 = (bf16[2,4,16,576]{3,2,1,0:T(8,128)(2,1)S(1)}, bf16[2,4,16,576]{3,2,1,0:T(8,128)(2,1)S(1)}, u32[]{:S(2)}, u32[]{:S(2)}) collective-permute-start(bf16[2,4,16,576]{3,2,1,0:T(8,128)(2,1)S(1)} %collective-permute-done.7), channel_id=1, source_target_pairs={{0,64},{64,128},{128,192},{192,256},{256,320},{320,384},{384,448},... | collective-permute-start | bytes 442376 | tf_op jit(solution)/shard_map/ppermute | solution.py:27
  66.0 7.3 %collective-permute-start.5 = (bf16[2,4,16,576]{3,2,1,0:T(8,128)(2,1)S(1)}, bf16[2,4,16,576]{3,2,1,0:T(8,128)(2,1)S(1)}, u32[]{:S(2)}, u32[]{:S(2)}) collective-permute-start(bf16[2,4,16,576]{3,2,1,0:T(8,128)(2,1)S(1)} %collective-permute-done.4), channel_id=1, source_target_pairs={{0,704},{64,0},{128,64},{192,128},{256,192},{320,256},{384,320},{4... | collective-permute-start | bytes 442376 | tf_op jit(solution)/shard_map/ppermute | solution.py:30
  71.0 7.3 %collective-permute-start.9 = (bf16[2,4,16,576]{3,2,1,0:T(8,128)(2,1)S(1)}, bf16[2,4,16,576]{3,2,1,0:T(8,128)(2,1)S(1)}, u32[]{:S(2)}, u32[]{:S(2)}) collective-permute-start(bf16[2,4,16,576]{3,2,1,0:T(8,128)(2,1)S(1)} %collective-permute-done.8), channel_id=1, source_target_pairs={{0,64},{64,128},{128,192},{192,256},{256,320},{320,384},{384,448},... | collective-permute-start | bytes 442376 | tf_op jit(solution)/shard_map/ppermute | solution.py:27
  73.2 14.4 %collective-permute-start.6 = (bf16[2,4,16,576]{3,2,1,0:T(8,128)(2,1)S(1)}, bf16[2,4,16,576]{3,2,1,0:T(8,128)(2,1)S(1)}, u32[]{:S(2)}, u32[]{:S(2)}) collective-permute-start(bf16[2,4,16,576]{3,2,1,0:T(8,128)(2,1)S(1)} %collective-permute-done.5), channel_id=1, source_target_pairs={{0,704},{64,0},{128,64},{192,128},{256,192},{320,256},{384,320},{4... | collective-permute-start | bytes 442376 | tf_op jit(solution)/shard_map/ppermute | solution.py:30
  78.3 7.3 %collective-permute-start.10 = (bf16[2,4,16,576]{3,2,1,0:T(8,128)(2,1)S(1)}, bf16[2,4,16,576]{3,2,1,0:T(8,128)(2,1)S(1)}, u32[]{:S(2)}, u32[]{:S(2)}) collective-permute-start(bf16[2,4,16,576]{3,2,1,0:T(8,128)(2,1)S(1)} %collective-permute-done.9), channel_id=1, source_target_pairs={{0,64},{64,128},{128,192},{192,256},{256,320},{320,384},{384,448},... | collective-permute-start | bytes 442376 | tf_op jit(solution)/shard_map/ppermute | solution.py:27
  85.5 8.4 %collective-permute-start.11 = (bf16[2,4,16,576]{3,2,1,0:T(8,128)(2,1)S(1)}, bf16[2,4,16,576]{3,2,1,0:T(8,128)(2,1)S(1)}, u32[]{:S(2)}, u32[]{:S(2)}) collective-permute-start(bf16[2,4,16,576]{3,2,1,0:T(8,128)(2,1)S(1)} %collective-permute-done.10), channel_id=1, source_target_pairs={{0,64},{64,128},{128,192},{192,256},{256,320},{320,384},{384,448},... | collective-permute-start | bytes 442376 | tf_op jit(solution)/shard_map/ppermute | solution.py:27
  106.4 1.4 copy-start.2
  106.4 1.5 copy-start.3
  111.6 11.8 %collective-permute-start.12 = (f32[32,6,432]{2,0,1:T(8,128)S(1)}, f32[32,6,432]{2,0,1:T(8,128)S(1)}, u32[]{:S(2)}, u32[]{:S(2)}) collective-permute-start(f32[32,6,432]{2,0,1:T(8,128)S(1)} %dynamic-slice_bitcast_fusion), channel_id=1, source_target_pairs={{0,1},{1,0},{2,3},{3,2},{4,5},{5,4},{6,7},{7,6},{8,9},{9,8},{10,11... | collective-permute-start | bytes 995336 | tf_op jit(solution)/shard_map/ppermute | solution.py:131
  124.5 26.3 %all-to-all-start = ((f32[32,6,432]{2,1,0:T(8,128)}), f32[32,6,432]{2,1,0:T(8,128)}, u32[]{:S(2)}, u32[]{:S(2)}) async-start(f32[32,6,432]{2,1,0:T(8,128)} %copy.133), calls=%async_computation | async-start | bytes 1048576 | tf_op jit(solution)/shard_map/all_to_all | solution.py:132

commit v6 on v5

--- a/solution.py
+++ b/solution.py
@@ -78,23 +78,38 @@
     extended = jnp.concatenate([previous, activated])
     first_frame = lax.axis_index("tm") * frames
     tap_mask = make_mask(clip_ids[0], first_frame, frames)
-    patches = extract(extended, tap_mask)
-    conv_rows = jnp.dot(patches, conv_weight, preferred_element_type=jnp.float32).astype(
-        jnp.bfloat16
+    kernel = conv_weight.reshape(3, 3, 3, channels, outputs)
+    tap_scale = tap_mask[:, :, None, None, None]
+    taps = jnp.stack([extended[tap_t : tap_t + frames] for tap_t in range(3)], axis=1)
+    masked_taps = taps * tap_scale.astype(taps.dtype)
+    conv_rows = lax.conv_general_dilated(
+        masked_taps,
+        kernel,
+        (1, 1, 1),
+        ((0, 0), (1, 1), (1, 1)),
+        dimension_numbers=("NDHWC", "DHWIO", "NDHWC"),
+        preferred_element_type=jnp.float32,
+    ).astype(jnp.bfloat16)
+    taps_grad = lax.conv_general_dilated(
+        out_cotangent[0][:, None],
+        kernel[::-1, ::-1, ::-1],
+        (1, 1, 1),
+        ((2, 2), (1, 1), (1, 1)),
+        dimension_numbers=("NDHWC", "DHWOI", "NDHWC"),
+        preferred_element_type=jnp.float32,
     )
-    cotangent_rows = out_cotangent[0].reshape(-1, outputs)
-    patch_grad = jnp.dot(cotangent_rows, conv_weight.T, preferred_element_type=jnp.float32)
-    unused, pull_patch = jax.vjp(
-        lambda field: extract(field, tap_mask), extended.astype(jnp.float32)
+    masked_grad = taps_grad * tap_scale
+    extended_grad = sum(
+        jnp.pad(masked_grad[:, tap_t], ((tap_t, 2 - tap_t), (0, 0), (0, 0), (0, 0)))
+        for tap_t in range(3)
     )
-    extended_grad = pull_patch(patch_grad)[0]
     returned = from_behind(extended_grad[:2], "tm", -1)
     own_grad = extended_grad[2:] + returned
     unused, pull_norm = jax.vjp(lambda field: activate(field, norm_gain), video.astype(jnp.float32))
     video_grad = pull_norm(own_grad)[0].astype(jnp.bfloat16)
     chain_len = lax.axis_size("tm")
     scale = 1.0 / math.sqrt(lax.axis_size(DATA) * chain_len * frames * height * width)
-    kernel_rows = patches.shape[1]
+    kernel_rows = conv_weight.shape[0]
     slab_rows = kernel_rows // chain_len
     slab_start = lax.axis_index("tm") * slab_rows
     tap_lo = slab_start // channels

time: 154 us -> 136 us (0.88)
  other arithmetic: 30.7 us -> 9.69 us
  waiting for transfers between devices: 21.7 us -> 25.4 us
  local copies, waits for them, and re-layouts: 20 us -> 22.9 us
  starting transfers between devices: 67 us -> 65.2 us
    unnamed x28 -> x2, other arithmetic: 18.3 us -> 0.3 us
    dot_general x2 -> x0, matrix products: 7.67 us -> none  [the longest x1 4.04 us: shards(): jnp.dot(cotangent_rows, conv_weight.T, preferred_element_type=jnp.float32)]
    conv_general_dilated x0 -> x2, matrix products: none -> 6.82 us  [the longest x1 3.43 us: shards(): lax.conv_general_dilated(out_cotangent[0][:, None], kernel[::-1, ::-1, ::...]
    unnamed x33 -> x51, local copies, waits for them, and re-layouts: 0.64 us -> 6.08 us
    all_to_all x1, waiting for transfers between devices: 6.72 us -> 11.3 us  [shards(): reduced_t = lax.all_to_all(pair_sum, 'dq', 0, 0, tiled=False).sum(axis=0)]
    another operation x1, local copies, waits for them, and re-layouts: 2.49 us -> 0.1 us  [shards(): out_cotangent[0][:, None]]
    reshape x1, local copies, waits for them, and re-layouts: 2 us -> 0.04 us  [shards(): conv_out = conv_rows.reshape(1, frames, height, width, outputs)]
  transfers between devices with their start and end apart: 14 -> 14, of which waited for: 7 -> 7; matrix products, arithmetic and copies ran while one was open for 27% -> 15% of each run, Pallas kernels for 0% -> 0%
where the time goes in v6:
time: 136 us; the launch traced here: 135 us
  starting transfers between devices  65.2 us (48%)
  waiting for transfers between devices  25.4 us (19%)
  local copies, waits for them, and re-layouts  22.9 us (17%)
  matrix products  10.2 us (7%)
  other arithmetic  9.69 us (7%)
  between operations  1.7 us (1%)
    ppermute x5, starting transfers between devices, ring_gather(): moving = lax.ppermute(moving, axis, ring_route(axis, -1))  31.3 us
    ppermute x5, starting transfers between devices, ring_gather(): lax.ppermute(from_behind_list[-1], axis, ring_route(axis, 1))  11.8 us
    all_to_all x1, waiting for transfers between devices, shards(): reduced_t = lax.all_to_all(pair_sum, 'dq', 0, 0, tiled=False).sum(axis=0)  11.3 us
    ppermute x5, waiting for transfers between devices, ring_gather(): lax.ppermute(from_behind_list[-1], axis, ring_route(axis, 1))  10.4 us
    all_to_all x1, starting transfers between devices, shards(): reduced_t = lax.all_to_all(pair_sum, 'dq', 0, 0, tiled=False).sum(axis=0)  9.67 us
    ppermute x1, starting transfers between devices, shards(): pair_sum = kept + lax.ppermute(sent, 'dc', [(0, 1), (1, 0)])  9.24 us
    unnamed x51, local copies, waits for them, and re-layouts  6.08 us
    reshape x4, local copies, waits for them, and re-layouts, shards(): (window * weight_t[:, None, None, None]).reshape(-1, channels)  5.43 us
  transfers between devices with their start and end apart: 14, of which 7 were waited for; matrix products, arithmetic and copies ran while one was open for 15% of the time, Pallas kernels for 0%

profile of v6, /device:TPU:1, one launch (start us, length us, event | category | flops | bytes accessed | tf_op | source)
XLA Modules:
  0.0 135.1 jit_solution(16094034888954370113)
XLA Ops:
  2.6 15.1 %collective-permute-start.2 = (bf16[2,4,16,576]{3,1,2,0:T(4,128)(2,1)S(1)}, bf16[2,4,16,576]{3,1,2,0:T(4,128)(2,1)S(1)}, u32[]{:S(2)}, u32[]{:S(2)}) collective-permute-start(bf16[2,4,16,576]{3,1,2,0:T(4,128)(2,1)S(1)} %pad_maximum_fusion), channel_id=1, source_target_pairs={{0,704},{64,0},{128,64},{192,128},{256,192},{320,256},{384,320},{4... | collective-permute-start | bytes 442376 | tf_op jit(solution)/shard_map/ppermute | solution.py:30
  17.8 1.9 %collective-permute-start = (bf16[2,4,16,576]{3,1,2,0:T(4,128)(2,1)S(1)}, bf16[2,4,16,576]{3,1,2,0:T(4,128)(2,1)S(1)}, u32[]{:S(2)}, u32[]{:S(2)}) collective-permute-start(bf16[2,4,16,576]{3,1,2,0:T(4,128)(2,1)S(1)} %pad_maximum_fusion), channel_id=1, source_target_pairs={{0,64},{64,128},{128,192},{192,256},{256,320},{320,384},{384,448},... | collective-permute-start | bytes 442376 | tf_op jit(solution)/shard_map/ppermute | solution.py:76
  22.1 1.0 copy.86
  23.7 3.4 %fusion.14 = f32[3,4,16,3,192]{4,2,3,1,0:T(8,128)S(1)} fusion(bf16[3,3,3,192,384]{4,3,2,1,0:T(8,128)(2,1)} %bitcast.128, f32[3,4,16,3,192]{4,1,3,2,0:T(4,128)S(1)} %bitcast.138, pred[16,3]{0,1:T(4,128)(4,1)S(1)} %copy-done.8, bf16[1,4,2,8,5,384]{5,2,4,3,1,0:T(2,128)(2,1)S(1)} %fusion.24), kind=kOutput, calls=%fused_computation.29 | convolution fusion | flops 637231104 | bytes 5111856 | tf_op jit(solution)/shard_map/conv_general_dilated | solution.py:93
  27.7 1.3 collective-permute-start.1
  29.4 1.2 gather_fusion.2
  33.1 4.0 %collective-permute-start.7 = (bf16[2,4,16,576]{3,1,2,0:T(4,128)(2,1)S(1)}, bf16[2,4,16,576]{3,1,2,0:T(4,128)(2,1)S(1)}, u32[]{:S(2)}, u32[]{:S(2)}) collective-permute-start(bf16[2,4,16,576]{3,1,2,0:T(4,128)(2,1)S(1)} %collective-permute-done), channel_id=1, source_target_pairs={{0,64},{64,128},{128,192},{192,256},{256,320},{320,384},{384,448},... | collective-permute-start | bytes 442376 | tf_op jit(solution)/shard_map/ppermute | solution.py:27
  37.1 1.6 %fusion.47 = (f32[2,4,16]{1,2,0:T(8,128)}, f32[2,4,16,192]{3,1,2,0:T(4,128)}, bf16[2,4,16,192]{3,1,2,0:T(4,128)(2,1)S(1)}, bf16[2,4,16,192]{3,1,2,0:T(4,128)(2,1)S(1)}) fusion(bf16[1,2,4,16,192]{4,3,2,1,0:T(8,128)(2,1)S(1)} %copy-done, f32[192]{0:T(256)S(1)} %copy-done.10, f32[2,4,16]{1,2,0:T(8,128)S(1)} %fusion.55, ...), kind=kLoop, calls=%fused_computation.103 | loop fusion | flops 638848 | bytes 493824 | tf_op jit(solution)/shard_map/transpose(jvp())/reduce_sum | solution.py:41
  38.8 2.5 %collective-permute-start.3 = (bf16[2,4,16,576]{3,1,2,0:T(4,128)(2,1)S(1)}, bf16[2,4,16,576]{3,1,2,0:T(4,128)(2,1)S(1)}, u32[]{:S(2)}, u32[]{:S(2)}) collective-permute-start(bf16[2,4,16,576]{3,1,2,0:T(4,128)(2,1)S(1)} %collective-permute-done.2), channel_id=1, source_target_pairs={{0,704},{64,0},{128,64},{192,128},{256,192},{320,256},{384,320},{4... | collective-permute-start | bytes 442376 | tf_op jit(solution)/shard_map/ppermute | solution.py:30
  42.2 2.6 %collective-permute-done.3 = bf16[2,4,16,576]{3,1,2,0:T(4,128)(2,1)S(1)} collective-permute-done((bf16[2,4,16,576]{3,1,2,0:T(4,128)(2,1)S(1)}, bf16[2,4,16,576]{3,1,2,0:T(4,128)(2,1)S(1)}, u32[]{:S(2)}, u32[]{:S(2)}) %collective-permute-start.3) | collective-permute-done | bytes 147488 | tf_op jit(solution)/shard_map/ppermute | solution.py:30
  44.8 3.7 %collective-permute-start.4 = (bf16[2,4,16,576]{3,1,2,0:T(4,128)(2,1)S(1)}, bf16[2,4,16,576]{3,1,2,0:T(4,128)(2,1)S(1)}, u32[]{:S(2)}, u32[]{:S(2)}) collective-permute-start(bf16[2,4,16,576]{3,1,2,0:T(4,128)(2,1)S(1)} %collective-permute-done.3), channel_id=1, source_target_pairs={{0,704},{64,0},{128,64},{192,128},{256,192},{320,256},{384,320},{4... | collective-permute-start | bytes 442376 | tf_op jit(solution)/shard_map/ppermute | solution.py:30
  48.6 1.9 %collective-permute-start.8 = (bf16[2,4,16,576]{3,1,2,0:T(4,128)(2,1)S(1)}, bf16[2,4,16,576]{3,1,2,0:T(4,128)(2,1)S(1)}, u32[]{:S(2)}, u32[]{:S(2)}) collective-permute-start(bf16[2,4,16,576]{3,1,2,0:T(4,128)(2,1)S(1)} %collective-permute-done.7), channel_id=1, source_target_pairs={{0,64},{64,128},{128,192},{192,256},{256,320},{320,384},{384,448},... | collective-permute-start | bytes 442376 | tf_op jit(solution)/shard_map/ppermute | solution.py:27
  50.9 4.9 %collective-permute-start.5 = (bf16[2,4,16,576]{3,1,2,0:T(4,128)(2,1)S(1)}, bf16[2,4,16,576]{3,1,2,0:T(4,128)(2,1)S(1)}, u32[]{:S(2)}, u32[]{:S(2)}) collective-permute-start(bf16[2,4,16,576]{3,1,2,0:T(4,128)(2,1)S(1)} %collective-permute-done.4), channel_id=1, source_target_pairs={{0,704},{64,0},{128,64},{192,128},{256,192},{320,256},{384,320},{4... | collective-permute-start | bytes 442376 | tf_op jit(solution)/shard_map/ppermute | solution.py:30
  55.8 1.9 %collective-permute-start.9 = (bf16[2,4,16,576]{3,1,2,0:T(4,128)(2,1)S(1)}, bf16[2,4,16,576]{3,1,2,0:T(4,128)(2,1)S(1)}, u32[]{:S(2)}, u32[]{:S(2)}) collective-permute-start(bf16[2,4,16,576]{3,1,2,0:T(4,128)(2,1)S(1)} %collective-permute-done.8), channel_id=1, source_target_pairs={{0,64},{64,128},{128,192},{192,256},{256,320},{320,384},{384,448},... | collective-permute-start | bytes 442376 | tf_op jit(solution)/shard_map/ppermute | solution.py:27
  58.0 5.0 %collective-permute-start.6 = (bf16[2,4,16,576]{3,1,2,0:T(4,128)(2,1)S(1)}, bf16[2,4,16,576]{3,1,2,0:T(4,128)(2,1)S(1)}, u32[]{:S(2)}, u32[]{:S(2)}) collective-permute-start(bf16[2,4,16,576]{3,1,2,0:T(4,128)(2,1)S(1)} %collective-permute-done.5), channel_id=1, source_target_pairs={{0,704},{64,0},{128,64},{192,128},{256,192},{320,256},{384,320},{4... | collective-permute-start | bytes 442376 | tf_op jit(solution)/shard_map/ppermute | solution.py:30
  63.1 1.9 %collective-permute-start.10 = (bf16[2,4,16,576]{3,1,2,0:T(4,128)(2,1)S(1)}, bf16[2,4,16,576]{3,1,2,0:T(4,128)(2,1)S(1)}, u32[]{:S(2)}, u32[]{:S(2)}) collective-permute-start(bf16[2,4,16,576]{3,1,2,0:T(4,128)(2,1)S(1)} %collective-permute-done.9), channel_id=1, source_target_pairs={{0,64},{64,128},{128,192},{192,256},{256,320},{320,384},{384,448},... | collective-permute-start | bytes 442376 | tf_op jit(solution)/shard_map/ppermute | solution.py:27
  65.1 5.3 %collective-permute-done.10 = bf16[2,4,16,576]{3,1,2,0:T(4,128)(2,1)S(1)} collective-permute-done((bf16[2,4,16,576]{3,1,2,0:T(4,128)(2,1)S(1)}, bf16[2,4,16,576]{3,1,2,0:T(4,128)(2,1)S(1)}, u32[]{:S(2)}, u32[]{:S(2)}) %collective-permute-start.10) | collective-permute-done | bytes 147488 | tf_op jit(solution)/shard_map/ppermute | solution.py:27
  70.4 2.1 %collective-permute-start.11 = (bf16[2,4,16,576]{3,1,2,0:T(4,128)(2,1)S(1)}, bf16[2,4,16,576]{3,1,2,0:T(4,128)(2,1)S(1)}, u32[]{:S(2)}, u32[]{:S(2)}) collective-permute-start(bf16[2,4,16,576]{3,1,2,0:T(4,128)(2,1)S(1)} %collective-permute-done.10), channel_id=1, source_target_pairs={{0,64},{64,128},{128,192},{192,256},{256,320},{320,384},{384,448},... | collective-permute-start | bytes 442376 | tf_op jit(solution)/shard_map/ppermute | solution.py:27
  72.5 5.1 %collective-permute-done.11 = bf16[2,4,16,576]{3,1,2,0:T(4,128)(2,1)S(1)} collective-permute-done((bf16[2,4,16,576]{3,1,2,0:T(4,128)(2,1)S(1)}, bf16[2,4,16,576]{3,1,2,0:T(4,128)(2,1)S(1)}, u32[]{:S(2)}, u32[]{:S(2)}) %collective-permute-start.11) | collective-permute-done | bytes 147488 | tf_op jit(solution)/shard_map/ppermute | solution.py:27
  81.9 2.5 %fusion.20 = (bf16[24,4,16,192]{3,2,1,0:T(8,128)(2,1)S(1)}, bf16[24,4,16,192]{3,2,1,0:T(8,128)(2,1)}, bf16[24,4,16,192]{3,2,1,0:T(8,128)(2,1)S(1)}) fusion(s32[]{:T(128)S(6)} %select_n.210, s32[]{:T(128)S(6)} %select_n.213, s32[]{:T(128)S(6)} %select_n.215, bf16[24,4,16,192]{3,2,1,0:T(8,128)(2,1)S(1)} %fusion.7, bf16[24]{0:T(256)(128)(2,1)S(1)} %get-tuple-element.12, ...), kind=kLoop, calls=%fused_computation.37 | loop fusion | flops 3538944 | bytes 2359476 | tf_op jit(solution)/shard_map/mul | solution.py:132
  84.4 2.2 %copy.77 = bf16[1536,192]{0,1:T(8,128)(2,1)} copy(bf16[1536,192]{1,0:T(8,128)(2,1)} %bitcast.137) | data formatting | bytes 1179648 | tf_op jit(solution)/shard_map/reshape | solution.py:132
  86.6 1.1 copy.78
  87.6 1.1 copy.79
  88.7 1.2 fusion.17
  89.9 1.1 copy.76
  91.6 1.4 %dot_general.8 = bf16[32,2,6,1536]{3,2,1,0:T(8,128)(2,1)} reshape(bf16[384,1536]{1,0:T(8,128)(2,1)S(1)} %copy.75) | data formatting | bytes 2359296 | tf_op jit(solution)/shard_map/dot_general | solution.py:134
  93.0 3.4 %fusion.12 = f32[32,2,6,432]{3,0,2,1:T(8,128)S(1)} fusion(s32[]{:T(128)S(6)} %select_n.217, bf16[1536,192]{0,1:T(8,128)(2,1)} %copy.76, bf16[1536,192]{0,1:T(8,128)(2,1)S(1)} %copy-done.3, bf16[1536,192]{0,1:T(8,128)(2,1)} %copy.78, bf16[1536,192]{0,1:T(8,128)(2,1)} %copy.79, bf16[32,2,6,1536]{3,2,1,0:T(8,128)(2,1)} %dot_general.8), kind=kOutput, calls=%fused_computation.27 | convolution fusion | flops 514916352 | bytes 4202500 | tf_op jit(solution)/shard_map/dot_general | solution.py:134
  96.5 9.2 %collective-permute-start.12 = (f32[32,6,432]{2,0,1:T(8,128)S(1)}, f32[32,6,432]{2,0,1:T(8,128)S(1)}, u32[]{:S(2)}, u32[]{:S(2)}) collective-permute-start(f32[32,6,432]{2,0,1:T(8,128)S(1)} %dynamic-slice_bitcast_fusion), channel_id=1, source_target_pairs={{0,1},{1,0},{2,3},{3,2},{4,5},{5,4},{6,7},{7,6},{8,9},{9,8},{10,11... | collective-permute-start | bytes 995336 | tf_op jit(solution)/shard_map/ppermute | solution.py:146
  107.1 1.0 copy.81
  108.2 9.7 %all-to-all-start = ((f32[32,6,432]{2,1,0:T(8,128)}), f32[32,6,432]{2,1,0:T(8,128)S(1)}, u32[]{:S(2)}, u32[]{:S(2)}) async-start(f32[32,6,432]{2,1,0:T(8,128)} %copy.81), calls=%async_computation | async-start | bytes 1048576 | tf_op jit(solution)/shard_map/all_to_all | solution.py:147
  118.9 3.4 %fusion.16 = bf16[1,4,16,3,384]{4,2,3,1,0:T(8,128)(2,1)S(1)} fusion(bf16[3,3,3,192,384]{4,3,2,1,0:T(8,128)(2,1)} %bitcast.129, bf16[3,4,2,8,5,192]{5,2,4,3,1,0:T(2,128)(2,1)S(1)} %fusion.21, pred[16,3]{0,1:T(4,128)(4,1)S(1)} %copy-done.9), kind=kOutput, calls=%fused_computation.32 | convolution fusion | flops 637157376 | bytes 4497456 | tf_op jit(solution)/shard_map/conv_general_dilated | solution.py:85
  123.1 11.3 %all-to-all-done = f32[32,6,432]{2,1,0:T(8,128)S(1)} async-done(((f32[32,6,432]{2,1,0:T(8,128)}), f32[32,6,432]{2,1,0:T(8,128)S(1)}, u32[]{:S(2)}, u32[]{:S(2)}) %all-to-all-start) | async-done | bytes 331808 | tf_op jit(solution)/shard_map/all_to_all | solution.py:147
  (122 shorter events, 18.4 us)
Async XLA Ops:
  0.6 23.0 %copy-start.8 = (pred[16,3]{0,1:T(4,128)(4,1)S(1)}, pred[16,3]{0,1:T(4,128)(4,1)}, u32[]{:S(2)}) copy-start(pred[16,3]{0,1:T(4,128)(4,1)} %constant.183) | copy-start | bytes 148
  2.6 36.1 %collective-permute-start.2 = (bf16[2,4,16,576]{3,1,2,0:T(4,128)(2,1)S(1)}, bf16[2,4,16,576]{3,1,2,0:T(4,128)(2,1)S(1)}, u32[]{:S(2)}, u32[]{:S(2)}) collective-permute-start(bf16[2,4,16,576]{3,1,2,0:T(4,128)(2,1)S(1)} %pad_maximum_fusion), channel_id=1, source_target_pairs={{0,704},{64,0},{128,64},{192,128},{256,192},{320,256},{384,320},{4... | collective-permute-start | bytes 442376 | tf_op jit(solution)/shard_map/ppermute | solution.py:30
  17.8 15.2 %collective-permute-start = (bf16[2,4,16,576]{3,1,2,0:T(4,128)(2,1)S(1)}, bf16[2,4,16,576]{3,1,2,0:T(4,128)(2,1)S(1)}, u32[]{:S(2)}, u32[]{:S(2)}) collective-permute-start(bf16[2,4,16,576]{3,1,2,0:T(4,128)(2,1)S(1)} %pad_maximum_fusion), channel_id=1, source_target_pairs={{0,64},{64,128},{128,192},{192,256},{256,320},{320,384},{384,448},... | collective-permute-start | bytes 442376 | tf_op jit(solution)/shard_map/ppermute | solution.py:76
  23.6 5.4 %copy-start = (bf16[1,2,4,16,192]{4,3,2,1,0:T(8,128)(2,1)S(1)}, bf16[1,2,4,16,192]{4,3,2,1,0:T(8,128)(2,1)}, u32[]{:S(2)}) copy-start(bf16[1,2,4,16,192]{4,3,2,1,0:T(8,128)(2,1)} %param.5) | copy-start | bytes 147460
  23.6 5.5 %copy-start.11 = (s32[1,24]{1,0:T(1,128)S(1)}, s32[1,24]{1,0:T(1,128)}, u32[]{:S(2)}) copy-start(s32[1,24]{1,0:T(1,128)} %param.6) | copy-start | bytes 292
  27.7 9.4 %collective-permute-start.1 = (f32[2,4,16,192]{3,1,2,0:T(4,128)S(1)}, f32[2,4,16,192]{3,1,2,0:T(4,128)S(1)}, u32[]{:S(2)}, u32[]{:S(2)}) collective-permute-start(f32[2,4,16,192]{3,1,2,0:T(4,128)S(1)} %slice.64), channel_id=1, source_target_pairs={{64,0},{128,64},{192,128},{256,192},{320,256},{384,320},{448,384},... | collective-permute-start | bytes 294920 | tf_op jit(solution)/shard_map/ppermute | solution.py:14
  29.2 2.2 %copy-start.5 = (f32[2,4,16]{1,2,0:T(8,128)}, f32[2,4,16]{1,2,0:T(8,128)S(1)}, u32[]{:S(2)}) copy-start(f32[2,4,16]{1,2,0:T(8,128)S(1)} %fusion.38) | copy-start | bytes 1540
  29.4 2.1 %copy-start.10 = (f32[192]{0:T(256)S(1)}, f32[192]{0:T(256)}, u32[]{:S(2)}) copy-start(f32[192]{0:T(256)} %param.7) | copy-start | bytes 2308
  33.1 15.5 %collective-permute-start.7 = (bf16[2,4,16,576]{3,1,2,0:T(4,128)(2,1)S(1)}, bf16[2,4,16,576]{3,1,2,0:T(4,128)(2,1)S(1)}, u32[]{:S(2)}, u32[]{:S(2)}) collective-permute-start(bf16[2,4,16,576]{3,1,2,0:T(4,128)(2,1)S(1)} %collective-permute-done), channel_id=1, source_target_pairs={{0,64},{64,128},{128,192},{192,256},{256,320},{320,384},{384,448},... | collective-permute-start | bytes 442376 | tf_op jit(solution)/shard_map/ppermute | solution.py:27
  38.8 6.1 %collective-permute-start.3 = (bf16[2,4,16,576]{3,1,2,0:T(4,128)(2,1)S(1)}, bf16[2,4,16,576]{3,1,2,0:T(4,128)(2,1)S(1)}, u32[]{:S(2)}, u32[]{:S(2)}) collective-permute-start(bf16[2,4,16,576]{3,1,2,0:T(4,128)(2,1)S(1)} %collective-permute-done.2), channel_id=1, source_target_pairs={{0,704},{64,0},{128,64},{192,128},{256,192},{320,256},{384,320},{4... | collective-permute-start | bytes 442376 | tf_op jit(solution)/shard_map/ppermute | solution.py:30
  44.8 6.1 %collective-permute-start.4 = (bf16[2,4,16,576]{3,1,2,0:T(4,128)(2,1)S(1)}, bf16[2,4,16,576]{3,1,2,0:T(4,128)(2,1)S(1)}, u32[]{:S(2)}, u32[]{:S(2)}) collective-permute-start(bf16[2,4,16,576]{3,1,2,0:T(4,128)(2,1)S(1)} %collective-permute-done.3), channel_id=1, source_target_pairs={{0,704},{64,0},{128,64},{192,128},{256,192},{320,256},{384,320},{4... | collective-permute-start | bytes 442376 | tf_op jit(solution)/shard_map/ppermute | solution.py:30
  48.6 7.3 %collective-permute-start.8 = (bf16[2,4,16,576]{3,1,2,0:T(4,128)(2,1)S(1)}, bf16[2,4,16,576]{3,1,2,0:T(4,128)(2,1)S(1)}, u32[]{:S(2)}, u32[]{:S(2)}) collective-permute-start(bf16[2,4,16,576]{3,1,2,0:T(4,128)(2,1)S(1)} %collective-permute-done.7), channel_id=1, source_target_pairs={{0,64},{64,128},{128,192},{192,256},{256,320},{320,384},{384,448},... | collective-permute-start | bytes 442376 | tf_op jit(solution)/shard_map/ppermute | solution.py:27
  50.9 7.2 %collective-permute-start.5 = (bf16[2,4,16,576]{3,1,2,0:T(4,128)(2,1)S(1)}, bf16[2,4,16,576]{3,1,2,0:T(4,128)(2,1)S(1)}, u32[]{:S(2)}, u32[]{:S(2)}) collective-permute-start(bf16[2,4,16,576]{3,1,2,0:T(4,128)(2,1)S(1)} %collective-permute-done.4), channel_id=1, source_target_pairs={{0,704},{64,0},{128,64},{192,128},{256,192},{320,256},{384,320},{4... | collective-permute-start | bytes 442376 | tf_op jit(solution)/shard_map/ppermute | solution.py:30
  55.8 7.3 %collective-permute-start.9 = (bf16[2,4,16,576]{3,1,2,0:T(4,128)(2,1)S(1)}, bf16[2,4,16,576]{3,1,2,0:T(4,128)(2,1)S(1)}, u32[]{:S(2)}, u32[]{:S(2)}) collective-permute-start(bf16[2,4,16,576]{3,1,2,0:T(4,128)(2,1)S(1)} %collective-permute-done.8), channel_id=1, source_target_pairs={{0,64},{64,128},{128,192},{192,256},{256,320},{320,384},{384,448},... | collective-permute-start | bytes 442376 | tf_op jit(solution)/shard_map/ppermute | solution.py:27
  58.0 14.4 %collective-permute-start.6 = (bf16[2,4,16,576]{3,1,2,0:T(4,128)(2,1)S(1)}, bf16[2,4,16,576]{3,1,2,0:T(4,128)(2,1)S(1)}, u32[]{:S(2)}, u32[]{:S(2)}) collective-permute-start(bf16[2,4,16,576]{3,1,2,0:T(4,128)(2,1)S(1)} %collective-permute-done.5), channel_id=1, source_target_pairs={{0,704},{64,0},{128,64},{192,128},{256,192},{320,256},{384,320},{4... | collective-permute-start | bytes 442376 | tf_op jit(solution)/shard_map/ppermute | solution.py:30
  63.1 7.3 %collective-permute-start.10 = (bf16[2,4,16,576]{3,1,2,0:T(4,128)(2,1)S(1)}, bf16[2,4,16,576]{3,1,2,0:T(4,128)(2,1)S(1)}, u32[]{:S(2)}, u32[]{:S(2)}) collective-permute-start(bf16[2,4,16,576]{3,1,2,0:T(4,128)(2,1)S(1)} %collective-permute-done.9), channel_id=1, source_target_pairs={{0,64},{64,128},{128,192},{192,256},{256,320},{320,384},{384,448},... | collective-permute-start | bytes 442376 | tf_op jit(solution)/shard_map/ppermute | solution.py:27
  70.4 7.3 %collective-permute-start.11 = (bf16[2,4,16,576]{3,1,2,0:T(4,128)(2,1)S(1)}, bf16[2,4,16,576]{3,1,2,0:T(4,128)(2,1)S(1)}, u32[]{:S(2)}, u32[]{:S(2)}) collective-permute-start(bf16[2,4,16,576]{3,1,2,0:T(4,128)(2,1)S(1)} %collective-permute-done.10), channel_id=1, source_target_pairs={{0,64},{64,128},{128,192},{192,256},{256,320},{320,384},{384,448},... | collective-permute-start | bytes 442376 | tf_op jit(solution)/shard_map/ppermute | solution.py:27
  88.7 4.3 %copy-start.3 = (bf16[1536,192]{0,1:T(8,128)(2,1)S(1)}, bf16[1536,192]{0,1:T(8,128)(2,1)}, u32[]{:S(2)}) copy-start(bf16[1536,192]{0,1:T(8,128)(2,1)} %copy.77) | copy-start | bytes 1769476
  93.0 12.7 %copy-start.6 = (f32[2,4,16]{1,2,0:T(8,128)S(1)}, f32[2,4,16]{1,2,0:T(8,128)}, u32[]{:S(2)}) copy-start(f32[2,4,16]{1,2,0:T(8,128)} %copy-done.5) | copy-start | bytes 1540
  93.0 12.8 %copy-start.7 = (f32[2,4,16]{1,2,0:T(8,128)S(1)}, f32[2,4,16]{1,2,0:T(8,128)}, u32[]{:S(2)}) copy-start(f32[2,4,16]{1,2,0:T(8,128)} %get-tuple-element.16) | copy-start | bytes 1540
  93.0 12.8 %copy-start.2 = (bf16[3,4,2,16,192]{4,1,3,2,0:T(4,128)(2,1)S(1)}, bf16[3,4,2,16,192]{4,1,3,2,0:T(4,128)(2,1)}, u32[]{:S(2)}) copy-start(bf16[3,4,2,16,192]{4,1,3,2,0:T(4,128)(2,1)} %fusion.27) | copy-start | bytes 442372
  93.0 13.4 %copy-start.1 = (bf16[1,2,4,16,192]{4,3,2,1,0:T(8,128)(2,1)S(1)}, bf16[1,2,4,16,192]{4,3,2,1,0:T(8,128)(2,1)}, u32[]{:S(2)}) copy-start(bf16[1,2,4,16,192]{4,3,2,1,0:T(8,128)(2,1)} %param.5) | copy-start | bytes 147460
  93.0 13.4 %copy-start.4 = (f32[2,4,16,192]{3,1,2,0:T(4,128)S(1)}, f32[2,4,16,192]{3,1,2,0:T(4,128)}, u32[]{:S(2)}) copy-start(f32[2,4,16,192]{3,1,2,0:T(4,128)} %get-tuple-element.17) | copy-start | bytes 294916
  96.4 22.5 %copy-start.9 = (pred[16,3]{0,1:T(4,128)(4,1)S(1)}, pred[16,3]{0,1:T(4,128)(4,1)}, u32[]{:S(2)}) copy-start(pred[16,3]{0,1:T(4,128)(4,1)} %constant.183) | copy-start | bytes 148
  96.5 10.6 %collective-permute-start.12 = (f32[32,6,432]{2,0,1:T(8,128)S(1)}, f32[32,6,432]{2,0,1:T(8,128)S(1)}, u32[]{:S(2)}, u32[]{:S(2)}) collective-permute-start(f32[32,6,432]{2,0,1:T(8,128)S(1)} %dynamic-slice_bitcast_fusion), channel_id=1, source_target_pairs={{0,1},{1,0},{2,3},{3,2},{4,5},{5,4},{6,7},{7,6},{8,9},{9,8},{10,11... | collective-permute-start | bytes 995336 | tf_op jit(solution)/shard_map/ppermute | solution.py:146
  108.2 26.3 %all-to-all-start = ((f32[32,6,432]{2,1,0:T(8,128)}), f32[32,6,432]{2,1,0:T(8,128)S(1)}, u32[]{:S(2)}, u32[]{:S(2)}) async-start(f32[32,6,432]{2,1,0:T(8,128)} %copy.81), calls=%async_computation | async-start | bytes 1048576 | tf_op jit(solution)/shard_map/all_to_all | solution.py:147

commit v7 on v6

--- a/solution.py
+++ b/solution.py
@@ -19,20 +19,20 @@
     return [(i, (i + step) % size) for i in range(size)]
 
 
-def ring_gather(block, axis, first_behind):
+def ring_blocks(block, axis, first_behind):
     size = lax.axis_size(axis)
-    from_ahead = []
-    from_behind_list = [first_behind]
-    for unused in range(size // 2 - 1):
-        from_behind_list.append(lax.ppermute(from_behind_list[-1], axis, ring_route(axis, 1)))
+    relative = [None] * size
+    relative[0] = block
+    relative[size - 1] = first_behind
+    moving = first_behind
+    for step in range(2, size // 2 + 1):
+        moving = lax.ppermute(moving, axis, ring_route(axis, 1))
+        relative[size - step] = moving
     moving = block
-    for unused in range(size - 1 - size // 2):
+    for step in range(1, size - size // 2):
         moving = lax.ppermute(moving, axis, ring_route(axis, -1))
-        from_ahead.append(moving)
-    relative = [block] + from_ahead + from_behind_list[::-1]
-    stacked = jnp.stack(relative, axis=0)
-    ordered = jnp.roll(stacked, lax.axis_index(axis), axis=0)
-    return ordered.reshape((-1,) + block.shape[1:])
+        relative[step] = moving
+    return relative
 
 
 def activate(video, norm_gain):
@@ -114,29 +114,41 @@
     slab_start = lax.axis_index("tm") * slab_rows
     tap_lo = slab_start // channels
     slab_offset = slab_start - tap_lo * channels
-    group_both = ring_gather(both, "tm", first_behind)
-    group_video = activate(group_both[..., :channels], norm_gain).astype(jnp.bfloat16)
-    group_cot = group_both[..., channels:]
-    group_frames = group_video.shape[0]
-    group_mask = make_mask(clip_ids[0], 0, group_frames).astype(jnp.bfloat16)
-    group_pad = jnp.pad(group_video, ((2, 0), (1, 1), (1, 1), (0, 0)))
+    blocks = ring_blocks(both, "tm", first_behind)
+    block_acts = [activated] + [
+        activate(block[..., :channels], norm_gain).astype(jnp.bfloat16) for block in blocks[1:-1]
+    ] + [previous]
+    group_mask = make_mask(clip_ids[0], 0, frames * chain_len).astype(jnp.bfloat16)
     tap_count = -(-(slab_rows + channels - 1) // channels)
-    columns = []
+    tap_params = []
     for step in range(tap_count):
         tap = jnp.minimum(tap_lo + step, 26)
-        tap_t, tap_h, tap_w = (tap // 9, tap // 3 % 3, tap % 3)
-        window = lax.dynamic_slice(
-            group_pad, (tap_t, tap_h, tap_w, 0), (group_frames, height, width, channels)
+        tap_params.append((tap // 9, tap // 3 % 3, tap % 3))
+    me = lax.axis_index("tm")
+    total = None
+    for rel in range(chain_len):
+        ext_pad = jnp.pad(
+            jnp.concatenate([block_acts[rel - 1], block_acts[rel]]),
+            ((0, 0), (1, 1), (1, 1), (0, 0)),
         )
-        weight_t = lax.dynamic_index_in_dim(group_mask, tap_t, 1, keepdims=False)
-        columns.append((window * weight_t[:, None, None, None]).reshape(-1, channels))
-    slab_patches = lax.dynamic_slice_in_dim(jnp.concatenate(columns, axis=1), slab_offset, slab_rows, 1)
-    slab_t = lax.dot_general(
-        group_cot.reshape(-1, outputs),
-        slab_patches,
-        (((0,), (0,)), ((), ())),
-        preferred_element_type=jnp.float32,
-    )
+        owner = (me + rel) % chain_len
+        block_mask = lax.dynamic_slice_in_dim(group_mask, owner * frames, frames, 0)
+        columns = []
+        for tap_t, tap_h, tap_w in tap_params:
+            window = lax.dynamic_slice(
+                ext_pad, (tap_t, tap_h, tap_w, 0), (frames, height, width, channels)
+            )
+            weight_t = lax.dynamic_index_in_dim(block_mask, tap_t, 1, keepdims=False)
+            columns.append((window * weight_t[:, None, None, None]).reshape(-1, channels))
+        block_cot = blocks[rel][..., channels:].reshape(-1, outputs)
+        term = lax.dot_general(
+            block_cot,
+            jnp.concatenate(columns, axis=1),
+            (((0,), (0,)), ((), ())),
+            preferred_element_type=jnp.float32,
+        )
+        total = term if total is None else total + term
+    slab_t = lax.dynamic_slice_in_dim(total, slab_offset, slab_rows, 1)
     chips = lax.axis_size("dq")
     cores = lax.axis_size("dc")
     pieces = slab_t.reshape(chips, cores, outputs // (chips * cores), slab_rows)

time: 136 us -> 134 us (0.985)
  local copies, waits for them, and re-layouts: 22.9 us -> 12.3 us
  waiting for transfers between devices: 25.4 us -> 32.8 us
  starting transfers between devices: 65.2 us -> 62.2 us
  matrix products: 10.2 us -> 12.4 us
    ppermute x10, waiting for transfers between devices: 13.5 us -> 20.9 us  [the longest x5 18.3 us: ring_blocks(): moving = lax.ppermute(moving, axis, ring_route(axis, 1))]
    reshape x4 -> x1, local copies, waits for them, and re-layouts: 5.43 us -> 0.12 us  [shards(): pieces = slab_t.reshape(chips, cores, outputs // (chips * cores), slab_rows)]
    ppermute x10, starting transfers between devices: 43.1 us -> 39.8 us  [the longest x5 25.5 us: ring_blocks(): moving = lax.ppermute(moving, axis, ring_route(axis, -1))]
    unnamed x51 -> x16, local copies, waits for them, and re-layouts: 6.08 us -> 3.47 us
    dot_general x1 -> x12, matrix products: 3.41 us -> 5.62 us  [shards(): lax.dot_general(block_cot, jnp.concatenate(columns, axis=1), (((0,), (0,)...]
    dot_general x2 -> x0, local copies, waits for them, and re-layouts: 2 us -> none  [shards(): lax.dot_general(group_cot.reshape(-1, outputs), slab_patches, (((0,), (0,...]
    mul x2 -> x13, other arithmetic: 3.65 us -> 2.93 us  [shards(): window * weight_t[:, None, None, None]]
  transfers between devices with their start and end apart: 14 -> 14, of which waited for: 7 -> 11; matrix products, arithmetic and copies ran while one was open for 15% -> 16% of each run, Pallas kernels for 0% -> 0%
where the time goes in v7:
time: 134 us; the launch traced here: 133 us
  starting transfers between devices  62.2 us (46%)
  waiting for transfers between devices  32.8 us (24%)
  matrix products  12.4 us (9%)
  local copies, waits for them, and re-layouts  12.3 us (9%)
  other arithmetic  10.2 us (8%)
  between operations  2.72 us (2%)
    ppermute x5, starting transfers between devices, ring_blocks(): moving = lax.ppermute(moving, axis, ring_route(axis, -1))  25.5 us
    ppermute x5, waiting for transfers between devices, ring_blocks(): moving = lax.ppermute(moving, axis, ring_route(axis, 1))  18.3 us
    ppermute x5, starting transfers between devices, ring_blocks(): moving = lax.ppermute(moving, axis, ring_route(axis, 1))  14.3 us
    all_to_all x1, waiting for transfers between devices, shards(): reduced_t = lax.all_to_all(pair_sum, 'dq', 0, 0, tiled=False).sum(axis=0)  11.3 us
    all_to_all x1, starting transfers between devices, shards(): reduced_t = lax.all_to_all(pair_sum, 'dq', 0, 0, tiled=False).sum(axis=0)  9.67 us
    ppermute x1, starting transfers between devices, shards(): pair_sum = kept + lax.ppermute(sent, 'dc', [(0, 1), (1, 0)])  9.54 us
    dot_general x12, matrix products, shards(): lax.dot_general(block_cot, jnp.concatenate(columns, axis=1), (((0,), (0,)...  5.62 us
    unnamed x16, local copies, waits for them, and re-layouts  3.47 us
  transfers between devices with their start and end apart: 14, of which 11 were waited for; matrix products, arithmetic and copies ran while one was open for 16% of the time, Pallas kernels for 0%

profile of v7, /device:TPU:1, one launch (start us, length us, event | category | flops | bytes accessed | tf_op | source)
XLA Modules:
  0.0 132.7 jit_solution(7720372606014587928)
XLA Ops:
  0.6 0.9 copy.133
  1.6 0.9 copy.132
  2.6 15.1 %collective-permute-start.2 = (bf16[2,4,16,576]{3,1,2,0:T(4,128)(2,1)S(1)}, bf16[2,4,16,576]{3,1,2,0:T(4,128)(2,1)S(1)}, u32[]{:S(2)}, u32[]{:S(2)}) collective-permute-start(bf16[2,4,16,576]{3,1,2,0:T(4,128)(2,1)S(1)} %pad_maximum_fusion), channel_id=1, source_target_pairs={{0,704},{64,0},{128,64},{192,128},{256,192},{320,256},{384,320},{4... | collective-permute-start | bytes 442376 | tf_op jit(solution)/shard_map/ppermute | solution.py:33
  17.8 1.9 %collective-permute-start = (bf16[2,4,16,576]{3,1,2,0:T(4,128)(2,1)S(1)}, bf16[2,4,16,576]{3,1,2,0:T(4,128)(2,1)S(1)}, u32[]{:S(2)}, u32[]{:S(2)}) collective-permute-start(bf16[2,4,16,576]{3,1,2,0:T(4,128)(2,1)S(1)} %pad_maximum_fusion), channel_id=1, source_target_pairs={{0,64},{64,128},{128,192},{192,256},{256,320},{320,384},{384,448},... | collective-permute-start | bytes 442376 | tf_op jit(solution)/shard_map/ppermute | solution.py:76
  19.8 0.7 pad_dynamic-slice_fusion.4
  22.8 3.4 %fusion = f32[3,4,16,3,192]{4,2,3,1,0:T(8,128)S(1)} fusion(bf16[3,3,3,192,384]{4,3,2,1,0:T(8,128)(2,1)} %bitcast.153, f32[3,4,16,3,192]{4,1,3,2,0:T(4,128)S(1)} %bitcast.155, pred[16,3]{0,1:T(4,128)(4,1)S(1)} %copy-done.2, bf16[1,4,2,8,5,384]{5,2,4,3,1,0:T(2,128)(2,1)S(1)} %fusion.8), kind=kOutput, calls=%fused_computation.12 | convolution fusion | flops 637231104 | bytes 5111856 | tf_op jit(solution)/shard_map/conv_general_dilated | solution.py:93
  26.8 1.3 collective-permute-start.1
  29.3 0.7 gather_fusion.3
  30.0 1.2 gather_fusion.2
  31.4 0.7 dynamic-slice_reduce_fusion.27
  32.7 4.6 %collective-permute-start.3 = (bf16[2,4,16,576]{3,1,2,0:T(4,128)(2,1)S(1)}, bf16[2,4,16,576]{3,1,2,0:T(4,128)(2,1)S(1)}, u32[]{:S(2)}, u32[]{:S(2)}) collective-permute-start(bf16[2,4,16,576]{3,1,2,0:T(4,128)(2,1)S(1)} %collective-permute-done.2), channel_id=1, source_target_pairs={{0,704},{64,0},{128,64},{192,128},{256,192},{320,256},{384,320},{4... | collective-permute-start | bytes 442376 | tf_op jit(solution)/shard_map/ppermute | solution.py:33
  37.4 1.9 %collective-permute-start.7 = (bf16[2,4,16,576]{3,1,2,0:T(4,128)(2,1)S(1)}, bf16[2,4,16,576]{3,1,2,0:T(4,128)(2,1)S(1)}, u32[]{:S(2)}, u32[]{:S(2)}) collective-permute-start(bf16[2,4,16,576]{3,1,2,0:T(4,128)(2,1)S(1)} %collective-permute-done), channel_id=1, source_target_pairs={{0,64},{64,128},{128,192},{192,256},{256,320},{320,384},{384,448},... | collective-permute-start | bytes 442376 | tf_op jit(solution)/shard_map/ppermute | solution.py:29
  40.3 4.4 %collective-permute-done.7 = bf16[2,4,16,576]{3,1,2,0:T(4,128)(2,1)S(1)} collective-permute-done((bf16[2,4,16,576]{3,1,2,0:T(4,128)(2,1)S(1)}, bf16[2,4,16,576]{3,1,2,0:T(4,128)(2,1)S(1)}, u32[]{:S(2)}, u32[]{:S(2)}) %collective-permute-start.7) | collective-permute-done | bytes 147488 | tf_op jit(solution)/shard_map/ppermute | solution.py:29
  44.9 1.9 %collective-permute-start.4 = (bf16[2,4,16,576]{3,1,2,0:T(4,128)(2,1)S(1)}, bf16[2,4,16,576]{3,1,2,0:T(4,128)(2,1)S(1)}, u32[]{:S(2)}, u32[]{:S(2)}) collective-permute-start(bf16[2,4,16,576]{3,1,2,0:T(4,128)(2,1)S(1)} %collective-permute-done.3), channel_id=1, source_target_pairs={{0,704},{64,0},{128,64},{192,128},{256,192},{320,256},{384,320},{4... | collective-permute-start | bytes 442376 | tf_op jit(solution)/shard_map/ppermute | solution.py:33
  46.9 3.4 %collective-permute-start.8 = (bf16[2,4,16,576]{3,1,2,0:T(4,128)(2,1)S(1)}, bf16[2,4,16,576]{3,1,2,0:T(4,128)(2,1)S(1)}, u32[]{:S(2)}, u32[]{:S(2)}) collective-permute-start(bf16[2,4,16,576]{3,1,2,0:T(4,128)(2,1)S(1)} %collective-permute-done.7), channel_id=1, source_target_pairs={{0,64},{64,128},{128,192},{192,256},{256,320},{320,384},{384,448},... | collective-permute-start | bytes 442376 | tf_op jit(solution)/shard_map/ppermute | solution.py:29
  51.2 3.0 %collective-permute-done.8 = bf16[2,4,16,576]{3,1,2,0:T(4,128)(2,1)S(1)} collective-permute-done((bf16[2,4,16,576]{3,1,2,0:T(4,128)(2,1)S(1)}, bf16[2,4,16,576]{3,1,2,0:T(4,128)(2,1)S(1)}, u32[]{:S(2)}, u32[]{:S(2)}) %collective-permute-start.8) | collective-permute-done | bytes 147488 | tf_op jit(solution)/shard_map/ppermute | solution.py:29
  54.3 1.9 %collective-permute-start.5 = (bf16[2,4,16,576]{3,1,2,0:T(4,128)(2,1)S(1)}, bf16[2,4,16,576]{3,1,2,0:T(4,128)(2,1)S(1)}, u32[]{:S(2)}, u32[]{:S(2)}) collective-permute-start(bf16[2,4,16,576]{3,1,2,0:T(4,128)(2,1)S(1)} %collective-permute-done.4), channel_id=1, source_target_pairs={{0,704},{64,0},{128,64},{192,128},{256,192},{320,256},{384,320},{4... | collective-permute-start | bytes 442376 | tf_op jit(solution)/shard_map/ppermute | solution.py:33
  56.4 3.4 %collective-permute-start.9 = (bf16[2,4,16,576]{3,1,2,0:T(4,128)(2,1)S(1)}, bf16[2,4,16,576]{3,1,2,0:T(4,128)(2,1)S(1)}, u32[]{:S(2)}, u32[]{:S(2)}) collective-permute-start(bf16[2,4,16,576]{3,1,2,0:T(4,128)(2,1)S(1)} %collective-permute-done.8), channel_id=1, source_target_pairs={{0,64},{64,128},{128,192},{192,256},{256,320},{320,384},{384,448},... | collective-permute-start | bytes 442376 | tf_op jit(solution)/shard_map/ppermute | solution.py:29
  60.5 3.1 %collective-permute-done.9 = bf16[2,4,16,576]{3,1,2,0:T(4,128)(2,1)S(1)} collective-permute-done((bf16[2,4,16,576]{3,1,2,0:T(4,128)(2,1)S(1)}, bf16[2,4,16,576]{3,1,2,0:T(4,128)(2,1)S(1)}, u32[]{:S(2)}, u32[]{:S(2)}) %collective-permute-start.9) | collective-permute-done | bytes 147488 | tf_op jit(solution)/shard_map/ppermute | solution.py:29
  66.2 1.9 %collective-permute-start.6 = (bf16[2,4,16,576]{3,1,2,0:T(4,128)(2,1)S(1)}, bf16[2,4,16,576]{3,1,2,0:T(4,128)(2,1)S(1)}, u32[]{:S(2)}, u32[]{:S(2)}) collective-permute-start(bf16[2,4,16,576]{3,1,2,0:T(4,128)(2,1)S(1)} %collective-permute-done.5), channel_id=1, source_target_pairs={{0,704},{64,0},{128,64},{192,128},{256,192},{320,256},{384,320},{4... | collective-permute-start | bytes 442376 | tf_op jit(solution)/shard_map/ppermute | solution.py:33
  68.2 3.4 %collective-permute-start.10 = (bf16[2,4,16,576]{3,1,2,0:T(4,128)(2,1)S(1)}, bf16[2,4,16,576]{3,1,2,0:T(4,128)(2,1)S(1)}, u32[]{:S(2)}, u32[]{:S(2)}) collective-permute-start(bf16[2,4,16,576]{3,1,2,0:T(4,128)(2,1)S(1)} %collective-permute-done.9), channel_id=1, source_target_pairs={{0,64},{64,128},{128,192},{192,256},{256,320},{320,384},{384,448},... | collective-permute-start | bytes 442376 | tf_op jit(solution)/shard_map/ppermute | solution.py:29
  71.5 0.7 collective-permute-done.6
  72.6 2.9 %collective-permute-done.10 = bf16[2,4,16,576]{3,1,2,0:T(4,128)(2,1)S(1)} collective-permute-done((bf16[2,4,16,576]{3,1,2,0:T(4,128)(2,1)S(1)}, bf16[2,4,16,576]{3,1,2,0:T(4,128)(2,1)S(1)}, u32[]{:S(2)}, u32[]{:S(2)}) %collective-permute-start.10) | collective-permute-done | bytes 147488 | tf_op jit(solution)/shard_map/ppermute | solution.py:29
  75.7 2.3 %collective-permute-start.11 = (bf16[2,4,16,576]{3,1,2,0:T(4,128)(2,1)S(1)}, bf16[2,4,16,576]{3,1,2,0:T(4,128)(2,1)S(1)}, u32[]{:S(2)}, u32[]{:S(2)}) collective-permute-start(bf16[2,4,16,576]{3,1,2,0:T(4,128)(2,1)S(1)} %collective-permute-done.10), channel_id=1, source_target_pairs={{0,64},{64,128},{128,192},{192,256},{256,320},{320,384},{384,448},... | collective-permute-start | bytes 442376 | tf_op jit(solution)/shard_map/ppermute | solution.py:29
  78.1 4.9 %collective-permute-done.11 = bf16[2,4,16,576]{3,1,2,0:T(4,128)(2,1)S(1)} collective-permute-done((bf16[2,4,16,576]{3,1,2,0:T(4,128)(2,1)S(1)}, bf16[2,4,16,576]{3,1,2,0:T(4,128)(2,1)S(1)}, u32[]{:S(2)}, u32[]{:S(2)}) %collective-permute-start.11) | collective-permute-done | bytes 147488 | tf_op jit(solution)/shard_map/ppermute | solution.py:29
  83.1 0.9 fusion.181
  84.9 0.8 select_maximum_fusion.6
  93.8 9.5 %collective-permute-start.12 = (f32[32,6,432]{2,1,0:T(8,128)S(1)}, f32[32,6,432]{2,1,0:T(8,128)S(1)}, u32[]{:S(2)}, u32[]{:S(2)}) collective-permute-start(f32[32,6,432]{2,1,0:T(8,128)S(1)} %dynamic-slice_bitcast_fusion), channel_id=1, source_target_pairs={{0,1},{1,0},{2,3},{3,2},{4,5},{5,4},{6,7},{7,6},{8,9},{9,8},{10,11... | collective-permute-start | bytes 995336 | tf_op jit(solution)/shard_map/ppermute | solution.py:158
  104.9 0.9 bitcast_add_fusion
  105.8 9.7 %all-to-all-start = ((f32[32,6,432]{2,1,0:T(8,128)}), f32[32,6,432]{2,1,0:T(8,128)S(1)}, u32[]{:S(2)}, u32[]{:S(2)}) async-start(f32[32,6,432]{2,1,0:T(8,128)} %bitcast_add_fusion), calls=%async_computation | async-start | bytes 1048576 | tf_op jit(solution)/shard_map/all_to_all | solution.py:159
  116.5 3.4 %fusion.1 = bf16[1,4,16,3,384]{4,2,3,1,0:T(8,128)(2,1)S(1)} fusion(bf16[3,3,3,192,384]{4,3,2,1,0:T(8,128)(2,1)} %bitcast.154, bf16[3,4,2,8,5,192]{5,2,4,3,1,0:T(2,128)(2,1)S(1)} %fusion.5, pred[16,3]{0,1:T(4,128)(4,1)S(1)} %copy-done.2), kind=kOutput, calls=%fused_computation.14 | convolution fusion | flops 637157376 | bytes 4497456 | tf_op jit(solution)/shard_map/conv_general_dilated | solution.py:85
  120.7 11.3 %all-to-all-done = f32[32,6,432]{2,1,0:T(8,128)S(1)} async-done(((f32[32,6,432]{2,1,0:T(8,128)}), f32[32,6,432]{2,1,0:T(8,128)S(1)}, u32[]{:S(2)}, u32[]{:S(2)}) %all-to-all-start) | async-done | bytes 331808 | tf_op jit(solution)/shard_map/all_to_all | solution.py:159
  (191 shorter events, 22.9 us)
Async XLA Ops:
  0.6 21.5 %copy-start.1 = (bf16[1,2,4,16,384]{4,3,2,1,0:T(8,128)(2,1)S(1)}, bf16[1,2,4,16,384]{4,3,2,1,0:T(8,128)(2,1)}, u32[]{:S(2)}) copy-start(bf16[1,2,4,16,384]{4,3,2,1,0:T(8,128)(2,1)} %param.9) | copy-start | bytes 294916
  2.6 29.6 %collective-permute-start.2 = (bf16[2,4,16,576]{3,1,2,0:T(4,128)(2,1)S(1)}, bf16[2,4,16,576]{3,1,2,0:T(4,128)(2,1)S(1)}, u32[]{:S(2)}, u32[]{:S(2)}) collective-permute-start(bf16[2,4,16,576]{3,1,2,0:T(4,128)(2,1)S(1)} %pad_maximum_fusion), channel_id=1, source_target_pairs={{0,704},{64,0},{128,64},{192,128},{256,192},{320,256},{384,320},{4... | collective-permute-start | bytes 442376 | tf_op jit(solution)/shard_map/ppermute | solution.py:33
  17.8 14.8 %collective-permute-start = (bf16[2,4,16,576]{3,1,2,0:T(4,128)(2,1)S(1)}, bf16[2,4,16,576]{3,1,2,0:T(4,128)(2,1)S(1)}, u32[]{:S(2)}, u32[]{:S(2)}) collective-permute-start(bf16[2,4,16,576]{3,1,2,0:T(4,128)(2,1)S(1)} %pad_maximum_fusion), channel_id=1, source_target_pairs={{0,64},{64,128},{128,192},{192,256},{256,320},{320,384},{384,448},... | collective-permute-start | bytes 442376 | tf_op jit(solution)/shard_map/ppermute | solution.py:76
  21.2 1.6 %copy-start.2 = (pred[16,3]{0,1:T(4,128)(4,1)S(1)}, pred[16,3]{0,1:T(4,128)(4,1)}, u32[]{:S(2)}) copy-start(pred[16,3]{0,1:T(4,128)(4,1)} %constant.813) | copy-start | bytes 148
  26.5 2.1 %copy-start.4 = (s32[1,24]{1,0:T(1,128)S(1)}, s32[1,24]{1,0:T(1,128)}, u32[]{:S(2)}) copy-start(s32[1,24]{1,0:T(1,128)} %param.6) | copy-start | bytes 292
  26.5 2.2 %copy-start = (bf16[1,2,4,16,192]{4,3,2,1,0:T(8,128)(2,1)S(1)}, bf16[1,2,4,16,192]{4,3,2,1,0:T(8,128)(2,1)}, u32[]{:S(2)}) copy-start(bf16[1,2,4,16,192]{4,3,2,1,0:T(8,128)(2,1)} %param.5) | copy-start | bytes 147460
  26.8 56.3 %collective-permute-start.1 = (f32[2,4,16,192]{3,1,2,0:T(4,128)S(1)}, f32[2,4,16,192]{3,1,2,0:T(4,128)S(1)}, u32[]{:S(2)}, u32[]{:S(2)}) collective-permute-start(f32[2,4,16,192]{3,1,2,0:T(4,128)S(1)} %slice.142), channel_id=1, source_target_pairs={{64,0},{128,64},{192,128},{256,192},{320,256},{384,320},{448,384},... | collective-permute-start | bytes 294920 | tf_op jit(solution)/shard_map/ppermute | solution.py:14
  30.0 2.1 %copy-start.3 = (f32[192]{0:T(256)S(1)}, f32[192]{0:T(256)}, u32[]{:S(2)}) copy-start(f32[192]{0:T(256)} %param.7) | copy-start | bytes 2308
  32.7 7.3 %collective-permute-start.3 = (bf16[2,4,16,576]{3,1,2,0:T(4,128)(2,1)S(1)}, bf16[2,4,16,576]{3,1,2,0:T(4,128)(2,1)S(1)}, u32[]{:S(2)}, u32[]{:S(2)}) collective-permute-start(bf16[2,4,16,576]{3,1,2,0:T(4,128)(2,1)S(1)} %collective-permute-done.2), channel_id=1, source_target_pairs={{0,704},{64,0},{128,64},{192,128},{256,192},{320,256},{384,320},{4... | collective-permute-start | bytes 442376 | tf_op jit(solution)/shard_map/ppermute | solution.py:33
  37.4 7.3 %collective-permute-start.7 = (bf16[2,4,16,576]{3,1,2,0:T(4,128)(2,1)S(1)}, bf16[2,4,16,576]{3,1,2,0:T(4,128)(2,1)S(1)}, u32[]{:S(2)}, u32[]{:S(2)}) collective-permute-start(bf16[2,4,16,576]{3,1,2,0:T(4,128)(2,1)S(1)} %collective-permute-done), channel_id=1, source_target_pairs={{0,64},{64,128},{128,192},{192,256},{256,320},{320,384},{384,448},... | collective-permute-start | bytes 442376 | tf_op jit(solution)/shard_map/ppermute | solution.py:29
  44.9 6.1 %collective-permute-start.4 = (bf16[2,4,16,576]{3,1,2,0:T(4,128)(2,1)S(1)}, bf16[2,4,16,576]{3,1,2,0:T(4,128)(2,1)S(1)}, u32[]{:S(2)}, u32[]{:S(2)}) collective-permute-start(bf16[2,4,16,576]{3,1,2,0:T(4,128)(2,1)S(1)} %collective-permute-done.3), channel_id=1, source_target_pairs={{0,704},{64,0},{128,64},{192,128},{256,192},{320,256},{384,320},{4... | collective-permute-start | bytes 442376 | tf_op jit(solution)/shard_map/ppermute | solution.py:33
  46.9 7.3 %collective-permute-start.8 = (bf16[2,4,16,576]{3,1,2,0:T(4,128)(2,1)S(1)}, bf16[2,4,16,576]{3,1,2,0:T(4,128)(2,1)S(1)}, u32[]{:S(2)}, u32[]{:S(2)}) collective-permute-start(bf16[2,4,16,576]{3,1,2,0:T(4,128)(2,1)S(1)} %collective-permute-done.7), channel_id=1, source_target_pairs={{0,64},{64,128},{128,192},{192,256},{256,320},{320,384},{384,448},... | collective-permute-start | bytes 442376 | tf_op jit(solution)/shard_map/ppermute | solution.py:29
  54.3 6.1 %collective-permute-start.5 = (bf16[2,4,16,576]{3,1,2,0:T(4,128)(2,1)S(1)}, bf16[2,4,16,576]{3,1,2,0:T(4,128)(2,1)S(1)}, u32[]{:S(2)}, u32[]{:S(2)}) collective-permute-start(bf16[2,4,16,576]{3,1,2,0:T(4,128)(2,1)S(1)} %collective-permute-done.4), channel_id=1, source_target_pairs={{0,704},{64,0},{128,64},{192,128},{256,192},{320,256},{384,320},{4... | collective-permute-start | bytes 442376 | tf_op jit(solution)/shard_map/ppermute | solution.py:33
  56.4 7.3 %collective-permute-start.9 = (bf16[2,4,16,576]{3,1,2,0:T(4,128)(2,1)S(1)}, bf16[2,4,16,576]{3,1,2,0:T(4,128)(2,1)S(1)}, u32[]{:S(2)}, u32[]{:S(2)}) collective-permute-start(bf16[2,4,16,576]{3,1,2,0:T(4,128)(2,1)S(1)} %collective-permute-done.8), channel_id=1, source_target_pairs={{0,64},{64,128},{128,192},{192,256},{256,320},{320,384},{384,448},... | collective-permute-start | bytes 442376 | tf_op jit(solution)/shard_map/ppermute | solution.py:29
  66.2 6.1 %collective-permute-start.6 = (bf16[2,4,16,576]{3,1,2,0:T(4,128)(2,1)S(1)}, bf16[2,4,16,576]{3,1,2,0:T(4,128)(2,1)S(1)}, u32[]{:S(2)}, u32[]{:S(2)}) collective-permute-start(bf16[2,4,16,576]{3,1,2,0:T(4,128)(2,1)S(1)} %collective-permute-done.5), channel_id=1, source_target_pairs={{0,704},{64,0},{128,64},{192,128},{256,192},{320,256},{384,320},{4... | collective-permute-start | bytes 442376 | tf_op jit(solution)/shard_map/ppermute | solution.py:33
  68.2 7.3 %collective-permute-start.10 = (bf16[2,4,16,576]{3,1,2,0:T(4,128)(2,1)S(1)}, bf16[2,4,16,576]{3,1,2,0:T(4,128)(2,1)S(1)}, u32[]{:S(2)}, u32[]{:S(2)}) collective-permute-start(bf16[2,4,16,576]{3,1,2,0:T(4,128)(2,1)S(1)} %collective-permute-done.9), channel_id=1, source_target_pairs={{0,64},{64,128},{128,192},{192,256},{256,320},{320,384},{384,448},... | collective-permute-start | bytes 442376 | tf_op jit(solution)/shard_map/ppermute | solution.py:29
  75.7 7.3 %collective-permute-start.11 = (bf16[2,4,16,576]{3,1,2,0:T(4,128)(2,1)S(1)}, bf16[2,4,16,576]{3,1,2,0:T(4,128)(2,1)S(1)}, u32[]{:S(2)}, u32[]{:S(2)}) collective-permute-start(bf16[2,4,16,576]{3,1,2,0:T(4,128)(2,1)S(1)} %collective-permute-done.10), channel_id=1, source_target_pairs={{0,64},{64,128},{128,192},{192,256},{256,320},{320,384},{384,448},... | collective-permute-start | bytes 442376 | tf_op jit(solution)/shard_map/ppermute | solution.py:29
  93.8 11.1 %collective-permute-start.12 = (f32[32,6,432]{2,1,0:T(8,128)S(1)}, f32[32,6,432]{2,1,0:T(8,128)S(1)}, u32[]{:S(2)}, u32[]{:S(2)}) collective-permute-start(f32[32,6,432]{2,1,0:T(8,128)S(1)} %dynamic-slice_bitcast_fusion), channel_id=1, source_target_pairs={{0,1},{1,0},{2,3},{3,2},{4,5},{5,4},{6,7},{7,6},{8,9},{9,8},{10,11... | collective-permute-start | bytes 995336 | tf_op jit(solution)/shard_map/ppermute | solution.py:158
  105.8 26.3 %all-to-all-start = ((f32[32,6,432]{2,1,0:T(8,128)}), f32[32,6,432]{2,1,0:T(8,128)S(1)}, u32[]{:S(2)}, u32[]{:S(2)}) async-start(f32[32,6,432]{2,1,0:T(8,128)} %bitcast_add_fusion), calls=%async_computation | async-start | bytes 1048576 | tf_op jit(solution)/shard_map/all_to_all | solution.py:159

commit v8 on v7

--- a/solution.py
+++ b/solution.py
@@ -114,19 +114,21 @@
     slab_start = lax.axis_index("tm") * slab_rows
     tap_lo = slab_start // channels
     slab_offset = slab_start - tap_lo * channels
-    blocks = ring_blocks(both, "tm", first_behind)
-    block_acts = [activated] + [
-        activate(block[..., :channels], norm_gain).astype(jnp.bfloat16) for block in blocks[1:-1]
-    ] + [previous]
     group_mask = make_mask(clip_ids[0], 0, frames * chain_len).astype(jnp.bfloat16)
-    tap_count = -(-(slab_rows + channels - 1) // channels)
+    tap_count = max(
+        -(-(slab_rows * index % channels + slab_rows) // channels) for index in range(chain_len)
+    )
     tap_params = []
     for step in range(tap_count):
         tap = jnp.minimum(tap_lo + step, 26)
         tap_params.append((tap // 9, tap // 3 % 3, tap % 3))
     me = lax.axis_index("tm")
-    total = None
-    for rel in range(chain_len):
+    blocks = [None] * chain_len
+    block_acts = [None] * chain_len
+    blocks[0], block_acts[0] = both, activated
+    blocks[-1], block_acts[-1] = first_behind, previous
+
+    def block_term(rel):
         ext_pad = jnp.pad(
             jnp.concatenate([block_acts[rel - 1], block_acts[rel]]),
             ((0, 0), (1, 1), (1, 1), (0, 0)),
@@ -141,13 +143,48 @@
             weight_t = lax.dynamic_index_in_dim(block_mask, tap_t, 1, keepdims=False)
             columns.append((window * weight_t[:, None, None, None]).reshape(-1, channels))
         block_cot = blocks[rel][..., channels:].reshape(-1, outputs)
-        term = lax.dot_general(
+        return lax.dot_general(
             block_cot,
             jnp.concatenate(columns, axis=1),
             (((0,), (0,)), ((), ())),
             preferred_element_type=jnp.float32,
         )
-        total = term if total is None else total + term
+
+    pending = list(range(chain_len))
+
+    def add_ready(total):
+        for rel in list(pending):
+            if block_acts[rel] is not None and block_acts[rel - 1] is not None:
+                term = block_term(rel)
+                total = term if total is None else total + term
+                pending.remove(rel)
+        return total
+
+    total = None
+    forward_steps = chain_len // 2
+    backward_steps = chain_len - 1 - forward_steps
+    forward_moving = first_behind
+    backward_moving = lax.ppermute(both, "tm", ring_route("tm", -1))
+    arrived = [(chain_len - 1, None), (1, backward_moving)]
+    for step in range(2, forward_steps + 1):
+        total = add_ready(total)
+        if total is not None:
+            forward_moving, backward_moving, total = lax.optimization_barrier(
+                (forward_moving, backward_moving, total)
+            )
+        for rel, block in arrived:
+            if block is not None:
+                blocks[rel] = block
+                block_acts[rel] = activate(block[..., :channels], norm_gain).astype(jnp.bfloat16)
+        forward_moving = lax.ppermute(forward_moving, "tm", ring_route("tm", 1))
+        arrived = [(chain_len - step, forward_moving)]
+        if step <= backward_steps:
+            backward_moving = lax.ppermute(backward_moving, "tm", ring_route("tm", -1))
+            arrived.append((step, backward_moving))
+    for rel, block in arrived:
+        blocks[rel] = block
+        block_acts[rel] = activate(block[..., :channels], norm_gain).astype(jnp.bfloat16)
+    total = add_ready(total)
     slab_t = lax.dynamic_slice_in_dim(total, slab_offset, slab_rows, 1)
     chips = lax.axis_size("dq")
     cores = lax.axis_size("dc")

time: 134 us -> 129 us (0.963)
  waiting for transfers between devices: 32.8 us -> 24.7 us
  starting transfers between devices: 62.2 us -> 66.5 us
    ppermute x10, waiting for transfers between devices: 20.9 us -> 9.15 us  [the longest x4 4.99 us: shards(): backward_moving = lax.ppermute(backward_moving, 'tm', ring_route('tm', -1))]
    ppermute x10, starting transfers between devices: 39.8 us -> 44.7 us  [the longest x4 17.3 us: shards(): backward_moving = lax.ppermute(backward_moving, 'tm', ring_route('tm', -1))]
    all_to_all x1, waiting for transfers between devices: 11.3 us -> 15.3 us  [shards(): reduced_t = lax.all_to_all(pair_sum, 'dq', 0, 0, tiled=False).sum(axis=0)]
    mul x13 -> x12, other arithmetic: 2.93 us -> 2.28 us  [block_term(): window * weight_t[:, None, None, None]]
  transfers between devices with their start and end apart: 14 -> 14, of which waited for: 11 -> 7; matrix products, arithmetic and copies ran while one was open for 16% -> 17% of each run, Pallas kernels for 0% -> 0%
where the time goes in v8:
time: 129 us
  starting transfers between devices  66.5 us (52%)
  waiting for transfers between devices  24.7 us (19%)
  local copies, waits for them, and re-layouts  13 us (10%)
  matrix products  11.8 us (9%)
  other arithmetic  10.1 us (8%)
  between operations  2.54 us (2%)
    ppermute x4, starting transfers between devices, shards(): backward_moving = lax.ppermute(backward_moving, 'tm', ring_route('tm', -1))  17.3 us
    all_to_all x1, waiting for transfers between devices, shards(): reduced_t = lax.all_to_all(pair_sum, 'dq', 0, 0, tiled=False).sum(axis=0)  15.3 us
    ppermute x1, starting transfers between devices, shards(): backward_moving = lax.ppermute(both, 'tm', ring_route('tm', -1))  15.1 us
    ppermute x5, starting transfers between devices, shards(): forward_moving = lax.ppermute(forward_moving, 'tm', ring_route('tm', 1))  12.4 us
    all_to_all x1, starting transfers between devices, shards(): reduced_t = lax.all_to_all(pair_sum, 'dq', 0, 0, tiled=False).sum(axis=0)  9.67 us
    ppermute x1, starting transfers between devices, shards(): pair_sum = kept + lax.ppermute(sent, 'dc', [(0, 1), (1, 0)])  8.9 us
    ppermute x4, waiting for transfers between devices, shards(): backward_moving = lax.ppermute(backward_moving, 'tm', ring_route('tm', -1))  4.99 us
    dot_general x12, matrix products, block_term(): lax.dot_general(block_cot, jnp.concatenate(columns, axis=1), (((0,), (0,)...  4.96 us
  transfers between devices with their start and end apart: 14, of which 7 were waited for; matrix products, arithmetic and copies ran while one was open for 17% of the time, Pallas kernels for 0%

profile of v8, /device:TPU:1, one launch (start us, length us, event | category | flops | bytes accessed | tf_op | source)
XLA Modules:
  0.0 128.6 jit_solution(3328303638011263990)
XLA Ops:
  0.6 0.9 copy.120
  1.6 0.9 copy.121
  2.6 15.1 %collective-permute-start.2 = (bf16[2,4,16,576]{3,1,2,0:T(4,128)(2,1)S(1)}, bf16[2,4,16,576]{3,1,2,0:T(4,128)(2,1)S(1)}, u32[]{:S(2)}, u32[]{:S(2)}) collective-permute-start(bf16[2,4,16,576]{3,1,2,0:T(4,128)(2,1)S(1)} %pad_maximum_fusion), channel_id=1, source_target_pairs={{0,704},{64,0},{128,64},{192,128},{256,192},{320,256},{384,320},{4... | collective-permute-start | bytes 442376 | tf_op jit(solution)/shard_map/ppermute | solution.py:167
  17.8 1.9 %collective-permute-start = (bf16[2,4,16,576]{3,1,2,0:T(4,128)(2,1)S(1)}, bf16[2,4,16,576]{3,1,2,0:T(4,128)(2,1)S(1)}, u32[]{:S(2)}, u32[]{:S(2)}) collective-permute-start(bf16[2,4,16,576]{3,1,2,0:T(4,128)(2,1)S(1)} %pad_maximum_fusion), channel_id=1, source_target_pairs={{0,64},{64,128},{128,192},{192,256},{256,320},{320,384},{384,448},... | collective-permute-start | bytes 442376 | tf_op jit(solution)/shard_map/ppermute | solution.py:76
  19.8 0.7 pad_dynamic-slice_fusion.3
  20.5 0.6 gather_fusion
  21.3 0.6 gather_fusion.1
  22.1 1.0 copy.96
  23.7 3.4 %fusion = f32[3,4,16,3,192]{4,2,3,1,0:T(8,128)S(1)} fusion(bf16[3,3,3,192,384]{4,3,2,1,0:T(8,128)(2,1)} %bitcast.141, f32[3,4,16,3,192]{4,1,3,2,0:T(4,128)S(1)} %bitcast.143, pred[16,3]{0,1:T(4,128)(4,1)S(1)} %copy-done.3, bf16[1,4,2,8,5,384]{5,2,4,3,1,0:T(2,128)(2,1)S(1)} %fusion.8), kind=kOutput, calls=%fused_computation.7 | convolution fusion | flops 637231104 | bytes 5111856 | tf_op jit(solution)/shard_map/conv_general_dilated | solution.py:93
  27.7 1.3 %collective-permute-start.1 = (f32[2,4,16,192]{3,1,2,0:T(4,128)S(1)}, f32[2,4,16,192]{3,1,2,0:T(4,128)S(1)}, u32[]{:S(2)}, u32[]{:S(2)}) collective-permute-start(f32[2,4,16,192]{3,1,2,0:T(4,128)S(1)} %slice.142), channel_id=1, source_target_pairs={{64,0},{128,64},{192,128},{256,192},{320,256},{384,320},{448,384},... | collective-permute-start | bytes 294920 | tf_op jit(solution)/shard_map/ppermute | solution.py:14
  29.9 1.2 gather_fusion.2
  31.3 0.7 gather_fusion.3
  35.7 3.8 %collective-permute-start.3 = (bf16[2,4,16,576]{3,1,2,0:T(4,128)(2,1)S(1)}, bf16[2,4,16,576]{3,1,2,0:T(4,128)(2,1)S(1)}, u32[]{:S(2)}, u32[]{:S(2)}) collective-permute-start(bf16[2,4,16,576]{3,1,2,0:T(4,128)(2,1)S(1)} %collective-permute-done), channel_id=1, source_target_pairs={{0,64},{64,128},{128,192},{192,256},{256,320},{320,384},{384,448},... | collective-permute-start | bytes 442376 | tf_op jit(solution)/shard_map/ppermute | solution.py:179
  39.5 2.7 %collective-permute-start.4 = (bf16[2,4,16,576]{3,1,2,0:T(4,128)(2,1)S(1)}, bf16[2,4,16,576]{3,1,2,0:T(4,128)(2,1)S(1)}, u32[]{:S(2)}, u32[]{:S(2)}) collective-permute-start(bf16[2,4,16,576]{3,1,2,0:T(4,128)(2,1)S(1)} %collective-permute-done.2), channel_id=1, source_target_pairs={{0,704},{64,0},{128,64},{192,128},{256,192},{320,256},{384,320},{4... | collective-permute-start | bytes 442376 | tf_op jit(solution)/shard_map/ppermute | solution.py:182
  43.9 1.9 %collective-permute-done.4 = bf16[2,4,16,576]{3,1,2,0:T(4,128)(2,1)S(1)} collective-permute-done((bf16[2,4,16,576]{3,1,2,0:T(4,128)(2,1)S(1)}, bf16[2,4,16,576]{3,1,2,0:T(4,128)(2,1)S(1)}, u32[]{:S(2)}, u32[]{:S(2)}) %collective-permute-start.4) | collective-permute-done | bytes 147488 | tf_op jit(solution)/shard_map/ppermute | solution.py:182
  45.8 1.9 %collective-permute-start.5 = (bf16[2,4,16,576]{3,1,2,0:T(4,128)(2,1)S(1)}, bf16[2,4,16,576]{3,1,2,0:T(4,128)(2,1)S(1)}, u32[]{:S(2)}, u32[]{:S(2)}) collective-permute-start(bf16[2,4,16,576]{3,1,2,0:T(4,128)(2,1)S(1)} %collective-permute-done.3), channel_id=1, source_target_pairs={{0,64},{64,128},{128,192},{192,256},{256,320},{320,384},{384,448},... | collective-permute-start | bytes 442376 | tf_op jit(solution)/shard_map/ppermute | solution.py:179
  47.7 4.6 %collective-permute-start.6 = (bf16[2,4,16,576]{3,1,2,0:T(4,128)(2,1)S(1)}, bf16[2,4,16,576]{3,1,2,0:T(4,128)(2,1)S(1)}, u32[]{:S(2)}, u32[]{:S(2)}) collective-permute-start(bf16[2,4,16,576]{3,1,2,0:T(4,128)(2,1)S(1)} %collective-permute-done.4), channel_id=1, source_target_pairs={{0,704},{64,0},{128,64},{192,128},{256,192},{320,256},{384,320},{4... | collective-permute-start | bytes 442376 | tf_op jit(solution)/shard_map/ppermute | solution.py:182
  53.2 1.3 %collective-permute-done.6 = bf16[2,4,16,576]{3,1,2,0:T(4,128)(2,1)S(1)} collective-permute-done((bf16[2,4,16,576]{3,1,2,0:T(4,128)(2,1)S(1)}, bf16[2,4,16,576]{3,1,2,0:T(4,128)(2,1)S(1)}, u32[]{:S(2)}, u32[]{:S(2)}) %collective-permute-start.6) | collective-permute-done | bytes 147488 | tf_op jit(solution)/shard_map/ppermute | solution.py:182
  56.8 1.9 %collective-permute-start.7 = (bf16[2,4,16,576]{3,1,2,0:T(4,128)(2,1)S(1)}, bf16[2,4,16,576]{3,1,2,0:T(4,128)(2,1)S(1)}, u32[]{:S(2)}, u32[]{:S(2)}) collective-permute-start(bf16[2,4,16,576]{3,1,2,0:T(4,128)(2,1)S(1)} %collective-permute-done.5), channel_id=1, source_target_pairs={{0,64},{64,128},{128,192},{192,256},{256,320},{320,384},{384,448},... | collective-permute-start | bytes 442376 | tf_op jit(solution)/shard_map/ppermute | solution.py:179
  58.7 5.2 %collective-permute-start.8 = (bf16[2,4,16,576]{3,1,2,0:T(4,128)(2,1)S(1)}, bf16[2,4,16,576]{3,1,2,0:T(4,128)(2,1)S(1)}, u32[]{:S(2)}, u32[]{:S(2)}) collective-permute-start(bf16[2,4,16,576]{3,1,2,0:T(4,128)(2,1)S(1)} %collective-permute-done.6), channel_id=1, source_target_pairs={{0,704},{64,0},{128,64},{192,128},{256,192},{320,256},{384,320},{4... | collective-permute-start | bytes 442376 | tf_op jit(solution)/shard_map/ppermute | solution.py:182
  66.2 1.9 %collective-permute-start.9 = (bf16[2,4,16,576]{3,1,2,0:T(4,128)(2,1)S(1)}, bf16[2,4,16,576]{3,1,2,0:T(4,128)(2,1)S(1)}, u32[]{:S(2)}, u32[]{:S(2)}) collective-permute-start(bf16[2,4,16,576]{3,1,2,0:T(4,128)(2,1)S(1)} %collective-permute-done.7), channel_id=1, source_target_pairs={{0,64},{64,128},{128,192},{192,256},{256,320},{320,384},{384,448},... | collective-permute-start | bytes 442376 | tf_op jit(solution)/shard_map/ppermute | solution.py:179
  68.2 4.8 %collective-permute-start.10 = (bf16[2,4,16,576]{3,1,2,0:T(4,128)(2,1)S(1)}, bf16[2,4,16,576]{3,1,2,0:T(4,128)(2,1)S(1)}, u32[]{:S(2)}, u32[]{:S(2)}) collective-permute-start(bf16[2,4,16,576]{3,1,2,0:T(4,128)(2,1)S(1)} %collective-permute-done.8), channel_id=1, source_target_pairs={{0,704},{64,0},{128,64},{192,128},{256,192},{320,256},{384,320},{4... | collective-permute-start | bytes 442376 | tf_op jit(solution)/shard_map/ppermute | solution.py:182
  73.5 1.7 %collective-permute-done.10 = bf16[2,4,16,576]{3,1,2,0:T(4,128)(2,1)S(1)} collective-permute-done((bf16[2,4,16,576]{3,1,2,0:T(4,128)(2,1)S(1)}, bf16[2,4,16,576]{3,1,2,0:T(4,128)(2,1)S(1)}, u32[]{:S(2)}, u32[]{:S(2)}) %collective-permute-start.10) | collective-permute-done | bytes 147488 | tf_op jit(solution)/shard_map/ppermute | solution.py:182
  77.1 2.8 %collective-permute-start.11 = (bf16[2,4,16,576]{3,1,2,0:T(4,128)(2,1)S(1)}, bf16[2,4,16,576]{3,1,2,0:T(4,128)(2,1)S(1)}, u32[]{:S(2)}, u32[]{:S(2)}) collective-permute-start(bf16[2,4,16,576]{3,1,2,0:T(4,128)(2,1)S(1)} %collective-permute-done.9), channel_id=1, source_target_pairs={{0,64},{64,128},{128,192},{192,256},{256,320},{320,384},{384,448},... | collective-permute-start | bytes 442376 | tf_op jit(solution)/shard_map/ppermute | solution.py:179
  80.9 4.0 %collective-permute-done.11 = bf16[2,4,16,576]{3,1,2,0:T(4,128)(2,1)S(1)} collective-permute-done((bf16[2,4,16,576]{3,1,2,0:T(4,128)(2,1)S(1)}, bf16[2,4,16,576]{3,1,2,0:T(4,128)(2,1)S(1)}, u32[]{:S(2)}, u32[]{:S(2)}) %collective-permute-start.11) | collective-permute-done | bytes 147488 | tf_op jit(solution)/shard_map/ppermute | solution.py:179
  88.2 8.9 %collective-permute-start.12 = (f32[32,6,432]{2,1,0:T(8,128)S(1)}, f32[32,6,432]{2,1,0:T(8,128)S(1)}, u32[]{:S(2)}, u32[]{:S(2)}) collective-permute-start(f32[32,6,432]{2,1,0:T(8,128)S(1)} %dynamic-slice_bitcast_fusion), channel_id=1, source_target_pairs={{0,1},{1,0},{2,3},{3,2},{4,5},{5,4},{6,7},{7,6},{8,9},{9,8},{10,11... | collective-permute-start | bytes 995336 | tf_op jit(solution)/shard_map/ppermute | solution.py:195
  97.1 3.4 %fusion.1 = bf16[1,4,16,3,384]{4,2,3,1,0:T(8,128)(2,1)S(1)} fusion(bf16[3,3,3,192,384]{4,3,2,1,0:T(8,128)(2,1)} %bitcast.142, bf16[3,4,2,8,5,192]{5,2,4,3,1,0:T(2,128)(2,1)S(1)} %fusion.5, pred[16,3]{0,1:T(4,128)(4,1)S(1)} %copy-done.3), kind=kOutput, calls=%fused_computation.9 | convolution fusion | flops 637157376 | bytes 4497456 | tf_op jit(solution)/shard_map/conv_general_dilated | solution.py:85
  100.5 0.9 bitcast_add_fusion
  101.4 9.7 %all-to-all-start = ((f32[32,6,432]{2,1,0:T(8,128)}), f32[32,6,432]{2,1,0:T(8,128)S(1)}, u32[]{:S(2)}, u32[]{:S(2)}) async-start(f32[32,6,432]{2,1,0:T(8,128)} %bitcast_add_fusion), calls=%async_computation | async-start | bytes 1048576 | tf_op jit(solution)/shard_map/all_to_all | solution.py:196
  111.1 0.7 copy.93
  112.0 0.6 copy.94
  112.6 15.3 %all-to-all-done = f32[32,6,432]{2,1,0:T(8,128)S(1)} async-done(((f32[32,6,432]{2,1,0:T(8,128)}), f32[32,6,432]{2,1,0:T(8,128)S(1)}, u32[]{:S(2)}, u32[]{:S(2)}) %all-to-all-start) | async-done | bytes 331808 | tf_op jit(solution)/shard_map/all_to_all | solution.py:196
  (186 shorter events, 19.5 us)
Async XLA Ops:
  0.6 23.0 %copy-start.3 = (pred[16,3]{0,1:T(4,128)(4,1)S(1)}, pred[16,3]{0,1:T(4,128)(4,1)}, u32[]{:S(2)}) copy-start(pred[16,3]{0,1:T(4,128)(4,1)} %constant.659) | copy-start | bytes 148
  2.6 30.3 %collective-permute-start.2 = (bf16[2,4,16,576]{3,1,2,0:T(4,128)(2,1)S(1)}, bf16[2,4,16,576]{3,1,2,0:T(4,128)(2,1)S(1)}, u32[]{:S(2)}, u32[]{:S(2)}) collective-permute-start(bf16[2,4,16,576]{3,1,2,0:T(4,128)(2,1)S(1)} %pad_maximum_fusion), channel_id=1, source_target_pairs={{0,704},{64,0},{128,64},{192,128},{256,192},{320,256},{384,320},{4... | collective-permute-start | bytes 442376 | tf_op jit(solution)/shard_map/ppermute | solution.py:167
  17.8 15.3 %collective-permute-start = (bf16[2,4,16,576]{3,1,2,0:T(4,128)(2,1)S(1)}, bf16[2,4,16,576]{3,1,2,0:T(4,128)(2,1)S(1)}, u32[]{:S(2)}, u32[]{:S(2)}) collective-permute-start(bf16[2,4,16,576]{3,1,2,0:T(4,128)(2,1)S(1)} %pad_maximum_fusion), channel_id=1, source_target_pairs={{0,64},{64,128},{128,192},{192,256},{256,320},{320,384},{384,448},... | collective-permute-start | bytes 442376 | tf_op jit(solution)/shard_map/ppermute | solution.py:76
  23.6 5.4 %copy-start = (bf16[1,2,4,16,192]{4,3,2,1,0:T(8,128)(2,1)S(1)}, bf16[1,2,4,16,192]{4,3,2,1,0:T(8,128)(2,1)}, u32[]{:S(2)}) copy-start(bf16[1,2,4,16,192]{4,3,2,1,0:T(8,128)(2,1)} %param.5) | copy-start | bytes 147460
  23.6 5.6 %copy-start.4 = (s32[1,24]{1,0:T(1,128)S(1)}, s32[1,24]{1,0:T(1,128)}, u32[]{:S(2)}) copy-start(s32[1,24]{1,0:T(1,128)} %param.6) | copy-start | bytes 292
  27.7 5.7 %collective-permute-start.1 = (f32[2,4,16,192]{3,1,2,0:T(4,128)S(1)}, f32[2,4,16,192]{3,1,2,0:T(4,128)S(1)}, u32[]{:S(2)}, u32[]{:S(2)}) collective-permute-start(f32[2,4,16,192]{3,1,2,0:T(4,128)S(1)} %slice.142), channel_id=1, source_target_pairs={{64,0},{128,64},{192,128},{256,192},{320,256},{384,320},{448,384},... | collective-permute-start | bytes 294920 | tf_op jit(solution)/shard_map/ppermute | solution.py:14
  29.9 2.8 %copy-start.2 = (f32[192]{0:T(256)S(1)}, f32[192]{0:T(256)}, u32[]{:S(2)}) copy-start(f32[192]{0:T(256)} %param.7) | copy-start | bytes 2308
  31.2 4.1 %copy-start.1 = (bf16[1,2,4,16,384]{4,3,2,1,0:T(8,128)(2,1)S(1)}, bf16[1,2,4,16,384]{4,3,2,1,0:T(8,128)(2,1)}, u32[]{:S(2)}) copy-start(bf16[1,2,4,16,384]{4,3,2,1,0:T(8,128)(2,1)} %param.9) | copy-start | bytes 294916
  35.7 8.2 %collective-permute-start.3 = (bf16[2,4,16,576]{3,1,2,0:T(4,128)(2,1)S(1)}, bf16[2,4,16,576]{3,1,2,0:T(4,128)(2,1)S(1)}, u32[]{:S(2)}, u32[]{:S(2)}) collective-permute-start(bf16[2,4,16,576]{3,1,2,0:T(4,128)(2,1)S(1)} %collective-permute-done), channel_id=1, source_target_pairs={{0,64},{64,128},{128,192},{192,256},{256,320},{320,384},{384,448},... | collective-permute-start | bytes 442376 | tf_op jit(solution)/shard_map/ppermute | solution.py:179
  39.5 6.3 %collective-permute-start.4 = (bf16[2,4,16,576]{3,1,2,0:T(4,128)(2,1)S(1)}, bf16[2,4,16,576]{3,1,2,0:T(4,128)(2,1)S(1)}, u32[]{:S(2)}, u32[]{:S(2)}) collective-permute-start(bf16[2,4,16,576]{3,1,2,0:T(4,128)(2,1)S(1)} %collective-permute-done.2), channel_id=1, source_target_pairs={{0,704},{64,0},{128,64},{192,128},{256,192},{320,256},{384,320},{4... | collective-permute-start | bytes 442376 | tf_op jit(solution)/shard_map/ppermute | solution.py:182
  45.8 7.3 %collective-permute-start.5 = (bf16[2,4,16,576]{3,1,2,0:T(4,128)(2,1)S(1)}, bf16[2,4,16,576]{3,1,2,0:T(4,128)(2,1)S(1)}, u32[]{:S(2)}, u32[]{:S(2)}) collective-permute-start(bf16[2,4,16,576]{3,1,2,0:T(4,128)(2,1)S(1)} %collective-permute-done.3), channel_id=1, source_target_pairs={{0,64},{64,128},{128,192},{192,256},{256,320},{320,384},{384,448},... | collective-permute-start | bytes 442376 | tf_op jit(solution)/shard_map/ppermute | solution.py:179
  47.7 6.8 %collective-permute-start.6 = (bf16[2,4,16,576]{3,1,2,0:T(4,128)(2,1)S(1)}, bf16[2,4,16,576]{3,1,2,0:T(4,128)(2,1)S(1)}, u32[]{:S(2)}, u32[]{:S(2)}) collective-permute-start(bf16[2,4,16,576]{3,1,2,0:T(4,128)(2,1)S(1)} %collective-permute-done.4), channel_id=1, source_target_pairs={{0,704},{64,0},{128,64},{192,128},{256,192},{320,256},{384,320},{4... | collective-permute-start | bytes 442376 | tf_op jit(solution)/shard_map/ppermute | solution.py:182
  56.8 8.1 %collective-permute-start.7 = (bf16[2,4,16,576]{3,1,2,0:T(4,128)(2,1)S(1)}, bf16[2,4,16,576]{3,1,2,0:T(4,128)(2,1)S(1)}, u32[]{:S(2)}, u32[]{:S(2)}) collective-permute-start(bf16[2,4,16,576]{3,1,2,0:T(4,128)(2,1)S(1)} %collective-permute-done.5), channel_id=1, source_target_pairs={{0,64},{64,128},{128,192},{192,256},{256,320},{320,384},{384,448},... | collective-permute-start | bytes 442376 | tf_op jit(solution)/shard_map/ppermute | solution.py:179
  58.7 7.5 %collective-permute-start.8 = (bf16[2,4,16,576]{3,1,2,0:T(4,128)(2,1)S(1)}, bf16[2,4,16,576]{3,1,2,0:T(4,128)(2,1)S(1)}, u32[]{:S(2)}, u32[]{:S(2)}) collective-permute-start(bf16[2,4,16,576]{3,1,2,0:T(4,128)(2,1)S(1)} %collective-permute-done.6), channel_id=1, source_target_pairs={{0,704},{64,0},{128,64},{192,128},{256,192},{320,256},{384,320},{4... | collective-permute-start | bytes 442376 | tf_op jit(solution)/shard_map/ppermute | solution.py:182
  66.2 9.1 %collective-permute-start.9 = (bf16[2,4,16,576]{3,1,2,0:T(4,128)(2,1)S(1)}, bf16[2,4,16,576]{3,1,2,0:T(4,128)(2,1)S(1)}, u32[]{:S(2)}, u32[]{:S(2)}) collective-permute-start(bf16[2,4,16,576]{3,1,2,0:T(4,128)(2,1)S(1)} %collective-permute-done.7), channel_id=1, source_target_pairs={{0,64},{64,128},{128,192},{192,256},{256,320},{320,384},{384,448},... | collective-permute-start | bytes 442376 | tf_op jit(solution)/shard_map/ppermute | solution.py:179
  68.2 7.0 %collective-permute-start.10 = (bf16[2,4,16,576]{3,1,2,0:T(4,128)(2,1)S(1)}, bf16[2,4,16,576]{3,1,2,0:T(4,128)(2,1)S(1)}, u32[]{:S(2)}, u32[]{:S(2)}) collective-permute-start(bf16[2,4,16,576]{3,1,2,0:T(4,128)(2,1)S(1)} %collective-permute-done.8), channel_id=1, source_target_pairs={{0,704},{64,0},{128,64},{192,128},{256,192},{320,256},{384,320},{4... | collective-permute-start | bytes 442376 | tf_op jit(solution)/shard_map/ppermute | solution.py:182
  77.1 7.7 %collective-permute-start.11 = (bf16[2,4,16,576]{3,1,2,0:T(4,128)(2,1)S(1)}, bf16[2,4,16,576]{3,1,2,0:T(4,128)(2,1)S(1)}, u32[]{:S(2)}, u32[]{:S(2)}) collective-permute-start(bf16[2,4,16,576]{3,1,2,0:T(4,128)(2,1)S(1)} %collective-permute-done.9), channel_id=1, source_target_pairs={{0,64},{64,128},{128,192},{192,256},{256,320},{320,384},{384,448},... | collective-permute-start | bytes 442376 | tf_op jit(solution)/shard_map/ppermute | solution.py:179
  88.2 12.4 %collective-permute-start.12 = (f32[32,6,432]{2,1,0:T(8,128)S(1)}, f32[32,6,432]{2,1,0:T(8,128)S(1)}, u32[]{:S(2)}, u32[]{:S(2)}) collective-permute-start(f32[32,6,432]{2,1,0:T(8,128)S(1)} %dynamic-slice_bitcast_fusion), channel_id=1, source_target_pairs={{0,1},{1,0},{2,3},{3,2},{4,5},{5,4},{6,7},{7,6},{8,9},{9,8},{10,11... | collective-permute-start | bytes 995336 | tf_op jit(solution)/shard_map/ppermute | solution.py:195
  101.4 26.5 %all-to-all-start = ((f32[32,6,432]{2,1,0:T(8,128)}), f32[32,6,432]{2,1,0:T(8,128)S(1)}, u32[]{:S(2)}, u32[]{:S(2)}) async-start(f32[32,6,432]{2,1,0:T(8,128)} %bitcast_add_fusion), calls=%async_computation | async-start | bytes 1048576 | tf_op jit(solution)/shard_map/all_to_all | solution.py:196

commit v9 on v8

--- a/solution.py
+++ b/solution.py
@@ -76,37 +76,6 @@
     first_behind = lax.ppermute(both, "tm", ring_route("tm", 1))
     previous = activate(first_behind[..., :channels], norm_gain).astype(jnp.bfloat16)
     extended = jnp.concatenate([previous, activated])
-    first_frame = lax.axis_index("tm") * frames
-    tap_mask = make_mask(clip_ids[0], first_frame, frames)
-    kernel = conv_weight.reshape(3, 3, 3, channels, outputs)
-    tap_scale = tap_mask[:, :, None, None, None]
-    taps = jnp.stack([extended[tap_t : tap_t + frames] for tap_t in range(3)], axis=1)
-    masked_taps = taps * tap_scale.astype(taps.dtype)
-    conv_rows = lax.conv_general_dilated(
-        masked_taps,
-        kernel,
-        (1, 1, 1),
-        ((0, 0), (1, 1), (1, 1)),
-        dimension_numbers=("NDHWC", "DHWIO", "NDHWC"),
-        preferred_element_type=jnp.float32,
-    ).astype(jnp.bfloat16)
-    taps_grad = lax.conv_general_dilated(
-        out_cotangent[0][:, None],
-        kernel[::-1, ::-1, ::-1],
-        (1, 1, 1),
-        ((2, 2), (1, 1), (1, 1)),
-        dimension_numbers=("NDHWC", "DHWOI", "NDHWC"),
-        preferred_element_type=jnp.float32,
-    )
-    masked_grad = taps_grad * tap_scale
-    extended_grad = sum(
-        jnp.pad(masked_grad[:, tap_t], ((tap_t, 2 - tap_t), (0, 0), (0, 0), (0, 0)))
-        for tap_t in range(3)
-    )
-    returned = from_behind(extended_grad[:2], "tm", -1)
-    own_grad = extended_grad[2:] + returned
-    unused, pull_norm = jax.vjp(lambda field: activate(field, norm_gain), video.astype(jnp.float32))
-    video_grad = pull_norm(own_grad)[0].astype(jnp.bfloat16)
     chain_len = lax.axis_size("tm")
     scale = 1.0 / math.sqrt(lax.axis_size(DATA) * chain_len * frames * height * width)
     kernel_rows = conv_weight.shape[0]
@@ -150,6 +119,40 @@
             preferred_element_type=jnp.float32,
         )
 
+    def conv_section(extended, cotangent, conv_weight, video):
+        first_frame = lax.axis_index("tm") * frames
+        tap_mask = make_mask(clip_ids[0], first_frame, frames)
+        kernel = conv_weight.reshape(3, 3, 3, channels, outputs)
+        tap_scale = tap_mask[:, :, None, None, None]
+        taps = jnp.stack([extended[tap_t : tap_t + frames] for tap_t in range(3)], axis=1)
+        masked_taps = taps * tap_scale.astype(taps.dtype)
+        conv_rows = lax.conv_general_dilated(
+            masked_taps,
+            kernel,
+            (1, 1, 1),
+            ((0, 0), (1, 1), (1, 1)),
+            dimension_numbers=("NDHWC", "DHWIO", "NDHWC"),
+            preferred_element_type=jnp.float32,
+        ).astype(jnp.bfloat16)
+        taps_grad = lax.conv_general_dilated(
+            cotangent[:, None],
+            kernel[::-1, ::-1, ::-1],
+            (1, 1, 1),
+            ((2, 2), (1, 1), (1, 1)),
+            dimension_numbers=("NDHWC", "DHWOI", "NDHWC"),
+            preferred_element_type=jnp.float32,
+        )
+        masked_grad = taps_grad * tap_scale
+        extended_grad = sum(
+            jnp.pad(masked_grad[:, tap_t], ((tap_t, 2 - tap_t), (0, 0), (0, 0), (0, 0)))
+            for tap_t in range(3)
+        )
+        returned = from_behind(extended_grad[:2], "tm", -1)
+        own_grad = extended_grad[2:] + returned
+        unused, pull_norm = jax.vjp(lambda field: activate(field, norm_gain), video.astype(jnp.float32))
+        video_grad = pull_norm(own_grad)[0].astype(jnp.bfloat16)
+        return conv_rows, video_grad
+
     pending = list(range(chain_len))
 
     def add_ready(total):
@@ -161,6 +164,7 @@
         return total
 
     total = None
+    conv_inputs = (extended, out_cotangent[0], conv_weight, video)
     forward_steps = chain_len // 2
     backward_steps = chain_len - 1 - forward_steps
     forward_moving = first_behind
@@ -168,7 +172,16 @@
     arrived = [(chain_len - 1, None), (1, backward_moving)]
     for step in range(2, forward_steps + 1):
         total = add_ready(total)
-        if total is not None:
+        if step == 3:
+            forward_moving, backward_moving, total, conv_inputs = lax.optimization_barrier(
+                (forward_moving, backward_moving, total, conv_inputs)
+            )
+            conv_results = conv_section(*conv_inputs)
+        elif step == 4:
+            forward_moving, backward_moving, total, conv_results = lax.optimization_barrier(
+                (forward_moving, backward_moving, total, conv_results)
+            )
+        elif total is not None:
             forward_moving, backward_moving, total = lax.optimization_barrier(
                 (forward_moving, backward_moving, total)
             )
@@ -193,6 +206,7 @@
     kept = lax.dynamic_index_in_dim(pieces, core, 1, keepdims=False)
     sent = lax.dynamic_index_in_dim(pieces, 1 - core, 1, keepdims=False)
     pair_sum = kept + lax.ppermute(sent, "dc", [(0, 1), (1, 0)])
+    conv_rows, video_grad = conv_results
     reduced_t = lax.all_to_all(pair_sum, "dq", 0, 0, tiled=False).sum(axis=0)
     grad_weight = reduced_t.T * scale
     conv_out = conv_rows.reshape(1, frames, height, width, outputs)

time: 129 us -> 123 us (0.953)
  matrix products: 11.8 us -> 7.5 us
  local copies, waits for them, and re-layouts: 13 us -> 8.9 us
  waiting for transfers between devices: 24.7 us -> 27.7 us
    conv_general_dilated x2, matrix products: 6.83 us -> 2.53 us  [the longest x1 1.27 us: conv_section(): lax.conv_general_dilated(cotangent[:, None], kernel[::-1, ::-1, ::-1], (1...]
    unnamed x16 -> x18, local copies, waits for them, and re-layouts: 4.34 us -> 1.08 us
    ppermute x1, starting transfers between devices: 1.92 us -> 4.83 us  [shards(): first_behind = lax.ppermute(both, 'tm', ring_route('tm', 1))]
    ppermute x1, starting transfers between devices: 15.1 us -> 12.2 us  [shards(): backward_moving = lax.ppermute(both, 'tm', ring_route('tm', -1))]
    ppermute x4, waiting for transfers between devices: 4.99 us -> 3.09 us  [shards(): backward_moving = lax.ppermute(backward_moving, 'tm', ring_route('tm', -1))]
    ppermute x5, starting transfers between devices: 12.4 us -> 10.6 us  [shards(): forward_moving = lax.ppermute(forward_moving, 'tm', ring_route('tm', 1))]
    ppermute x5, waiting for transfers between devices: 4.15 us -> 5.71 us  [shards(): forward_moving = lax.ppermute(forward_moving, 'tm', ring_route('tm', 1))]
    ppermute x1, waiting for transfers between devices: 0.01 us -> 1.51 us  [shards(): pair_sum = kept + lax.ppermute(sent, 'dc', [(0, 1), (1, 0)])]
  transfers between devices with their start and end apart: 14 -> 14, of which waited for: 7 -> 8; matrix products, arithmetic and copies ran while one was open for 17% -> 13% of each run, Pallas kernels for 0% -> 0%
where the time goes in v9:
time: 123 us; the launch traced here: 122 us
  starting transfers between devices  66.3 us (54%)
  waiting for transfers between devices  27.7 us (23%)
  other arithmetic  9.81 us (8%)
  local copies, waits for them, and re-layouts  8.9 us (7%)
  matrix products  7.5 us (6%)
  between operations  2.23 us (2%)
    ppermute x4, starting transfers between devices, shards(): backward_moving = lax.ppermute(backward_moving, 'tm', ring_route('tm', -1))  18.5 us
    all_to_all x1, waiting for transfers between devices, shards(): reduced_t = lax.all_to_all(pair_sum, 'dq', 0, 0, tiled=False).sum(axis=0)  15.9 us
    ppermute x1, starting transfers between devices, shards(): backward_moving = lax.ppermute(both, 'tm', ring_route('tm', -1))  12.2 us
    ppermute x5, starting transfers between devices, shards(): forward_moving = lax.ppermute(forward_moving, 'tm', ring_route('tm', 1))  10.6 us
    all_to_all x1, starting transfers between devices, shards(): reduced_t = lax.all_to_all(pair_sum, 'dq', 0, 0, tiled=False).sum(axis=0)  9.67 us
    ppermute x1, starting transfers between devices, shards(): pair_sum = kept + lax.ppermute(sent, 'dc', [(0, 1), (1, 0)])  9.23 us
    ppermute x5, waiting for transfers between devices, shards(): forward_moving = lax.ppermute(forward_moving, 'tm', ring_route('tm', 1))  5.71 us
    dot_general x12, matrix products, block_term(): lax.dot_general(block_cot, jnp.concatenate(columns, axis=1), (((0,), (0,)...  4.96 us
  transfers between devices with their start and end apart: 14, of which 8 were waited for; matrix products, arithmetic and copies ran while one was open for 13% of the time, Pallas kernels for 0%

profile of v9, /device:TPU:1, one launch (start us, length us, event | category | flops | bytes accessed | tf_op | source)
XLA Modules:
  0.0 122.4 jit_solution(3562612988700042948)
XLA Ops:
  0.6 1.0 pad_maximum_fusion
  1.6 4.8 %collective-permute-start = (bf16[2,4,16,576]{3,2,1,0:T(8,128)(2,1)S(1)}, bf16[2,4,16,576]{3,2,1,0:T(8,128)(2,1)S(1)}, u32[]{:S(2)}, u32[]{:S(2)}) collective-permute-start(bf16[2,4,16,576]{3,2,1,0:T(8,128)(2,1)S(1)} %pad_maximum_fusion), channel_id=1, source_target_pairs={{0,64},{64,128},{128,192},{192,256},{256,320},{320,384},{384,448},... | collective-permute-start | bytes 442376 | tf_op jit(solution)/shard_map/ppermute | solution.py:76
  6.5 12.2 %collective-permute-start.1 = (bf16[2,4,16,576]{3,2,1,0:T(8,128)(2,1)S(1)}, bf16[2,4,16,576]{3,2,1,0:T(8,128)(2,1)S(1)}, u32[]{:S(2)}, u32[]{:S(2)}) collective-permute-start(bf16[2,4,16,576]{3,2,1,0:T(8,128)(2,1)S(1)} %pad_maximum_fusion), channel_id=1, source_target_pairs={{0,704},{64,0},{128,64},{192,128},{256,192},{320,256},{384,320},{4... | collective-permute-start | bytes 442376 | tf_op jit(solution)/shard_map/ppermute | solution.py:171
  18.8 0.9 fusion.97
  20.2 0.7 concatenate.82
  21.1 1.2 %gather_fusion = s32[72]{0:T(128)S(1)} fusion(s32[26]{0:T(128)S(1)} %concatenate.82, s32[1024]{0:T(1024)S(1)} %pad_clamp_fusion.3), kind=kCustom, calls=%fused_computation | custom fusion | bytes 864 | tf_op jit(solution)/shard_map/gather | solution.py:50
  22.5 0.7 gather_fusion.1
  23.5 0.6 gather_fusion.2
  24.2 0.6 gather_fusion.3
  27.1 2.1 %collective-permute-start.2 = (bf16[2,4,16,576]{3,2,1,0:T(8,128)(2,1)S(1)}, bf16[2,4,16,576]{3,2,1,0:T(8,128)(2,1)S(1)}, u32[]{:S(2)}, u32[]{:S(2)}) collective-permute-start(bf16[2,4,16,576]{3,2,1,0:T(8,128)(2,1)S(1)} %collective-permute-done), channel_id=1, source_target_pairs={{0,64},{64,128},{128,192},{192,256},{256,320},{320,384},{384,448},... | collective-permute-start | bytes 442376 | tf_op jit(solution)/shard_map/ppermute | solution.py:192
  29.1 4.6 %collective-permute-start.3 = (bf16[2,4,16,576]{3,2,1,0:T(8,128)(2,1)S(1)}, bf16[2,4,16,576]{3,2,1,0:T(8,128)(2,1)S(1)}, u32[]{:S(2)}, u32[]{:S(2)}) collective-permute-start(bf16[2,4,16,576]{3,2,1,0:T(8,128)(2,1)S(1)} %collective-permute-done.1), channel_id=1, source_target_pairs={{0,704},{64,0},{128,64},{192,128},{256,192},{320,256},{384,320},{4... | collective-permute-start | bytes 442376 | tf_op jit(solution)/shard_map/ppermute | solution.py:195
  35.0 0.9 collective-permute-done.3
  35.9 1.9 %collective-permute-start.4 = (bf16[2,4,16,576]{3,2,1,0:T(8,128)(2,1)S(1)}, bf16[2,4,16,576]{3,2,1,0:T(8,128)(2,1)S(1)}, u32[]{:S(2)}, u32[]{:S(2)}) collective-permute-start(bf16[2,4,16,576]{3,2,1,0:T(8,128)(2,1)S(1)} %collective-permute-done.2), channel_id=1, source_target_pairs={{0,64},{64,128},{128,192},{192,256},{256,320},{320,384},{384,448},... | collective-permute-start | bytes 442376 | tf_op jit(solution)/shard_map/ppermute | solution.py:192
  37.9 5.0 %collective-permute-start.5 = (bf16[2,4,16,576]{3,2,1,0:T(8,128)(2,1)S(1)}, bf16[2,4,16,576]{3,2,1,0:T(8,128)(2,1)S(1)}, u32[]{:S(2)}, u32[]{:S(2)}) collective-permute-start(bf16[2,4,16,576]{3,2,1,0:T(8,128)(2,1)S(1)} %collective-permute-done.3), channel_id=1, source_target_pairs={{0,704},{64,0},{128,64},{192,128},{256,192},{320,256},{384,320},{4... | collective-permute-start | bytes 442376 | tf_op jit(solution)/shard_map/ppermute | solution.py:195
  43.9 1.3 %fusion = f32[3,4,16,3,192]{4,2,3,1,0:T(8,128)S(1)} fusion(bf16[3,3,3,192,384]{4,3,2,1,0:T(8,128)(2,1)S(1)} %bitcast.129, f32[3,4,16,3,192]{4,1,3,2,0:T(4,128)S(1)} %bitcast.135, pred[16,3]{0,1:T(4,128)(4,1)S(1)} %copy-done.4, bf16[1,4,2,8,5,384]{5,2,4,3,1,0:T(2,128)(2,1)S(1)} %fusion.8), kind=kOutput, calls=%fused_computation.7 | convolution fusion | flops 637231104 | bytes 5111856 | tf_op jit(solution)/shard_map/conv_general_dilated | solution.py:137
  45.9 1.3 %collective-permute-start.6 = (f32[2,4,16,192]{3,2,1,0:T(8,128)S(1)}, f32[2,4,16,192]{3,2,1,0:T(8,128)S(1)}, u32[]{:S(2)}, u32[]{:S(2)}) collective-permute-start(f32[2,4,16,192]{3,2,1,0:T(8,128)S(1)} %slice.154), channel_id=1, source_target_pairs={{64,0},{128,64},{192,128},{256,192},{320,256},{384,320},{448,384},... | collective-permute-start | bytes 294920 | tf_op jit(solution)/shard_map/ppermute | solution.py:14
  48.3 1.3 %fusion.1 = bf16[1,4,16,3,384]{4,2,3,1,0:T(8,128)(2,1)S(1)} fusion(bf16[3,3,3,192,384]{4,3,2,1,0:T(8,128)(2,1)S(1)} %bitcast.130, bf16[3,4,2,8,5,192]{5,2,4,3,1,0:T(2,128)(2,1)S(1)} %fusion.5, pred[16,3]{0,1:T(4,128)(4,1)S(1)} %copy-done.4), kind=kOutput, calls=%fused_computation.9 | convolution fusion | flops 637157376 | bytes 4497456 | tf_op jit(solution)/shard_map/conv_general_dilated | solution.py:129
  50.2 1.4 %collective-permute-done.6 = f32[2,4,16,192]{3,2,1,0:T(8,128)S(1)} collective-permute-done((f32[2,4,16,192]{3,2,1,0:T(8,128)S(1)}, f32[2,4,16,192]{3,2,1,0:T(8,128)S(1)}, u32[]{:S(2)}, u32[]{:S(2)}) %collective-permute-start.6) | collective-permute-done | bytes 98336 | tf_op jit(solution)/shard_map/ppermute | solution.py:14
  52.1 0.7 fusion.188
  53.9 2.6 %collective-permute-start.7 = (bf16[2,4,16,576]{3,2,1,0:T(8,128)(2,1)S(1)}, bf16[2,4,16,576]{3,2,1,0:T(8,128)(2,1)S(1)}, u32[]{:S(2)}, u32[]{:S(2)}) collective-permute-start(bf16[2,4,16,576]{3,2,1,0:T(8,128)(2,1)S(1)} %collective-permute-done.4), channel_id=1, source_target_pairs={{0,64},{64,128},{128,192},{192,256},{256,320},{320,384},{384,448},... | collective-permute-start | bytes 442376 | tf_op jit(solution)/shard_map/ppermute | solution.py:192
  56.5 3.9 %collective-permute-start.8 = (bf16[2,4,16,576]{3,2,1,0:T(8,128)(2,1)S(1)}, bf16[2,4,16,576]{3,2,1,0:T(8,128)(2,1)S(1)}, u32[]{:S(2)}, u32[]{:S(2)}) collective-permute-start(bf16[2,4,16,576]{3,2,1,0:T(8,128)(2,1)S(1)} %collective-permute-done.5), channel_id=1, source_target_pairs={{0,704},{64,0},{128,64},{192,128},{256,192},{320,256},{384,320},{4... | collective-permute-start | bytes 442376 | tf_op jit(solution)/shard_map/ppermute | solution.py:195
  62.7 2.1 %collective-permute-start.9 = (bf16[2,4,16,576]{3,2,1,0:T(8,128)(2,1)S(1)}, bf16[2,4,16,576]{3,2,1,0:T(8,128)(2,1)S(1)}, u32[]{:S(2)}, u32[]{:S(2)}) collective-permute-start(bf16[2,4,16,576]{3,2,1,0:T(8,128)(2,1)S(1)} %collective-permute-done.7), channel_id=1, source_target_pairs={{0,64},{64,128},{128,192},{192,256},{256,320},{320,384},{384,448},... | collective-permute-start | bytes 442376 | tf_op jit(solution)/shard_map/ppermute | solution.py:192
  64.8 5.0 %collective-permute-start.10 = (bf16[2,4,16,576]{3,2,1,0:T(8,128)(2,1)S(1)}, bf16[2,4,16,576]{3,2,1,0:T(8,128)(2,1)S(1)}, u32[]{:S(2)}, u32[]{:S(2)}) collective-permute-start(bf16[2,4,16,576]{3,2,1,0:T(8,128)(2,1)S(1)} %collective-permute-done.8), channel_id=1, source_target_pairs={{0,704},{64,0},{128,64},{192,128},{256,192},{320,256},{384,320},{4... | collective-permute-start | bytes 442376 | tf_op jit(solution)/shard_map/ppermute | solution.py:195
  70.2 1.6 %collective-permute-done.10 = bf16[2,4,16,576]{3,2,1,0:T(8,128)(2,1)S(1)} collective-permute-done((bf16[2,4,16,576]{3,2,1,0:T(8,128)(2,1)S(1)}, bf16[2,4,16,576]{3,2,1,0:T(8,128)(2,1)S(1)}, u32[]{:S(2)}, u32[]{:S(2)}) %collective-permute-start.10) | collective-permute-done | bytes 147488 | tf_op jit(solution)/shard_map/ppermute | solution.py:195
  73.4 1.9 %collective-permute-start.11 = (bf16[2,4,16,576]{3,2,1,0:T(8,128)(2,1)S(1)}, bf16[2,4,16,576]{3,2,1,0:T(8,128)(2,1)S(1)}, u32[]{:S(2)}, u32[]{:S(2)}) collective-permute-start(bf16[2,4,16,576]{3,2,1,0:T(8,128)(2,1)S(1)} %collective-permute-done.9), channel_id=1, source_target_pairs={{0,64},{64,128},{128,192},{192,256},{256,320},{320,384},{384,448},... | collective-permute-start | bytes 442376 | tf_op jit(solution)/shard_map/ppermute | solution.py:192
  76.1 5.1 %collective-permute-done.11 = bf16[2,4,16,576]{3,2,1,0:T(8,128)(2,1)S(1)} collective-permute-done((bf16[2,4,16,576]{3,2,1,0:T(8,128)(2,1)S(1)}, bf16[2,4,16,576]{3,2,1,0:T(8,128)(2,1)S(1)}, u32[]{:S(2)}, u32[]{:S(2)}) %collective-permute-start.11) | collective-permute-done | bytes 147488 | tf_op jit(solution)/shard_map/ppermute | solution.py:192
  83.9 9.2 %collective-permute-start.12 = (f32[32,6,432]{2,1,0:T(8,128)S(1)}, f32[32,6,432]{2,1,0:T(8,128)S(1)}, u32[]{:S(2)}, u32[]{:S(2)}) collective-permute-start(f32[32,6,432]{2,1,0:T(8,128)S(1)} %dynamic-slice_bitcast_fusion), channel_id=1, source_target_pairs={{0,1},{1,0},{2,3},{3,2},{4,5},{5,4},{6,7},{7,6},{8,9},{9,8},{10,11... | collective-permute-start | bytes 995336 | tf_op jit(solution)/shard_map/ppermute | solution.py:208
  93.1 1.5 %collective-permute-done.12 = f32[32,6,432]{2,1,0:T(8,128)S(1)} collective-permute-done((f32[32,6,432]{2,1,0:T(8,128)S(1)}, f32[32,6,432]{2,1,0:T(8,128)S(1)}, u32[]{:S(2)}, u32[]{:S(2)}) %collective-permute-start.12) | collective-permute-done | bytes 331808 | tf_op jit(solution)/shard_map/ppermute | solution.py:208
  94.6 0.9 bitcast_add_fusion
  95.5 9.7 %all-to-all-start = ((f32[32,6,432]{2,1,0:T(8,128)}), f32[32,6,432]{2,1,0:T(8,128)S(1)}, u32[]{:S(2)}, u32[]{:S(2)}) async-start(f32[32,6,432]{2,1,0:T(8,128)} %bitcast_add_fusion), calls=%async_computation | async-start | bytes 1048576 | tf_op jit(solution)/shard_map/all_to_all | solution.py:210
  105.2 0.7 copy.45
  105.8 15.9 %all-to-all-done = f32[32,6,432]{2,1,0:T(8,128)S(1)} async-done(((f32[32,6,432]{2,1,0:T(8,128)}), f32[32,6,432]{2,1,0:T(8,128)S(1)}, u32[]{:S(2)}, u32[]{:S(2)}) %all-to-all-start) | async-done | bytes 331808 | tf_op jit(solution)/shard_map/all_to_all | solution.py:210
  (142 shorter events, 16.8 us)
Async XLA Ops:
  1.6 24.2 %collective-permute-start = (bf16[2,4,16,576]{3,2,1,0:T(8,128)(2,1)S(1)}, bf16[2,4,16,576]{3,2,1,0:T(8,128)(2,1)S(1)}, u32[]{:S(2)}, u32[]{:S(2)}) collective-permute-start(bf16[2,4,16,576]{3,2,1,0:T(8,128)(2,1)S(1)} %pad_maximum_fusion), channel_id=1, source_target_pairs={{0,64},{64,128},{128,192},{192,256},{256,320},{320,384},{384,448},... | collective-permute-start | bytes 442376 | tf_op jit(solution)/shard_map/ppermute | solution.py:76
  6.5 19.3 %collective-permute-start.1 = (bf16[2,4,16,576]{3,2,1,0:T(8,128)(2,1)S(1)}, bf16[2,4,16,576]{3,2,1,0:T(8,128)(2,1)S(1)}, u32[]{:S(2)}, u32[]{:S(2)}) collective-permute-start(bf16[2,4,16,576]{3,2,1,0:T(8,128)(2,1)S(1)} %pad_maximum_fusion), channel_id=1, source_target_pairs={{0,704},{64,0},{128,64},{192,128},{256,192},{320,256},{384,320},{4... | collective-permute-start | bytes 442376 | tf_op jit(solution)/shard_map/ppermute | solution.py:171
  21.1 2.2 %copy-start.5 = (s32[1,24]{1,0:T(1,128)S(1)}, s32[1,24]{1,0:T(1,128)}, u32[]{:S(2)}) copy-start(s32[1,24]{1,0:T(1,128)} %param.6) | copy-start | bytes 292
  21.1 4.9 %copy-start.1 = (bf16[1,2,4,16,192]{4,3,2,1,0:T(8,128)(2,1)S(1)}, bf16[1,2,4,16,192]{4,3,2,1,0:T(8,128)(2,1)}, u32[]{:S(2)}) copy-start(bf16[1,2,4,16,192]{4,3,2,1,0:T(8,128)(2,1)} %param.5) | copy-start | bytes 147460
  21.1 4.9 %copy-start.3 = (f32[192]{0:T(256)S(1)}, f32[192]{0:T(256)}, u32[]{:S(2)}) copy-start(f32[192]{0:T(256)} %param.7) | copy-start | bytes 2308
  22.3 4.3 %copy-start.2 = (bf16[1,2,4,16,384]{4,3,2,1,0:T(8,128)(2,1)S(1)}, bf16[1,2,4,16,384]{4,3,2,1,0:T(8,128)(2,1)}, u32[]{:S(2)}) copy-start(bf16[1,2,4,16,384]{4,3,2,1,0:T(8,128)(2,1)} %param.9) | copy-start | bytes 294916
  26.3 17.6 %copy-start = (bf16[5184,384]{1,0:T(8,128)(2,1)S(1)}, bf16[5184,384]{1,0:T(8,128)(2,1)}, u32[]{:S(2)}) copy-start(bf16[5184,384]{1,0:T(8,128)(2,1)} %param.8) | copy-start | bytes 11943940
  26.3 17.6 %copy-start.4 = (pred[16,3]{0,1:T(4,128)(4,1)S(1)}, pred[16,3]{0,1:T(4,128)(4,1)}, u32[]{:S(2)}) copy-start(pred[16,3]{0,1:T(4,128)(4,1)} %constant.660) | copy-start | bytes 148
  27.1 8.0 %collective-permute-start.2 = (bf16[2,4,16,576]{3,2,1,0:T(8,128)(2,1)S(1)}, bf16[2,4,16,576]{3,2,1,0:T(8,128)(2,1)S(1)}, u32[]{:S(2)}, u32[]{:S(2)}) collective-permute-start(bf16[2,4,16,576]{3,2,1,0:T(8,128)(2,1)S(1)} %collective-permute-done), channel_id=1, source_target_pairs={{0,64},{64,128},{128,192},{192,256},{256,320},{320,384},{384,448},... | collective-permute-start | bytes 442376 | tf_op jit(solution)/shard_map/ppermute | solution.py:192
  29.1 6.8 %collective-permute-start.3 = (bf16[2,4,16,576]{3,2,1,0:T(8,128)(2,1)S(1)}, bf16[2,4,16,576]{3,2,1,0:T(8,128)(2,1)S(1)}, u32[]{:S(2)}, u32[]{:S(2)}) collective-permute-start(bf16[2,4,16,576]{3,2,1,0:T(8,128)(2,1)S(1)} %collective-permute-done.1), channel_id=1, source_target_pairs={{0,704},{64,0},{128,64},{192,128},{256,192},{320,256},{384,320},{4... | collective-permute-start | bytes 442376 | tf_op jit(solution)/shard_map/ppermute | solution.py:195
  35.9 14.0 %collective-permute-start.4 = (bf16[2,4,16,576]{3,2,1,0:T(8,128)(2,1)S(1)}, bf16[2,4,16,576]{3,2,1,0:T(8,128)(2,1)S(1)}, u32[]{:S(2)}, u32[]{:S(2)}) collective-permute-start(bf16[2,4,16,576]{3,2,1,0:T(8,128)(2,1)S(1)} %collective-permute-done.2), channel_id=1, source_target_pairs={{0,64},{64,128},{128,192},{192,256},{256,320},{320,384},{384,448},... | collective-permute-start | bytes 442376 | tf_op jit(solution)/shard_map/ppermute | solution.py:192
  37.9 12.2 %collective-permute-start.5 = (bf16[2,4,16,576]{3,2,1,0:T(8,128)(2,1)S(1)}, bf16[2,4,16,576]{3,2,1,0:T(8,128)(2,1)S(1)}, u32[]{:S(2)}, u32[]{:S(2)}) collective-permute-start(bf16[2,4,16,576]{3,2,1,0:T(8,128)(2,1)S(1)} %collective-permute-done.3), channel_id=1, source_target_pairs={{0,704},{64,0},{128,64},{192,128},{256,192},{320,256},{384,320},{4... | collective-permute-start | bytes 442376 | tf_op jit(solution)/shard_map/ppermute | solution.py:195
  45.9 5.7 %collective-permute-start.6 = (f32[2,4,16,192]{3,2,1,0:T(8,128)S(1)}, f32[2,4,16,192]{3,2,1,0:T(8,128)S(1)}, u32[]{:S(2)}, u32[]{:S(2)}) collective-permute-start(f32[2,4,16,192]{3,2,1,0:T(8,128)S(1)} %slice.154), channel_id=1, source_target_pairs={{64,0},{128,64},{192,128},{256,192},{320,256},{384,320},{448,384},... | collective-permute-start | bytes 294920 | tf_op jit(solution)/shard_map/ppermute | solution.py:14
  53.9 7.3 %collective-permute-start.7 = (bf16[2,4,16,576]{3,2,1,0:T(8,128)(2,1)S(1)}, bf16[2,4,16,576]{3,2,1,0:T(8,128)(2,1)S(1)}, u32[]{:S(2)}, u32[]{:S(2)}) collective-permute-start(bf16[2,4,16,576]{3,2,1,0:T(8,128)(2,1)S(1)} %collective-permute-done.4), channel_id=1, source_target_pairs={{0,64},{64,128},{128,192},{192,256},{256,320},{320,384},{384,448},... | collective-permute-start | bytes 442376 | tf_op jit(solution)/shard_map/ppermute | solution.py:192
  56.5 6.1 %collective-permute-start.8 = (bf16[2,4,16,576]{3,2,1,0:T(8,128)(2,1)S(1)}, bf16[2,4,16,576]{3,2,1,0:T(8,128)(2,1)S(1)}, u32[]{:S(2)}, u32[]{:S(2)}) collective-permute-start(bf16[2,4,16,576]{3,2,1,0:T(8,128)(2,1)S(1)} %collective-permute-done.5), channel_id=1, source_target_pairs={{0,704},{64,0},{128,64},{192,128},{256,192},{320,256},{384,320},{4... | collective-permute-start | bytes 442376 | tf_op jit(solution)/shard_map/ppermute | solution.py:195
  62.7 9.3 %collective-permute-start.9 = (bf16[2,4,16,576]{3,2,1,0:T(8,128)(2,1)S(1)}, bf16[2,4,16,576]{3,2,1,0:T(8,128)(2,1)S(1)}, u32[]{:S(2)}, u32[]{:S(2)}) collective-permute-start(bf16[2,4,16,576]{3,2,1,0:T(8,128)(2,1)S(1)} %collective-permute-done.7), channel_id=1, source_target_pairs={{0,64},{64,128},{128,192},{192,256},{256,320},{320,384},{384,448},... | collective-permute-start | bytes 442376 | tf_op jit(solution)/shard_map/ppermute | solution.py:192
  64.8 7.1 %collective-permute-start.10 = (bf16[2,4,16,576]{3,2,1,0:T(8,128)(2,1)S(1)}, bf16[2,4,16,576]{3,2,1,0:T(8,128)(2,1)S(1)}, u32[]{:S(2)}, u32[]{:S(2)}) collective-permute-start(bf16[2,4,16,576]{3,2,1,0:T(8,128)(2,1)S(1)} %collective-permute-done.8), channel_id=1, source_target_pairs={{0,704},{64,0},{128,64},{192,128},{256,192},{320,256},{384,320},{4... | collective-permute-start | bytes 442376 | tf_op jit(solution)/shard_map/ppermute | solution.py:195
  73.4 7.7 %collective-permute-start.11 = (bf16[2,4,16,576]{3,2,1,0:T(8,128)(2,1)S(1)}, bf16[2,4,16,576]{3,2,1,0:T(8,128)(2,1)S(1)}, u32[]{:S(2)}, u32[]{:S(2)}) collective-permute-start(bf16[2,4,16,576]{3,2,1,0:T(8,128)(2,1)S(1)} %collective-permute-done.9), channel_id=1, source_target_pairs={{0,64},{64,128},{128,192},{192,256},{256,320},{320,384},{384,448},... | collective-permute-start | bytes 442376 | tf_op jit(solution)/shard_map/ppermute | solution.py:192
  83.9 10.8 %collective-permute-start.12 = (f32[32,6,432]{2,1,0:T(8,128)S(1)}, f32[32,6,432]{2,1,0:T(8,128)S(1)}, u32[]{:S(2)}, u32[]{:S(2)}) collective-permute-start(f32[32,6,432]{2,1,0:T(8,128)S(1)} %dynamic-slice_bitcast_fusion), channel_id=1, source_target_pairs={{0,1},{1,0},{2,3},{3,2},{4,5},{5,4},{6,7},{7,6},{8,9},{9,8},{10,11... | collective-permute-start | bytes 995336 | tf_op jit(solution)/shard_map/ppermute | solution.py:208
  95.5 26.3 %all-to-all-start = ((f32[32,6,432]{2,1,0:T(8,128)}), f32[32,6,432]{2,1,0:T(8,128)S(1)}, u32[]{:S(2)}, u32[]{:S(2)}) async-start(f32[32,6,432]{2,1,0:T(8,128)} %bitcast_add_fusion), calls=%async_computation | async-start | bytes 1048576 | tf_op jit(solution)/shard_map/all_to_all | solution.py:210

commit v10 on v9

--- a/solution.py
+++ b/solution.py
@@ -119,7 +119,7 @@
             preferred_element_type=jnp.float32,
         )
 
-    def conv_section(extended, cotangent, conv_weight, video):
+    def forward_section(extended, conv_weight):
         first_frame = lax.axis_index("tm") * frames
         tap_mask = make_mask(clip_ids[0], first_frame, frames)
         kernel = conv_weight.reshape(3, 3, 3, channels, outputs)
@@ -134,6 +134,13 @@
             dimension_numbers=("NDHWC", "DHWIO", "NDHWC"),
             preferred_element_type=jnp.float32,
         ).astype(jnp.bfloat16)
+        return conv_rows
+
+    def backward_section(cotangent, conv_weight, video):
+        first_frame = lax.axis_index("tm") * frames
+        tap_mask = make_mask(clip_ids[0], first_frame, frames)
+        kernel = conv_weight.reshape(3, 3, 3, channels, outputs)
+        tap_scale = tap_mask[:, :, None, None, None]
         taps_grad = lax.conv_general_dilated(
             cotangent[:, None],
             kernel[::-1, ::-1, ::-1],
@@ -151,7 +158,7 @@
         own_grad = extended_grad[2:] + returned
         unused, pull_norm = jax.vjp(lambda field: activate(field, norm_gain), video.astype(jnp.float32))
         video_grad = pull_norm(own_grad)[0].astype(jnp.bfloat16)
-        return conv_rows, video_grad
+        return video_grad
 
     pending = list(range(chain_len))
 
@@ -164,7 +171,8 @@
         return total
 
     total = None
-    conv_inputs = (extended, out_cotangent[0], conv_weight, video)
+    conv_inputs = (extended, conv_weight)
+    grad_inputs = (out_cotangent[0], conv_weight, video)
     forward_steps = chain_len // 2
     backward_steps = chain_len - 1 - forward_steps
     forward_moving = first_behind
@@ -176,10 +184,21 @@
             forward_moving, backward_moving, total, conv_inputs = lax.optimization_barrier(
                 (forward_moving, backward_moving, total, conv_inputs)
             )
-            conv_results = conv_section(*conv_inputs)
+            conv_rows = forward_section(*conv_inputs)
         elif step == 4:
-            forward_moving, backward_moving, total, conv_results = lax.optimization_barrier(
-                (forward_moving, backward_moving, total, conv_results)
+            forward_moving, backward_moving, total, conv_rows, grad_inputs = (
+                lax.optimization_barrier(
+                    (forward_moving, backward_moving, total, conv_rows, grad_inputs)
+                )
+            )
+        elif step == 5:
+            forward_moving, backward_moving, total, grad_inputs = lax.optimization_barrier(
+                (forward_moving, backward_moving, total, grad_inputs)
+            )
+            video_grad = backward_section(*grad_inputs)
+        elif step == 6:
+            forward_moving, backward_moving, total, video_grad = lax.optimization_barrier(
+                (forward_moving, backward_moving, total, video_grad)
             )
         elif total is not None:
             forward_moving, backward_moving, total = lax.optimization_barrier(
@@ -206,7 +225,6 @@
     kept = lax.dynamic_index_in_dim(pieces, core, 1, keepdims=False)
     sent = lax.dynamic_index_in_dim(pieces, 1 - core, 1, keepdims=False)
     pair_sum = kept + lax.ppermute(sent, "dc", [(0, 1), (1, 0)])
-    conv_rows, video_grad = conv_results
     reduced_t = lax.all_to_all(pair_sum, "dq", 0, 0, tiled=False).sum(axis=0)
     grad_weight = reduced_t.T * scale
     conv_out = conv_rows.reshape(1, frames, height, width, outputs)

time: 123 us -> 123 us (level)
    ppermute x1, waiting for transfers between devices: 1.41 us -> 3.64 us  [from_behind(): return lax.ppermute(block, axis, route)]
    ppermute x4, waiting for transfers between devices: 3.09 us -> 1.34 us  [shards(): backward_moving = lax.ppermute(backward_moving, 'tm', ring_route('tm', -1))]
  transfers between devices with their start and end apart: 14 -> 14, of which waited for: 8 -> 7; matrix products, arithmetic and copies ran while one was open for 13% -> 15% of each run, Pallas kernels for 0% -> 0%
where the time goes in v10:
time: 123 us; the launch traced here: 122 us
  starting transfers between devices  66.2 us (54%)
  waiting for transfers between devices  27.6 us (22%)
  other arithmetic  9.87 us (8%)
  local copies, waits for them, and re-layouts  8.91 us (7%)
  matrix products  7.52 us (6%)
  between operations  2.24 us (2%)
    ppermute x4, starting transfers between devices, shards(): backward_moving = lax.ppermute(backward_moving, 'tm', ring_route('tm', -1))  19.2 us
    all_to_all x1, waiting for transfers between devices, shards(): reduced_t = lax.all_to_all(pair_sum, 'dq', 0, 0, tiled=False).sum(axis=0)  15.9 us
    ppermute x1, starting transfers between devices, shards(): backward_moving = lax.ppermute(both, 'tm', ring_route('tm', -1))  12.2 us
    ppermute x5, starting transfers between devices, shards(): forward_moving = lax.ppermute(forward_moving, 'tm', ring_route('tm', 1))  9.84 us
    all_to_all x1, starting transfers between devices, shards(): reduced_t = lax.all_to_all(pair_sum, 'dq', 0, 0, tiled=False).sum(axis=0)  9.67 us
    ppermute x1, starting transfers between devices, shards(): pair_sum = kept + lax.ppermute(sent, 'dc', [(0, 1), (1, 0)])  8.92 us
    ppermute x5, waiting for transfers between devices, shards(): forward_moving = lax.ppermute(forward_moving, 'tm', ring_route('tm', 1))  5.2 us
    dot_general x12, matrix products, block_term(): lax.dot_general(block_cot, jnp.concatenate(columns, axis=1), (((0,), (0,)...  4.98 us
  transfers between devices with their start and end apart: 14, of which 7 were waited for; matrix products, arithmetic and copies ran while one was open for 15% of the time, Pallas kernels for 0%

profile of v10, /device:TPU:1, one launch (start us, length us, event | category | flops | bytes accessed | tf_op | source)
XLA Modules:
  0.0 122.3 jit_solution(7712020509676320908)
XLA Ops:
  0.6 1.0 pad_maximum_fusion
  1.6 4.8 %collective-permute-start = (bf16[2,4,16,576]{3,2,1,0:T(8,128)(2,1)S(1)}, bf16[2,4,16,576]{3,2,1,0:T(8,128)(2,1)S(1)}, u32[]{:S(2)}, u32[]{:S(2)}) collective-permute-start(bf16[2,4,16,576]{3,2,1,0:T(8,128)(2,1)S(1)} %pad_maximum_fusion), channel_id=1, source_target_pairs={{0,64},{64,128},{128,192},{192,256},{256,320},{320,384},{384,448},... | collective-permute-start | bytes 442376 | tf_op jit(solution)/shard_map/ppermute | solution.py:76
  6.5 12.2 %collective-permute-start.1 = (bf16[2,4,16,576]{3,2,1,0:T(8,128)(2,1)S(1)}, bf16[2,4,16,576]{3,2,1,0:T(8,128)(2,1)S(1)}, u32[]{:S(2)}, u32[]{:S(2)}) collective-permute-start(bf16[2,4,16,576]{3,2,1,0:T(8,128)(2,1)S(1)} %pad_maximum_fusion), channel_id=1, source_target_pairs={{0,704},{64,0},{128,64},{192,128},{256,192},{320,256},{384,320},{4... | collective-permute-start | bytes 442376 | tf_op jit(solution)/shard_map/ppermute | solution.py:179
  18.8 0.9 fusion.97
  20.2 0.7 concatenate.83
  21.1 1.2 %gather_fusion = s32[72]{0:T(128)S(1)} fusion(s32[26]{0:T(128)S(1)} %concatenate.83, s32[1024]{0:T(1024)S(1)} %pad_clamp_fusion.3), kind=kCustom, calls=%fused_computation | custom fusion | bytes 864 | tf_op jit(solution)/shard_map/gather | solution.py:50
  22.5 0.7 gather_fusion.1
  23.5 0.6 gather_fusion.2
  24.2 0.6 gather_fusion.3
  27.1 2.2 %collective-permute-start.2 = (bf16[2,4,16,576]{3,2,1,0:T(8,128)(2,1)S(1)}, bf16[2,4,16,576]{3,2,1,0:T(8,128)(2,1)S(1)}, u32[]{:S(2)}, u32[]{:S(2)}) collective-permute-start(bf16[2,4,16,576]{3,2,1,0:T(8,128)(2,1)S(1)} %collective-permute-done), channel_id=1, source_target_pairs={{0,64},{64,128},{128,192},{192,256},{256,320},{320,384},{384,448},... | collective-permute-start | bytes 442376 | tf_op jit(solution)/shard_map/ppermute | solution.py:211
  29.2 4.6 %collective-permute-start.3 = (bf16[2,4,16,576]{3,2,1,0:T(8,128)(2,1)S(1)}, bf16[2,4,16,576]{3,2,1,0:T(8,128)(2,1)S(1)}, u32[]{:S(2)}, u32[]{:S(2)}) collective-permute-start(bf16[2,4,16,576]{3,2,1,0:T(8,128)(2,1)S(1)} %collective-permute-done.1), channel_id=1, source_target_pairs={{0,704},{64,0},{128,64},{192,128},{256,192},{320,256},{384,320},{4... | collective-permute-start | bytes 442376 | tf_op jit(solution)/shard_map/ppermute | solution.py:214
  35.2 0.9 collective-permute-done.3
  36.1 1.9 %collective-permute-start.4 = (bf16[2,4,16,576]{3,2,1,0:T(8,128)(2,1)S(1)}, bf16[2,4,16,576]{3,2,1,0:T(8,128)(2,1)S(1)}, u32[]{:S(2)}, u32[]{:S(2)}) collective-permute-start(bf16[2,4,16,576]{3,2,1,0:T(8,128)(2,1)S(1)} %collective-permute-done.2), channel_id=1, source_target_pairs={{0,64},{64,128},{128,192},{192,256},{256,320},{320,384},{384,448},... | collective-permute-start | bytes 442376 | tf_op jit(solution)/shard_map/ppermute | solution.py:211
  38.0 5.0 %collective-permute-start.5 = (bf16[2,4,16,576]{3,2,1,0:T(8,128)(2,1)S(1)}, bf16[2,4,16,576]{3,2,1,0:T(8,128)(2,1)S(1)}, u32[]{:S(2)}, u32[]{:S(2)}) collective-permute-start(bf16[2,4,16,576]{3,2,1,0:T(8,128)(2,1)S(1)} %collective-permute-done.3), channel_id=1, source_target_pairs={{0,704},{64,0},{128,64},{192,128},{256,192},{320,256},{384,320},{4... | collective-permute-start | bytes 442376 | tf_op jit(solution)/shard_map/ppermute | solution.py:214
  44.3 1.3 %fusion.1 = bf16[1,4,16,3,384]{4,2,3,1,0:T(8,128)(2,1)S(1)} fusion(bf16[3,3,3,192,384]{4,3,2,1,0:T(8,128)(2,1)S(1)} %bitcast.130, bf16[3,4,2,8,5,192]{5,2,4,3,1,0:T(2,128)(2,1)S(1)} %fusion.5, pred[16,3]{0,1:T(4,128)(4,1)S(1)} %copy-done.4), kind=kOutput, calls=%fused_computation.9 | convolution fusion | flops 637157376 | bytes 4497456 | tf_op jit(solution)/shard_map/conv_general_dilated | solution.py:129
  47.6 1.9 %collective-permute-start.6 = (bf16[2,4,16,576]{3,2,1,0:T(8,128)(2,1)S(1)}, bf16[2,4,16,576]{3,2,1,0:T(8,128)(2,1)S(1)}, u32[]{:S(2)}, u32[]{:S(2)}) collective-permute-start(bf16[2,4,16,576]{3,2,1,0:T(8,128)(2,1)S(1)} %collective-permute-done.4), channel_id=1, source_target_pairs={{0,64},{64,128},{128,192},{192,256},{256,320},{320,384},{384,448},... | collective-permute-start | bytes 442376 | tf_op jit(solution)/shard_map/ppermute | solution.py:211
  49.6 4.6 %collective-permute-start.7 = (bf16[2,4,16,576]{3,2,1,0:T(8,128)(2,1)S(1)}, bf16[2,4,16,576]{3,2,1,0:T(8,128)(2,1)S(1)}, u32[]{:S(2)}, u32[]{:S(2)}) collective-permute-start(bf16[2,4,16,576]{3,2,1,0:T(8,128)(2,1)S(1)} %collective-permute-done.5), channel_id=1, source_target_pairs={{0,704},{64,0},{128,64},{192,128},{256,192},{320,256},{384,320},{4... | collective-permute-start | bytes 442376 | tf_op jit(solution)/shard_map/ppermute | solution.py:214
  56.4 1.9 %collective-permute-start.8 = (bf16[2,4,16,576]{3,2,1,0:T(8,128)(2,1)S(1)}, bf16[2,4,16,576]{3,2,1,0:T(8,128)(2,1)S(1)}, u32[]{:S(2)}, u32[]{:S(2)}) collective-permute-start(bf16[2,4,16,576]{3,2,1,0:T(8,128)(2,1)S(1)} %collective-permute-done.6), channel_id=1, source_target_pairs={{0,64},{64,128},{128,192},{192,256},{256,320},{320,384},{384,448},... | collective-permute-start | bytes 442376 | tf_op jit(solution)/shard_map/ppermute | solution.py:211
  58.3 5.0 %collective-permute-start.9 = (bf16[2,4,16,576]{3,2,1,0:T(8,128)(2,1)S(1)}, bf16[2,4,16,576]{3,2,1,0:T(8,128)(2,1)S(1)}, u32[]{:S(2)}, u32[]{:S(2)}) collective-permute-start(bf16[2,4,16,576]{3,2,1,0:T(8,128)(2,1)S(1)} %collective-permute-done.7), channel_id=1, source_target_pairs={{0,704},{64,0},{128,64},{192,128},{256,192},{320,256},{384,320},{4... | collective-permute-start | bytes 442376 | tf_op jit(solution)/shard_map/ppermute | solution.py:214
  64.2 1.3 %fusion = f32[3,4,16,3,192]{4,2,3,1,0:T(8,128)S(1)} fusion(bf16[3,3,3,192,384]{4,3,2,1,0:T(8,128)(2,1)S(1)} %bitcast.131, f32[3,4,16,3,192]{4,1,3,2,0:T(4,128)S(1)} %bitcast.132, pred[16,3]{0,1:T(4,128)(4,1)S(1)} %copy-done.4, bf16[1,4,2,8,5,384]{5,2,4,3,1,0:T(2,128)(2,1)S(1)} %fusion.8), kind=kOutput, calls=%fused_computation.7 | convolution fusion | flops 637231104 | bytes 5111856 | tf_op jit(solution)/shard_map/conv_general_dilated | solution.py:144
  66.2 1.5 %collective-permute-start.10 = (f32[2,4,16,192]{3,2,1,0:T(8,128)S(1)}, f32[2,4,16,192]{3,2,1,0:T(8,128)S(1)}, u32[]{:S(2)}, u32[]{:S(2)}) collective-permute-start(f32[2,4,16,192]{3,2,1,0:T(8,128)S(1)} %slice.162), channel_id=1, source_target_pairs={{64,0},{128,64},{192,128},{256,192},{320,256},{384,320},{448,384},... | collective-permute-start | bytes 294920 | tf_op jit(solution)/shard_map/ppermute | solution.py:14
  68.2 3.6 %collective-permute-done.10 = f32[2,4,16,192]{3,2,1,0:T(8,128)S(1)} collective-permute-done((f32[2,4,16,192]{3,2,1,0:T(8,128)S(1)}, f32[2,4,16,192]{3,2,1,0:T(8,128)S(1)}, u32[]{:S(2)}, u32[]{:S(2)}) %collective-permute-start.10) | collective-permute-done | bytes 98336 | tf_op jit(solution)/shard_map/ppermute | solution.py:14
  72.3 0.7 fusion.188
  74.0 1.9 %collective-permute-start.11 = (bf16[2,4,16,576]{3,2,1,0:T(8,128)(2,1)S(1)}, bf16[2,4,16,576]{3,2,1,0:T(8,128)(2,1)S(1)}, u32[]{:S(2)}, u32[]{:S(2)}) collective-permute-start(bf16[2,4,16,576]{3,2,1,0:T(8,128)(2,1)S(1)} %collective-permute-done.8), channel_id=1, source_target_pairs={{0,64},{64,128},{128,192},{192,256},{256,320},{320,384},{384,448},... | collective-permute-start | bytes 442376 | tf_op jit(solution)/shard_map/ppermute | solution.py:211
  76.7 4.6 %collective-permute-done.11 = bf16[2,4,16,576]{3,2,1,0:T(8,128)(2,1)S(1)} collective-permute-done((bf16[2,4,16,576]{3,2,1,0:T(8,128)(2,1)S(1)}, bf16[2,4,16,576]{3,2,1,0:T(8,128)(2,1)S(1)}, u32[]{:S(2)}, u32[]{:S(2)}) %collective-permute-start.11) | collective-permute-done | bytes 147488 | tf_op jit(solution)/shard_map/ppermute | solution.py:211
  84.1 8.9 %collective-permute-start.12 = (f32[32,6,432]{2,1,0:T(8,128)S(1)}, f32[32,6,432]{2,1,0:T(8,128)S(1)}, u32[]{:S(2)}, u32[]{:S(2)}) collective-permute-start(f32[32,6,432]{2,1,0:T(8,128)S(1)} %dynamic-slice_bitcast_fusion), channel_id=1, source_target_pairs={{0,1},{1,0},{2,3},{3,2},{4,5},{5,4},{6,7},{7,6},{8,9},{9,8},{10,11... | collective-permute-start | bytes 995336 | tf_op jit(solution)/shard_map/ppermute | solution.py:227
  93.0 1.5 %collective-permute-done.12 = f32[32,6,432]{2,1,0:T(8,128)S(1)} collective-permute-done((f32[32,6,432]{2,1,0:T(8,128)S(1)}, f32[32,6,432]{2,1,0:T(8,128)S(1)}, u32[]{:S(2)}, u32[]{:S(2)}) %collective-permute-start.12) | collective-permute-done | bytes 331808 | tf_op jit(solution)/shard_map/ppermute | solution.py:227
  94.5 0.9 bitcast_add_fusion
  95.4 9.7 %all-to-all-start = ((f32[32,6,432]{2,1,0:T(8,128)}), f32[32,6,432]{2,1,0:T(8,128)S(1)}, u32[]{:S(2)}, u32[]{:S(2)}) async-start(f32[32,6,432]{2,1,0:T(8,128)} %bitcast_add_fusion), calls=%async_computation | async-start | bytes 1048576 | tf_op jit(solution)/shard_map/all_to_all | solution.py:228
  105.1 0.7 copy.45
  105.7 15.9 %all-to-all-done = f32[32,6,432]{2,1,0:T(8,128)S(1)} async-done(((f32[32,6,432]{2,1,0:T(8,128)}), f32[32,6,432]{2,1,0:T(8,128)S(1)}, u32[]{:S(2)}, u32[]{:S(2)}) %all-to-all-start) | async-done | bytes 331808 | tf_op jit(solution)/shard_map/all_to_all | solution.py:228
  121.7 0.6 multiply_bitcast_fusion
  (142 shorter events, 16.0 us)
Async XLA Ops:
  1.6 24.2 %collective-permute-start = (bf16[2,4,16,576]{3,2,1,0:T(8,128)(2,1)S(1)}, bf16[2,4,16,576]{3,2,1,0:T(8,128)(2,1)S(1)}, u32[]{:S(2)}, u32[]{:S(2)}) collective-permute-start(bf16[2,4,16,576]{3,2,1,0:T(8,128)(2,1)S(1)} %pad_maximum_fusion), channel_id=1, source_target_pairs={{0,64},{64,128},{128,192},{192,256},{256,320},{320,384},{384,448},... | collective-permute-start | bytes 442376 | tf_op jit(solution)/shard_map/ppermute | solution.py:76
  6.5 19.3 %collective-permute-start.1 = (bf16[2,4,16,576]{3,2,1,0:T(8,128)(2,1)S(1)}, bf16[2,4,16,576]{3,2,1,0:T(8,128)(2,1)S(1)}, u32[]{:S(2)}, u32[]{:S(2)}) collective-permute-start(bf16[2,4,16,576]{3,2,1,0:T(8,128)(2,1)S(1)} %pad_maximum_fusion), channel_id=1, source_target_pairs={{0,704},{64,0},{128,64},{192,128},{256,192},{320,256},{384,320},{4... | collective-permute-start | bytes 442376 | tf_op jit(solution)/shard_map/ppermute | solution.py:179
  21.1 2.2 %copy-start.5 = (s32[1,24]{1,0:T(1,128)S(1)}, s32[1,24]{1,0:T(1,128)}, u32[]{:S(2)}) copy-start(s32[1,24]{1,0:T(1,128)} %param.6) | copy-start | bytes 292
  21.1 4.9 %copy-start.1 = (bf16[1,2,4,16,192]{4,3,2,1,0:T(8,128)(2,1)S(1)}, bf16[1,2,4,16,192]{4,3,2,1,0:T(8,128)(2,1)}, u32[]{:S(2)}) copy-start(bf16[1,2,4,16,192]{4,3,2,1,0:T(8,128)(2,1)} %param.5) | copy-start | bytes 147460
  21.1 4.9 %copy-start.3 = (f32[192]{0:T(256)S(1)}, f32[192]{0:T(256)}, u32[]{:S(2)}) copy-start(f32[192]{0:T(256)} %param.7) | copy-start | bytes 2308
  22.3 4.3 %copy-start.2 = (bf16[1,2,4,16,384]{4,3,2,1,0:T(8,128)(2,1)S(1)}, bf16[1,2,4,16,384]{4,3,2,1,0:T(8,128)(2,1)}, u32[]{:S(2)}) copy-start(bf16[1,2,4,16,384]{4,3,2,1,0:T(8,128)(2,1)} %param.9) | copy-start | bytes 294916
  26.6 17.7 %copy-start = (bf16[5184,384]{1,0:T(8,128)(2,1)S(1)}, bf16[5184,384]{1,0:T(8,128)(2,1)}, u32[]{:S(2)}) copy-start(bf16[5184,384]{1,0:T(8,128)(2,1)} %param.8) | copy-start | bytes 11943940
  26.6 17.6 %copy-start.4 = (pred[16,3]{0,1:T(4,128)(4,1)S(1)}, pred[16,3]{0,1:T(4,128)(4,1)}, u32[]{:S(2)}) copy-start(pred[16,3]{0,1:T(4,128)(4,1)} %constant.660) | copy-start | bytes 148
  27.1 8.1 %collective-permute-start.2 = (bf16[2,4,16,576]{3,2,1,0:T(8,128)(2,1)S(1)}, bf16[2,4,16,576]{3,2,1,0:T(8,128)(2,1)S(1)}, u32[]{:S(2)}, u32[]{:S(2)}) collective-permute-start(bf16[2,4,16,576]{3,2,1,0:T(8,128)(2,1)S(1)} %collective-permute-done), channel_id=1, source_target_pairs={{0,64},{64,128},{128,192},{192,256},{256,320},{320,384},{384,448},... | collective-permute-start | bytes 442376 | tf_op jit(solution)/shard_map/ppermute | solution.py:211
  29.2 6.8 %collective-permute-start.3 = (bf16[2,4,16,576]{3,2,1,0:T(8,128)(2,1)S(1)}, bf16[2,4,16,576]{3,2,1,0:T(8,128)(2,1)S(1)}, u32[]{:S(2)}, u32[]{:S(2)}) collective-permute-start(bf16[2,4,16,576]{3,2,1,0:T(8,128)(2,1)S(1)} %collective-permute-done.1), channel_id=1, source_target_pairs={{0,704},{64,0},{128,64},{192,128},{256,192},{320,256},{384,320},{4... | collective-permute-start | bytes 442376 | tf_op jit(solution)/shard_map/ppermute | solution.py:214
  36.1 11.6 %collective-permute-start.4 = (bf16[2,4,16,576]{3,2,1,0:T(8,128)(2,1)S(1)}, bf16[2,4,16,576]{3,2,1,0:T(8,128)(2,1)S(1)}, u32[]{:S(2)}, u32[]{:S(2)}) collective-permute-start(bf16[2,4,16,576]{3,2,1,0:T(8,128)(2,1)S(1)} %collective-permute-done.2), channel_id=1, source_target_pairs={{0,64},{64,128},{128,192},{192,256},{256,320},{320,384},{384,448},... | collective-permute-start | bytes 442376 | tf_op jit(solution)/shard_map/ppermute | solution.py:211
  38.0 8.0 %collective-permute-start.5 = (bf16[2,4,16,576]{3,2,1,0:T(8,128)(2,1)S(1)}, bf16[2,4,16,576]{3,2,1,0:T(8,128)(2,1)S(1)}, u32[]{:S(2)}, u32[]{:S(2)}) collective-permute-start(bf16[2,4,16,576]{3,2,1,0:T(8,128)(2,1)S(1)} %collective-permute-done.3), channel_id=1, source_target_pairs={{0,704},{64,0},{128,64},{192,128},{256,192},{320,256},{384,320},{4... | collective-permute-start | bytes 442376 | tf_op jit(solution)/shard_map/ppermute | solution.py:214
  47.6 7.4 %collective-permute-start.6 = (bf16[2,4,16,576]{3,2,1,0:T(8,128)(2,1)S(1)}, bf16[2,4,16,576]{3,2,1,0:T(8,128)(2,1)S(1)}, u32[]{:S(2)}, u32[]{:S(2)}) collective-permute-start(bf16[2,4,16,576]{3,2,1,0:T(8,128)(2,1)S(1)} %collective-permute-done.4), channel_id=1, source_target_pairs={{0,64},{64,128},{128,192},{192,256},{256,320},{320,384},{384,448},... | collective-permute-start | bytes 442376 | tf_op jit(solution)/shard_map/ppermute | solution.py:211
  49.6 6.8 %collective-permute-start.7 = (bf16[2,4,16,576]{3,2,1,0:T(8,128)(2,1)S(1)}, bf16[2,4,16,576]{3,2,1,0:T(8,128)(2,1)S(1)}, u32[]{:S(2)}, u32[]{:S(2)}) collective-permute-start(bf16[2,4,16,576]{3,2,1,0:T(8,128)(2,1)S(1)} %collective-permute-done.5), channel_id=1, source_target_pairs={{0,704},{64,0},{128,64},{192,128},{256,192},{320,256},{384,320},{4... | collective-permute-start | bytes 442376 | tf_op jit(solution)/shard_map/ppermute | solution.py:214
  56.4 11.7 %collective-permute-start.8 = (bf16[2,4,16,576]{3,2,1,0:T(8,128)(2,1)S(1)}, bf16[2,4,16,576]{3,2,1,0:T(8,128)(2,1)S(1)}, u32[]{:S(2)}, u32[]{:S(2)}) collective-permute-start(bf16[2,4,16,576]{3,2,1,0:T(8,128)(2,1)S(1)} %collective-permute-done.6), channel_id=1, source_target_pairs={{0,64},{64,128},{128,192},{192,256},{256,320},{320,384},{384,448},... | collective-permute-start | bytes 442376 | tf_op jit(solution)/shard_map/ppermute | solution.py:211
  58.3 9.7 %collective-permute-start.9 = (bf16[2,4,16,576]{3,2,1,0:T(8,128)(2,1)S(1)}, bf16[2,4,16,576]{3,2,1,0:T(8,128)(2,1)S(1)}, u32[]{:S(2)}, u32[]{:S(2)}) collective-permute-start(bf16[2,4,16,576]{3,2,1,0:T(8,128)(2,1)S(1)} %collective-permute-done.7), channel_id=1, source_target_pairs={{0,704},{64,0},{128,64},{192,128},{256,192},{320,256},{384,320},{4... | collective-permute-start | bytes 442376 | tf_op jit(solution)/shard_map/ppermute | solution.py:214
  66.2 5.7 %collective-permute-start.10 = (f32[2,4,16,192]{3,2,1,0:T(8,128)S(1)}, f32[2,4,16,192]{3,2,1,0:T(8,128)S(1)}, u32[]{:S(2)}, u32[]{:S(2)}) collective-permute-start(f32[2,4,16,192]{3,2,1,0:T(8,128)S(1)} %slice.162), channel_id=1, source_target_pairs={{64,0},{128,64},{192,128},{256,192},{320,256},{384,320},{448,384},... | collective-permute-start | bytes 294920 | tf_op jit(solution)/shard_map/ppermute | solution.py:14
  74.0 7.3 %collective-permute-start.11 = (bf16[2,4,16,576]{3,2,1,0:T(8,128)(2,1)S(1)}, bf16[2,4,16,576]{3,2,1,0:T(8,128)(2,1)S(1)}, u32[]{:S(2)}, u32[]{:S(2)}) collective-permute-start(bf16[2,4,16,576]{3,2,1,0:T(8,128)(2,1)S(1)} %collective-permute-done.8), channel_id=1, source_target_pairs={{0,64},{64,128},{128,192},{192,256},{256,320},{320,384},{384,448},... | collective-permute-start | bytes 442376 | tf_op jit(solution)/shard_map/ppermute | solution.py:211
  84.1 10.4 %collective-permute-start.12 = (f32[32,6,432]{2,1,0:T(8,128)S(1)}, f32[32,6,432]{2,1,0:T(8,128)S(1)}, u32[]{:S(2)}, u32[]{:S(2)}) collective-permute-start(f32[32,6,432]{2,1,0:T(8,128)S(1)} %dynamic-slice_bitcast_fusion), channel_id=1, source_target_pairs={{0,1},{1,0},{2,3},{3,2},{4,5},{5,4},{6,7},{7,6},{8,9},{9,8},{10,11... | collective-permute-start | bytes 995336 | tf_op jit(solution)/shard_map/ppermute | solution.py:227
  95.4 26.3 %all-to-all-start = ((f32[32,6,432]{2,1,0:T(8,128)}), f32[32,6,432]{2,1,0:T(8,128)S(1)}, u32[]{:S(2)}, u32[]{:S(2)}) async-start(f32[32,6,432]{2,1,0:T(8,128)} %bitcast_add_fusion), calls=%async_computation | async-start | bytes 1048576 | tf_op jit(solution)/shard_map/all_to_all | solution.py:228

commit v11 on v10

--- a/solution.py
+++ b/solution.py
@@ -225,7 +225,9 @@
     kept = lax.dynamic_index_in_dim(pieces, core, 1, keepdims=False)
     sent = lax.dynamic_index_in_dim(pieces, 1 - core, 1, keepdims=False)
     pair_sum = kept + lax.ppermute(sent, "dc", [(0, 1), (1, 0)])
-    reduced_t = lax.all_to_all(pair_sum, "dq", 0, 0, tiled=False).sum(axis=0)
+    reduced_t = lax.all_to_all(pair_sum.astype(jnp.bfloat16), "dq", 0, 0, tiled=False).astype(
+        jnp.float32
+    ).sum(axis=0)
     grad_weight = reduced_t.T * scale
     conv_out = conv_rows.reshape(1, frames, height, width, outputs)
     return (conv_out, video_grad[None], grad_weight)

time: 123 us -> 118 us (0.959)
  waiting for transfers between devices: 27.6 us -> 22.6 us
    all_to_all x1, waiting for transfers between devices: 15.9 us -> 10.9 us  [shards(): lax.all_to_all(pair_sum.astype(jnp.bfloat16), 'dq', 0, 0, tiled=False)]
where the time goes in v11:
time: 118 us; the launch traced here: 117 us
  starting transfers between devices  66.2 us (56%)
  waiting for transfers between devices  22.6 us (19%)
  other arithmetic  9.77 us (8%)
  local copies, waits for them, and re-layouts  8.91 us (8%)
  matrix products  7.52 us (6%)
  between operations  2.24 us (2%)
    ppermute x4, starting transfers between devices, shards(): backward_moving = lax.ppermute(backward_moving, 'tm', ring_route('tm', -1))  19.2 us
    ppermute x1, starting transfers between devices, shards(): backward_moving = lax.ppermute(both, 'tm', ring_route('tm', -1))  12.2 us
    all_to_all x1, waiting for transfers between devices, shards(): lax.all_to_all(pair_sum.astype(jnp.bfloat16), 'dq', 0, 0, tiled=False)  10.9 us
    ppermute x5, starting transfers between devices, shards(): forward_moving = lax.ppermute(forward_moving, 'tm', ring_route('tm', 1))  9.84 us
    all_to_all x1, starting transfers between devices, shards(): lax.all_to_all(pair_sum.astype(jnp.bfloat16), 'dq', 0, 0, tiled=False)  9.67 us
    ppermute x1, starting transfers between devices, shards(): pair_sum = kept + lax.ppermute(sent, 'dc', [(0, 1), (1, 0)])  8.92 us
    ppermute x5, waiting for transfers between devices, shards(): forward_moving = lax.ppermute(forward_moving, 'tm', ring_route('tm', 1))  5.2 us
    dot_general x12, matrix products, block_term(): lax.dot_general(block_cot, jnp.concatenate(columns, axis=1), (((0,), (0,)...  4.98 us
  transfers between devices with their start and end apart: 14, of which 7 were waited for; matrix products, arithmetic and copies ran while one was open for 15% of the time, Pallas kernels for 0%

profile of v11, /device:TPU:1, one launch (start us, length us, event | category | flops | bytes accessed | tf_op | source)
XLA Modules:
  0.0 117.2 jit_solution(16657237808545422193)
XLA Ops:
  0.6 1.0 pad_maximum_fusion
  1.6 4.8 %collective-permute-start = (bf16[2,4,16,576]{3,2,1,0:T(8,128)(2,1)S(1)}, bf16[2,4,16,576]{3,2,1,0:T(8,128)(2,1)S(1)}, u32[]{:S(2)}, u32[]{:S(2)}) collective-permute-start(bf16[2,4,16,576]{3,2,1,0:T(8,128)(2,1)S(1)} %pad_maximum_fusion), channel_id=1, source_target_pairs={{0,64},{64,128},{128,192},{192,256},{256,320},{320,384},{384,448},... | collective-permute-start | bytes 442376 | tf_op jit(solution)/shard_map/ppermute | solution.py:76
  6.5 12.2 %collective-permute-start.1 = (bf16[2,4,16,576]{3,2,1,0:T(8,128)(2,1)S(1)}, bf16[2,4,16,576]{3,2,1,0:T(8,128)(2,1)S(1)}, u32[]{:S(2)}, u32[]{:S(2)}) collective-permute-start(bf16[2,4,16,576]{3,2,1,0:T(8,128)(2,1)S(1)} %pad_maximum_fusion), channel_id=1, source_target_pairs={{0,704},{64,0},{128,64},{192,128},{256,192},{320,256},{384,320},{4... | collective-permute-start | bytes 442376 | tf_op jit(solution)/shard_map/ppermute | solution.py:179
  18.8 0.9 fusion.98
  20.2 0.7 concatenate.83
  21.1 1.2 %gather_fusion = s32[72]{0:T(128)S(1)} fusion(s32[26]{0:T(128)S(1)} %concatenate.83, s32[1024]{0:T(1024)S(1)} %pad_clamp_fusion.3), kind=kCustom, calls=%fused_computation | custom fusion | bytes 864 | tf_op jit(solution)/shard_map/gather | solution.py:50
  22.5 0.7 gather_fusion.1
  23.5 0.6 gather_fusion.2
  24.2 0.6 gather_fusion.3
  27.1 2.2 %collective-permute-start.2 = (bf16[2,4,16,576]{3,2,1,0:T(8,128)(2,1)S(1)}, bf16[2,4,16,576]{3,2,1,0:T(8,128)(2,1)S(1)}, u32[]{:S(2)}, u32[]{:S(2)}) collective-permute-start(bf16[2,4,16,576]{3,2,1,0:T(8,128)(2,1)S(1)} %collective-permute-done), channel_id=1, source_target_pairs={{0,64},{64,128},{128,192},{192,256},{256,320},{320,384},{384,448},... | collective-permute-start | bytes 442376 | tf_op jit(solution)/shard_map/ppermute | solution.py:211
  29.2 4.6 %collective-permute-start.3 = (bf16[2,4,16,576]{3,2,1,0:T(8,128)(2,1)S(1)}, bf16[2,4,16,576]{3,2,1,0:T(8,128)(2,1)S(1)}, u32[]{:S(2)}, u32[]{:S(2)}) collective-permute-start(bf16[2,4,16,576]{3,2,1,0:T(8,128)(2,1)S(1)} %collective-permute-done.1), channel_id=1, source_target_pairs={{0,704},{64,0},{128,64},{192,128},{256,192},{320,256},{384,320},{4... | collective-permute-start | bytes 442376 | tf_op jit(solution)/shard_map/ppermute | solution.py:214
  35.2 0.9 collective-permute-done.3
  36.1 1.9 %collective-permute-start.4 = (bf16[2,4,16,576]{3,2,1,0:T(8,128)(2,1)S(1)}, bf16[2,4,16,576]{3,2,1,0:T(8,128)(2,1)S(1)}, u32[]{:S(2)}, u32[]{:S(2)}) collective-permute-start(bf16[2,4,16,576]{3,2,1,0:T(8,128)(2,1)S(1)} %collective-permute-done.2), channel_id=1, source_target_pairs={{0,64},{64,128},{128,192},{192,256},{256,320},{320,384},{384,448},... | collective-permute-start | bytes 442376 | tf_op jit(solution)/shard_map/ppermute | solution.py:211
  38.0 5.0 %collective-permute-start.5 = (bf16[2,4,16,576]{3,2,1,0:T(8,128)(2,1)S(1)}, bf16[2,4,16,576]{3,2,1,0:T(8,128)(2,1)S(1)}, u32[]{:S(2)}, u32[]{:S(2)}) collective-permute-start(bf16[2,4,16,576]{3,2,1,0:T(8,128)(2,1)S(1)} %collective-permute-done.3), channel_id=1, source_target_pairs={{0,704},{64,0},{128,64},{192,128},{256,192},{320,256},{384,320},{4... | collective-permute-start | bytes 442376 | tf_op jit(solution)/shard_map/ppermute | solution.py:214
  44.3 1.3 %fusion.1 = bf16[1,4,16,3,384]{4,2,3,1,0:T(8,128)(2,1)S(1)} fusion(bf16[3,3,3,192,384]{4,3,2,1,0:T(8,128)(2,1)S(1)} %bitcast.132, bf16[3,4,2,8,5,192]{5,2,4,3,1,0:T(2,128)(2,1)S(1)} %fusion.6, pred[16,3]{0,1:T(4,128)(4,1)S(1)} %copy-done.4), kind=kOutput, calls=%fused_computation.9 | convolution fusion | flops 637157376 | bytes 4497456 | tf_op jit(solution)/shard_map/conv_general_dilated | solution.py:129
  47.6 1.9 %collective-permute-start.6 = (bf16[2,4,16,576]{3,2,1,0:T(8,128)(2,1)S(1)}, bf16[2,4,16,576]{3,2,1,0:T(8,128)(2,1)S(1)}, u32[]{:S(2)}, u32[]{:S(2)}) collective-permute-start(bf16[2,4,16,576]{3,2,1,0:T(8,128)(2,1)S(1)} %collective-permute-done.4), channel_id=1, source_target_pairs={{0,64},{64,128},{128,192},{192,256},{256,320},{320,384},{384,448},... | collective-permute-start | bytes 442376 | tf_op jit(solution)/shard_map/ppermute | solution.py:211
  49.6 4.6 %collective-permute-start.7 = (bf16[2,4,16,576]{3,2,1,0:T(8,128)(2,1)S(1)}, bf16[2,4,16,576]{3,2,1,0:T(8,128)(2,1)S(1)}, u32[]{:S(2)}, u32[]{:S(2)}) collective-permute-start(bf16[2,4,16,576]{3,2,1,0:T(8,128)(2,1)S(1)} %collective-permute-done.5), channel_id=1, source_target_pairs={{0,704},{64,0},{128,64},{192,128},{256,192},{320,256},{384,320},{4... | collective-permute-start | bytes 442376 | tf_op jit(solution)/shard_map/ppermute | solution.py:214
  56.4 1.9 %collective-permute-start.8 = (bf16[2,4,16,576]{3,2,1,0:T(8,128)(2,1)S(1)}, bf16[2,4,16,576]{3,2,1,0:T(8,128)(2,1)S(1)}, u32[]{:S(2)}, u32[]{:S(2)}) collective-permute-start(bf16[2,4,16,576]{3,2,1,0:T(8,128)(2,1)S(1)} %collective-permute-done.6), channel_id=1, source_target_pairs={{0,64},{64,128},{128,192},{192,256},{256,320},{320,384},{384,448},... | collective-permute-start | bytes 442376 | tf_op jit(solution)/shard_map/ppermute | solution.py:211
  58.3 5.0 %collective-permute-start.9 = (bf16[2,4,16,576]{3,2,1,0:T(8,128)(2,1)S(1)}, bf16[2,4,16,576]{3,2,1,0:T(8,128)(2,1)S(1)}, u32[]{:S(2)}, u32[]{:S(2)}) collective-permute-start(bf16[2,4,16,576]{3,2,1,0:T(8,128)(2,1)S(1)} %collective-permute-done.7), channel_id=1, source_target_pairs={{0,704},{64,0},{128,64},{192,128},{256,192},{320,256},{384,320},{4... | collective-permute-start | bytes 442376 | tf_op jit(solution)/shard_map/ppermute | solution.py:214
  64.2 1.3 %fusion = f32[3,4,16,3,192]{4,2,3,1,0:T(8,128)S(1)} fusion(bf16[3,3,3,192,384]{4,3,2,1,0:T(8,128)(2,1)S(1)} %bitcast.133, f32[3,4,16,3,192]{4,1,3,2,0:T(4,128)S(1)} %bitcast.134, pred[16,3]{0,1:T(4,128)(4,1)S(1)} %copy-done.4, bf16[1,4,2,8,5,384]{5,2,4,3,1,0:T(2,128)(2,1)S(1)} %fusion.9), kind=kOutput, calls=%fused_computation.7 | convolution fusion | flops 637231104 | bytes 5111856 | tf_op jit(solution)/shard_map/conv_general_dilated | solution.py:144
  66.2 1.5 %collective-permute-start.10 = (f32[2,4,16,192]{3,2,1,0:T(8,128)S(1)}, f32[2,4,16,192]{3,2,1,0:T(8,128)S(1)}, u32[]{:S(2)}, u32[]{:S(2)}) collective-permute-start(f32[2,4,16,192]{3,2,1,0:T(8,128)S(1)} %slice.162), channel_id=1, source_target_pairs={{64,0},{128,64},{192,128},{256,192},{320,256},{384,320},{448,384},... | collective-permute-start | bytes 294920 | tf_op jit(solution)/shard_map/ppermute | solution.py:14
  68.2 3.6 %collective-permute-done.10 = f32[2,4,16,192]{3,2,1,0:T(8,128)S(1)} collective-permute-done((f32[2,4,16,192]{3,2,1,0:T(8,128)S(1)}, f32[2,4,16,192]{3,2,1,0:T(8,128)S(1)}, u32[]{:S(2)}, u32[]{:S(2)}) %collective-permute-start.10) | collective-permute-done | bytes 98336 | tf_op jit(solution)/shard_map/ppermute | solution.py:14
  72.3 0.7 fusion.189
  74.0 1.9 %collective-permute-start.11 = (bf16[2,4,16,576]{3,2,1,0:T(8,128)(2,1)S(1)}, bf16[2,4,16,576]{3,2,1,0:T(8,128)(2,1)S(1)}, u32[]{:S(2)}, u32[]{:S(2)}) collective-permute-start(bf16[2,4,16,576]{3,2,1,0:T(8,128)(2,1)S(1)} %collective-permute-done.8), channel_id=1, source_target_pairs={{0,64},{64,128},{128,192},{192,256},{256,320},{320,384},{384,448},... | collective-permute-start | bytes 442376 | tf_op jit(solution)/shard_map/ppermute | solution.py:211
  76.7 4.6 %collective-permute-done.11 = bf16[2,4,16,576]{3,2,1,0:T(8,128)(2,1)S(1)} collective-permute-done((bf16[2,4,16,576]{3,2,1,0:T(8,128)(2,1)S(1)}, bf16[2,4,16,576]{3,2,1,0:T(8,128)(2,1)S(1)}, u32[]{:S(2)}, u32[]{:S(2)}) %collective-permute-start.11) | collective-permute-done | bytes 147488 | tf_op jit(solution)/shard_map/ppermute | solution.py:211
  84.1 8.9 %collective-permute-start.12 = (f32[32,6,432]{2,1,0:T(8,128)S(1)}, f32[32,6,432]{2,1,0:T(8,128)S(1)}, u32[]{:S(2)}, u32[]{:S(2)}) collective-permute-start(f32[32,6,432]{2,1,0:T(8,128)S(1)} %dynamic-slice_bitcast_fusion), channel_id=1, source_target_pairs={{0,1},{1,0},{2,3},{3,2},{4,5},{5,4},{6,7},{7,6},{8,9},{9,8},{10,11... | collective-permute-start | bytes 995336 | tf_op jit(solution)/shard_map/ppermute | solution.py:227
  93.0 1.5 %collective-permute-done.12 = f32[32,6,432]{2,1,0:T(8,128)S(1)} collective-permute-done((f32[32,6,432]{2,1,0:T(8,128)S(1)}, f32[32,6,432]{2,1,0:T(8,128)S(1)}, u32[]{:S(2)}, u32[]{:S(2)}) %collective-permute-start.12) | collective-permute-done | bytes 331808 | tf_op jit(solution)/shard_map/ppermute | solution.py:227
  94.5 0.8 fusion.5
  95.3 9.7 %all-to-all-start = ((bf16[32,6,432]{2,1,0:T(8,128)(2,1)}), bf16[32,6,432]{2,1,0:T(8,128)(2,1)S(1)}, u32[]{:S(2)}, u32[]{:S(2)}) async-start(bf16[32,6,432]{2,1,0:T(8,128)(2,1)} %fusion.5), calls=%async_computation | async-start | bytes 524288 | tf_op jit(solution)/shard_map/all_to_all | solution.py:228
  105.0 0.7 copy.45
  105.6 10.9 %all-to-all-done = bf16[32,6,432]{2,1,0:T(8,128)(2,1)S(1)} async-done(((bf16[32,6,432]{2,1,0:T(8,128)(2,1)}), bf16[32,6,432]{2,1,0:T(8,128)(2,1)S(1)}, u32[]{:S(2)}, u32[]{:S(2)}) %all-to-all-start) | async-done | bytes 165920 | tf_op jit(solution)/shard_map/all_to_all | solution.py:228
  116.6 0.6 multiply_bitcast_fusion
  (142 shorter events, 16.0 us)
Async XLA Ops:
  1.6 24.2 %collective-permute-start = (bf16[2,4,16,576]{3,2,1,0:T(8,128)(2,1)S(1)}, bf16[2,4,16,576]{3,2,1,0:T(8,128)(2,1)S(1)}, u32[]{:S(2)}, u32[]{:S(2)}) collective-permute-start(bf16[2,4,16,576]{3,2,1,0:T(8,128)(2,1)S(1)} %pad_maximum_fusion), channel_id=1, source_target_pairs={{0,64},{64,128},{128,192},{192,256},{256,320},{320,384},{384,448},... | collective-permute-start | bytes 442376 | tf_op jit(solution)/shard_map/ppermute | solution.py:76
  6.5 19.3 %collective-permute-start.1 = (bf16[2,4,16,576]{3,2,1,0:T(8,128)(2,1)S(1)}, bf16[2,4,16,576]{3,2,1,0:T(8,128)(2,1)S(1)}, u32[]{:S(2)}, u32[]{:S(2)}) collective-permute-start(bf16[2,4,16,576]{3,2,1,0:T(8,128)(2,1)S(1)} %pad_maximum_fusion), channel_id=1, source_target_pairs={{0,704},{64,0},{128,64},{192,128},{256,192},{320,256},{384,320},{4... | collective-permute-start | bytes 442376 | tf_op jit(solution)/shard_map/ppermute | solution.py:179
  21.1 2.2 %copy-start.5 = (s32[1,24]{1,0:T(1,128)S(1)}, s32[1,24]{1,0:T(1,128)}, u32[]{:S(2)}) copy-start(s32[1,24]{1,0:T(1,128)} %param.6) | copy-start | bytes 292
  21.1 4.9 %copy-start.1 = (bf16[1,2,4,16,192]{4,3,2,1,0:T(8,128)(2,1)S(1)}, bf16[1,2,4,16,192]{4,3,2,1,0:T(8,128)(2,1)}, u32[]{:S(2)}) copy-start(bf16[1,2,4,16,192]{4,3,2,1,0:T(8,128)(2,1)} %param.5) | copy-start | bytes 147460
  21.1 4.9 %copy-start.3 = (f32[192]{0:T(256)S(1)}, f32[192]{0:T(256)}, u32[]{:S(2)}) copy-start(f32[192]{0:T(256)} %param.7) | copy-start | bytes 2308
  22.3 4.3 %copy-start.2 = (bf16[1,2,4,16,384]{4,3,2,1,0:T(8,128)(2,1)S(1)}, bf16[1,2,4,16,384]{4,3,2,1,0:T(8,128)(2,1)}, u32[]{:S(2)}) copy-start(bf16[1,2,4,16,384]{4,3,2,1,0:T(8,128)(2,1)} %param.9) | copy-start | bytes 294916
  26.6 17.7 %copy-start = (bf16[5184,384]{1,0:T(8,128)(2,1)S(1)}, bf16[5184,384]{1,0:T(8,128)(2,1)}, u32[]{:S(2)}) copy-start(bf16[5184,384]{1,0:T(8,128)(2,1)} %param.8) | copy-start | bytes 11943940
  26.6 17.6 %copy-start.4 = (pred[16,3]{0,1:T(4,128)(4,1)S(1)}, pred[16,3]{0,1:T(4,128)(4,1)}, u32[]{:S(2)}) copy-start(pred[16,3]{0,1:T(4,128)(4,1)} %constant.660) | copy-start | bytes 148
  27.1 8.1 %collective-permute-start.2 = (bf16[2,4,16,576]{3,2,1,0:T(8,128)(2,1)S(1)}, bf16[2,4,16,576]{3,2,1,0:T(8,128)(2,1)S(1)}, u32[]{:S(2)}, u32[]{:S(2)}) collective-permute-start(bf16[2,4,16,576]{3,2,1,0:T(8,128)(2,1)S(1)} %collective-permute-done), channel_id=1, source_target_pairs={{0,64},{64,128},{128,192},{192,256},{256,320},{320,384},{384,448},... | collective-permute-start | bytes 442376 | tf_op jit(solution)/shard_map/ppermute | solution.py:211
  29.2 6.8 %collective-permute-start.3 = (bf16[2,4,16,576]{3,2,1,0:T(8,128)(2,1)S(1)}, bf16[2,4,16,576]{3,2,1,0:T(8,128)(2,1)S(1)}, u32[]{:S(2)}, u32[]{:S(2)}) collective-permute-start(bf16[2,4,16,576]{3,2,1,0:T(8,128)(2,1)S(1)} %collective-permute-done.1), channel_id=1, source_target_pairs={{0,704},{64,0},{128,64},{192,128},{256,192},{320,256},{384,320},{4... | collective-permute-start | bytes 442376 | tf_op jit(solution)/shard_map/ppermute | solution.py:214
  36.1 11.6 %collective-permute-start.4 = (bf16[2,4,16,576]{3,2,1,0:T(8,128)(2,1)S(1)}, bf16[2,4,16,576]{3,2,1,0:T(8,128)(2,1)S(1)}, u32[]{:S(2)}, u32[]{:S(2)}) collective-permute-start(bf16[2,4,16,576]{3,2,1,0:T(8,128)(2,1)S(1)} %collective-permute-done.2), channel_id=1, source_target_pairs={{0,64},{64,128},{128,192},{192,256},{256,320},{320,384},{384,448},... | collective-permute-start | bytes 442376 | tf_op jit(solution)/shard_map/ppermute | solution.py:211
  38.0 8.0 %collective-permute-start.5 = (bf16[2,4,16,576]{3,2,1,0:T(8,128)(2,1)S(1)}, bf16[2,4,16,576]{3,2,1,0:T(8,128)(2,1)S(1)}, u32[]{:S(2)}, u32[]{:S(2)}) collective-permute-start(bf16[2,4,16,576]{3,2,1,0:T(8,128)(2,1)S(1)} %collective-permute-done.3), channel_id=1, source_target_pairs={{0,704},{64,0},{128,64},{192,128},{256,192},{320,256},{384,320},{4... | collective-permute-start | bytes 442376 | tf_op jit(solution)/shard_map/ppermute | solution.py:214
  47.6 7.4 %collective-permute-start.6 = (bf16[2,4,16,576]{3,2,1,0:T(8,128)(2,1)S(1)}, bf16[2,4,16,576]{3,2,1,0:T(8,128)(2,1)S(1)}, u32[]{:S(2)}, u32[]{:S(2)}) collective-permute-start(bf16[2,4,16,576]{3,2,1,0:T(8,128)(2,1)S(1)} %collective-permute-done.4), channel_id=1, source_target_pairs={{0,64},{64,128},{128,192},{192,256},{256,320},{320,384},{384,448},... | collective-permute-start | bytes 442376 | tf_op jit(solution)/shard_map/ppermute | solution.py:211
  49.6 6.8 %collective-permute-start.7 = (bf16[2,4,16,576]{3,2,1,0:T(8,128)(2,1)S(1)}, bf16[2,4,16,576]{3,2,1,0:T(8,128)(2,1)S(1)}, u32[]{:S(2)}, u32[]{:S(2)}) collective-permute-start(bf16[2,4,16,576]{3,2,1,0:T(8,128)(2,1)S(1)} %collective-permute-done.5), channel_id=1, source_target_pairs={{0,704},{64,0},{128,64},{192,128},{256,192},{320,256},{384,320},{4... | collective-permute-start | bytes 442376 | tf_op jit(solution)/shard_map/ppermute | solution.py:214
  56.4 11.7 %collective-permute-start.8 = (bf16[2,4,16,576]{3,2,1,0:T(8,128)(2,1)S(1)}, bf16[2,4,16,576]{3,2,1,0:T(8,128)(2,1)S(1)}, u32[]{:S(2)}, u32[]{:S(2)}) collective-permute-start(bf16[2,4,16,576]{3,2,1,0:T(8,128)(2,1)S(1)} %collective-permute-done.6), channel_id=1, source_target_pairs={{0,64},{64,128},{128,192},{192,256},{256,320},{320,384},{384,448},... | collective-permute-start | bytes 442376 | tf_op jit(solution)/shard_map/ppermute | solution.py:211
  58.3 9.7 %collective-permute-start.9 = (bf16[2,4,16,576]{3,2,1,0:T(8,128)(2,1)S(1)}, bf16[2,4,16,576]{3,2,1,0:T(8,128)(2,1)S(1)}, u32[]{:S(2)}, u32[]{:S(2)}) collective-permute-start(bf16[2,4,16,576]{3,2,1,0:T(8,128)(2,1)S(1)} %collective-permute-done.7), channel_id=1, source_target_pairs={{0,704},{64,0},{128,64},{192,128},{256,192},{320,256},{384,320},{4... | collective-permute-start | bytes 442376 | tf_op jit(solution)/shard_map/ppermute | solution.py:214
  66.2 5.7 %collective-permute-start.10 = (f32[2,4,16,192]{3,2,1,0:T(8,128)S(1)}, f32[2,4,16,192]{3,2,1,0:T(8,128)S(1)}, u32[]{:S(2)}, u32[]{:S(2)}) collective-permute-start(f32[2,4,16,192]{3,2,1,0:T(8,128)S(1)} %slice.162), channel_id=1, source_target_pairs={{64,0},{128,64},{192,128},{256,192},{320,256},{384,320},{448,384},... | collective-permute-start | bytes 294920 | tf_op jit(solution)/shard_map/ppermute | solution.py:14
  74.0 7.3 %collective-permute-start.11 = (bf16[2,4,16,576]{3,2,1,0:T(8,128)(2,1)S(1)}, bf16[2,4,16,576]{3,2,1,0:T(8,128)(2,1)S(1)}, u32[]{:S(2)}, u32[]{:S(2)}) collective-permute-start(bf16[2,4,16,576]{3,2,1,0:T(8,128)(2,1)S(1)} %collective-permute-done.8), channel_id=1, source_target_pairs={{0,64},{64,128},{128,192},{192,256},{256,320},{320,384},{384,448},... | collective-permute-start | bytes 442376 | tf_op jit(solution)/shard_map/ppermute | solution.py:211
  84.1 10.4 %collective-permute-start.12 = (f32[32,6,432]{2,1,0:T(8,128)S(1)}, f32[32,6,432]{2,1,0:T(8,128)S(1)}, u32[]{:S(2)}, u32[]{:S(2)}) collective-permute-start(f32[32,6,432]{2,1,0:T(8,128)S(1)} %dynamic-slice_bitcast_fusion), channel_id=1, source_target_pairs={{0,1},{1,0},{2,3},{3,2},{4,5},{5,4},{6,7},{7,6},{8,9},{9,8},{10,11... | collective-permute-start | bytes 995336 | tf_op jit(solution)/shard_map/ppermute | solution.py:227
  95.3 21.3 %all-to-all-start = ((bf16[32,6,432]{2,1,0:T(8,128)(2,1)}), bf16[32,6,432]{2,1,0:T(8,128)(2,1)S(1)}, u32[]{:S(2)}, u32[]{:S(2)}) async-start(bf16[32,6,432]{2,1,0:T(8,128)(2,1)} %fusion.5), calls=%async_computation | async-start | bytes 524288 | tf_op jit(solution)/shard_map/all_to_all | solution.py:228

commit v12 on v11

--- a/solution.py
+++ b/solution.py
@@ -73,7 +73,10 @@
     outputs = conv_weight.shape[1]
     activated = activate(video, norm_gain).astype(jnp.bfloat16)
     both = jnp.concatenate([video, out_cotangent[0]], axis=-1)
-    first_behind = lax.ppermute(both, "tm", ring_route("tm", 1))
+    block_shape = both.shape
+    dense = both.reshape(-1, 128)
+    dense_behind = lax.ppermute(dense, "tm", ring_route("tm", 1))
+    first_behind = dense_behind.reshape(block_shape)
     previous = activate(first_behind[..., :channels], norm_gain).astype(jnp.bfloat16)
     extended = jnp.concatenate([previous, activated])
     chain_len = lax.axis_size("tm")
@@ -175,8 +178,8 @@
     grad_inputs = (out_cotangent[0], conv_weight, video)
     forward_steps = chain_len // 2
     backward_steps = chain_len - 1 - forward_steps
-    forward_moving = first_behind
-    backward_moving = lax.ppermute(both, "tm", ring_route("tm", -1))
+    forward_moving = dense_behind
+    backward_moving = lax.ppermute(dense, "tm", ring_route("tm", -1))
     arrived = [(chain_len - 1, None), (1, backward_moving)]
     for step in range(2, forward_steps + 1):
         total = add_ready(total)
@@ -206,7 +209,7 @@
             )
         for rel, block in arrived:
             if block is not None:
-                blocks[rel] = block
+                blocks[rel] = block = block.reshape(block_shape)
                 block_acts[rel] = activate(block[..., :channels], norm_gain).astype(jnp.bfloat16)
         forward_moving = lax.ppermute(forward_moving, "tm", ring_route("tm", 1))
         arrived = [(chain_len - step, forward_moving)]
@@ -214,7 +217,7 @@
             backward_moving = lax.ppermute(backward_moving, "tm", ring_route("tm", -1))
             arrived.append((step, backward_moving))
     for rel, block in arrived:
-        blocks[rel] = block
+        blocks[rel] = block = block.reshape(block_shape)
         block_acts[rel] = activate(block[..., :channels], norm_gain).astype(jnp.bfloat16)
     total = add_ready(total)
     slab_t = lax.dynamic_slice_in_dim(total, slab_offset, slab_rows, 1)

time: 118 us -> 129 us (1.093)
  local copies, waits for them, and re-layouts: 8.91 us -> 17.2 us
  matrix products: 7.52 us -> 9.68 us
    reshape x0 -> x12, local copies, waits for them, and re-layouts: none -> 5.56 us  [the longest x10 5.21 us: shards(): blocks[rel] = block = block.reshape(block_shape)]
    conv_general_dilated x1, matrix products: 1.27 us -> 3.42 us  [forward_section(): lax.conv_general_dilated(masked_taps, kernel, (1, 1, 1), ((0, 0), (1, 1),...]
  transfers between devices with their start and end apart: 14 -> 14, of which waited for: 7 -> 6; matrix products, arithmetic and copies ran while one was open for 15% -> 19% of each run, Pallas kernels for 0% -> 0%
where the time goes in v12:
time: 129 us; the launch traced here: 128 us
  starting transfers between devices  65.6 us (51%)
  waiting for transfers between devices  22.4 us (17%)
  local copies, waits for them, and re-layouts  17.2 us (13%)
  other arithmetic  10.4 us (8%)
  matrix products  9.68 us (8%)
  between operations  2.61 us (2%)
    ppermute x4, starting transfers between devices, shards(): backward_moving = lax.ppermute(backward_moving, 'tm', ring_route('tm', -1))  19.2 us
    ppermute x1, starting transfers between devices, shards(): backward_moving = lax.ppermute(dense, 'tm', ring_route('tm', -1))  12.2 us
    all_to_all x1, waiting for transfers between devices, shards(): lax.all_to_all(pair_sum.astype(jnp.bfloat16), 'dq', 0, 0, tiled=False)  10.9 us
    ppermute x5, starting transfers between devices, shards(): forward_moving = lax.ppermute(forward_moving, 'tm', ring_route('tm', 1))  9.74 us
    all_to_all x1, starting transfers between devices, shards(): lax.all_to_all(pair_sum.astype(jnp.bfloat16), 'dq', 0, 0, tiled=False)  9.66 us
    ppermute x1, starting transfers between devices, shards(): pair_sum = kept + lax.ppermute(sent, 'dc', [(0, 1), (1, 0)])  8.59 us
    reshape x10, local copies, waits for them, and re-layouts, shards(): blocks[rel] = block = block.reshape(block_shape)  5.21 us
    dot_general x12, matrix products, block_term(): lax.dot_general(block_cot, jnp.concatenate(columns, axis=1), (((0,), (0,)...  4.98 us
  transfers between devices with their start and end apart: 14, of which 6 were waited for; matrix products, arithmetic and copies ran while one was open for 19% of the time, Pallas kernels for 0%

profile of v12, /device:TPU:1, one launch (start us, length us, event | category | flops | bytes accessed | tf_op | source)
XLA Modules:
  0.0 127.8 jit_solution(138119968238273868)
XLA Ops:
  0.6 1.0 pad_maximum_fusion
  1.8 4.8 %collective-permute-start = (bf16[576,128]{1,0:T(8,128)(2,1)S(1)}, bf16[576,128]{1,0:T(8,128)(2,1)S(1)}, u32[]{:S(2)}, u32[]{:S(2)}) collective-permute-start(bf16[576,128]{1,0:T(8,128)(2,1)S(1)} %reshape.505), channel_id=1, source_target_pairs={{0,64},{64,128},{128,192},{192,256},{256,320},{320,384},{384,448},... | collective-permute-start | bytes 442376 | tf_op jit(solution)/shard_map/ppermute | solution.py:78
  6.7 12.2 %collective-permute-start.1 = (bf16[576,128]{1,0:T(8,128)(2,1)S(1)}, bf16[576,128]{1,0:T(8,128)(2,1)S(1)}, u32[]{:S(2)}, u32[]{:S(2)}) collective-permute-start(bf16[576,128]{1,0:T(8,128)(2,1)S(1)} %reshape.505), channel_id=1, source_target_pairs={{0,704},{64,0},{128,64},{192,128},{256,192},{320,256},{384,320},{4... | collective-permute-start | bytes 442376 | tf_op jit(solution)/shard_map/ppermute | solution.py:182
  19.0 0.9 fusion.98
  21.3 1.2 gather_fusion
  25.4 1.1 dynamic-slice_reduce_fusion.11
  28.2 1.9 %collective-permute-start.2 = (bf16[576,128]{1,0:T(8,128)(2,1)S(1)}, bf16[576,128]{1,0:T(8,128)(2,1)}, u32[]{:S(2)}, u32[]{:S(2)}) collective-permute-start(bf16[576,128]{1,0:T(8,128)(2,1)S(1)} %collective-permute-done), channel_id=1, source_target_pairs={{0,64},{64,128},{128,192},{192,256},{256,320},{320,384},{384,448},... | collective-permute-start | bytes 442376 | tf_op jit(solution)/shard_map/ppermute | solution.py:214
  30.1 4.6 %collective-permute-start.3 = (bf16[576,128]{1,0:T(8,128)(2,1)S(1)}, bf16[576,128]{1,0:T(8,128)(2,1)S(1)}, u32[]{:S(2)}, u32[]{:S(2)}) collective-permute-start(bf16[576,128]{1,0:T(8,128)(2,1)S(1)} %collective-permute-done.1), channel_id=1, source_target_pairs={{0,704},{64,0},{128,64},{192,128},{256,192},{320,256},{384,320},{4... | collective-permute-start | bytes 442376 | tf_op jit(solution)/shard_map/ppermute | solution.py:217
  35.3 1.4 %collective-permute-done.3 = bf16[576,128]{1,0:T(8,128)(2,1)S(1)} collective-permute-done((bf16[576,128]{1,0:T(8,128)(2,1)S(1)}, bf16[576,128]{1,0:T(8,128)(2,1)S(1)}, u32[]{:S(2)}, u32[]{:S(2)}) %collective-permute-start.3) | collective-permute-done | bytes 147488 | tf_op jit(solution)/shard_map/ppermute | solution.py:217
  37.8 1.1 reshape.521
  39.1 1.9 %collective-permute-start.4 = (bf16[576,128]{1,0:T(8,128)(2,1)}, bf16[576,128]{1,0:T(8,128)(2,1)}, u32[]{:S(2)}, u32[]{:S(2)}) collective-permute-start(bf16[576,128]{1,0:T(8,128)(2,1)} %collective-permute-done.2), channel_id=1, source_target_pairs={{0,64},{64,128},{128,192},{192,256},{256,320},{320,384},{384,448},... | collective-permute-start | bytes 442376 | tf_op jit(solution)/shard_map/ppermute | solution.py:214
  41.0 5.0 %collective-permute-start.5 = (bf16[576,128]{1,0:T(8,128)(2,1)S(1)}, bf16[576,128]{1,0:T(8,128)(2,1)}, u32[]{:S(2)}, u32[]{:S(2)}) collective-permute-start(bf16[576,128]{1,0:T(8,128)(2,1)S(1)} %collective-permute-done.3), channel_id=1, source_target_pairs={{0,704},{64,0},{128,64},{192,128},{256,192},{320,256},{384,320},{4... | collective-permute-start | bytes 442376 | tf_op jit(solution)/shard_map/ppermute | solution.py:217
  47.2 3.4 %fusion.1 = bf16[1,4,16,3,384]{4,2,3,1,0:T(8,128)(2,1)S(1)} fusion(bf16[3,3,3,192,384]{4,3,2,1,0:T(8,128)(2,1)} %bitcast.134, bf16[3,4,2,8,5,192]{5,2,4,3,1,0:T(2,128)(2,1)S(1)} %fusion.6, pred[16,3]{0,1:T(4,128)(4,1)S(1)} %copy-done.12), kind=kOutput, calls=%fused_computation.9 | convolution fusion | flops 637157376 | bytes 4497456 | tf_op jit(solution)/shard_map/conv_general_dilated | solution.py:132
  51.4 1.1 reshape.527
  54.2 1.9 %collective-permute-start.6 = (bf16[576,128]{1,0:T(8,128)(2,1)}, bf16[576,128]{1,0:T(8,128)(2,1)}, u32[]{:S(2)}, u32[]{:S(2)}) collective-permute-start(bf16[576,128]{1,0:T(8,128)(2,1)} %collective-permute-done.4), channel_id=1, source_target_pairs={{0,64},{64,128},{128,192},{192,256},{256,320},{320,384},{384,448},... | collective-permute-start | bytes 442376 | tf_op jit(solution)/shard_map/ppermute | solution.py:214
  56.2 4.6 %collective-permute-start.7 = (bf16[576,128]{1,0:T(8,128)(2,1)}, bf16[576,128]{1,0:T(8,128)(2,1)S(1)}, u32[]{:S(2)}, u32[]{:S(2)}) collective-permute-start(bf16[576,128]{1,0:T(8,128)(2,1)} %collective-permute-done.5), channel_id=1, source_target_pairs={{0,704},{64,0},{128,64},{192,128},{256,192},{320,256},{384,320},{4... | collective-permute-start | bytes 442376 | tf_op jit(solution)/shard_map/ppermute | solution.py:217
  60.8 1.1 reshape.533
  64.2 1.1 reshape.543
  66.3 2.1 %collective-permute-start.8 = (bf16[576,128]{1,0:T(8,128)(2,1)}, bf16[576,128]{1,0:T(8,128)(2,1)S(1)}, u32[]{:S(2)}, u32[]{:S(2)}) collective-permute-start(bf16[576,128]{1,0:T(8,128)(2,1)} %collective-permute-done.6), channel_id=1, source_target_pairs={{0,64},{64,128},{128,192},{192,256},{256,320},{320,384},{384,448},... | collective-permute-start | bytes 442376 | tf_op jit(solution)/shard_map/ppermute | solution.py:214
  68.4 5.1 %collective-permute-start.9 = (bf16[576,128]{1,0:T(8,128)(2,1)S(1)}, bf16[576,128]{1,0:T(8,128)(2,1)S(1)}, u32[]{:S(2)}, u32[]{:S(2)}) collective-permute-start(bf16[576,128]{1,0:T(8,128)(2,1)S(1)} %copy-done.10), channel_id=1, source_target_pairs={{0,704},{64,0},{128,64},{192,128},{256,192},{320,256},{384,320},{4... | collective-permute-start | bytes 442376 | tf_op jit(solution)/shard_map/ppermute | solution.py:217
  74.3 1.3 fusion
  76.3 1.3 %collective-permute-start.10 = (f32[2,4,16,192]{3,2,1,0:T(8,128)S(1)}, f32[2,4,16,192]{3,2,1,0:T(8,128)S(1)}, u32[]{:S(2)}, u32[]{:S(2)}) collective-permute-start(f32[2,4,16,192]{3,2,1,0:T(8,128)S(1)} %slice.162), channel_id=1, source_target_pairs={{64,0},{128,64},{192,128},{256,192},{320,256},{384,320},{448,384},... | collective-permute-start | bytes 294920 | tf_op jit(solution)/shard_map/ppermute | solution.py:14
  78.7 3.3 %collective-permute-done.10 = f32[2,4,16,192]{3,2,1,0:T(8,128)S(1)} collective-permute-done((f32[2,4,16,192]{3,2,1,0:T(8,128)S(1)}, f32[2,4,16,192]{3,2,1,0:T(8,128)S(1)}, u32[]{:S(2)}, u32[]{:S(2)}) %collective-permute-start.10) | collective-permute-done | bytes 98336 | tf_op jit(solution)/shard_map/ppermute | solution.py:14
  82.0 0.9 fusion.169
  83.0 0.7 fusion.189
  84.8 1.9 %collective-permute-start.11 = (bf16[576,128]{1,0:T(8,128)(2,1)S(1)}, bf16[576,128]{1,0:T(8,128)(2,1)S(1)}, u32[]{:S(2)}, u32[]{:S(2)}) collective-permute-start(bf16[576,128]{1,0:T(8,128)(2,1)S(1)} %copy-done.8), channel_id=1, source_target_pairs={{0,64},{64,128},{128,192},{192,256},{256,320},{320,384},{384,448},... | collective-permute-start | bytes 442376 | tf_op jit(solution)/shard_map/ppermute | solution.py:214
  87.3 4.6 %collective-permute-done.11 = bf16[576,128]{1,0:T(8,128)(2,1)S(1)} collective-permute-done((bf16[576,128]{1,0:T(8,128)(2,1)S(1)}, bf16[576,128]{1,0:T(8,128)(2,1)S(1)}, u32[]{:S(2)}, u32[]{:S(2)}) %collective-permute-start.11) | collective-permute-done | bytes 147488 | tf_op jit(solution)/shard_map/ppermute | solution.py:214
  95.0 8.6 %collective-permute-start.12 = (f32[32,6,432]{2,1,0:T(8,128)S(1)}, f32[32,6,432]{2,1,0:T(8,128)S(1)}, u32[]{:S(2)}, u32[]{:S(2)}) collective-permute-start(f32[32,6,432]{2,1,0:T(8,128)S(1)} %dynamic-slice_bitcast_fusion), channel_id=1, source_target_pairs={{0,1},{1,0},{2,3},{3,2},{4,5},{5,4},{6,7},{7,6},{8,9},{9,8},{10,11... | collective-permute-start | bytes 995336 | tf_op jit(solution)/shard_map/ppermute | solution.py:230
  103.6 1.5 %collective-permute-done.12 = f32[32,6,432]{2,1,0:T(8,128)S(1)} collective-permute-done((f32[32,6,432]{2,1,0:T(8,128)S(1)}, f32[32,6,432]{2,1,0:T(8,128)S(1)}, u32[]{:S(2)}, u32[]{:S(2)}) %collective-permute-start.12) | collective-permute-done | bytes 331808 | tf_op jit(solution)/shard_map/ppermute | solution.py:230
  105.1 0.8 fusion.5
  105.9 9.7 %all-to-all-start = ((bf16[32,6,432]{2,1,0:T(8,128)(2,1)}), bf16[32,6,432]{2,1,0:T(8,128)(2,1)S(1)}, u32[]{:S(2)}, u32[]{:S(2)}) async-start(bf16[32,6,432]{2,1,0:T(8,128)(2,1)} %fusion.5), calls=%async_computation | async-start | bytes 524288 | tf_op jit(solution)/shard_map/all_to_all | solution.py:231
  116.2 10.9 %all-to-all-done = bf16[32,6,432]{2,1,0:T(8,128)(2,1)S(1)} async-done(((bf16[32,6,432]{2,1,0:T(8,128)(2,1)}), bf16[32,6,432]{2,1,0:T(8,128)(2,1)S(1)}, u32[]{:S(2)}, u32[]{:S(2)}) %all-to-all-start) | async-done | bytes 165920 | tf_op jit(solution)/shard_map/all_to_all | solution.py:231
  (202 shorter events, 22.2 us)
Async XLA Ops:
  1.8 25.0 %collective-permute-start = (bf16[576,128]{1,0:T(8,128)(2,1)S(1)}, bf16[576,128]{1,0:T(8,128)(2,1)S(1)}, u32[]{:S(2)}, u32[]{:S(2)}) collective-permute-start(bf16[576,128]{1,0:T(8,128)(2,1)S(1)} %reshape.505), channel_id=1, source_target_pairs={{0,64},{64,128},{128,192},{192,256},{256,320},{320,384},{384,448},... | collective-permute-start | bytes 442376 | tf_op jit(solution)/shard_map/ppermute | solution.py:78
  6.7 19.8 %collective-permute-start.1 = (bf16[576,128]{1,0:T(8,128)(2,1)S(1)}, bf16[576,128]{1,0:T(8,128)(2,1)S(1)}, u32[]{:S(2)}, u32[]{:S(2)}) collective-permute-start(bf16[576,128]{1,0:T(8,128)(2,1)S(1)} %reshape.505), channel_id=1, source_target_pairs={{0,704},{64,0},{128,64},{192,128},{256,192},{320,256},{384,320},{4... | collective-permute-start | bytes 442376 | tf_op jit(solution)/shard_map/ppermute | solution.py:182
  28.2 9.6 %collective-permute-start.2 = (bf16[576,128]{1,0:T(8,128)(2,1)S(1)}, bf16[576,128]{1,0:T(8,128)(2,1)}, u32[]{:S(2)}, u32[]{:S(2)}) collective-permute-start(bf16[576,128]{1,0:T(8,128)(2,1)S(1)} %collective-permute-done), channel_id=1, source_target_pairs={{0,64},{64,128},{128,192},{192,256},{256,320},{320,384},{384,448},... | collective-permute-start | bytes 442376 | tf_op jit(solution)/shard_map/ppermute | solution.py:214
  30.1 6.7 %collective-permute-start.3 = (bf16[576,128]{1,0:T(8,128)(2,1)S(1)}, bf16[576,128]{1,0:T(8,128)(2,1)S(1)}, u32[]{:S(2)}, u32[]{:S(2)}) collective-permute-start(bf16[576,128]{1,0:T(8,128)(2,1)S(1)} %collective-permute-done.1), channel_id=1, source_target_pairs={{0,704},{64,0},{128,64},{192,128},{256,192},{320,256},{384,320},{4... | collective-permute-start | bytes 442376 | tf_op jit(solution)/shard_map/ppermute | solution.py:217
  34.7 12.5 %copy-start.12 = (pred[16,3]{0,1:T(4,128)(4,1)S(1)}, pred[16,3]{0,1:T(4,128)(4,1)}, u32[]{:S(2)}) copy-start(pred[16,3]{0,1:T(4,128)(4,1)} %constant.660) | copy-start | bytes 148
  39.1 15.2 %collective-permute-start.4 = (bf16[576,128]{1,0:T(8,128)(2,1)}, bf16[576,128]{1,0:T(8,128)(2,1)}, u32[]{:S(2)}, u32[]{:S(2)}) collective-permute-start(bf16[576,128]{1,0:T(8,128)(2,1)} %collective-permute-done.2), channel_id=1, source_target_pairs={{0,64},{64,128},{128,192},{192,256},{256,320},{320,384},{384,448},... | collective-permute-start | bytes 442376 | tf_op jit(solution)/shard_map/ppermute | solution.py:214
  41.0 10.4 %collective-permute-start.5 = (bf16[576,128]{1,0:T(8,128)(2,1)S(1)}, bf16[576,128]{1,0:T(8,128)(2,1)}, u32[]{:S(2)}, u32[]{:S(2)}) collective-permute-start(bf16[576,128]{1,0:T(8,128)(2,1)S(1)} %collective-permute-done.3), channel_id=1, source_target_pairs={{0,704},{64,0},{128,64},{192,128},{256,192},{320,256},{384,320},{4... | collective-permute-start | bytes 442376 | tf_op jit(solution)/shard_map/ppermute | solution.py:217
  53.6 12.1 %copy-start.26 = (bf16[2]{0:T(256)(128)(2,1)S(1)}, bf16[2]{0:T(256)(128)(2,1)}, u32[]{:S(2)}) copy-start(bf16[2]{0:T(256)(128)(2,1)} %get-tuple-element.75) | copy-start | bytes 16
  53.7 12.1 %copy-start.27 = (bf16[2]{0:T(256)(128)(2,1)S(1)}, bf16[2]{0:T(256)(128)(2,1)}, u32[]{:S(2)}) copy-start(bf16[2]{0:T(256)(128)(2,1)} %get-tuple-element.76) | copy-start | bytes 16
  53.7 12.1 %copy-start.28 = (bf16[2]{0:T(256)(128)(2,1)S(1)}, bf16[2]{0:T(256)(128)(2,1)}, u32[]{:S(2)}) copy-start(bf16[2]{0:T(256)(128)(2,1)} %get-tuple-element.77) | copy-start | bytes 16
  54.2 9.9 %collective-permute-start.6 = (bf16[576,128]{1,0:T(8,128)(2,1)}, bf16[576,128]{1,0:T(8,128)(2,1)}, u32[]{:S(2)}, u32[]{:S(2)}) collective-permute-start(bf16[576,128]{1,0:T(8,128)(2,1)} %collective-permute-done.4), channel_id=1, source_target_pairs={{0,64},{64,128},{128,192},{192,256},{256,320},{320,384},{384,448},... | collective-permute-start | bytes 442376 | tf_op jit(solution)/shard_map/ppermute | solution.py:214
  56.2 7.0 %collective-permute-start.7 = (bf16[576,128]{1,0:T(8,128)(2,1)}, bf16[576,128]{1,0:T(8,128)(2,1)S(1)}, u32[]{:S(2)}, u32[]{:S(2)}) collective-permute-start(bf16[576,128]{1,0:T(8,128)(2,1)} %collective-permute-done.5), channel_id=1, source_target_pairs={{0,704},{64,0},{128,64},{192,128},{256,192},{320,256},{384,320},{4... | collective-permute-start | bytes 442376 | tf_op jit(solution)/shard_map/ppermute | solution.py:217
  65.2 9.0 %copy-start = (bf16[5184,384]{1,0:T(8,128)(2,1)S(1)}, bf16[5184,384]{1,0:T(8,128)(2,1)}, u32[]{:S(2)}) copy-start(bf16[5184,384]{1,0:T(8,128)(2,1)} %param.8) | copy-start | bytes 11943940
  66.3 11.7 %collective-permute-start.8 = (bf16[576,128]{1,0:T(8,128)(2,1)}, bf16[576,128]{1,0:T(8,128)(2,1)S(1)}, u32[]{:S(2)}, u32[]{:S(2)}) collective-permute-start(bf16[576,128]{1,0:T(8,128)(2,1)} %collective-permute-done.6), channel_id=1, source_target_pairs={{0,64},{64,128},{128,192},{192,256},{256,320},{320,384},{384,448},... | collective-permute-start | bytes 442376 | tf_op jit(solution)/shard_map/ppermute | solution.py:214
  68.4 9.4 %collective-permute-start.9 = (bf16[576,128]{1,0:T(8,128)(2,1)S(1)}, bf16[576,128]{1,0:T(8,128)(2,1)S(1)}, u32[]{:S(2)}, u32[]{:S(2)}) collective-permute-start(bf16[576,128]{1,0:T(8,128)(2,1)S(1)} %copy-done.10), channel_id=1, source_target_pairs={{0,704},{64,0},{128,64},{192,128},{256,192},{320,256},{384,320},{4... | collective-permute-start | bytes 442376 | tf_op jit(solution)/shard_map/ppermute | solution.py:217
  75.6 8.2 %copy-start.20 = (bf16[2]{0:T(256)(128)(2,1)S(1)}, bf16[2]{0:T(256)(128)(2,1)}, u32[]{:S(2)}) copy-start(bf16[2]{0:T(256)(128)(2,1)} %get-tuple-element.72) | copy-start | bytes 16
  75.6 8.2 %copy-start.21 = (bf16[2]{0:T(256)(128)(2,1)S(1)}, bf16[2]{0:T(256)(128)(2,1)}, u32[]{:S(2)}) copy-start(bf16[2]{0:T(256)(128)(2,1)} %get-tuple-element.73) | copy-start | bytes 16
  75.6 8.2 %copy-start.22 = (bf16[2]{0:T(256)(128)(2,1)S(1)}, bf16[2]{0:T(256)(128)(2,1)}, u32[]{:S(2)}) copy-start(bf16[2]{0:T(256)(128)(2,1)} %get-tuple-element.74) | copy-start | bytes 16
  75.7 8.3 %copy-start.4 = (bf16[2,4,16,384]{3,2,1,0:T(8,128)(2,1)S(1)}, bf16[2,4,16,384]{3,2,1,0:T(8,128)(2,1)}, u32[]{:S(2)}) copy-start(bf16[2,4,16,384]{3,2,1,0:T(8,128)(2,1)} %slice.150) | copy-start | bytes 294916
  76.3 5.7 %collective-permute-start.10 = (f32[2,4,16,192]{3,2,1,0:T(8,128)S(1)}, f32[2,4,16,192]{3,2,1,0:T(8,128)S(1)}, u32[]{:S(2)}, u32[]{:S(2)}) collective-permute-start(f32[2,4,16,192]{3,2,1,0:T(8,128)S(1)} %slice.162), channel_id=1, source_target_pairs={{64,0},{128,64},{192,128},{256,192},{320,256},{384,320},{448,384},... | collective-permute-start | bytes 294920 | tf_op jit(solution)/shard_map/ppermute | solution.py:14
  77.6 9.1 %copy-start.19 = (bf16[2]{0:T(256)(128)(2,1)S(1)}, bf16[2]{0:T(256)(128)(2,1)}, u32[]{:S(2)}) copy-start(bf16[2]{0:T(256)(128)(2,1)} %get-tuple-element.68) | copy-start | bytes 16
  82.9 9.5 %copy-start.6 = (bf16[2,4,16,192]{3,2,1,0:T(8,128)(2,1)S(1)}, bf16[2,4,16,192]{3,2,1,0:T(8,128)(2,1)}, u32[]{:S(2)}) copy-start(bf16[2,4,16,192]{3,2,1,0:T(8,128)(2,1)} %get-tuple-element.150) | copy-start | bytes 147460
  83.8 8.9 %copy-start.16 = (bf16[2]{0:T(256)(128)(2,1)S(1)}, bf16[2]{0:T(256)(128)(2,1)}, u32[]{:S(2)}) copy-start(bf16[2]{0:T(256)(128)(2,1)} %get-tuple-element.58) | copy-start | bytes 16
  83.8 8.9 %copy-start.17 = (bf16[2]{0:T(256)(128)(2,1)S(1)}, bf16[2]{0:T(256)(128)(2,1)}, u32[]{:S(2)}) copy-start(bf16[2]{0:T(256)(128)(2,1)} %get-tuple-element.59) | copy-start | bytes 16
  83.8 8.9 %copy-start.18 = (bf16[2]{0:T(256)(128)(2,1)S(1)}, bf16[2]{0:T(256)(128)(2,1)}, u32[]{:S(2)}) copy-start(bf16[2]{0:T(256)(128)(2,1)} %get-tuple-element.60) | copy-start | bytes 16
  84.4 8.8 %copy-start.13 = (bf16[2]{0:T(256)(128)(2,1)S(1)}, bf16[2]{0:T(256)(128)(2,1)}, u32[]{:S(2)}) copy-start(bf16[2]{0:T(256)(128)(2,1)} %get-tuple-element.61) | copy-start | bytes 16
  84.4 8.8 %copy-start.14 = (bf16[2]{0:T(256)(128)(2,1)S(1)}, bf16[2]{0:T(256)(128)(2,1)}, u32[]{:S(2)}) copy-start(bf16[2]{0:T(256)(128)(2,1)} %get-tuple-element.62) | copy-start | bytes 16
  84.4 8.8 %copy-start.15 = (bf16[2]{0:T(256)(128)(2,1)S(1)}, bf16[2]{0:T(256)(128)(2,1)}, u32[]{:S(2)}) copy-start(bf16[2]{0:T(256)(128)(2,1)} %get-tuple-element.63) | copy-start | bytes 16
  84.8 7.1 %collective-permute-start.11 = (bf16[576,128]{1,0:T(8,128)(2,1)S(1)}, bf16[576,128]{1,0:T(8,128)(2,1)S(1)}, u32[]{:S(2)}, u32[]{:S(2)}) collective-permute-start(bf16[576,128]{1,0:T(8,128)(2,1)S(1)} %copy-done.8), channel_id=1, source_target_pairs={{0,64},{64,128},{128,192},{192,256},{256,320},{320,384},{384,448},... | collective-permute-start | bytes 442376 | tf_op jit(solution)/shard_map/ppermute | solution.py:214
  94.5 21.0 %copy-start.3 = (bf16[2,1,4,16,384]{4,2,3,0,1:T(4,128)(2,1)S(1)}, bf16[2,1,4,16,384]{4,2,3,0,1:T(4,128)(2,1)}, u32[]{:S(2)}) copy-start(bf16[2,1,4,16,384]{4,2,3,0,1:T(4,128)(2,1)} %slice_bitcast_fusion) | copy-start | bytes 294916
  95.0 10.1 %collective-permute-start.12 = (f32[32,6,432]{2,1,0:T(8,128)S(1)}, f32[32,6,432]{2,1,0:T(8,128)S(1)}, u32[]{:S(2)}, u32[]{:S(2)}) collective-permute-start(f32[32,6,432]{2,1,0:T(8,128)S(1)} %dynamic-slice_bitcast_fusion), channel_id=1, source_target_pairs={{0,1},{1,0},{2,3},{3,2},{4,5},{5,4},{6,7},{7,6},{8,9},{9,8},{10,11... | collective-permute-start | bytes 995336 | tf_op jit(solution)/shard_map/ppermute | solution.py:230
  105.9 21.2 %all-to-all-start = ((bf16[32,6,432]{2,1,0:T(8,128)(2,1)}), bf16[32,6,432]{2,1,0:T(8,128)(2,1)S(1)}, u32[]{:S(2)}, u32[]{:S(2)}) async-start(bf16[32,6,432]{2,1,0:T(8,128)(2,1)} %fusion.5), calls=%async_computation | async-start | bytes 524288 | tf_op jit(solution)/shard_map/all_to_all | solution.py:231
  (12 other events, 42.8 us)

commit v13 on v11

--- a/solution.py
+++ b/solution.py
@@ -200,7 +200,7 @@
             forward_moving, backward_moving, total, video_grad = lax.optimization_barrier(
                 (forward_moving, backward_moving, total, video_grad)
             )
-        elif total is not None:
+        elif total is not None and step > 2:
             forward_moving, backward_moving, total = lax.optimization_barrier(
                 (forward_moving, backward_moving, total)
             )

time: 118 us -> 118 us (level)
  no operation moved by 1% of the time
where the time goes in v13:
time: 118 us; the launch traced here: 117 us
  starting transfers between devices  66 us (56%)
  waiting for transfers between devices  22.7 us (19%)
  other arithmetic  9.78 us (8%)
  local copies, waits for them, and re-layouts  8.91 us (8%)
  matrix products  7.51 us (6%)
  between operations  2.24 us (2%)
    ppermute x4, starting transfers between devices, shards(): backward_moving = lax.ppermute(backward_moving, 'tm', ring_route('tm', -1))  19.2 us
    ppermute x1, starting transfers between devices, shards(): backward_moving = lax.ppermute(both, 'tm', ring_route('tm', -1))  12.2 us
    all_to_all x1, waiting for transfers between devices, shards(): lax.all_to_all(pair_sum.astype(jnp.bfloat16), 'dq', 0, 0, tiled=False)  10.9 us
    ppermute x5, starting transfers between devices, shards(): forward_moving = lax.ppermute(forward_moving, 'tm', ring_route('tm', 1))  9.71 us
    all_to_all x1, starting transfers between devices, shards(): lax.all_to_all(pair_sum.astype(jnp.bfloat16), 'dq', 0, 0, tiled=False)  9.67 us
    ppermute x1, starting transfers between devices, shards(): pair_sum = kept + lax.ppermute(sent, 'dc', [(0, 1), (1, 0)])  8.92 us
    ppermute x5, waiting for transfers between devices, shards(): forward_moving = lax.ppermute(forward_moving, 'tm', ring_route('tm', 1))  5.32 us
    dot_general x12, matrix products, block_term(): lax.dot_general(block_cot, jnp.concatenate(columns, axis=1), (((0,), (0,)...  4.97 us
  transfers between devices with their start and end apart: 14, of which 7 were waited for; matrix products, arithmetic and copies ran while one was open for 15% of the time, Pallas kernels for 0%

profile of v13, /device:TPU:1, one launch (start us, length us, event | category | flops | bytes accessed | tf_op | source)
XLA Modules:
  0.0 117.2 jit_solution(12930968536561764140)
XLA Ops:
  0.6 1.0 pad_maximum_fusion
  1.6 4.8 %collective-permute-start = (bf16[2,4,16,576]{3,2,1,0:T(8,128)(2,1)S(1)}, bf16[2,4,16,576]{3,2,1,0:T(8,128)(2,1)S(1)}, u32[]{:S(2)}, u32[]{:S(2)}) collective-permute-start(bf16[2,4,16,576]{3,2,1,0:T(8,128)(2,1)S(1)} %pad_maximum_fusion), channel_id=1, source_target_pairs={{0,64},{64,128},{128,192},{192,256},{256,320},{320,384},{384,448},... | collective-permute-start | bytes 442376 | tf_op jit(solution)/shard_map/ppermute | solution.py:76
  6.5 12.2 %collective-permute-start.2 = (bf16[2,4,16,576]{3,2,1,0:T(8,128)(2,1)S(1)}, bf16[2,4,16,576]{3,2,1,0:T(8,128)(2,1)S(1)}, u32[]{:S(2)}, u32[]{:S(2)}) collective-permute-start(bf16[2,4,16,576]{3,2,1,0:T(8,128)(2,1)S(1)} %pad_maximum_fusion), channel_id=1, source_target_pairs={{0,704},{64,0},{128,64},{192,128},{256,192},{320,256},{384,320},{4... | collective-permute-start | bytes 442376 | tf_op jit(solution)/shard_map/ppermute | solution.py:179
  18.8 0.9 fusion.92
  20.2 0.7 concatenate.83
  21.1 1.2 %gather_fusion = s32[72]{0:T(128)S(1)} fusion(s32[26]{0:T(128)S(1)} %concatenate.83, s32[1024]{0:T(1024)S(1)} %pad_clamp_fusion.3), kind=kCustom, calls=%fused_computation | custom fusion | bytes 864 | tf_op jit(solution)/shard_map/gather | solution.py:50
  22.5 0.7 gather_fusion.1
  23.5 0.6 gather_fusion.2
  24.2 0.6 gather_fusion.3
  27.1 2.1 %collective-permute-start.1 = (bf16[2,4,16,576]{3,2,1,0:T(8,128)(2,1)S(1)}, bf16[2,4,16,576]{3,2,1,0:T(8,128)(2,1)S(1)}, u32[]{:S(2)}, u32[]{:S(2)}) collective-permute-start(bf16[2,4,16,576]{3,2,1,0:T(8,128)(2,1)S(1)} %collective-permute-done), channel_id=1, source_target_pairs={{0,64},{64,128},{128,192},{192,256},{256,320},{320,384},{384,448},... | collective-permute-start | bytes 442376 | tf_op jit(solution)/shard_map/ppermute | solution.py:211
  29.1 4.6 %collective-permute-start.3 = (bf16[2,4,16,576]{3,2,1,0:T(8,128)(2,1)S(1)}, bf16[2,4,16,576]{3,2,1,0:T(8,128)(2,1)S(1)}, u32[]{:S(2)}, u32[]{:S(2)}) collective-permute-start(bf16[2,4,16,576]{3,2,1,0:T(8,128)(2,1)S(1)} %collective-permute-done.2), channel_id=1, source_target_pairs={{0,704},{64,0},{128,64},{192,128},{256,192},{320,256},{384,320},{4... | collective-permute-start | bytes 442376 | tf_op jit(solution)/shard_map/ppermute | solution.py:214
  34.3 0.7 collective-permute-done.1
  35.0 0.9 collective-permute-done.3
  35.9 1.9 %collective-permute-start.4 = (bf16[2,4,16,576]{3,2,1,0:T(8,128)(2,1)S(1)}, bf16[2,4,16,576]{3,2,1,0:T(8,128)(2,1)S(1)}, u32[]{:S(2)}, u32[]{:S(2)}) collective-permute-start(bf16[2,4,16,576]{3,2,1,0:T(8,128)(2,1)S(1)} %collective-permute-done.1), channel_id=1, source_target_pairs={{0,64},{64,128},{128,192},{192,256},{256,320},{320,384},{384,448},... | collective-permute-start | bytes 442376 | tf_op jit(solution)/shard_map/ppermute | solution.py:211
  37.9 5.0 %collective-permute-start.5 = (bf16[2,4,16,576]{3,2,1,0:T(8,128)(2,1)S(1)}, bf16[2,4,16,576]{3,2,1,0:T(8,128)(2,1)S(1)}, u32[]{:S(2)}, u32[]{:S(2)}) collective-permute-start(bf16[2,4,16,576]{3,2,1,0:T(8,128)(2,1)S(1)} %collective-permute-done.3), channel_id=1, source_target_pairs={{0,704},{64,0},{128,64},{192,128},{256,192},{320,256},{384,320},{4... | collective-permute-start | bytes 442376 | tf_op jit(solution)/shard_map/ppermute | solution.py:214
  44.2 1.3 %fusion.1 = bf16[1,4,16,3,384]{4,2,3,1,0:T(8,128)(2,1)S(1)} fusion(bf16[3,3,3,192,384]{4,3,2,1,0:T(8,128)(2,1)S(1)} %bitcast.132, bf16[3,4,2,8,5,192]{5,2,4,3,1,0:T(2,128)(2,1)S(1)} %fusion.6, pred[16,3]{0,1:T(4,128)(4,1)S(1)} %copy-done.4), kind=kOutput, calls=%fused_computation.11 | convolution fusion | flops 637157376 | bytes 4497456 | tf_op jit(solution)/shard_map/conv_general_dilated | solution.py:129
  47.6 1.9 %collective-permute-start.6 = (bf16[2,4,16,576]{3,2,1,0:T(8,128)(2,1)S(1)}, bf16[2,4,16,576]{3,2,1,0:T(8,128)(2,1)S(1)}, u32[]{:S(2)}, u32[]{:S(2)}) collective-permute-start(bf16[2,4,16,576]{3,2,1,0:T(8,128)(2,1)S(1)} %collective-permute-done.4), channel_id=1, source_target_pairs={{0,64},{64,128},{128,192},{192,256},{256,320},{320,384},{384,448},... | collective-permute-start | bytes 442376 | tf_op jit(solution)/shard_map/ppermute | solution.py:211
  49.5 4.6 %collective-permute-start.7 = (bf16[2,4,16,576]{3,2,1,0:T(8,128)(2,1)S(1)}, bf16[2,4,16,576]{3,2,1,0:T(8,128)(2,1)S(1)}, u32[]{:S(2)}, u32[]{:S(2)}) collective-permute-start(bf16[2,4,16,576]{3,2,1,0:T(8,128)(2,1)S(1)} %collective-permute-done.5), channel_id=1, source_target_pairs={{0,704},{64,0},{128,64},{192,128},{256,192},{320,256},{384,320},{4... | collective-permute-start | bytes 442376 | tf_op jit(solution)/shard_map/ppermute | solution.py:214
  56.4 1.9 %collective-permute-start.8 = (bf16[2,4,16,576]{3,2,1,0:T(8,128)(2,1)S(1)}, bf16[2,4,16,576]{3,2,1,0:T(8,128)(2,1)S(1)}, u32[]{:S(2)}, u32[]{:S(2)}) collective-permute-start(bf16[2,4,16,576]{3,2,1,0:T(8,128)(2,1)S(1)} %collective-permute-done.6), channel_id=1, source_target_pairs={{0,64},{64,128},{128,192},{192,256},{256,320},{320,384},{384,448},... | collective-permute-start | bytes 442376 | tf_op jit(solution)/shard_map/ppermute | solution.py:211
  58.3 5.0 %collective-permute-start.9 = (bf16[2,4,16,576]{3,2,1,0:T(8,128)(2,1)S(1)}, bf16[2,4,16,576]{3,2,1,0:T(8,128)(2,1)S(1)}, u32[]{:S(2)}, u32[]{:S(2)}) collective-permute-start(bf16[2,4,16,576]{3,2,1,0:T(8,128)(2,1)S(1)} %collective-permute-done.7), channel_id=1, source_target_pairs={{0,704},{64,0},{128,64},{192,128},{256,192},{320,256},{384,320},{4... | collective-permute-start | bytes 442376 | tf_op jit(solution)/shard_map/ppermute | solution.py:214
  64.2 1.3 %fusion = f32[3,4,16,3,192]{4,2,3,1,0:T(8,128)S(1)} fusion(bf16[3,3,3,192,384]{4,3,2,1,0:T(8,128)(2,1)S(1)} %bitcast.133, f32[3,4,16,3,192]{4,1,3,2,0:T(4,128)S(1)} %bitcast.134, pred[16,3]{0,1:T(4,128)(4,1)S(1)} %copy-done.4, bf16[1,4,2,8,5,384]{5,2,4,3,1,0:T(2,128)(2,1)S(1)} %fusion.9), kind=kOutput, calls=%fused_computation.9 | convolution fusion | flops 637231104 | bytes 5111856 | tf_op jit(solution)/shard_map/conv_general_dilated | solution.py:144
  66.2 1.5 %collective-permute-start.10 = (f32[2,4,16,192]{3,2,1,0:T(8,128)S(1)}, f32[2,4,16,192]{3,2,1,0:T(8,128)S(1)}, u32[]{:S(2)}, u32[]{:S(2)}) collective-permute-start(f32[2,4,16,192]{3,2,1,0:T(8,128)S(1)} %slice.162), channel_id=1, source_target_pairs={{64,0},{128,64},{192,128},{256,192},{320,256},{384,320},{448,384},... | collective-permute-start | bytes 294920 | tf_op jit(solution)/shard_map/ppermute | solution.py:14
  68.2 3.6 %collective-permute-done.10 = f32[2,4,16,192]{3,2,1,0:T(8,128)S(1)} collective-permute-done((f32[2,4,16,192]{3,2,1,0:T(8,128)S(1)}, f32[2,4,16,192]{3,2,1,0:T(8,128)S(1)}, u32[]{:S(2)}, u32[]{:S(2)}) %collective-permute-start.10) | collective-permute-done | bytes 98336 | tf_op jit(solution)/shard_map/ppermute | solution.py:14
  72.3 0.7 fusion.183
  74.0 1.9 %collective-permute-start.11 = (bf16[2,4,16,576]{3,2,1,0:T(8,128)(2,1)S(1)}, bf16[2,4,16,576]{3,2,1,0:T(8,128)(2,1)S(1)}, u32[]{:S(2)}, u32[]{:S(2)}) collective-permute-start(bf16[2,4,16,576]{3,2,1,0:T(8,128)(2,1)S(1)} %collective-permute-done.8), channel_id=1, source_target_pairs={{0,64},{64,128},{128,192},{192,256},{256,320},{320,384},{384,448},... | collective-permute-start | bytes 442376 | tf_op jit(solution)/shard_map/ppermute | solution.py:211
  76.7 4.6 %collective-permute-done.11 = bf16[2,4,16,576]{3,2,1,0:T(8,128)(2,1)S(1)} collective-permute-done((bf16[2,4,16,576]{3,2,1,0:T(8,128)(2,1)S(1)}, bf16[2,4,16,576]{3,2,1,0:T(8,128)(2,1)S(1)}, u32[]{:S(2)}, u32[]{:S(2)}) %collective-permute-start.11) | collective-permute-done | bytes 147488 | tf_op jit(solution)/shard_map/ppermute | solution.py:211
  84.1 8.9 %collective-permute-start.12 = (f32[32,6,432]{2,1,0:T(8,128)S(1)}, f32[32,6,432]{2,1,0:T(8,128)S(1)}, u32[]{:S(2)}, u32[]{:S(2)}) collective-permute-start(f32[32,6,432]{2,1,0:T(8,128)S(1)} %dynamic-slice_bitcast_fusion), channel_id=1, source_target_pairs={{0,1},{1,0},{2,3},{3,2},{4,5},{5,4},{6,7},{7,6},{8,9},{9,8},{10,11... | collective-permute-start | bytes 995336 | tf_op jit(solution)/shard_map/ppermute | solution.py:227
  93.0 1.5 %collective-permute-done.12 = f32[32,6,432]{2,1,0:T(8,128)S(1)} collective-permute-done((f32[32,6,432]{2,1,0:T(8,128)S(1)}, f32[32,6,432]{2,1,0:T(8,128)S(1)}, u32[]{:S(2)}, u32[]{:S(2)}) %collective-permute-start.12) | collective-permute-done | bytes 331808 | tf_op jit(solution)/shard_map/ppermute | solution.py:227
  94.5 0.8 fusion.5
  95.3 9.7 %all-to-all-start = ((bf16[32,6,432]{2,1,0:T(8,128)(2,1)}), bf16[32,6,432]{2,1,0:T(8,128)(2,1)S(1)}, u32[]{:S(2)}, u32[]{:S(2)}) async-start(bf16[32,6,432]{2,1,0:T(8,128)(2,1)} %fusion.5), calls=%async_computation | async-start | bytes 524288 | tf_op jit(solution)/shard_map/all_to_all | solution.py:228
  104.9 0.7 copy.45
  105.6 10.9 %all-to-all-done = bf16[32,6,432]{2,1,0:T(8,128)(2,1)S(1)} async-done(((bf16[32,6,432]{2,1,0:T(8,128)(2,1)}), bf16[32,6,432]{2,1,0:T(8,128)(2,1)S(1)}, u32[]{:S(2)}, u32[]{:S(2)}) %all-to-all-start) | async-done | bytes 165920 | tf_op jit(solution)/shard_map/all_to_all | solution.py:228
  (142 shorter events, 16.1 us)
Async XLA Ops:
  1.6 24.2 %collective-permute-start = (bf16[2,4,16,576]{3,2,1,0:T(8,128)(2,1)S(1)}, bf16[2,4,16,576]{3,2,1,0:T(8,128)(2,1)S(1)}, u32[]{:S(2)}, u32[]{:S(2)}) collective-permute-start(bf16[2,4,16,576]{3,2,1,0:T(8,128)(2,1)S(1)} %pad_maximum_fusion), channel_id=1, source_target_pairs={{0,64},{64,128},{128,192},{192,256},{256,320},{320,384},{384,448},... | collective-permute-start | bytes 442376 | tf_op jit(solution)/shard_map/ppermute | solution.py:76
  6.5 19.3 %collective-permute-start.2 = (bf16[2,4,16,576]{3,2,1,0:T(8,128)(2,1)S(1)}, bf16[2,4,16,576]{3,2,1,0:T(8,128)(2,1)S(1)}, u32[]{:S(2)}, u32[]{:S(2)}) collective-permute-start(bf16[2,4,16,576]{3,2,1,0:T(8,128)(2,1)S(1)} %pad_maximum_fusion), channel_id=1, source_target_pairs={{0,704},{64,0},{128,64},{192,128},{256,192},{320,256},{384,320},{4... | collective-permute-start | bytes 442376 | tf_op jit(solution)/shard_map/ppermute | solution.py:179
  21.1 2.2 %copy-start.5 = (s32[1,24]{1,0:T(1,128)S(1)}, s32[1,24]{1,0:T(1,128)}, u32[]{:S(2)}) copy-start(s32[1,24]{1,0:T(1,128)} %param.6) | copy-start | bytes 292
  21.1 4.9 %copy-start.1 = (bf16[1,2,4,16,192]{4,3,2,1,0:T(8,128)(2,1)S(1)}, bf16[1,2,4,16,192]{4,3,2,1,0:T(8,128)(2,1)}, u32[]{:S(2)}) copy-start(bf16[1,2,4,16,192]{4,3,2,1,0:T(8,128)(2,1)} %param.5) | copy-start | bytes 147460
  21.1 4.9 %copy-start.3 = (f32[192]{0:T(256)S(1)}, f32[192]{0:T(256)}, u32[]{:S(2)}) copy-start(f32[192]{0:T(256)} %param.7) | copy-start | bytes 2308
  22.3 4.3 %copy-start.2 = (bf16[1,2,4,16,384]{4,3,2,1,0:T(8,128)(2,1)S(1)}, bf16[1,2,4,16,384]{4,3,2,1,0:T(8,128)(2,1)}, u32[]{:S(2)}) copy-start(bf16[1,2,4,16,384]{4,3,2,1,0:T(8,128)(2,1)} %param.9) | copy-start | bytes 294916
  26.2 17.9 %copy-start = (bf16[5184,384]{1,0:T(8,128)(2,1)S(1)}, bf16[5184,384]{1,0:T(8,128)(2,1)}, u32[]{:S(2)}) copy-start(bf16[5184,384]{1,0:T(8,128)(2,1)} %param.8) | copy-start | bytes 11943940
  26.3 17.9 %copy-start.4 = (pred[16,3]{0,1:T(4,128)(4,1)S(1)}, pred[16,3]{0,1:T(4,128)(4,1)}, u32[]{:S(2)}) copy-start(pred[16,3]{0,1:T(4,128)(4,1)} %constant.660) | copy-start | bytes 148
  27.1 8.0 %collective-permute-start.1 = (bf16[2,4,16,576]{3,2,1,0:T(8,128)(2,1)S(1)}, bf16[2,4,16,576]{3,2,1,0:T(8,128)(2,1)S(1)}, u32[]{:S(2)}, u32[]{:S(2)}) collective-permute-start(bf16[2,4,16,576]{3,2,1,0:T(8,128)(2,1)S(1)} %collective-permute-done), channel_id=1, source_target_pairs={{0,64},{64,128},{128,192},{192,256},{256,320},{320,384},{384,448},... | collective-permute-start | bytes 442376 | tf_op jit(solution)/shard_map/ppermute | solution.py:211
  29.1 6.8 %collective-permute-start.3 = (bf16[2,4,16,576]{3,2,1,0:T(8,128)(2,1)S(1)}, bf16[2,4,16,576]{3,2,1,0:T(8,128)(2,1)S(1)}, u32[]{:S(2)}, u32[]{:S(2)}) collective-permute-start(bf16[2,4,16,576]{3,2,1,0:T(8,128)(2,1)S(1)} %collective-permute-done.2), channel_id=1, source_target_pairs={{0,704},{64,0},{128,64},{192,128},{256,192},{320,256},{384,320},{4... | collective-permute-start | bytes 442376 | tf_op jit(solution)/shard_map/ppermute | solution.py:214
  35.9 11.7 %collective-permute-start.4 = (bf16[2,4,16,576]{3,2,1,0:T(8,128)(2,1)S(1)}, bf16[2,4,16,576]{3,2,1,0:T(8,128)(2,1)S(1)}, u32[]{:S(2)}, u32[]{:S(2)}) collective-permute-start(bf16[2,4,16,576]{3,2,1,0:T(8,128)(2,1)S(1)} %collective-permute-done.1), channel_id=1, source_target_pairs={{0,64},{64,128},{128,192},{192,256},{256,320},{320,384},{384,448},... | collective-permute-start | bytes 442376 | tf_op jit(solution)/shard_map/ppermute | solution.py:211
  37.9 8.0 %collective-permute-start.5 = (bf16[2,4,16,576]{3,2,1,0:T(8,128)(2,1)S(1)}, bf16[2,4,16,576]{3,2,1,0:T(8,128)(2,1)S(1)}, u32[]{:S(2)}, u32[]{:S(2)}) collective-permute-start(bf16[2,4,16,576]{3,2,1,0:T(8,128)(2,1)S(1)} %collective-permute-done.3), channel_id=1, source_target_pairs={{0,704},{64,0},{128,64},{192,128},{256,192},{320,256},{384,320},{4... | collective-permute-start | bytes 442376 | tf_op jit(solution)/shard_map/ppermute | solution.py:214
  47.6 7.4 %collective-permute-start.6 = (bf16[2,4,16,576]{3,2,1,0:T(8,128)(2,1)S(1)}, bf16[2,4,16,576]{3,2,1,0:T(8,128)(2,1)S(1)}, u32[]{:S(2)}, u32[]{:S(2)}) collective-permute-start(bf16[2,4,16,576]{3,2,1,0:T(8,128)(2,1)S(1)} %collective-permute-done.4), channel_id=1, source_target_pairs={{0,64},{64,128},{128,192},{192,256},{256,320},{320,384},{384,448},... | collective-permute-start | bytes 442376 | tf_op jit(solution)/shard_map/ppermute | solution.py:211
  49.5 6.8 %collective-permute-start.7 = (bf16[2,4,16,576]{3,2,1,0:T(8,128)(2,1)S(1)}, bf16[2,4,16,576]{3,2,1,0:T(8,128)(2,1)S(1)}, u32[]{:S(2)}, u32[]{:S(2)}) collective-permute-start(bf16[2,4,16,576]{3,2,1,0:T(8,128)(2,1)S(1)} %collective-permute-done.5), channel_id=1, source_target_pairs={{0,704},{64,0},{128,64},{192,128},{256,192},{320,256},{384,320},{4... | collective-permute-start | bytes 442376 | tf_op jit(solution)/shard_map/ppermute | solution.py:214
  56.4 11.7 %collective-permute-start.8 = (bf16[2,4,16,576]{3,2,1,0:T(8,128)(2,1)S(1)}, bf16[2,4,16,576]{3,2,1,0:T(8,128)(2,1)S(1)}, u32[]{:S(2)}, u32[]{:S(2)}) collective-permute-start(bf16[2,4,16,576]{3,2,1,0:T(8,128)(2,1)S(1)} %collective-permute-done.6), channel_id=1, source_target_pairs={{0,64},{64,128},{128,192},{192,256},{256,320},{320,384},{384,448},... | collective-permute-start | bytes 442376 | tf_op jit(solution)/shard_map/ppermute | solution.py:211
  58.3 9.7 %collective-permute-start.9 = (bf16[2,4,16,576]{3,2,1,0:T(8,128)(2,1)S(1)}, bf16[2,4,16,576]{3,2,1,0:T(8,128)(2,1)S(1)}, u32[]{:S(2)}, u32[]{:S(2)}) collective-permute-start(bf16[2,4,16,576]{3,2,1,0:T(8,128)(2,1)S(1)} %collective-permute-done.7), channel_id=1, source_target_pairs={{0,704},{64,0},{128,64},{192,128},{256,192},{320,256},{384,320},{4... | collective-permute-start | bytes 442376 | tf_op jit(solution)/shard_map/ppermute | solution.py:214
  66.2 5.7 %collective-permute-start.10 = (f32[2,4,16,192]{3,2,1,0:T(8,128)S(1)}, f32[2,4,16,192]{3,2,1,0:T(8,128)S(1)}, u32[]{:S(2)}, u32[]{:S(2)}) collective-permute-start(f32[2,4,16,192]{3,2,1,0:T(8,128)S(1)} %slice.162), channel_id=1, source_target_pairs={{64,0},{128,64},{192,128},{256,192},{320,256},{384,320},{448,384},... | collective-permute-start | bytes 294920 | tf_op jit(solution)/shard_map/ppermute | solution.py:14
  74.0 7.3 %collective-permute-start.11 = (bf16[2,4,16,576]{3,2,1,0:T(8,128)(2,1)S(1)}, bf16[2,4,16,576]{3,2,1,0:T(8,128)(2,1)S(1)}, u32[]{:S(2)}, u32[]{:S(2)}) collective-permute-start(bf16[2,4,16,576]{3,2,1,0:T(8,128)(2,1)S(1)} %collective-permute-done.8), channel_id=1, source_target_pairs={{0,64},{64,128},{128,192},{192,256},{256,320},{320,384},{384,448},... | collective-permute-start | bytes 442376 | tf_op jit(solution)/shard_map/ppermute | solution.py:211
  84.1 10.4 %collective-permute-start.12 = (f32[32,6,432]{2,1,0:T(8,128)S(1)}, f32[32,6,432]{2,1,0:T(8,128)S(1)}, u32[]{:S(2)}, u32[]{:S(2)}) collective-permute-start(f32[32,6,432]{2,1,0:T(8,128)S(1)} %dynamic-slice_bitcast_fusion), channel_id=1, source_target_pairs={{0,1},{1,0},{2,3},{3,2},{4,5},{5,4},{6,7},{7,6},{8,9},{9,8},{10,11... | collective-permute-start | bytes 995336 | tf_op jit(solution)/shard_map/ppermute | solution.py:227
  95.3 21.3 %all-to-all-start = ((bf16[32,6,432]{2,1,0:T(8,128)(2,1)}), bf16[32,6,432]{2,1,0:T(8,128)(2,1)S(1)}, u32[]{:S(2)}, u32[]{:S(2)}) async-start(bf16[32,6,432]{2,1,0:T(8,128)(2,1)} %fusion.5), calls=%async_computation | async-start | bytes 524288 | tf_op jit(solution)/shard_map/all_to_all | solution.py:228

commit v14 on v13

--- a/solution.py
+++ b/solution.py
@@ -195,11 +195,11 @@
             forward_moving, backward_moving, total, grad_inputs = lax.optimization_barrier(
                 (forward_moving, backward_moving, total, grad_inputs)
             )
+        elif step == 6:
+            forward_moving, backward_moving, total, grad_inputs = lax.optimization_barrier(
+                (forward_moving, backward_moving, total, grad_inputs)
+            )
             video_grad = backward_section(*grad_inputs)
-        elif step == 6:
-            forward_moving, backward_moving, total, video_grad = lax.optimization_barrier(
-                (forward_moving, backward_moving, total, video_grad)
-            )
         elif total is not None and step > 2:
             forward_moving, backward_moving, total = lax.optimization_barrier(
                 (forward_moving, backward_moving, total)
@@ -217,6 +217,7 @@
         blocks[rel] = block
         block_acts[rel] = activate(block[..., :channels], norm_gain).astype(jnp.bfloat16)
     total = add_ready(total)
+    total, video_grad = lax.optimization_barrier((total, video_grad))
     slab_t = lax.dynamic_slice_in_dim(total, slab_offset, slab_rows, 1)
     chips = lax.axis_size("dq")
     cores = lax.axis_size("dc")

time: 118 us -> 120 us (1.017)
  starting transfers between devices: 66 us -> 68.7 us
    ppermute x1, waiting for transfers between devices: 3.64 us -> 0.01 us  [from_behind(): return lax.ppermute(block, axis, route)]
    ppermute x4, waiting for transfers between devices: 1.32 us -> 4.04 us  [shards(): backward_moving = lax.ppermute(backward_moving, 'tm', ring_route('tm', -1))]
    ppermute x5, starting transfers between devices: 9.71 us -> 11.7 us  [shards(): forward_moving = lax.ppermute(forward_moving, 'tm', ring_route('tm', 1))]
  transfers between devices with their start and end apart: 14 -> 14, of which waited for: 7 -> 9; matrix products, arithmetic and copies ran while one was open for 15% -> 9% of each run, Pallas kernels for 0% -> 0%
where the time goes in v14:
time: 120 us; the launch traced here: 119 us
  starting transfers between devices  68.7 us (57%)
  waiting for transfers between devices  21.7 us (18%)
  other arithmetic  9.46 us (8%)
  local copies, waits for them, and re-layouts  8.98 us (7%)
  matrix products  7.55 us (6%)
  between operations  2.22 us (2%)
    ppermute x4, starting transfers between devices, shards(): backward_moving = lax.ppermute(backward_moving, 'tm', ring_route('tm', -1))  19.8 us
    ppermute x1, starting transfers between devices, shards(): backward_moving = lax.ppermute(both, 'tm', ring_route('tm', -1))  12.2 us
    ppermute x5, starting transfers between devices, shards(): forward_moving = lax.ppermute(forward_moving, 'tm', ring_route('tm', 1))  11.7 us
    all_to_all x1, waiting for transfers between devices, shards(): lax.all_to_all(pair_sum.astype(jnp.bfloat16), 'dq', 0, 0, tiled=False)  10.9 us
    all_to_all x1, starting transfers between devices, shards(): lax.all_to_all(pair_sum.astype(jnp.bfloat16), 'dq', 0, 0, tiled=False)  9.67 us
    ppermute x1, starting transfers between devices, shards(): pair_sum = kept + lax.ppermute(sent, 'dc', [(0, 1), (1, 0)])  9.23 us
    ppermute x5, waiting for transfers between devices, shards(): forward_moving = lax.ppermute(forward_moving, 'tm', ring_route('tm', 1))  5.25 us
    dot_general x12, matrix products, block_term(): lax.dot_general(block_cot, jnp.concatenate(columns, axis=1), (((0,), (0,)...  5.01 us
  transfers between devices with their start and end apart: 14, of which 9 were waited for; matrix products, arithmetic and copies ran while one was open for 9% of the time, Pallas kernels for 0%

profile of v14, /device:TPU:1, one launch (start us, length us, event | category | flops | bytes accessed | tf_op | source)
XLA Modules:
  0.0 118.7 jit_solution(9446078136966523555)
XLA Ops:
  0.6 1.0 pad_maximum_fusion
  1.6 4.8 %collective-permute-start = (bf16[2,4,16,576]{3,2,1,0:T(8,128)(2,1)S(1)}, bf16[2,4,16,576]{3,2,1,0:T(8,128)(2,1)S(1)}, u32[]{:S(2)}, u32[]{:S(2)}) collective-permute-start(bf16[2,4,16,576]{3,2,1,0:T(8,128)(2,1)S(1)} %pad_maximum_fusion), channel_id=1, source_target_pairs={{0,64},{64,128},{128,192},{192,256},{256,320},{320,384},{384,448},... | collective-permute-start | bytes 442376 | tf_op jit(solution)/shard_map/ppermute | solution.py:76
  6.5 12.2 %collective-permute-start.2 = (bf16[2,4,16,576]{3,2,1,0:T(8,128)(2,1)S(1)}, bf16[2,4,16,576]{3,2,1,0:T(8,128)(2,1)S(1)}, u32[]{:S(2)}, u32[]{:S(2)}) collective-permute-start(bf16[2,4,16,576]{3,2,1,0:T(8,128)(2,1)S(1)} %pad_maximum_fusion), channel_id=1, source_target_pairs={{0,704},{64,0},{128,64},{192,128},{256,192},{320,256},{384,320},{4... | collective-permute-start | bytes 442376 | tf_op jit(solution)/shard_map/ppermute | solution.py:179
  19.3 0.9 fusion.94
  20.3 0.7 concatenate.83
  21.2 1.2 %gather_fusion = s32[72]{0:T(128)S(1)} fusion(s32[26]{0:T(128)S(1)} %concatenate.83, s32[1024]{0:T(1024)S(1)} %pad_clamp_fusion.3), kind=kCustom, calls=%fused_computation | custom fusion | bytes 864 | tf_op jit(solution)/shard_map/gather | solution.py:50
  22.6 0.7 gather_fusion.1
  25.8 1.9 %collective-permute-start.1 = (bf16[2,4,16,576]{3,2,1,0:T(8,128)(2,1)S(1)}, bf16[2,4,16,576]{3,2,1,0:T(8,128)(2,1)S(1)}, u32[]{:S(2)}, u32[]{:S(2)}) collective-permute-start(bf16[2,4,16,576]{3,2,1,0:T(8,128)(2,1)S(1)} %collective-permute-done), channel_id=1, source_target_pairs={{0,64},{64,128},{128,192},{192,256},{256,320},{320,384},{384,448},... | collective-permute-start | bytes 442376 | tf_op jit(solution)/shard_map/ppermute | solution.py:211
  27.8 4.6 %collective-permute-start.3 = (bf16[2,4,16,576]{3,2,1,0:T(8,128)(2,1)S(1)}, bf16[2,4,16,576]{3,2,1,0:T(8,128)(2,1)S(1)}, u32[]{:S(2)}, u32[]{:S(2)}) collective-permute-start(bf16[2,4,16,576]{3,2,1,0:T(8,128)(2,1)S(1)} %collective-permute-done.2), channel_id=1, source_target_pairs={{0,704},{64,0},{128,64},{192,128},{256,192},{320,256},{384,320},{4... | collective-permute-start | bytes 442376 | tf_op jit(solution)/shard_map/ppermute | solution.py:214
  32.7 0.9 collective-permute-done.1
  33.7 0.9 collective-permute-done.3
  37.8 1.3 %fusion.1 = bf16[1,4,16,3,384]{4,2,3,1,0:T(8,128)(2,1)S(1)} fusion(bf16[3,3,3,192,384]{4,3,2,1,0:T(8,128)(2,1)S(1)} %bitcast.132, bf16[3,4,2,8,5,192]{5,2,4,3,1,0:T(2,128)(2,1)S(1)} %fusion.6, pred[16,3]{0,1:T(4,128)(4,1)S(1)} %copy-done.3), kind=kOutput, calls=%fused_computation.11 | convolution fusion | flops 637157376 | bytes 4497456 | tf_op jit(solution)/shard_map/conv_general_dilated | solution.py:129
  39.2 1.9 %collective-permute-start.4 = (bf16[2,4,16,576]{3,2,1,0:T(8,128)(2,1)S(1)}, bf16[2,4,16,576]{3,2,1,0:T(8,128)(2,1)S(1)}, u32[]{:S(2)}, u32[]{:S(2)}) collective-permute-start(bf16[2,4,16,576]{3,2,1,0:T(8,128)(2,1)S(1)} %collective-permute-done.1), channel_id=1, source_target_pairs={{0,64},{64,128},{128,192},{192,256},{256,320},{320,384},{384,448},... | collective-permute-start | bytes 442376 | tf_op jit(solution)/shard_map/ppermute | solution.py:211
  41.1 5.0 %collective-permute-start.5 = (bf16[2,4,16,576]{3,2,1,0:T(8,128)(2,1)S(1)}, bf16[2,4,16,576]{3,2,1,0:T(8,128)(2,1)S(1)}, u32[]{:S(2)}, u32[]{:S(2)}) collective-permute-start(bf16[2,4,16,576]{3,2,1,0:T(8,128)(2,1)S(1)} %collective-permute-done.3), channel_id=1, source_target_pairs={{0,704},{64,0},{128,64},{192,128},{256,192},{320,256},{384,320},{4... | collective-permute-start | bytes 442376 | tf_op jit(solution)/shard_map/ppermute | solution.py:214
  47.4 1.0 collective-permute-done.5
  48.4 1.9 %collective-permute-start.6 = (bf16[2,4,16,576]{3,2,1,0:T(8,128)(2,1)S(1)}, bf16[2,4,16,576]{3,2,1,0:T(8,128)(2,1)S(1)}, u32[]{:S(2)}, u32[]{:S(2)}) collective-permute-start(bf16[2,4,16,576]{3,2,1,0:T(8,128)(2,1)S(1)} %collective-permute-done.4), channel_id=1, source_target_pairs={{0,64},{64,128},{128,192},{192,256},{256,320},{320,384},{384,448},... | collective-permute-start | bytes 442376 | tf_op jit(solution)/shard_map/ppermute | solution.py:211
  50.3 5.0 %collective-permute-start.7 = (bf16[2,4,16,576]{3,2,1,0:T(8,128)(2,1)S(1)}, bf16[2,4,16,576]{3,2,1,0:T(8,128)(2,1)S(1)}, u32[]{:S(2)}, u32[]{:S(2)}) collective-permute-start(bf16[2,4,16,576]{3,2,1,0:T(8,128)(2,1)S(1)} %collective-permute-done.5), channel_id=1, source_target_pairs={{0,704},{64,0},{128,64},{192,128},{256,192},{320,256},{384,320},{4... | collective-permute-start | bytes 442376 | tf_op jit(solution)/shard_map/ppermute | solution.py:214
  56.2 1.4 %collective-permute-done.7 = bf16[2,4,16,576]{3,2,1,0:T(8,128)(2,1)S(1)} collective-permute-done((bf16[2,4,16,576]{3,2,1,0:T(8,128)(2,1)S(1)}, bf16[2,4,16,576]{3,2,1,0:T(8,128)(2,1)S(1)}, u32[]{:S(2)}, u32[]{:S(2)}) %collective-permute-start.7) | collective-permute-done | bytes 147488 | tf_op jit(solution)/shard_map/ppermute | solution.py:214
  59.3 1.9 %collective-permute-start.8 = (bf16[2,4,16,576]{3,2,1,0:T(8,128)(2,1)S(1)}, bf16[2,4,16,576]{3,2,1,0:T(8,128)(2,1)S(1)}, u32[]{:S(2)}, u32[]{:S(2)}) collective-permute-start(bf16[2,4,16,576]{3,2,1,0:T(8,128)(2,1)S(1)} %collective-permute-done.6), channel_id=1, source_target_pairs={{0,64},{64,128},{128,192},{192,256},{256,320},{320,384},{384,448},... | collective-permute-start | bytes 442376 | tf_op jit(solution)/shard_map/ppermute | solution.py:211
  61.2 5.2 %collective-permute-start.9 = (bf16[2,4,16,576]{3,2,1,0:T(8,128)(2,1)S(1)}, bf16[2,4,16,576]{3,2,1,0:T(8,128)(2,1)S(1)}, u32[]{:S(2)}, u32[]{:S(2)}) collective-permute-start(bf16[2,4,16,576]{3,2,1,0:T(8,128)(2,1)S(1)} %collective-permute-done.7), channel_id=1, source_target_pairs={{0,704},{64,0},{128,64},{192,128},{256,192},{320,256},{384,320},{4... | collective-permute-start | bytes 442376 | tf_op jit(solution)/shard_map/ppermute | solution.py:214
  67.7 0.8 collective-permute-done.9
  69.1 1.3 %fusion = f32[3,4,16,3,192]{4,2,3,1,0:T(8,128)S(1)} fusion(bf16[3,3,3,192,384]{4,3,2,1,0:T(8,128)(2,1)S(1)} %bitcast.133, f32[3,4,16,3,192]{4,1,3,2,0:T(4,128)S(1)} %bitcast.134, pred[16,3]{0,1:T(4,128)(4,1)S(1)} %copy-done.3, bf16[1,4,2,8,5,384]{5,2,4,3,1,0:T(2,128)(2,1)S(1)} %fusion.9), kind=kOutput, calls=%fused_computation.9 | convolution fusion | flops 637231104 | bytes 5111856 | tf_op jit(solution)/shard_map/conv_general_dilated | solution.py:144
  71.1 1.3 %collective-permute-start.11 = (f32[2,4,16,192]{3,2,1,0:T(8,128)S(1)}, f32[2,4,16,192]{3,2,1,0:T(8,128)S(1)}, u32[]{:S(2)}, u32[]{:S(2)}) collective-permute-start(f32[2,4,16,192]{3,2,1,0:T(8,128)S(1)} %slice.169), channel_id=1, source_target_pairs={{64,0},{128,64},{192,128},{256,192},{320,256},{384,320},{448,384},... | collective-permute-start | bytes 294920 | tf_op jit(solution)/shard_map/ppermute | solution.py:14
  72.4 4.0 %collective-permute-start.10 = (bf16[2,4,16,576]{3,2,1,0:T(8,128)(2,1)S(1)}, bf16[2,4,16,576]{3,2,1,0:T(8,128)(2,1)S(1)}, u32[]{:S(2)}, u32[]{:S(2)}) collective-permute-start(bf16[2,4,16,576]{3,2,1,0:T(8,128)(2,1)S(1)} %collective-permute-done.8), channel_id=1, source_target_pairs={{0,64},{64,128},{128,192},{192,256},{256,320},{320,384},{384,448},... | collective-permute-start | bytes 442376 | tf_op jit(solution)/shard_map/ppermute | solution.py:211
  76.9 4.0 %collective-permute-done.10 = bf16[2,4,16,576]{3,2,1,0:T(8,128)(2,1)S(1)} collective-permute-done((bf16[2,4,16,576]{3,2,1,0:T(8,128)(2,1)S(1)}, bf16[2,4,16,576]{3,2,1,0:T(8,128)(2,1)S(1)}, u32[]{:S(2)}, u32[]{:S(2)}) %collective-permute-start.10) | collective-permute-done | bytes 147488 | tf_op jit(solution)/shard_map/ppermute | solution.py:211
  81.4 0.7 fusion.185
  85.2 9.2 %collective-permute-start.12 = (f32[32,6,432]{2,1,0:T(8,128)S(1)}, f32[32,6,432]{2,1,0:T(8,128)S(1)}, u32[]{:S(2)}, u32[]{:S(2)}) collective-permute-start(f32[32,6,432]{2,1,0:T(8,128)S(1)} %dynamic-slice_bitcast_fusion), channel_id=1, source_target_pairs={{0,1},{1,0},{2,3},{3,2},{4,5},{5,4},{6,7},{7,6},{8,9},{9,8},{10,11... | collective-permute-start | bytes 995336 | tf_op jit(solution)/shard_map/ppermute | solution.py:228
  94.5 1.5 %collective-permute-done.12 = f32[32,6,432]{2,1,0:T(8,128)S(1)} collective-permute-done((f32[32,6,432]{2,1,0:T(8,128)S(1)}, f32[32,6,432]{2,1,0:T(8,128)S(1)}, u32[]{:S(2)}, u32[]{:S(2)}) %collective-permute-start.12) | collective-permute-done | bytes 331808 | tf_op jit(solution)/shard_map/ppermute | solution.py:228
  96.0 0.8 fusion.5
  96.7 9.7 %all-to-all-start = ((bf16[32,6,432]{2,1,0:T(8,128)(2,1)}), bf16[32,6,432]{2,1,0:T(8,128)(2,1)S(1)}, u32[]{:S(2)}, u32[]{:S(2)}) async-start(bf16[32,6,432]{2,1,0:T(8,128)(2,1)} %fusion.5), calls=%async_computation | async-start | bytes 524288 | tf_op jit(solution)/shard_map/all_to_all | solution.py:229
  106.4 0.7 copy.45
  107.1 10.9 %all-to-all-done = bf16[32,6,432]{2,1,0:T(8,128)(2,1)S(1)} async-done(((bf16[32,6,432]{2,1,0:T(8,128)(2,1)}), bf16[32,6,432]{2,1,0:T(8,128)(2,1)S(1)}, u32[]{:S(2)}, u32[]{:S(2)}) %all-to-all-start) | async-done | bytes 165920 | tf_op jit(solution)/shard_map/all_to_all | solution.py:229
  (138 shorter events, 17.0 us)
Async XLA Ops:
  1.6 24.1 %collective-permute-start = (bf16[2,4,16,576]{3,2,1,0:T(8,128)(2,1)S(1)}, bf16[2,4,16,576]{3,2,1,0:T(8,128)(2,1)S(1)}, u32[]{:S(2)}, u32[]{:S(2)}) collective-permute-start(bf16[2,4,16,576]{3,2,1,0:T(8,128)(2,1)S(1)} %pad_maximum_fusion), channel_id=1, source_target_pairs={{0,64},{64,128},{128,192},{192,256},{256,320},{320,384},{384,448},... | collective-permute-start | bytes 442376 | tf_op jit(solution)/shard_map/ppermute | solution.py:76
  6.5 21.3 %collective-permute-start.2 = (bf16[2,4,16,576]{3,2,1,0:T(8,128)(2,1)S(1)}, bf16[2,4,16,576]{3,2,1,0:T(8,128)(2,1)S(1)}, u32[]{:S(2)}, u32[]{:S(2)}) collective-permute-start(bf16[2,4,16,576]{3,2,1,0:T(8,128)(2,1)S(1)} %pad_maximum_fusion), channel_id=1, source_target_pairs={{0,704},{64,0},{128,64},{192,128},{256,192},{320,256},{384,320},{4... | collective-permute-start | bytes 442376 | tf_op jit(solution)/shard_map/ppermute | solution.py:179
  21.2 2.1 %copy-start.5 = (s32[1,24]{1,0:T(1,128)S(1)}, s32[1,24]{1,0:T(1,128)}, u32[]{:S(2)}) copy-start(s32[1,24]{1,0:T(1,128)} %param.6) | copy-start | bytes 292
  21.2 13.6 %copy-start.1 = (bf16[1,2,4,16,192]{4,3,2,1,0:T(8,128)(2,1)S(1)}, bf16[1,2,4,16,192]{4,3,2,1,0:T(8,128)(2,1)}, u32[]{:S(2)}) copy-start(bf16[1,2,4,16,192]{4,3,2,1,0:T(8,128)(2,1)} %param.5) | copy-start | bytes 147460
  21.2 13.6 %copy-start.4 = (f32[192]{0:T(256)S(1)}, f32[192]{0:T(256)}, u32[]{:S(2)}) copy-start(f32[192]{0:T(256)} %param.7) | copy-start | bytes 2308
  22.5 13.2 %copy-start.2 = (bf16[1,2,4,16,384]{4,3,2,1,0:T(8,128)(2,1)S(1)}, bf16[1,2,4,16,384]{4,3,2,1,0:T(8,128)(2,1)}, u32[]{:S(2)}) copy-start(bf16[1,2,4,16,384]{4,3,2,1,0:T(8,128)(2,1)} %param.9) | copy-start | bytes 294916
  25.8 7.9 %collective-permute-start.1 = (bf16[2,4,16,576]{3,2,1,0:T(8,128)(2,1)S(1)}, bf16[2,4,16,576]{3,2,1,0:T(8,128)(2,1)S(1)}, u32[]{:S(2)}, u32[]{:S(2)}) collective-permute-start(bf16[2,4,16,576]{3,2,1,0:T(8,128)(2,1)S(1)} %collective-permute-done), channel_id=1, source_target_pairs={{0,64},{64,128},{128,192},{192,256},{256,320},{320,384},{384,448},... | collective-permute-start | bytes 442376 | tf_op jit(solution)/shard_map/ppermute | solution.py:211
  27.8 6.8 %collective-permute-start.3 = (bf16[2,4,16,576]{3,2,1,0:T(8,128)(2,1)S(1)}, bf16[2,4,16,576]{3,2,1,0:T(8,128)(2,1)S(1)}, u32[]{:S(2)}, u32[]{:S(2)}) collective-permute-start(bf16[2,4,16,576]{3,2,1,0:T(8,128)(2,1)S(1)} %collective-permute-done.2), channel_id=1, source_target_pairs={{0,704},{64,0},{128,64},{192,128},{256,192},{320,256},{384,320},{4... | collective-permute-start | bytes 442376 | tf_op jit(solution)/shard_map/ppermute | solution.py:214
  35.3 2.5 %copy-start = (bf16[5184,384]{1,0:T(8,128)(2,1)S(1)}, bf16[5184,384]{1,0:T(8,128)(2,1)}, u32[]{:S(2)}) copy-start(bf16[5184,384]{1,0:T(8,128)(2,1)} %param.8) | copy-start | bytes 11943940
  35.3 2.5 %copy-start.3 = (pred[16,3]{0,1:T(4,128)(4,1)S(1)}, pred[16,3]{0,1:T(4,128)(4,1)}, u32[]{:S(2)}) copy-start(pred[16,3]{0,1:T(4,128)(4,1)} %constant.660) | copy-start | bytes 148
  39.2 8.2 %collective-permute-start.4 = (bf16[2,4,16,576]{3,2,1,0:T(8,128)(2,1)S(1)}, bf16[2,4,16,576]{3,2,1,0:T(8,128)(2,1)S(1)}, u32[]{:S(2)}, u32[]{:S(2)}) collective-permute-start(bf16[2,4,16,576]{3,2,1,0:T(8,128)(2,1)S(1)} %collective-permute-done.1), channel_id=1, source_target_pairs={{0,64},{64,128},{128,192},{192,256},{256,320},{320,384},{384,448},... | collective-permute-start | bytes 442376 | tf_op jit(solution)/shard_map/ppermute | solution.py:211
  41.1 7.3 %collective-permute-start.5 = (bf16[2,4,16,576]{3,2,1,0:T(8,128)(2,1)S(1)}, bf16[2,4,16,576]{3,2,1,0:T(8,128)(2,1)S(1)}, u32[]{:S(2)}, u32[]{:S(2)}) collective-permute-start(bf16[2,4,16,576]{3,2,1,0:T(8,128)(2,1)S(1)} %collective-permute-done.3), channel_id=1, source_target_pairs={{0,704},{64,0},{128,64},{192,128},{256,192},{320,256},{384,320},{4... | collective-permute-start | bytes 442376 | tf_op jit(solution)/shard_map/ppermute | solution.py:214
  48.4 7.7 %collective-permute-start.6 = (bf16[2,4,16,576]{3,2,1,0:T(8,128)(2,1)S(1)}, bf16[2,4,16,576]{3,2,1,0:T(8,128)(2,1)S(1)}, u32[]{:S(2)}, u32[]{:S(2)}) collective-permute-start(bf16[2,4,16,576]{3,2,1,0:T(8,128)(2,1)S(1)} %collective-permute-done.4), channel_id=1, source_target_pairs={{0,64},{64,128},{128,192},{192,256},{256,320},{320,384},{384,448},... | collective-permute-start | bytes 442376 | tf_op jit(solution)/shard_map/ppermute | solution.py:211
  50.3 7.3 %collective-permute-start.7 = (bf16[2,4,16,576]{3,2,1,0:T(8,128)(2,1)S(1)}, bf16[2,4,16,576]{3,2,1,0:T(8,128)(2,1)S(1)}, u32[]{:S(2)}, u32[]{:S(2)}) collective-permute-start(bf16[2,4,16,576]{3,2,1,0:T(8,128)(2,1)S(1)} %collective-permute-done.5), channel_id=1, source_target_pairs={{0,704},{64,0},{128,64},{192,128},{256,192},{320,256},{384,320},{4... | collective-permute-start | bytes 442376 | tf_op jit(solution)/shard_map/ppermute | solution.py:214
  59.3 8.4 %collective-permute-start.8 = (bf16[2,4,16,576]{3,2,1,0:T(8,128)(2,1)S(1)}, bf16[2,4,16,576]{3,2,1,0:T(8,128)(2,1)S(1)}, u32[]{:S(2)}, u32[]{:S(2)}) collective-permute-start(bf16[2,4,16,576]{3,2,1,0:T(8,128)(2,1)S(1)} %collective-permute-done.6), channel_id=1, source_target_pairs={{0,64},{64,128},{128,192},{192,256},{256,320},{320,384},{384,448},... | collective-permute-start | bytes 442376 | tf_op jit(solution)/shard_map/ppermute | solution.py:211
  61.2 7.3 %collective-permute-start.9 = (bf16[2,4,16,576]{3,2,1,0:T(8,128)(2,1)S(1)}, bf16[2,4,16,576]{3,2,1,0:T(8,128)(2,1)S(1)}, u32[]{:S(2)}, u32[]{:S(2)}) collective-permute-start(bf16[2,4,16,576]{3,2,1,0:T(8,128)(2,1)S(1)} %collective-permute-done.7), channel_id=1, source_target_pairs={{0,704},{64,0},{128,64},{192,128},{256,192},{320,256},{384,320},{4... | collective-permute-start | bytes 442376 | tf_op jit(solution)/shard_map/ppermute | solution.py:214
  71.1 10.0 %collective-permute-start.11 = (f32[2,4,16,192]{3,2,1,0:T(8,128)S(1)}, f32[2,4,16,192]{3,2,1,0:T(8,128)S(1)}, u32[]{:S(2)}, u32[]{:S(2)}) collective-permute-start(f32[2,4,16,192]{3,2,1,0:T(8,128)S(1)} %slice.169), channel_id=1, source_target_pairs={{64,0},{128,64},{192,128},{256,192},{320,256},{384,320},{448,384},... | collective-permute-start | bytes 294920 | tf_op jit(solution)/shard_map/ppermute | solution.py:14
  72.4 8.6 %collective-permute-start.10 = (bf16[2,4,16,576]{3,2,1,0:T(8,128)(2,1)S(1)}, bf16[2,4,16,576]{3,2,1,0:T(8,128)(2,1)S(1)}, u32[]{:S(2)}, u32[]{:S(2)}) collective-permute-start(bf16[2,4,16,576]{3,2,1,0:T(8,128)(2,1)S(1)} %collective-permute-done.8), channel_id=1, source_target_pairs={{0,64},{64,128},{128,192},{192,256},{256,320},{320,384},{384,448},... | collective-permute-start | bytes 442376 | tf_op jit(solution)/shard_map/ppermute | solution.py:211
  85.2 10.7 %collective-permute-start.12 = (f32[32,6,432]{2,1,0:T(8,128)S(1)}, f32[32,6,432]{2,1,0:T(8,128)S(1)}, u32[]{:S(2)}, u32[]{:S(2)}) collective-permute-start(f32[32,6,432]{2,1,0:T(8,128)S(1)} %dynamic-slice_bitcast_fusion), channel_id=1, source_target_pairs={{0,1},{1,0},{2,3},{3,2},{4,5},{5,4},{6,7},{7,6},{8,9},{9,8},{10,11... | collective-permute-start | bytes 995336 | tf_op jit(solution)/shard_map/ppermute | solution.py:228
  96.7 21.3 %all-to-all-start = ((bf16[32,6,432]{2,1,0:T(8,128)(2,1)}), bf16[32,6,432]{2,1,0:T(8,128)(2,1)S(1)}, u32[]{:S(2)}, u32[]{:S(2)}) async-start(bf16[32,6,432]{2,1,0:T(8,128)(2,1)} %fusion.5), calls=%async_computation | async-start | bytes 524288 | tf_op jit(solution)/shard_map/all_to_all | solution.py:229

commit v15 on v13

--- a/solution.py
+++ b/solution.py
@@ -224,7 +224,9 @@
     core = lax.axis_index("dc")
     kept = lax.dynamic_index_in_dim(pieces, core, 1, keepdims=False)
     sent = lax.dynamic_index_in_dim(pieces, 1 - core, 1, keepdims=False)
-    pair_sum = kept + lax.ppermute(sent, "dc", [(0, 1), (1, 0)])
+    pair_sum = kept + lax.ppermute(sent.astype(jnp.bfloat16), "dc", [(0, 1), (1, 0)]).astype(
+        jnp.float32
+    )
     reduced_t = lax.all_to_all(pair_sum.astype(jnp.bfloat16), "dq", 0, 0, tiled=False).astype(
         jnp.float32
     ).sum(axis=0)

time: 118 us -> 118 us (level)
  no operation moved by 1% of the time
where the time goes in v15:
time: 118 us; the launch traced here: 117 us
  starting transfers between devices  66 us (56%)
  waiting for transfers between devices  22.2 us (19%)
  local copies, waits for them, and re-layouts  9.82 us (8%)
  other arithmetic  9.25 us (8%)
  matrix products  7.51 us (6%)
  between operations  2.26 us (2%)
    ppermute x4, starting transfers between devices, shards(): backward_moving = lax.ppermute(backward_moving, 'tm', ring_route('tm', -1))  19.2 us
    ppermute x1, starting transfers between devices, shards(): backward_moving = lax.ppermute(both, 'tm', ring_route('tm', -1))  12.2 us
    all_to_all x1, waiting for transfers between devices, shards(): lax.all_to_all(pair_sum.astype(jnp.bfloat16), 'dq', 0, 0, tiled=False)  10.9 us
    ppermute x5, starting transfers between devices, shards(): forward_moving = lax.ppermute(forward_moving, 'tm', ring_route('tm', 1))  9.71 us
    all_to_all x1, starting transfers between devices, shards(): lax.all_to_all(pair_sum.astype(jnp.bfloat16), 'dq', 0, 0, tiled=False)  9.67 us
    ppermute x1, starting transfers between devices, shards(): lax.ppermute(sent.astype(jnp.bfloat16), 'dc', [(0, 1), (1, 0)])  8.93 us
    ppermute x5, waiting for transfers between devices, shards(): forward_moving = lax.ppermute(forward_moving, 'tm', ring_route('tm', 1))  5.32 us
    dot_general x12, matrix products, block_term(): lax.dot_general(block_cot, jnp.concatenate(columns, axis=1), (((0,), (0,)...  4.97 us
  transfers between devices with their start and end apart: 14, of which 7 were waited for; matrix products, arithmetic and copies ran while one was open for 15% of the time, Pallas kernels for 0%

profile of v15, /device:TPU:1, one launch (start us, length us, event | category | flops | bytes accessed | tf_op | source)
XLA Modules:
  0.0 117.1 jit_solution(5124986820527673160)
XLA Ops:
  0.6 1.0 pad_maximum_fusion
  1.6 4.8 %collective-permute-start = (bf16[2,4,16,576]{3,2,1,0:T(8,128)(2,1)S(1)}, bf16[2,4,16,576]{3,2,1,0:T(8,128)(2,1)S(1)}, u32[]{:S(2)}, u32[]{:S(2)}) collective-permute-start(bf16[2,4,16,576]{3,2,1,0:T(8,128)(2,1)S(1)} %pad_maximum_fusion), channel_id=1, source_target_pairs={{0,64},{64,128},{128,192},{192,256},{256,320},{320,384},{384,448},... | collective-permute-start | bytes 442376 | tf_op jit(solution)/shard_map/ppermute | solution.py:76
  6.5 12.2 %collective-permute-start.2 = (bf16[2,4,16,576]{3,2,1,0:T(8,128)(2,1)S(1)}, bf16[2,4,16,576]{3,2,1,0:T(8,128)(2,1)S(1)}, u32[]{:S(2)}, u32[]{:S(2)}) collective-permute-start(bf16[2,4,16,576]{3,2,1,0:T(8,128)(2,1)S(1)} %pad_maximum_fusion), channel_id=1, source_target_pairs={{0,704},{64,0},{128,64},{192,128},{256,192},{320,256},{384,320},{4... | collective-permute-start | bytes 442376 | tf_op jit(solution)/shard_map/ppermute | solution.py:179
  18.8 0.9 fusion.93
  20.2 0.7 concatenate.83
  21.1 1.2 %gather_fusion = s32[72]{0:T(128)S(1)} fusion(s32[26]{0:T(128)S(1)} %concatenate.83, s32[1024]{0:T(1024)S(1)} %pad_clamp_fusion.3), kind=kCustom, calls=%fused_computation | custom fusion | bytes 864 | tf_op jit(solution)/shard_map/gather | solution.py:50
  22.5 0.7 gather_fusion.1
  23.5 0.6 gather_fusion.2
  24.2 0.6 gather_fusion.3
  27.1 2.1 %collective-permute-start.1 = (bf16[2,4,16,576]{3,2,1,0:T(8,128)(2,1)S(1)}, bf16[2,4,16,576]{3,2,1,0:T(8,128)(2,1)S(1)}, u32[]{:S(2)}, u32[]{:S(2)}) collective-permute-start(bf16[2,4,16,576]{3,2,1,0:T(8,128)(2,1)S(1)} %collective-permute-done), channel_id=1, source_target_pairs={{0,64},{64,128},{128,192},{192,256},{256,320},{320,384},{384,448},... | collective-permute-start | bytes 442376 | tf_op jit(solution)/shard_map/ppermute | solution.py:211
  29.1 4.6 %collective-permute-start.3 = (bf16[2,4,16,576]{3,2,1,0:T(8,128)(2,1)S(1)}, bf16[2,4,16,576]{3,2,1,0:T(8,128)(2,1)S(1)}, u32[]{:S(2)}, u32[]{:S(2)}) collective-permute-start(bf16[2,4,16,576]{3,2,1,0:T(8,128)(2,1)S(1)} %collective-permute-done.2), channel_id=1, source_target_pairs={{0,704},{64,0},{128,64},{192,128},{256,192},{320,256},{384,320},{4... | collective-permute-start | bytes 442376 | tf_op jit(solution)/shard_map/ppermute | solution.py:214
  34.3 0.7 collective-permute-done.1
  35.0 0.9 collective-permute-done.3
  35.9 1.9 %collective-permute-start.4 = (bf16[2,4,16,576]{3,2,1,0:T(8,128)(2,1)S(1)}, bf16[2,4,16,576]{3,2,1,0:T(8,128)(2,1)S(1)}, u32[]{:S(2)}, u32[]{:S(2)}) collective-permute-start(bf16[2,4,16,576]{3,2,1,0:T(8,128)(2,1)S(1)} %collective-permute-done.1), channel_id=1, source_target_pairs={{0,64},{64,128},{128,192},{192,256},{256,320},{320,384},{384,448},... | collective-permute-start | bytes 442376 | tf_op jit(solution)/shard_map/ppermute | solution.py:211
  37.9 5.0 %collective-permute-start.5 = (bf16[2,4,16,576]{3,2,1,0:T(8,128)(2,1)S(1)}, bf16[2,4,16,576]{3,2,1,0:T(8,128)(2,1)S(1)}, u32[]{:S(2)}, u32[]{:S(2)}) collective-permute-start(bf16[2,4,16,576]{3,2,1,0:T(8,128)(2,1)S(1)} %collective-permute-done.3), channel_id=1, source_target_pairs={{0,704},{64,0},{128,64},{192,128},{256,192},{320,256},{384,320},{4... | collective-permute-start | bytes 442376 | tf_op jit(solution)/shard_map/ppermute | solution.py:214
  44.2 1.3 %fusion.1 = bf16[1,4,16,3,384]{4,2,3,1,0:T(8,128)(2,1)S(1)} fusion(bf16[3,3,3,192,384]{4,3,2,1,0:T(8,128)(2,1)S(1)} %bitcast.133, bf16[3,4,2,8,5,192]{5,2,4,3,1,0:T(2,128)(2,1)S(1)} %fusion.5, pred[16,3]{0,1:T(4,128)(4,1)S(1)} %copy-done.4), kind=kOutput, calls=%fused_computation.11 | convolution fusion | flops 637157376 | bytes 4497456 | tf_op jit(solution)/shard_map/conv_general_dilated | solution.py:129
  47.6 1.9 %collective-permute-start.6 = (bf16[2,4,16,576]{3,2,1,0:T(8,128)(2,1)S(1)}, bf16[2,4,16,576]{3,2,1,0:T(8,128)(2,1)S(1)}, u32[]{:S(2)}, u32[]{:S(2)}) collective-permute-start(bf16[2,4,16,576]{3,2,1,0:T(8,128)(2,1)S(1)} %collective-permute-done.4), channel_id=1, source_target_pairs={{0,64},{64,128},{128,192},{192,256},{256,320},{320,384},{384,448},... | collective-permute-start | bytes 442376 | tf_op jit(solution)/shard_map/ppermute | solution.py:211
  49.6 4.6 %collective-permute-start.7 = (bf16[2,4,16,576]{3,2,1,0:T(8,128)(2,1)S(1)}, bf16[2,4,16,576]{3,2,1,0:T(8,128)(2,1)S(1)}, u32[]{:S(2)}, u32[]{:S(2)}) collective-permute-start(bf16[2,4,16,576]{3,2,1,0:T(8,128)(2,1)S(1)} %collective-permute-done.5), channel_id=1, source_target_pairs={{0,704},{64,0},{128,64},{192,128},{256,192},{320,256},{384,320},{4... | collective-permute-start | bytes 442376 | tf_op jit(solution)/shard_map/ppermute | solution.py:214
  56.4 1.9 %collective-permute-start.8 = (bf16[2,4,16,576]{3,2,1,0:T(8,128)(2,1)S(1)}, bf16[2,4,16,576]{3,2,1,0:T(8,128)(2,1)S(1)}, u32[]{:S(2)}, u32[]{:S(2)}) collective-permute-start(bf16[2,4,16,576]{3,2,1,0:T(8,128)(2,1)S(1)} %collective-permute-done.6), channel_id=1, source_target_pairs={{0,64},{64,128},{128,192},{192,256},{256,320},{320,384},{384,448},... | collective-permute-start | bytes 442376 | tf_op jit(solution)/shard_map/ppermute | solution.py:211
  58.3 5.0 %collective-permute-start.9 = (bf16[2,4,16,576]{3,2,1,0:T(8,128)(2,1)S(1)}, bf16[2,4,16,576]{3,2,1,0:T(8,128)(2,1)S(1)}, u32[]{:S(2)}, u32[]{:S(2)}) collective-permute-start(bf16[2,4,16,576]{3,2,1,0:T(8,128)(2,1)S(1)} %collective-permute-done.7), channel_id=1, source_target_pairs={{0,704},{64,0},{128,64},{192,128},{256,192},{320,256},{384,320},{4... | collective-permute-start | bytes 442376 | tf_op jit(solution)/shard_map/ppermute | solution.py:214
  64.2 1.3 %fusion = f32[3,4,16,3,192]{4,2,3,1,0:T(8,128)S(1)} fusion(bf16[3,3,3,192,384]{4,3,2,1,0:T(8,128)(2,1)S(1)} %bitcast.134, f32[3,4,16,3,192]{4,1,3,2,0:T(4,128)S(1)} %bitcast.135, pred[16,3]{0,1:T(4,128)(4,1)S(1)} %copy-done.4, bf16[1,4,2,8,5,384]{5,2,4,3,1,0:T(2,128)(2,1)S(1)} %fusion.9), kind=kOutput, calls=%fused_computation.9 | convolution fusion | flops 637231104 | bytes 5111856 | tf_op jit(solution)/shard_map/conv_general_dilated | solution.py:144
  66.2 1.5 %collective-permute-start.10 = (f32[2,4,16,192]{3,2,1,0:T(8,128)S(1)}, f32[2,4,16,192]{3,2,1,0:T(8,128)S(1)}, u32[]{:S(2)}, u32[]{:S(2)}) collective-permute-start(f32[2,4,16,192]{3,2,1,0:T(8,128)S(1)} %slice.162), channel_id=1, source_target_pairs={{64,0},{128,64},{192,128},{256,192},{320,256},{384,320},{448,384},... | collective-permute-start | bytes 294920 | tf_op jit(solution)/shard_map/ppermute | solution.py:14
  68.2 3.6 %collective-permute-done.10 = f32[2,4,16,192]{3,2,1,0:T(8,128)S(1)} collective-permute-done((f32[2,4,16,192]{3,2,1,0:T(8,128)S(1)}, f32[2,4,16,192]{3,2,1,0:T(8,128)S(1)}, u32[]{:S(2)}, u32[]{:S(2)}) %collective-permute-start.10) | collective-permute-done | bytes 98336 | tf_op jit(solution)/shard_map/ppermute | solution.py:14
  72.3 0.7 fusion.184
  74.0 1.9 %collective-permute-start.11 = (bf16[2,4,16,576]{3,2,1,0:T(8,128)(2,1)S(1)}, bf16[2,4,16,576]{3,2,1,0:T(8,128)(2,1)S(1)}, u32[]{:S(2)}, u32[]{:S(2)}) collective-permute-start(bf16[2,4,16,576]{3,2,1,0:T(8,128)(2,1)S(1)} %collective-permute-done.8), channel_id=1, source_target_pairs={{0,64},{64,128},{128,192},{192,256},{256,320},{320,384},{384,448},... | collective-permute-start | bytes 442376 | tf_op jit(solution)/shard_map/ppermute | solution.py:211
  76.7 4.6 %collective-permute-done.11 = bf16[2,4,16,576]{3,2,1,0:T(8,128)(2,1)S(1)} collective-permute-done((bf16[2,4,16,576]{3,2,1,0:T(8,128)(2,1)S(1)}, bf16[2,4,16,576]{3,2,1,0:T(8,128)(2,1)S(1)}, u32[]{:S(2)}, u32[]{:S(2)}) %collective-permute-start.11) | collective-permute-done | bytes 147488 | tf_op jit(solution)/shard_map/ppermute | solution.py:211
  84.1 8.9 %collective-permute-start.12 = (bf16[32,6,432]{2,0,1:T(8,128)(2,1)S(1)}, bf16[32,6,432]{2,0,1:T(8,128)(2,1)S(1)}, u32[]{:S(2)}, u32[]{:S(2)}) collective-permute-start(bf16[32,6,432]{2,0,1:T(8,128)(2,1)S(1)} %bitcast.202), channel_id=1, source_target_pairs={{0,1},{1,0},{2,3},{3,2},{4,5},{5,4},{6,7},{7,6},{8,9},{9,8},{10,11... | collective-permute-start | bytes 497672 | tf_op jit(solution)/shard_map/ppermute | solution.py:227
  93.1 1.0 collective-permute-done.12
  94.3 0.8 copy.85
  95.1 9.7 %all-to-all-start = ((bf16[32,6,432]{2,1,0:T(8,128)(2,1)}), bf16[32,6,432]{2,1,0:T(8,128)(2,1)S(1)}, u32[]{:S(2)}, u32[]{:S(2)}) async-start(bf16[32,6,432]{2,1,0:T(8,128)(2,1)} %copy.85), calls=%async_computation | async-start | bytes 524288 | tf_op jit(solution)/shard_map/all_to_all | solution.py:230
  104.8 0.7 copy.86
  105.5 10.9 %all-to-all-done = bf16[32,6,432]{2,1,0:T(8,128)(2,1)S(1)} async-done(((bf16[32,6,432]{2,1,0:T(8,128)(2,1)}), bf16[32,6,432]{2,1,0:T(8,128)(2,1)S(1)}, u32[]{:S(2)}, u32[]{:S(2)}) %all-to-all-start) | async-done | bytes 165920 | tf_op jit(solution)/shard_map/all_to_all | solution.py:230
  (145 shorter events, 16.4 us)
Async XLA Ops:
  1.6 24.2 %collective-permute-start = (bf16[2,4,16,576]{3,2,1,0:T(8,128)(2,1)S(1)}, bf16[2,4,16,576]{3,2,1,0:T(8,128)(2,1)S(1)}, u32[]{:S(2)}, u32[]{:S(2)}) collective-permute-start(bf16[2,4,16,576]{3,2,1,0:T(8,128)(2,1)S(1)} %pad_maximum_fusion), channel_id=1, source_target_pairs={{0,64},{64,128},{128,192},{192,256},{256,320},{320,384},{384,448},... | collective-permute-start | bytes 442376 | tf_op jit(solution)/shard_map/ppermute | solution.py:76
  6.5 19.3 %collective-permute-start.2 = (bf16[2,4,16,576]{3,2,1,0:T(8,128)(2,1)S(1)}, bf16[2,4,16,576]{3,2,1,0:T(8,128)(2,1)S(1)}, u32[]{:S(2)}, u32[]{:S(2)}) collective-permute-start(bf16[2,4,16,576]{3,2,1,0:T(8,128)(2,1)S(1)} %pad_maximum_fusion), channel_id=1, source_target_pairs={{0,704},{64,0},{128,64},{192,128},{256,192},{320,256},{384,320},{4... | collective-permute-start | bytes 442376 | tf_op jit(solution)/shard_map/ppermute | solution.py:179
  21.1 2.2 %copy-start.5 = (s32[1,24]{1,0:T(1,128)S(1)}, s32[1,24]{1,0:T(1,128)}, u32[]{:S(2)}) copy-start(s32[1,24]{1,0:T(1,128)} %param.6) | copy-start | bytes 292
  21.1 4.9 %copy-start.1 = (bf16[1,2,4,16,192]{4,3,2,1,0:T(8,128)(2,1)S(1)}, bf16[1,2,4,16,192]{4,3,2,1,0:T(8,128)(2,1)}, u32[]{:S(2)}) copy-start(bf16[1,2,4,16,192]{4,3,2,1,0:T(8,128)(2,1)} %param.5) | copy-start | bytes 147460
  21.1 4.9 %copy-start.3 = (f32[192]{0:T(256)S(1)}, f32[192]{0:T(256)}, u32[]{:S(2)}) copy-start(f32[192]{0:T(256)} %param.7) | copy-start | bytes 2308
  22.3 4.3 %copy-start.2 = (bf16[1,2,4,16,384]{4,3,2,1,0:T(8,128)(2,1)S(1)}, bf16[1,2,4,16,384]{4,3,2,1,0:T(8,128)(2,1)}, u32[]{:S(2)}) copy-start(bf16[1,2,4,16,384]{4,3,2,1,0:T(8,128)(2,1)} %param.9) | copy-start | bytes 294916
  26.2 17.9 %copy-start = (bf16[5184,384]{1,0:T(8,128)(2,1)S(1)}, bf16[5184,384]{1,0:T(8,128)(2,1)}, u32[]{:S(2)}) copy-start(bf16[5184,384]{1,0:T(8,128)(2,1)} %param.8) | copy-start | bytes 11943940
  26.3 17.9 %copy-start.4 = (pred[16,3]{0,1:T(4,128)(4,1)S(1)}, pred[16,3]{0,1:T(4,128)(4,1)}, u32[]{:S(2)}) copy-start(pred[16,3]{0,1:T(4,128)(4,1)} %constant.660) | copy-start | bytes 148
  27.1 8.0 %collective-permute-start.1 = (bf16[2,4,16,576]{3,2,1,0:T(8,128)(2,1)S(1)}, bf16[2,4,16,576]{3,2,1,0:T(8,128)(2,1)S(1)}, u32[]{:S(2)}, u32[]{:S(2)}) collective-permute-start(bf16[2,4,16,576]{3,2,1,0:T(8,128)(2,1)S(1)} %collective-permute-done), channel_id=1, source_target_pairs={{0,64},{64,128},{128,192},{192,256},{256,320},{320,384},{384,448},... | collective-permute-start | bytes 442376 | tf_op jit(solution)/shard_map/ppermute | solution.py:211
  29.1 6.8 %collective-permute-start.3 = (bf16[2,4,16,576]{3,2,1,0:T(8,128)(2,1)S(1)}, bf16[2,4,16,576]{3,2,1,0:T(8,128)(2,1)S(1)}, u32[]{:S(2)}, u32[]{:S(2)}) collective-permute-start(bf16[2,4,16,576]{3,2,1,0:T(8,128)(2,1)S(1)} %collective-permute-done.2), channel_id=1, source_target_pairs={{0,704},{64,0},{128,64},{192,128},{256,192},{320,256},{384,320},{4... | collective-permute-start | bytes 442376 | tf_op jit(solution)/shard_map/ppermute | solution.py:214
  35.9 11.7 %collective-permute-start.4 = (bf16[2,4,16,576]{3,2,1,0:T(8,128)(2,1)S(1)}, bf16[2,4,16,576]{3,2,1,0:T(8,128)(2,1)S(1)}, u32[]{:S(2)}, u32[]{:S(2)}) collective-permute-start(bf16[2,4,16,576]{3,2,1,0:T(8,128)(2,1)S(1)} %collective-permute-done.1), channel_id=1, source_target_pairs={{0,64},{64,128},{128,192},{192,256},{256,320},{320,384},{384,448},... | collective-permute-start | bytes 442376 | tf_op jit(solution)/shard_map/ppermute | solution.py:211
  37.9 8.0 %collective-permute-start.5 = (bf16[2,4,16,576]{3,2,1,0:T(8,128)(2,1)S(1)}, bf16[2,4,16,576]{3,2,1,0:T(8,128)(2,1)S(1)}, u32[]{:S(2)}, u32[]{:S(2)}) collective-permute-start(bf16[2,4,16,576]{3,2,1,0:T(8,128)(2,1)S(1)} %collective-permute-done.3), channel_id=1, source_target_pairs={{0,704},{64,0},{128,64},{192,128},{256,192},{320,256},{384,320},{4... | collective-permute-start | bytes 442376 | tf_op jit(solution)/shard_map/ppermute | solution.py:214
  47.6 7.4 %collective-permute-start.6 = (bf16[2,4,16,576]{3,2,1,0:T(8,128)(2,1)S(1)}, bf16[2,4,16,576]{3,2,1,0:T(8,128)(2,1)S(1)}, u32[]{:S(2)}, u32[]{:S(2)}) collective-permute-start(bf16[2,4,16,576]{3,2,1,0:T(8,128)(2,1)S(1)} %collective-permute-done.4), channel_id=1, source_target_pairs={{0,64},{64,128},{128,192},{192,256},{256,320},{320,384},{384,448},... | collective-permute-start | bytes 442376 | tf_op jit(solution)/shard_map/ppermute | solution.py:211
  49.6 6.8 %collective-permute-start.7 = (bf16[2,4,16,576]{3,2,1,0:T(8,128)(2,1)S(1)}, bf16[2,4,16,576]{3,2,1,0:T(8,128)(2,1)S(1)}, u32[]{:S(2)}, u32[]{:S(2)}) collective-permute-start(bf16[2,4,16,576]{3,2,1,0:T(8,128)(2,1)S(1)} %collective-permute-done.5), channel_id=1, source_target_pairs={{0,704},{64,0},{128,64},{192,128},{256,192},{320,256},{384,320},{4... | collective-permute-start | bytes 442376 | tf_op jit(solution)/shard_map/ppermute | solution.py:214
  56.4 11.7 %collective-permute-start.8 = (bf16[2,4,16,576]{3,2,1,0:T(8,128)(2,1)S(1)}, bf16[2,4,16,576]{3,2,1,0:T(8,128)(2,1)S(1)}, u32[]{:S(2)}, u32[]{:S(2)}) collective-permute-start(bf16[2,4,16,576]{3,2,1,0:T(8,128)(2,1)S(1)} %collective-permute-done.6), channel_id=1, source_target_pairs={{0,64},{64,128},{128,192},{192,256},{256,320},{320,384},{384,448},... | collective-permute-start | bytes 442376 | tf_op jit(solution)/shard_map/ppermute | solution.py:211
  58.3 9.7 %collective-permute-start.9 = (bf16[2,4,16,576]{3,2,1,0:T(8,128)(2,1)S(1)}, bf16[2,4,16,576]{3,2,1,0:T(8,128)(2,1)S(1)}, u32[]{:S(2)}, u32[]{:S(2)}) collective-permute-start(bf16[2,4,16,576]{3,2,1,0:T(8,128)(2,1)S(1)} %collective-permute-done.7), channel_id=1, source_target_pairs={{0,704},{64,0},{128,64},{192,128},{256,192},{320,256},{384,320},{4... | collective-permute-start | bytes 442376 | tf_op jit(solution)/shard_map/ppermute | solution.py:214
  66.2 5.7 %collective-permute-start.10 = (f32[2,4,16,192]{3,2,1,0:T(8,128)S(1)}, f32[2,4,16,192]{3,2,1,0:T(8,128)S(1)}, u32[]{:S(2)}, u32[]{:S(2)}) collective-permute-start(f32[2,4,16,192]{3,2,1,0:T(8,128)S(1)} %slice.162), channel_id=1, source_target_pairs={{64,0},{128,64},{192,128},{256,192},{320,256},{384,320},{448,384},... | collective-permute-start | bytes 294920 | tf_op jit(solution)/shard_map/ppermute | solution.py:14
  74.0 7.3 %collective-permute-start.11 = (bf16[2,4,16,576]{3,2,1,0:T(8,128)(2,1)S(1)}, bf16[2,4,16,576]{3,2,1,0:T(8,128)(2,1)S(1)}, u32[]{:S(2)}, u32[]{:S(2)}) collective-permute-start(bf16[2,4,16,576]{3,2,1,0:T(8,128)(2,1)S(1)} %collective-permute-done.8), channel_id=1, source_target_pairs={{0,64},{64,128},{128,192},{192,256},{256,320},{320,384},{384,448},... | collective-permute-start | bytes 442376 | tf_op jit(solution)/shard_map/ppermute | solution.py:211
  84.1 10.0 %collective-permute-start.12 = (bf16[32,6,432]{2,0,1:T(8,128)(2,1)S(1)}, bf16[32,6,432]{2,0,1:T(8,128)(2,1)S(1)}, u32[]{:S(2)}, u32[]{:S(2)}) collective-permute-start(bf16[32,6,432]{2,0,1:T(8,128)(2,1)S(1)} %bitcast.202), channel_id=1, source_target_pairs={{0,1},{1,0},{2,3},{3,2},{4,5},{5,4},{6,7},{7,6},{8,9},{9,8},{10,11... | collective-permute-start | bytes 497672 | tf_op jit(solution)/shard_map/ppermute | solution.py:227
  95.1 21.3 %all-to-all-start = ((bf16[32,6,432]{2,1,0:T(8,128)(2,1)}), bf16[32,6,432]{2,1,0:T(8,128)(2,1)S(1)}, u32[]{:S(2)}, u32[]{:S(2)}) async-start(bf16[32,6,432]{2,1,0:T(8,128)(2,1)} %copy.85), calls=%async_computation | async-start | bytes 524288 | tf_op jit(solution)/shard_map/all_to_all | solution.py:230

commit v16 on v13

--- a/solution.py
+++ b/solution.py
@@ -208,6 +208,12 @@
             if block is not None:
                 blocks[rel] = block
                 block_acts[rel] = activate(block[..., :channels], norm_gain).astype(jnp.bfloat16)
+        if step > backward_steps and frames > 1:
+            half = frames // 2
+            front = lax.ppermute(forward_moving[:half], "tm", ring_route("tm", 1))
+            back = lax.ppermute(backward_moving[half:], "tm", ring_route("tm", -1))
+            arrived = [(chain_len - step, jnp.concatenate([front, back]))]
+            continue
         forward_moving = lax.ppermute(forward_moving, "tm", ring_route("tm", 1))
         arrived = [(chain_len - step, forward_moving)]
         if step <= backward_steps:

time: 118 us -> 119 us (level)
  starting transfers between devices: 66 us -> 70.6 us
  waiting for transfers between devices: 22.7 us -> 18.8 us
    ppermute x0 -> x2, starting transfers between devices: none -> 6.49 us  [the longest x1 4.57 us: shards(): back = lax.ppermute(backward_moving[half:], 'tm', ring_route('tm', -1))]
    ppermute x5 -> x4, waiting for transfers between devices: 5.32 us -> 0.72 us  [shards(): forward_moving = lax.ppermute(forward_moving, 'tm', ring_route('tm', 1))]
    ppermute x5 -> x4, starting transfers between devices: 9.71 us -> 7.79 us  [shards(): forward_moving = lax.ppermute(forward_moving, 'tm', ring_route('tm', 1))]
  transfers between devices with their start and end apart: 14 -> 15, of which waited for: 7 -> 7; matrix products, arithmetic and copies ran while one was open for 15% -> 15% of each run, Pallas kernels for 0% -> 0%
where the time goes in v16:
time: 119 us; the launch traced here: 118 us
  starting transfers between devices  70.6 us (59%)
  waiting for transfers between devices  18.8 us (16%)
  other arithmetic  9.76 us (8%)
  local copies, waits for them, and re-layouts  8.95 us (8%)
  matrix products  7.52 us (6%)
  between operations  2.28 us (2%)
    ppermute x4, starting transfers between devices, shards(): backward_moving = lax.ppermute(backward_moving, 'tm', ring_route('tm', -1))  19.2 us
    ppermute x1, starting transfers between devices, shards(): backward_moving = lax.ppermute(both, 'tm', ring_route('tm', -1))  12.2 us
    all_to_all x1, waiting for transfers between devices, shards(): lax.all_to_all(pair_sum.astype(jnp.bfloat16), 'dq', 0, 0, tiled=False)  10.9 us
    all_to_all x1, starting transfers between devices, shards(): lax.all_to_all(pair_sum.astype(jnp.bfloat16), 'dq', 0, 0, tiled=False)  9.65 us
    ppermute x1, starting transfers between devices, shards(): pair_sum = kept + lax.ppermute(sent, 'dc', [(0, 1), (1, 0)])  8.91 us
    ppermute x4, starting transfers between devices, shards(): forward_moving = lax.ppermute(forward_moving, 'tm', ring_route('tm', 1))  7.79 us
    dot_general x12, matrix products, block_term(): lax.dot_general(block_cot, jnp.concatenate(columns, axis=1), (((0,), (0,)...  4.98 us
    ppermute x1, starting transfers between devices, shards(): first_behind = lax.ppermute(both, 'tm', ring_route('tm', 1))  4.83 us
  transfers between devices with their start and end apart: 15, of which 7 were waited for; matrix products, arithmetic and copies ran while one was open for 15% of the time, Pallas kernels for 0%

profile of v16, /device:TPU:1, one launch (start us, length us, event | category | flops | bytes accessed | tf_op | source)
XLA Modules:
  0.0 117.9 jit_solution(9546511938885832923)
XLA Ops:
  0.6 1.0 pad_maximum_fusion
  1.6 4.8 %collective-permute-start = (bf16[2,4,16,576]{3,2,1,0:T(8,128)(2,1)S(1)}, bf16[2,4,16,576]{3,2,1,0:T(8,128)(2,1)S(1)}, u32[]{:S(2)}, u32[]{:S(2)}) collective-permute-start(bf16[2,4,16,576]{3,2,1,0:T(8,128)(2,1)S(1)} %pad_maximum_fusion), channel_id=1, source_target_pairs={{0,64},{64,128},{128,192},{192,256},{256,320},{320,384},{384,448},... | collective-permute-start | bytes 442376 | tf_op jit(solution)/shard_map/ppermute | solution.py:76
  6.5 12.2 %collective-permute-start.2 = (bf16[2,4,16,576]{3,2,1,0:T(8,128)(2,1)S(1)}, bf16[2,4,16,576]{3,2,1,0:T(8,128)(2,1)S(1)}, u32[]{:S(2)}, u32[]{:S(2)}) collective-permute-start(bf16[2,4,16,576]{3,2,1,0:T(8,128)(2,1)S(1)} %pad_maximum_fusion), channel_id=1, source_target_pairs={{0,704},{64,0},{128,64},{192,128},{256,192},{320,256},{384,320},{4... | collective-permute-start | bytes 442376 | tf_op jit(solution)/shard_map/ppermute | solution.py:179
  18.8 0.9 fusion.92
  20.2 0.7 concatenate.86
  21.1 1.2 %gather_fusion = s32[72]{0:T(128)S(1)} fusion(s32[26]{0:T(128)S(1)} %concatenate.86, s32[1024]{0:T(1024)S(1)} %pad_clamp_fusion.3), kind=kCustom, calls=%fused_computation | custom fusion | bytes 864 | tf_op jit(solution)/shard_map/gather | solution.py:50
  22.5 0.7 gather_fusion.1
  24.2 0.6 gather_fusion.3
  27.0 2.1 %collective-permute-start.1 = (bf16[2,4,16,576]{3,2,1,0:T(8,128)(2,1)S(1)}, bf16[2,4,16,576]{3,2,1,0:T(8,128)(2,1)S(1)}, u32[]{:S(2)}, u32[]{:S(2)}) collective-permute-start(bf16[2,4,16,576]{3,2,1,0:T(8,128)(2,1)S(1)} %collective-permute-done), channel_id=1, source_target_pairs={{0,64},{64,128},{128,192},{192,256},{256,320},{320,384},{384,448},... | collective-permute-start | bytes 442376 | tf_op jit(solution)/shard_map/ppermute | solution.py:217
  29.1 4.6 %collective-permute-start.3 = (bf16[2,4,16,576]{3,2,1,0:T(8,128)(2,1)S(1)}, bf16[2,4,16,576]{3,2,1,0:T(8,128)(2,1)S(1)}, u32[]{:S(2)}, u32[]{:S(2)}) collective-permute-start(bf16[2,4,16,576]{3,2,1,0:T(8,128)(2,1)S(1)} %collective-permute-done.2), channel_id=1, source_target_pairs={{0,704},{64,0},{128,64},{192,128},{256,192},{320,256},{384,320},{4... | collective-permute-start | bytes 442376 | tf_op jit(solution)/shard_map/ppermute | solution.py:220
  34.3 0.7 collective-permute-done.1
  35.0 0.9 collective-permute-done.3
  35.9 1.9 %collective-permute-start.4 = (bf16[2,4,16,576]{3,2,1,0:T(8,128)(2,1)S(1)}, bf16[2,4,16,576]{3,2,1,0:T(8,128)(2,1)S(1)}, u32[]{:S(2)}, u32[]{:S(2)}) collective-permute-start(bf16[2,4,16,576]{3,2,1,0:T(8,128)(2,1)S(1)} %collective-permute-done.1), channel_id=1, source_target_pairs={{0,64},{64,128},{128,192},{192,256},{256,320},{320,384},{384,448},... | collective-permute-start | bytes 442376 | tf_op jit(solution)/shard_map/ppermute | solution.py:217
  37.8 5.0 %collective-permute-start.5 = (bf16[2,4,16,576]{3,2,1,0:T(8,128)(2,1)S(1)}, bf16[2,4,16,576]{3,2,1,0:T(8,128)(2,1)S(1)}, u32[]{:S(2)}, u32[]{:S(2)}) collective-permute-start(bf16[2,4,16,576]{3,2,1,0:T(8,128)(2,1)S(1)} %collective-permute-done.3), channel_id=1, source_target_pairs={{0,704},{64,0},{128,64},{192,128},{256,192},{320,256},{384,320},{4... | collective-permute-start | bytes 442376 | tf_op jit(solution)/shard_map/ppermute | solution.py:220
  44.2 1.3 %fusion.1 = bf16[1,4,16,3,384]{4,2,3,1,0:T(8,128)(2,1)S(1)} fusion(bf16[3,3,3,192,384]{4,3,2,1,0:T(8,128)(2,1)S(1)} %bitcast.132, bf16[3,4,2,8,5,192]{5,2,4,3,1,0:T(2,128)(2,1)S(1)} %fusion.6, pred[16,3]{0,1:T(4,128)(4,1)S(1)} %copy-done.4), kind=kOutput, calls=%fused_computation.11 | convolution fusion | flops 637157376 | bytes 4497456 | tf_op jit(solution)/shard_map/conv_general_dilated | solution.py:129
  47.6 1.9 %collective-permute-start.6 = (bf16[2,4,16,576]{3,2,1,0:T(8,128)(2,1)S(1)}, bf16[2,4,16,576]{3,2,1,0:T(8,128)(2,1)S(1)}, u32[]{:S(2)}, u32[]{:S(2)}) collective-permute-start(bf16[2,4,16,576]{3,2,1,0:T(8,128)(2,1)S(1)} %collective-permute-done.4), channel_id=1, source_target_pairs={{0,64},{64,128},{128,192},{192,256},{256,320},{320,384},{384,448},... | collective-permute-start | bytes 442376 | tf_op jit(solution)/shard_map/ppermute | solution.py:217
  49.6 4.6 %collective-permute-start.7 = (bf16[2,4,16,576]{3,2,1,0:T(8,128)(2,1)S(1)}, bf16[2,4,16,576]{3,2,1,0:T(8,128)(2,1)S(1)}, u32[]{:S(2)}, u32[]{:S(2)}) collective-permute-start(bf16[2,4,16,576]{3,2,1,0:T(8,128)(2,1)S(1)} %collective-permute-done.5), channel_id=1, source_target_pairs={{0,704},{64,0},{128,64},{192,128},{256,192},{320,256},{384,320},{4... | collective-permute-start | bytes 442376 | tf_op jit(solution)/shard_map/ppermute | solution.py:220
  56.4 1.9 %collective-permute-start.8 = (bf16[2,4,16,576]{3,2,1,0:T(8,128)(2,1)S(1)}, bf16[2,4,16,576]{3,2,1,0:T(8,128)(2,1)S(1)}, u32[]{:S(2)}, u32[]{:S(2)}) collective-permute-start(bf16[2,4,16,576]{3,2,1,0:T(8,128)(2,1)S(1)} %collective-permute-done.6), channel_id=1, source_target_pairs={{0,64},{64,128},{128,192},{192,256},{256,320},{320,384},{384,448},... | collective-permute-start | bytes 442376 | tf_op jit(solution)/shard_map/ppermute | solution.py:217
  58.3 5.0 %collective-permute-start.9 = (bf16[2,4,16,576]{3,2,1,0:T(8,128)(2,1)S(1)}, bf16[2,4,16,576]{3,2,1,0:T(8,128)(2,1)S(1)}, u32[]{:S(2)}, u32[]{:S(2)}) collective-permute-start(bf16[2,4,16,576]{3,2,1,0:T(8,128)(2,1)S(1)} %collective-permute-done.7), channel_id=1, source_target_pairs={{0,704},{64,0},{128,64},{192,128},{256,192},{320,256},{384,320},{4... | collective-permute-start | bytes 442376 | tf_op jit(solution)/shard_map/ppermute | solution.py:220
  64.2 1.3 %fusion = f32[3,4,16,3,192]{4,2,3,1,0:T(8,128)S(1)} fusion(bf16[3,3,3,192,384]{4,3,2,1,0:T(8,128)(2,1)S(1)} %bitcast.133, f32[3,4,16,3,192]{4,1,3,2,0:T(4,128)S(1)} %bitcast.134, pred[16,3]{0,1:T(4,128)(4,1)S(1)} %copy-done.4, bf16[1,4,2,8,5,384]{5,2,4,3,1,0:T(2,128)(2,1)S(1)} %fusion.9), kind=kOutput, calls=%fused_computation.9 | convolution fusion | flops 637231104 | bytes 5111856 | tf_op jit(solution)/shard_map/conv_general_dilated | solution.py:144
  66.2 1.5 %collective-permute-start.10 = (f32[2,4,16,192]{3,2,1,0:T(8,128)S(1)}, f32[2,4,16,192]{3,2,1,0:T(8,128)S(1)}, u32[]{:S(2)}, u32[]{:S(2)}) collective-permute-start(f32[2,4,16,192]{3,2,1,0:T(8,128)S(1)} %slice.170), channel_id=1, source_target_pairs={{64,0},{128,64},{192,128},{256,192},{320,256},{384,320},{448,384},... | collective-permute-start | bytes 294920 | tf_op jit(solution)/shard_map/ppermute | solution.py:14
  68.2 3.6 %collective-permute-done.10 = f32[2,4,16,192]{3,2,1,0:T(8,128)S(1)} collective-permute-done((f32[2,4,16,192]{3,2,1,0:T(8,128)S(1)}, f32[2,4,16,192]{3,2,1,0:T(8,128)S(1)}, u32[]{:S(2)}, u32[]{:S(2)}) %collective-permute-start.10) | collective-permute-done | bytes 98336 | tf_op jit(solution)/shard_map/ppermute | solution.py:14
  72.3 0.7 fusion.183
  74.0 1.9 %collective-permute-start.11 = (bf16[1,4,16,576]{3,2,1,0:T(8,128)(2,1)S(1)}, bf16[1,4,16,576]{3,2,1,0:T(8,128)(2,1)S(1)}, u32[]{:S(2)}, u32[]{:S(2)}) collective-permute-start(bf16[1,4,16,576]{3,2,1,0:T(8,128)(2,1)S(1)} %slice.121), channel_id=1, source_target_pairs={{0,64},{64,128},{128,192},{192,256},{256,320},{320,384},{384,448},... | collective-permute-start | bytes 221192 | tf_op jit(solution)/shard_map/ppermute | solution.py:213
  76.0 4.6 %collective-permute-start.12 = (bf16[1,4,16,576]{3,2,1,0:T(8,128)(2,1)S(1)}, bf16[1,4,16,576]{3,2,1,0:T(8,128)(2,1)S(1)}, u32[]{:S(2)}, u32[]{:S(2)}) collective-permute-start(bf16[1,4,16,576]{3,2,1,0:T(8,128)(2,1)S(1)} %slice.122), channel_id=1, source_target_pairs={{0,704},{64,0},{128,64},{192,128},{256,192},{320,256},{384,320},{4... | collective-permute-start | bytes 221192 | tf_op jit(solution)/shard_map/ppermute | solution.py:214
  81.3 0.7 collective-permute-done.12
  84.8 8.9 %collective-permute-start.13 = (f32[32,6,432]{2,1,0:T(8,128)S(1)}, f32[32,6,432]{2,1,0:T(8,128)S(1)}, u32[]{:S(2)}, u32[]{:S(2)}) collective-permute-start(f32[32,6,432]{2,1,0:T(8,128)S(1)} %dynamic-slice_bitcast_fusion), channel_id=1, source_target_pairs={{0,1},{1,0},{2,3},{3,2},{4,5},{5,4},{6,7},{7,6},{8,9},{9,8},{10,11... | collective-permute-start | bytes 995336 | tf_op jit(solution)/shard_map/ppermute | solution.py:233
  93.7 1.5 %collective-permute-done.13 = f32[32,6,432]{2,1,0:T(8,128)S(1)} collective-permute-done((f32[32,6,432]{2,1,0:T(8,128)S(1)}, f32[32,6,432]{2,1,0:T(8,128)S(1)}, u32[]{:S(2)}, u32[]{:S(2)}) %collective-permute-start.13) | collective-permute-done | bytes 331808 | tf_op jit(solution)/shard_map/ppermute | solution.py:233
  95.2 0.8 fusion.5
  96.0 9.7 %all-to-all-start = ((bf16[32,6,432]{2,1,0:T(8,128)(2,1)}), bf16[32,6,432]{2,1,0:T(8,128)(2,1)S(1)}, u32[]{:S(2)}, u32[]{:S(2)}) async-start(bf16[32,6,432]{2,1,0:T(8,128)(2,1)} %fusion.5), calls=%async_computation | async-start | bytes 524288 | tf_op jit(solution)/shard_map/all_to_all | solution.py:234
  105.6 0.7 copy.45
  106.3 10.9 %all-to-all-done = bf16[32,6,432]{2,1,0:T(8,128)(2,1)S(1)} async-done(((bf16[32,6,432]{2,1,0:T(8,128)(2,1)}), bf16[32,6,432]{2,1,0:T(8,128)(2,1)S(1)}, u32[]{:S(2)}, u32[]{:S(2)}) %all-to-all-start) | async-done | bytes 165920 | tf_op jit(solution)/shard_map/all_to_all | solution.py:234
  (147 shorter events, 16.7 us)
Async XLA Ops:
  1.6 24.2 %collective-permute-start = (bf16[2,4,16,576]{3,2,1,0:T(8,128)(2,1)S(1)}, bf16[2,4,16,576]{3,2,1,0:T(8,128)(2,1)S(1)}, u32[]{:S(2)}, u32[]{:S(2)}) collective-permute-start(bf16[2,4,16,576]{3,2,1,0:T(8,128)(2,1)S(1)} %pad_maximum_fusion), channel_id=1, source_target_pairs={{0,64},{64,128},{128,192},{192,256},{256,320},{320,384},{384,448},... | collective-permute-start | bytes 442376 | tf_op jit(solution)/shard_map/ppermute | solution.py:76
  6.5 19.3 %collective-permute-start.2 = (bf16[2,4,16,576]{3,2,1,0:T(8,128)(2,1)S(1)}, bf16[2,4,16,576]{3,2,1,0:T(8,128)(2,1)S(1)}, u32[]{:S(2)}, u32[]{:S(2)}) collective-permute-start(bf16[2,4,16,576]{3,2,1,0:T(8,128)(2,1)S(1)} %pad_maximum_fusion), channel_id=1, source_target_pairs={{0,704},{64,0},{128,64},{192,128},{256,192},{320,256},{384,320},{4... | collective-permute-start | bytes 442376 | tf_op jit(solution)/shard_map/ppermute | solution.py:179
  21.1 2.2 %copy-start.5 = (s32[1,24]{1,0:T(1,128)S(1)}, s32[1,24]{1,0:T(1,128)}, u32[]{:S(2)}) copy-start(s32[1,24]{1,0:T(1,128)} %param.6) | copy-start | bytes 292
  21.1 4.9 %copy-start.1 = (bf16[1,2,4,16,192]{4,3,2,1,0:T(8,128)(2,1)S(1)}, bf16[1,2,4,16,192]{4,3,2,1,0:T(8,128)(2,1)}, u32[]{:S(2)}) copy-start(bf16[1,2,4,16,192]{4,3,2,1,0:T(8,128)(2,1)} %param.5) | copy-start | bytes 147460
  21.1 4.9 %copy-start.3 = (f32[192]{0:T(256)S(1)}, f32[192]{0:T(256)}, u32[]{:S(2)}) copy-start(f32[192]{0:T(256)} %param.7) | copy-start | bytes 2308
  22.3 4.3 %copy-start.2 = (bf16[1,2,4,16,384]{4,3,2,1,0:T(8,128)(2,1)S(1)}, bf16[1,2,4,16,384]{4,3,2,1,0:T(8,128)(2,1)}, u32[]{:S(2)}) copy-start(bf16[1,2,4,16,384]{4,3,2,1,0:T(8,128)(2,1)} %param.9) | copy-start | bytes 294916
  26.2 17.9 %copy-start = (bf16[5184,384]{1,0:T(8,128)(2,1)S(1)}, bf16[5184,384]{1,0:T(8,128)(2,1)}, u32[]{:S(2)}) copy-start(bf16[5184,384]{1,0:T(8,128)(2,1)} %param.8) | copy-start | bytes 11943940
  26.2 17.9 %copy-start.4 = (pred[16,3]{0,1:T(4,128)(4,1)S(1)}, pred[16,3]{0,1:T(4,128)(4,1)}, u32[]{:S(2)}) copy-start(pred[16,3]{0,1:T(4,128)(4,1)} %constant.660) | copy-start | bytes 148
  27.0 8.0 %collective-permute-start.1 = (bf16[2,4,16,576]{3,2,1,0:T(8,128)(2,1)S(1)}, bf16[2,4,16,576]{3,2,1,0:T(8,128)(2,1)S(1)}, u32[]{:S(2)}, u32[]{:S(2)}) collective-permute-start(bf16[2,4,16,576]{3,2,1,0:T(8,128)(2,1)S(1)} %collective-permute-done), channel_id=1, source_target_pairs={{0,64},{64,128},{128,192},{192,256},{256,320},{320,384},{384,448},... | collective-permute-start | bytes 442376 | tf_op jit(solution)/shard_map/ppermute | solution.py:217
  29.1 6.8 %collective-permute-start.3 = (bf16[2,4,16,576]{3,2,1,0:T(8,128)(2,1)S(1)}, bf16[2,4,16,576]{3,2,1,0:T(8,128)(2,1)S(1)}, u32[]{:S(2)}, u32[]{:S(2)}) collective-permute-start(bf16[2,4,16,576]{3,2,1,0:T(8,128)(2,1)S(1)} %collective-permute-done.2), channel_id=1, source_target_pairs={{0,704},{64,0},{128,64},{192,128},{256,192},{320,256},{384,320},{4... | collective-permute-start | bytes 442376 | tf_op jit(solution)/shard_map/ppermute | solution.py:220
  35.9 11.7 %collective-permute-start.4 = (bf16[2,4,16,576]{3,2,1,0:T(8,128)(2,1)S(1)}, bf16[2,4,16,576]{3,2,1,0:T(8,128)(2,1)S(1)}, u32[]{:S(2)}, u32[]{:S(2)}) collective-permute-start(bf16[2,4,16,576]{3,2,1,0:T(8,128)(2,1)S(1)} %collective-permute-done.1), channel_id=1, source_target_pairs={{0,64},{64,128},{128,192},{192,256},{256,320},{320,384},{384,448},... | collective-permute-start | bytes 442376 | tf_op jit(solution)/shard_map/ppermute | solution.py:217
  37.8 8.0 %collective-permute-start.5 = (bf16[2,4,16,576]{3,2,1,0:T(8,128)(2,1)S(1)}, bf16[2,4,16,576]{3,2,1,0:T(8,128)(2,1)S(1)}, u32[]{:S(2)}, u32[]{:S(2)}) collective-permute-start(bf16[2,4,16,576]{3,2,1,0:T(8,128)(2,1)S(1)} %collective-permute-done.3), channel_id=1, source_target_pairs={{0,704},{64,0},{128,64},{192,128},{256,192},{320,256},{384,320},{4... | collective-permute-start | bytes 442376 | tf_op jit(solution)/shard_map/ppermute | solution.py:220
  47.6 7.4 %collective-permute-start.6 = (bf16[2,4,16,576]{3,2,1,0:T(8,128)(2,1)S(1)}, bf16[2,4,16,576]{3,2,1,0:T(8,128)(2,1)S(1)}, u32[]{:S(2)}, u32[]{:S(2)}) collective-permute-start(bf16[2,4,16,576]{3,2,1,0:T(8,128)(2,1)S(1)} %collective-permute-done.4), channel_id=1, source_target_pairs={{0,64},{64,128},{128,192},{192,256},{256,320},{320,384},{384,448},... | collective-permute-start | bytes 442376 | tf_op jit(solution)/shard_map/ppermute | solution.py:217
  49.6 6.8 %collective-permute-start.7 = (bf16[2,4,16,576]{3,2,1,0:T(8,128)(2,1)S(1)}, bf16[2,4,16,576]{3,2,1,0:T(8,128)(2,1)S(1)}, u32[]{:S(2)}, u32[]{:S(2)}) collective-permute-start(bf16[2,4,16,576]{3,2,1,0:T(8,128)(2,1)S(1)} %collective-permute-done.5), channel_id=1, source_target_pairs={{0,704},{64,0},{128,64},{192,128},{256,192},{320,256},{384,320},{4... | collective-permute-start | bytes 442376 | tf_op jit(solution)/shard_map/ppermute | solution.py:220
  56.4 11.7 %collective-permute-start.8 = (bf16[2,4,16,576]{3,2,1,0:T(8,128)(2,1)S(1)}, bf16[2,4,16,576]{3,2,1,0:T(8,128)(2,1)S(1)}, u32[]{:S(2)}, u32[]{:S(2)}) collective-permute-start(bf16[2,4,16,576]{3,2,1,0:T(8,128)(2,1)S(1)} %collective-permute-done.6), channel_id=1, source_target_pairs={{0,64},{64,128},{128,192},{192,256},{256,320},{320,384},{384,448},... | collective-permute-start | bytes 442376 | tf_op jit(solution)/shard_map/ppermute | solution.py:217
  58.3 9.7 %collective-permute-start.9 = (bf16[2,4,16,576]{3,2,1,0:T(8,128)(2,1)S(1)}, bf16[2,4,16,576]{3,2,1,0:T(8,128)(2,1)S(1)}, u32[]{:S(2)}, u32[]{:S(2)}) collective-permute-start(bf16[2,4,16,576]{3,2,1,0:T(8,128)(2,1)S(1)} %collective-permute-done.7), channel_id=1, source_target_pairs={{0,704},{64,0},{128,64},{192,128},{256,192},{320,256},{384,320},{4... | collective-permute-start | bytes 442376 | tf_op jit(solution)/shard_map/ppermute | solution.py:220
  66.2 5.7 %collective-permute-start.10 = (f32[2,4,16,192]{3,2,1,0:T(8,128)S(1)}, f32[2,4,16,192]{3,2,1,0:T(8,128)S(1)}, u32[]{:S(2)}, u32[]{:S(2)}) collective-permute-start(f32[2,4,16,192]{3,2,1,0:T(8,128)S(1)} %slice.170), channel_id=1, source_target_pairs={{64,0},{128,64},{192,128},{256,192},{320,256},{384,320},{448,384},... | collective-permute-start | bytes 294920 | tf_op jit(solution)/shard_map/ppermute | solution.py:14
  74.0 7.3 %collective-permute-start.11 = (bf16[1,4,16,576]{3,2,1,0:T(8,128)(2,1)S(1)}, bf16[1,4,16,576]{3,2,1,0:T(8,128)(2,1)S(1)}, u32[]{:S(2)}, u32[]{:S(2)}) collective-permute-start(bf16[1,4,16,576]{3,2,1,0:T(8,128)(2,1)S(1)} %slice.121), channel_id=1, source_target_pairs={{0,64},{64,128},{128,192},{192,256},{256,320},{320,384},{384,448},... | collective-permute-start | bytes 221192 | tf_op jit(solution)/shard_map/ppermute | solution.py:213
  76.0 6.0 %collective-permute-start.12 = (bf16[1,4,16,576]{3,2,1,0:T(8,128)(2,1)S(1)}, bf16[1,4,16,576]{3,2,1,0:T(8,128)(2,1)S(1)}, u32[]{:S(2)}, u32[]{:S(2)}) collective-permute-start(bf16[1,4,16,576]{3,2,1,0:T(8,128)(2,1)S(1)} %slice.122), channel_id=1, source_target_pairs={{0,704},{64,0},{128,64},{192,128},{256,192},{320,256},{384,320},{4... | collective-permute-start | bytes 221192 | tf_op jit(solution)/shard_map/ppermute | solution.py:214
  84.8 10.4 %collective-permute-start.13 = (f32[32,6,432]{2,1,0:T(8,128)S(1)}, f32[32,6,432]{2,1,0:T(8,128)S(1)}, u32[]{:S(2)}, u32[]{:S(2)}) collective-permute-start(f32[32,6,432]{2,1,0:T(8,128)S(1)} %dynamic-slice_bitcast_fusion), channel_id=1, source_target_pairs={{0,1},{1,0},{2,3},{3,2},{4,5},{5,4},{6,7},{7,6},{8,9},{9,8},{10,11... | collective-permute-start | bytes 995336 | tf_op jit(solution)/shard_map/ppermute | solution.py:233
  96.0 21.2 %all-to-all-start = ((bf16[32,6,432]{2,1,0:T(8,128)(2,1)}), bf16[32,6,432]{2,1,0:T(8,128)(2,1)S(1)}, u32[]{:S(2)}, u32[]{:S(2)}) async-start(bf16[32,6,432]{2,1,0:T(8,128)(2,1)} %fusion.5), calls=%async_computation | async-start | bytes 524288 | tf_op jit(solution)/shard_map/all_to_all | solution.py:234
